TPU v7x, 32 devices: a whole 2x2x4 slice. The times are simulated.
32 devices in a mesh: snp: 8 (over z, y), samp: 4 (over x, core).
Axes of the slice: x: 2, y: 2, z: 4, core: 2. Of those that a mesh axis runs over, the one named last changes fastest.
Arguments:
- dosages: float32 [7168, 8192], P('snp', 'samp'), may hold values from 0 to 2, as said below
Outputs:
- linkage: float32 [7168, 3584], P('snp', 'samp')
Inputs may be any that keep to these rules, and one draw needn't show every extreme that they name: `dosages`: continuous imputed dosage of a SNP in a sample.
All inputs are finite; a program needn't handle non-finite values.
Results may differ from a plain program's by a relative error of at most 0.00096.
Values may be sent and summed in bfloat16 or wider, within the bound.
No kernel may reach another device: no remote copies, remote signals or barrier semaphores. Data moves between devices by JAX's collectives and lax.ppermute only.
A program may use at most 128 MiB of HBM per device.

v0:
```python
import jax
import jax.numpy as jnp
from jax import lax
from jax.sharding import PartitionSpec as P

BAND = 3
CHUNKS = 8


def moved(value, pairs):
    return lax.ppermute(value, "snp", pairs)


def standardize(values, sums, squares, total):
    mean = sums / total
    variance = squares / total - mean * mean
    return ((values - mean[:, None]) * lax.rsqrt(variance + 1e-05)[:, None]).astype(jnp.bfloat16)


def local_moments(values):
    return (jnp.sum(values, axis=1), jnp.sum(values * values, axis=1))


def joined(parts):
    parts = [p for p in parts if p is not None]
    return parts[0] if len(parts) == 1 else jnp.concatenate(parts, axis=0)


def local(dosages):
    total = dosages.shape[1] * lax.axis_size("samp")
    count = lax.axis_size("snp")
    groups = lax.axis_size("samp")
    sums, squares = local_moments(dosages)
    sums, squares = lax.psum((sums, squares), "samp")
    own_block = standardize(dosages, sums, squares, total)
    rows = own_block.shape[0]
    step = rows // CHUNKS
    pieces = [own_block[c * step:(c + 1) * step] for c in range(CHUNKS)]

    odd = list(range(1, count, 2))
    even = list(range(0, count, 2))
    z_down = [(s, s - 2) for s in range(2, count)]
    odd_to_even = [(s, s - 1) for s in odd]
    even_to_odd = [(s, s + 1) for s in even if s + 1 < count]

    me = lax.axis_index("samp")
    order = jnp.bitwise_xor(me, jnp.arange(BAND + 1, dtype=me.dtype))
    partner = [(j, j ^ 1) for j in range(groups)]
    across = [(j, j ^ 2) for j in range(groups)]

    names = ("two", "one_even", "one_odd", "three_even", "three_odd", "tiles", "first", "results")
    state = {name: [None] * CHUNKS for name in names}

    def finish(c):
        blocks = jnp.stack([
            pieces[c],
            state["one_even"][c] + state["one_odd"][c],
            state["two"][c],
            state["three_even"][c] + state["three_odd"][c],
        ])
        picked = jnp.take(blocks, order, axis=0).reshape((BAND + 1) * step, -1)
        state["tiles"][c] = jnp.einsum("ab,cb->ac", own_block, picked, preferred_element_type=jnp.float32)

    def tile(c, k):
        return state["tiles"][c][:, k * step:(k + 1) * step]

    for t in range(CHUNKS + 4):
        new = t if t < CHUNKS else None
        second = t - 1 if 0 <= t - 1 < CHUNKS else None
        third = t - 2 if 0 <= t - 2 < CHUNKS else None
        if new is not None or third is not None:
            sent = moved(joined([pieces[new] if new is not None else None,
                                 state["one_odd"][third] if third is not None else None]), z_down)
            if new is not None:
                state["two"][new] = sent[:step]
            if third is not None:
                state["three_odd"][third] = sent[-step:]
        if new is not None or second is not None:
            sent = moved(joined([pieces[new] if new is not None else None,
                                 state["two"][second] if second is not None else None]), odd_to_even)
            if new is not None:
                state["one_even"][new] = sent[:step]
            if second is not None:
                state["three_even"][second] = sent[-step:]
        if second is not None:
            state["one_odd"][second] = moved(state["two"][second], even_to_odd)
        if 0 <= t - 3 < CHUNKS:
            c = t - 3
            finish(c)
            payload = jnp.concatenate([tile(c, 1), tile(c, 3)], axis=1)
            state["first"][c] = lax.ppermute(payload, "samp", partner)
        if 0 <= t - 4 < CHUNKS:
            c = t - 4
            payload = tile(c, 2) + state["first"][c][:, step:]
            last = lax.ppermute(payload, "samp", across)
            state["results"][c] = tile(c, 0) + state["first"][c][:, :step] + last
        flat, tree = jax.tree.flatten(state)
        following = pieces[t + 1] if t + 1 < CHUNKS else own_block[:8]
        flat, following = lax.optimization_barrier((flat, following))
        state = {k: list(v) for k, v in jax.tree.unflatten(tree, flat).items()}
        if t + 1 < CHUNKS:
            pieces[t + 1] = following
    summed = jnp.concatenate(state["results"], axis=1)
    return summed / total


def solution(mesh):
    return jax.shard_map(
        local,
        mesh=mesh,
        in_specs=(P("snp", "samp"),),
        out_specs=P("snp", "samp"),
        check_vma=False,
    )
```

profile of v0, /device:TPU:0, one launch (start us, length us, event | category | flops | bytes accessed | tf_op | source)
XLA Modules:
  0.0 327.7 jit_solution(9216880892603769728)
XLA Ops:
  0.0 4.0 %fusion = (f32[896]{0:T(1024)S(1)}, f32[896]{0:T(1024)S(1)}) fusion(f32[896,2048]{1,0:T(8,128)} %param.3), kind=kLoop, calls=%fused_computation.94 | loop fusion | flops 5503232 | bytes 7347200 | tf_op jit(solution)/shard_map/reduce_sum | solution.py:21
  4.0 8.5 %all-reduce = (f32[896]{0:T(1024)S(1)}, f32[896]{0:T(1024)S(1)}) all-reduce(f32[896]{0:T(1024)S(1)} %get-tuple-element.301, f32[896]{0:T(1024)S(1)} %get-tuple-element.300), channel_id=1, replica_groups=mesh['snp'=8,'samp'=4] {'samp'}, use_global_device_ids=true, to_apply=%region_3.0 | all-reduce | flops 1792 | bytes 14336 | tf_op jit(solution)/shard_map/psum | solution.py:34
  12.5 3.8 %multiply_convert_fusion = bf16[896,2048]{1,0:T(8,128)(2,1)S(1)} fusion(f32[896,2048]{1,0:T(8,128)} %param.3, f32[896]{0:T(1024)S(1)} %get-tuple-element.368, f32[896]{0:T(1024)S(1)} %get-tuple-element.367), kind=kLoop, calls=%fused_computation.8 | loop fusion | flops 5505024 | bytes 11017216 | tf_op jit(solution)/shard_map/convert_element_type | solution.py:17
  21.4 10.1 %collective-permute-done = bf16[112,2048]{1,0:T(8,128)(2,1)S(1)} collective-permute-done((bf16[112,2048]{1,0:T(8,128)(2,1)S(1)}, bf16[112,2048]{1,0:T(8,128)(2,1)S(1)}, u32[]{:S(2)}, u32[]{:S(2)}) %collective-permute-start) | collective-permute-done | bytes 458784 | tf_op jit(solution)/shard_map/ppermute | solution.py:11
  34.2 4.6 %collective-permute-start.3 = (bf16[112,2048]{1,0:T(8,128)(2,1)S(1)}, bf16[112,2048]{1,0:T(8,128)(2,1)S(1)}, u32[]{:S(2)}, u32[]{:S(2)}) collective-permute-start(bf16[112,2048]{1,0:T(8,128)(2,1)S(1)} %collective-permute-done.1), channel_id=1, source_target_pairs={{0,4},{8,12},{16,20},{24,28},{1,5},{9,13},{17,21},{25,29},{2,6},{1... | collective-permute-start | bytes 1376264 | tf_op jit(solution)/shard_map/ppermute | solution.py:11
  40.2 14.4 %collective-permute-done.2 = bf16[224,2048]{1,0:T(8,128)(2,1)S(1)} collective-permute-done((bf16[224,2048]{1,0:T(8,128)(2,1)S(1)}, bf16[224,2048]{1,0:T(8,128)(2,1)S(1)}, u32[]{:S(2)}, u32[]{:S(2)}) %collective-permute-start.2) | collective-permute-done | bytes 917536 | tf_op jit(solution)/shard_map/ppermute | solution.py:11
  59.6 5.5 %collective-permute-start.6 = (bf16[112,2048]{1,0:T(8,128)(2,1)S(1)}, bf16[112,2048]{1,0:T(8,128)(2,1)S(1)}, u32[]{:S(2)}, u32[]{:S(2)}) collective-permute-start(bf16[112,2048]{1,0:T(8,128)(2,1)S(1)} %collective-permute-done.4), channel_id=1, source_target_pairs={{0,4},{8,12},{16,20},{24,28},{1,5},{9,13},{17,21},{25,29},{2,6},{1... | collective-permute-start | bytes 1376264 | tf_op jit(solution)/shard_map/ppermute | solution.py:11
  65.1 13.2 %collective-permute-done.7 = bf16[224,2048]{1,0:T(8,128)(2,1)} collective-permute-done((bf16[224,2048]{1,0:T(8,128)(2,1)}, bf16[224,2048]{1,0:T(8,128)(2,1)}, u32[]{:S(2)}, u32[]{:S(2)}) %collective-permute-start.7) | collective-permute-done | bytes 917536 | tf_op jit(solution)/shard_map/ppermute | solution.py:11
  79.5 2.2 fusion.21
  81.7 2.4 collective-permute-start.10
  95.4 10.9 %collective-permute-done.11 = bf16[224,2048]{1,0:T(8,128)(2,1)} collective-permute-done((bf16[224,2048]{1,0:T(8,128)(2,1)}, bf16[224,2048]{1,0:T(8,128)(2,1)}, u32[]{:S(2)}, u32[]{:S(2)}) %collective-permute-start.11) | collective-permute-done | bytes 917536 | tf_op jit(solution)/shard_map/ppermute | solution.py:11
  107.5 2.2 fusion.19
  110.7 5.4 %collective-permute-start.15 = (f32[896,112]{0,1:T(8,128)}, f32[896,112]{0,1:T(8,128)}, u32[]{:S(2)}, u32[]{:S(2)}) collective-permute-start(f32[896,112]{0,1:T(8,128)} %slice_add_fusion.7), channel_id=1, source_target_pairs={{0,2},{1,3},{2,0},{3,1},{4,6},{5,7},{6,4},{7,5},{8,10},{9,11},{10,... | collective-permute-start | bytes 1204232 | tf_op jit(solution)/shard_map/ppermute | solution.py:95
  118.1 2.5 pad_maximum_fusion.12
  134.0 7.3 %collective-permute-done.16 = bf16[224,2048]{1,0:T(8,128)(2,1)} collective-permute-done((bf16[224,2048]{1,0:T(8,128)(2,1)}, bf16[224,2048]{1,0:T(8,128)(2,1)}, u32[]{:S(2)}, u32[]{:S(2)}) %collective-permute-start.16) | collective-permute-done | bytes 917536 | tf_op jit(solution)/shard_map/ppermute | solution.py:11
  142.6 2.3 fusion.17
  149.0 2.5 pad_maximum_fusion.14
  166.1 6.8 %collective-permute-done.21 = bf16[224,2048]{1,0:T(8,128)(2,1)} collective-permute-done((bf16[224,2048]{1,0:T(8,128)(2,1)}, bf16[224,2048]{1,0:T(8,128)(2,1)}, u32[]{:S(2)}, u32[]{:S(2)}) %collective-permute-start.21) | collective-permute-done | bytes 917536 | tf_op jit(solution)/shard_map/ppermute | solution.py:11
  174.1 2.2 fusion.15
  181.1 2.5 pad_maximum_fusion.16
  198.1 7.2 %collective-permute-done.26 = bf16[224,2048]{1,0:T(8,128)(2,1)} collective-permute-done((bf16[224,2048]{1,0:T(8,128)(2,1)}, bf16[224,2048]{1,0:T(8,128)(2,1)}, u32[]{:S(2)}, u32[]{:S(2)}) %collective-permute-start.26) | collective-permute-done | bytes 917536 | tf_op jit(solution)/shard_map/ppermute | solution.py:11
  206.5 2.2 fusion.13
  213.1 2.5 pad_maximum_fusion.18
  230.2 6.8 %collective-permute-done.31 = bf16[224,2048]{1,0:T(8,128)(2,1)} collective-permute-done((bf16[224,2048]{1,0:T(8,128)(2,1)}, bf16[224,2048]{1,0:T(8,128)(2,1)}, u32[]{:S(2)}, u32[]{:S(2)}) %collective-permute-start.31) | collective-permute-done | bytes 917536 | tf_op jit(solution)/shard_map/ppermute | solution.py:11
  239.1 2.2 fusion.11
  257.4 4.4 %collective-permute-done.34 = f32[896,112]{0,1:T(8,128)S(1)} collective-permute-done((f32[896,112]{0,1:T(8,128)S(1)}, f32[896,112]{0,1:T(8,128)S(1)}, u32[]{:S(2)}, u32[]{:S(2)}) %collective-permute-start.34) | collective-permute-done | bytes 401440 | tf_op jit(solution)/shard_map/ppermute | solution.py:95
  263.3 4.1 %collective-permute-done.35 = bf16[112,2048]{1,0:T(8,128)(2,1)S(1)} collective-permute-done((bf16[112,2048]{1,0:T(8,128)(2,1)S(1)}, bf16[112,2048]{1,0:T(8,128)(2,1)S(1)}, u32[]{:S(2)}, u32[]{:S(2)}) %collective-permute-start.35) | collective-permute-done | bytes 458784 | tf_op jit(solution)/shard_map/ppermute | solution.py:11
  281.9 7.6 %collective-permute-done.38 = f32[896,112]{0,1:T(8,128)S(1)} collective-permute-done((f32[896,112]{0,1:T(8,128)S(1)}, f32[896,112]{0,1:T(8,128)S(1)}, u32[]{:S(2)}, u32[]{:S(2)}) %collective-permute-start.38) | collective-permute-done | bytes 401440 | tf_op jit(solution)/shard_map/ppermute | solution.py:95
  290.4 3.4 %collective-permute-done.39 = bf16[112,2048]{1,0:T(8,128)(2,1)S(1)} collective-permute-done((bf16[112,2048]{1,0:T(8,128)(2,1)S(1)}, bf16[112,2048]{1,0:T(8,128)(2,1)S(1)}, u32[]{:S(2)}, u32[]{:S(2)}) %collective-permute-start.39) | collective-permute-done | bytes 458784 | tf_op jit(solution)/shard_map/ppermute | solution.py:11
  304.8 8.8 %collective-permute-done.41 = f32[896,112]{0,1:T(8,128)S(1)} collective-permute-done((f32[896,112]{0,1:T(8,128)S(1)}, f32[896,112]{0,1:T(8,128)S(1)}, u32[]{:S(2)}, u32[]{:S(2)}) %collective-permute-start.41) | collective-permute-done | bytes 401440 | tf_op jit(solution)/shard_map/ppermute | solution.py:95
  315.3 7.9 %collective-permute-done.42 = f32[896,112]{0,1:T(8,128)S(1)} collective-permute-done((f32[896,112]{0,1:T(8,128)S(1)}, f32[896,112]{0,1:T(8,128)S(1)}, u32[]{:S(2)}, u32[]{:S(2)}) %collective-permute-start.42) | collective-permute-done | bytes 401440 | tf_op jit(solution)/shard_map/ppermute | solution.py:95
  324.8 3.0 copy.2
  (331 shorter events, 152.7 us)
Async XLA Ops:
  32.9 21.6 %collective-permute-start.2 = (bf16[224,2048]{1,0:T(8,128)(2,1)S(1)}, bf16[224,2048]{1,0:T(8,128)(2,1)S(1)}, u32[]{:S(2)}, u32[]{:S(2)}) collective-permute-start(bf16[224,2048]{1,0:T(8,128)(2,1)S(1)} %pad_maximum_fusion.20), channel_id=1, source_target_pairs={{4,0},{12,8},{20,16},{28,24},{5,1},{13,9},{21,17},{29,25},{6,2},{1... | collective-permute-start | bytes 2752520 | tf_op jit(solution)/shard_map/ppermute | solution.py:11
  34.2 21.2 %collective-permute-start.3 = (bf16[112,2048]{1,0:T(8,128)(2,1)S(1)}, bf16[112,2048]{1,0:T(8,128)(2,1)S(1)}, u32[]{:S(2)}, u32[]{:S(2)}) collective-permute-start(bf16[112,2048]{1,0:T(8,128)(2,1)S(1)} %collective-permute-done.1), channel_id=1, source_target_pairs={{0,4},{8,12},{16,20},{24,28},{1,5},{9,13},{17,21},{25,29},{2,6},{1... | collective-permute-start | bytes 1376264 | tf_op jit(solution)/shard_map/ppermute | solution.py:11
  38.9 16.6 %collective-permute-start.4 = (bf16[112,2048]{1,0:T(8,128)(2,1)S(1)}, bf16[112,2048]{1,0:T(8,128)(2,1)S(1)}, u32[]{:S(2)}, u32[]{:S(2)}) collective-permute-start(bf16[112,2048]{1,0:T(8,128)(2,1)S(1)} %get-tuple-element.154), channel_id=1, source_target_pairs={{8,0},{12,4},{16,8},{20,12},{24,16},{28,20},{9,1},{13,5},{17,9},{2... | collective-permute-start | bytes 1376264 | tf_op jit(solution)/shard_map/ppermute | solution.py:11
  57.0 21.3 %collective-permute-start.7 = (bf16[224,2048]{1,0:T(8,128)(2,1)}, bf16[224,2048]{1,0:T(8,128)(2,1)}, u32[]{:S(2)}, u32[]{:S(2)}) collective-permute-start(bf16[224,2048]{1,0:T(8,128)(2,1)} %get-tuple-element.365), channel_id=1, source_target_pairs={{8,0},{12,4},{16,8},{20,12},{24,16},{28,20},{9,1},{13,5},{17,9},{2... | collective-permute-start | bytes 2752520 | tf_op jit(solution)/shard_map/ppermute | solution.py:11
  58.2 21.3 %collective-permute-start.5 = (bf16[224,2048]{1,0:T(8,128)(2,1)}, bf16[224,2048]{1,0:T(8,128)(2,1)}, u32[]{:S(2)}, u32[]{:S(2)}) collective-permute-start(bf16[224,2048]{1,0:T(8,128)(2,1)} %get-tuple-element.366), channel_id=1, source_target_pairs={{4,0},{12,8},{20,16},{28,24},{5,1},{13,9},{21,17},{29,25},{6,2},{1... | collective-permute-start | bytes 2752520 | tf_op jit(solution)/shard_map/ppermute | solution.py:11
  59.6 22.1 %collective-permute-start.6 = (bf16[112,2048]{1,0:T(8,128)(2,1)S(1)}, bf16[112,2048]{1,0:T(8,128)(2,1)S(1)}, u32[]{:S(2)}, u32[]{:S(2)}) collective-permute-start(bf16[112,2048]{1,0:T(8,128)(2,1)S(1)} %collective-permute-done.4), channel_id=1, source_target_pairs={{0,4},{8,12},{16,20},{24,28},{1,5},{9,13},{17,21},{25,29},{2,6},{1... | collective-permute-start | bytes 1376264 | tf_op jit(solution)/shard_map/ppermute | solution.py:11
  81.7 28.0 %collective-permute-start.10 = (bf16[112,2048]{1,0:T(8,128)(2,1)S(1)}, bf16[112,2048]{1,0:T(8,128)(2,1)}, u32[]{:S(2)}, u32[]{:S(2)}) collective-permute-start(bf16[112,2048]{1,0:T(8,128)(2,1)S(1)} %get-tuple-element.192), channel_id=1, source_target_pairs={{0,4},{8,12},{16,20},{24,28},{1,5},{9,13},{17,21},{25,29},{2,6},{1... | collective-permute-start | bytes 1376264 | tf_op jit(solution)/shard_map/ppermute | solution.py:11
  85.5 20.8 %collective-permute-start.11 = (bf16[224,2048]{1,0:T(8,128)(2,1)}, bf16[224,2048]{1,0:T(8,128)(2,1)}, u32[]{:S(2)}, u32[]{:S(2)}) collective-permute-start(bf16[224,2048]{1,0:T(8,128)(2,1)} %get-tuple-element.363), channel_id=1, source_target_pairs={{8,0},{12,4},{16,8},{20,12},{24,16},{28,20},{9,1},{13,5},{17,9},{2... | collective-permute-start | bytes 2752520 | tf_op jit(solution)/shard_map/ppermute | solution.py:11
  87.0 20.6 %collective-permute-start.9 = (bf16[224,2048]{1,0:T(8,128)(2,1)}, bf16[224,2048]{1,0:T(8,128)(2,1)}, u32[]{:S(2)}, u32[]{:S(2)}) collective-permute-start(bf16[224,2048]{1,0:T(8,128)(2,1)} %get-tuple-element.364), channel_id=1, source_target_pairs={{4,0},{12,8},{20,16},{28,24},{5,1},{13,9},{21,17},{29,25},{6,2},{1... | collective-permute-start | bytes 2752520 | tf_op jit(solution)/shard_map/ppermute | solution.py:11
  95.4 14.4 %collective-permute-start.8 = (f32[896,224]{0,1:T(8,128)S(1)}, f32[896,224]{0,1:T(8,128)S(1)}, u32[]{:S(2)}, u32[]{:S(2)}) collective-permute-start(f32[896,224]{0,1:T(8,128)S(1)} %pad_maximum_fusion.21), channel_id=1, source_target_pairs={{0,1},{1,0},{2,3},{3,2},{4,5},{5,4},{6,7},{7,6},{8,9},{9,8},{10,11... | collective-permute-start | bytes 2408456 | tf_op jit(solution)/shard_map/ppermute | solution.py:91
  110.7 19.9 %collective-permute-start.15 = (f32[896,112]{0,1:T(8,128)}, f32[896,112]{0,1:T(8,128)}, u32[]{:S(2)}, u32[]{:S(2)}) collective-permute-start(f32[896,112]{0,1:T(8,128)} %slice_add_fusion.7), channel_id=1, source_target_pairs={{0,2},{1,3},{2,0},{3,1},{4,6},{5,7},{6,4},{7,5},{8,10},{9,11},{10,... | collective-permute-start | bytes 1204232 | tf_op jit(solution)/shard_map/ppermute | solution.py:95
  116.1 28.8 %collective-permute-start.14 = (bf16[112,2048]{1,0:T(8,128)(2,1)S(1)}, bf16[112,2048]{1,0:T(8,128)(2,1)}, u32[]{:S(2)}, u32[]{:S(2)}) collective-permute-start(bf16[112,2048]{1,0:T(8,128)(2,1)S(1)} %get-tuple-element.207), channel_id=1, source_target_pairs={{0,4},{8,12},{16,20},{24,28},{1,5},{9,13},{17,21},{25,29},{2,6},{1... | collective-permute-start | bytes 1376264 | tf_op jit(solution)/shard_map/ppermute | solution.py:11
  120.6 20.7 %collective-permute-start.16 = (bf16[224,2048]{1,0:T(8,128)(2,1)}, bf16[224,2048]{1,0:T(8,128)(2,1)}, u32[]{:S(2)}, u32[]{:S(2)}) collective-permute-start(bf16[224,2048]{1,0:T(8,128)(2,1)} %get-tuple-element.361), channel_id=1, source_target_pairs={{8,0},{12,4},{16,8},{20,12},{24,16},{28,20},{9,1},{13,5},{17,9},{2... | collective-permute-start | bytes 2752520 | tf_op jit(solution)/shard_map/ppermute | solution.py:11
  122.0 20.5 %collective-permute-start.13 = (bf16[224,2048]{1,0:T(8,128)(2,1)}, bf16[224,2048]{1,0:T(8,128)(2,1)}, u32[]{:S(2)}, u32[]{:S(2)}) collective-permute-start(bf16[224,2048]{1,0:T(8,128)(2,1)} %get-tuple-element.362), channel_id=1, source_target_pairs={{4,0},{12,8},{20,16},{28,24},{5,1},{13,9},{21,17},{29,25},{6,2},{1... | collective-permute-start | bytes 2752520 | tf_op jit(solution)/shard_map/ppermute | solution.py:11
  130.5 14.4 %collective-permute-start.12 = (f32[896,224]{0,1:T(8,128)S(1)}, f32[896,224]{0,1:T(8,128)S(1)}, u32[]{:S(2)}, u32[]{:S(2)}) collective-permute-start(f32[896,224]{0,1:T(8,128)S(1)} %pad_maximum_fusion.22), channel_id=1, source_target_pairs={{0,1},{1,0},{2,3},{3,2},{4,5},{5,4},{6,7},{7,6},{8,9},{9,8},{10,11... | collective-permute-start | bytes 2408456 | tf_op jit(solution)/shard_map/ppermute | solution.py:91
  146.5 16.1 %collective-permute-start.20 = (f32[896,112]{0,1:T(8,128)}, f32[896,112]{0,1:T(8,128)}, u32[]{:S(2)}, u32[]{:S(2)}) collective-permute-start(f32[896,112]{0,1:T(8,128)} %slice_add_fusion.6), channel_id=1, source_target_pairs={{0,2},{1,3},{2,0},{3,1},{4,6},{5,7},{6,4},{7,5},{8,10},{9,11},{10,... | collective-permute-start | bytes 1204232 | tf_op jit(solution)/shard_map/ppermute | solution.py:95
  147.0 29.4 %collective-permute-start.19 = (bf16[112,2048]{1,0:T(8,128)(2,1)S(1)}, bf16[112,2048]{1,0:T(8,128)(2,1)}, u32[]{:S(2)}, u32[]{:S(2)}) collective-permute-start(bf16[112,2048]{1,0:T(8,128)(2,1)S(1)} %get-tuple-element.223), channel_id=1, source_target_pairs={{0,4},{8,12},{16,20},{24,28},{1,5},{9,13},{17,21},{25,29},{2,6},{1... | collective-permute-start | bytes 1376264 | tf_op jit(solution)/shard_map/ppermute | solution.py:11
  151.5 21.4 %collective-permute-start.21 = (bf16[224,2048]{1,0:T(8,128)(2,1)}, bf16[224,2048]{1,0:T(8,128)(2,1)}, u32[]{:S(2)}, u32[]{:S(2)}) collective-permute-start(bf16[224,2048]{1,0:T(8,128)(2,1)} %get-tuple-element.359), channel_id=1, source_target_pairs={{8,0},{12,4},{16,8},{20,12},{24,16},{28,20},{9,1},{13,5},{17,9},{2... | collective-permute-start | bytes 2752520 | tf_op jit(solution)/shard_map/ppermute | solution.py:11
  153.0 21.2 %collective-permute-start.18 = (bf16[224,2048]{1,0:T(8,128)(2,1)}, bf16[224,2048]{1,0:T(8,128)(2,1)}, u32[]{:S(2)}, u32[]{:S(2)}) collective-permute-start(bf16[224,2048]{1,0:T(8,128)(2,1)} %get-tuple-element.360), channel_id=1, source_target_pairs={{4,0},{12,8},{20,16},{28,24},{5,1},{13,9},{21,17},{29,25},{6,2},{1... | collective-permute-start | bytes 2752520 | tf_op jit(solution)/shard_map/ppermute | solution.py:11
  162.6 13.8 %collective-permute-start.17 = (f32[896,224]{0,1:T(8,128)S(1)}, f32[896,224]{0,1:T(8,128)S(1)}, u32[]{:S(2)}, u32[]{:S(2)}) collective-permute-start(f32[896,224]{0,1:T(8,128)S(1)} %pad_maximum_fusion.23), channel_id=1, source_target_pairs={{0,1},{1,0},{2,3},{3,2},{4,5},{5,4},{6,7},{7,6},{8,9},{9,8},{10,11... | collective-permute-start | bytes 2408456 | tf_op jit(solution)/shard_map/ppermute | solution.py:91
  177.4 17.1 %collective-permute-start.25 = (f32[896,112]{0,1:T(8,128)}, f32[896,112]{0,1:T(8,128)}, u32[]{:S(2)}, u32[]{:S(2)}) collective-permute-start(f32[896,112]{0,1:T(8,128)} %slice_add_fusion.5), channel_id=1, source_target_pairs={{0,2},{1,3},{2,0},{3,1},{4,6},{5,7},{6,4},{7,5},{8,10},{9,11},{10,... | collective-permute-start | bytes 1204232 | tf_op jit(solution)/shard_map/ppermute | solution.py:95
  179.1 29.7 %collective-permute-start.24 = (bf16[112,2048]{1,0:T(8,128)(2,1)S(1)}, bf16[112,2048]{1,0:T(8,128)(2,1)}, u32[]{:S(2)}, u32[]{:S(2)}) collective-permute-start(bf16[112,2048]{1,0:T(8,128)(2,1)S(1)} %get-tuple-element.240), channel_id=1, source_target_pairs={{0,4},{8,12},{16,20},{24,28},{1,5},{9,13},{17,21},{25,29},{2,6},{1... | collective-permute-start | bytes 1376264 | tf_op jit(solution)/shard_map/ppermute | solution.py:11
  183.6 21.7 %collective-permute-start.26 = (bf16[224,2048]{1,0:T(8,128)(2,1)}, bf16[224,2048]{1,0:T(8,128)(2,1)}, u32[]{:S(2)}, u32[]{:S(2)}) collective-permute-start(bf16[224,2048]{1,0:T(8,128)(2,1)} %get-tuple-element.357), channel_id=1, source_target_pairs={{8,0},{12,4},{16,8},{20,12},{24,16},{28,20},{9,1},{13,5},{17,9},{2... | collective-permute-start | bytes 2752520 | tf_op jit(solution)/shard_map/ppermute | solution.py:11
  185.0 21.5 %collective-permute-start.23 = (bf16[224,2048]{1,0:T(8,128)(2,1)}, bf16[224,2048]{1,0:T(8,128)(2,1)}, u32[]{:S(2)}, u32[]{:S(2)}) collective-permute-start(bf16[224,2048]{1,0:T(8,128)(2,1)} %get-tuple-element.358), channel_id=1, source_target_pairs={{4,0},{12,8},{20,16},{28,24},{5,1},{13,9},{21,17},{29,25},{6,2},{1... | collective-permute-start | bytes 2752520 | tf_op jit(solution)/shard_map/ppermute | solution.py:11
  194.5 14.3 %collective-permute-start.22 = (f32[896,224]{0,1:T(8,128)S(1)}, f32[896,224]{0,1:T(8,128)S(1)}, u32[]{:S(2)}, u32[]{:S(2)}) collective-permute-start(f32[896,224]{0,1:T(8,128)S(1)} %pad_maximum_fusion.24), channel_id=1, source_target_pairs={{0,1},{1,0},{2,3},{3,2},{4,5},{5,4},{6,7},{7,6},{8,9},{9,8},{10,11... | collective-permute-start | bytes 2408456 | tf_op jit(solution)/shard_map/ppermute | solution.py:91
  210.5 16.3 %collective-permute-start.30 = (f32[896,112]{0,1:T(8,128)}, f32[896,112]{0,1:T(8,128)}, u32[]{:S(2)}, u32[]{:S(2)}) collective-permute-start(f32[896,112]{0,1:T(8,128)} %slice_add_fusion.4), channel_id=1, source_target_pairs={{0,2},{1,3},{2,0},{3,1},{4,6},{5,7},{6,4},{7,5},{8,10},{9,11},{10,... | collective-permute-start | bytes 1204232 | tf_op jit(solution)/shard_map/ppermute | solution.py:95
  211.0 30.3 %collective-permute-start.29 = (bf16[112,2048]{1,0:T(8,128)(2,1)S(1)}, bf16[112,2048]{1,0:T(8,128)(2,1)}, u32[]{:S(2)}, u32[]{:S(2)}) collective-permute-start(bf16[112,2048]{1,0:T(8,128)(2,1)S(1)} %get-tuple-element.257), channel_id=1, source_target_pairs={{0,4},{8,12},{16,20},{24,28},{1,5},{9,13},{17,21},{25,29},{2,6},{1... | collective-permute-start | bytes 1376264 | tf_op jit(solution)/shard_map/ppermute | solution.py:11
  215.7 21.4 %collective-permute-start.31 = (bf16[224,2048]{1,0:T(8,128)(2,1)}, bf16[224,2048]{1,0:T(8,128)(2,1)}, u32[]{:S(2)}, u32[]{:S(2)}) collective-permute-start(bf16[224,2048]{1,0:T(8,128)(2,1)} %get-tuple-element.355), channel_id=1, source_target_pairs={{8,0},{12,4},{16,8},{20,12},{24,16},{28,20},{9,1},{13,5},{17,9},{2... | collective-permute-start | bytes 2752520 | tf_op jit(solution)/shard_map/ppermute | solution.py:11
  217.1 22.0 %collective-permute-start.28 = (bf16[224,2048]{1,0:T(8,128)(2,1)}, bf16[224,2048]{1,0:T(8,128)(2,1)}, u32[]{:S(2)}, u32[]{:S(2)}) collective-permute-start(bf16[224,2048]{1,0:T(8,128)(2,1)} %get-tuple-element.356), channel_id=1, source_target_pairs={{4,0},{12,8},{20,16},{28,24},{5,1},{13,9},{21,17},{29,25},{6,2},{1... | collective-permute-start | bytes 2752520 | tf_op jit(solution)/shard_map/ppermute | solution.py:11
  226.7 14.6 %collective-permute-start.27 = (f32[896,224]{0,1:T(8,128)S(1)}, f32[896,224]{0,1:T(8,128)S(1)}, u32[]{:S(2)}, u32[]{:S(2)}) collective-permute-start(f32[896,224]{0,1:T(8,128)S(1)} %pad_maximum_fusion.25), channel_id=1, source_target_pairs={{0,1},{1,0},{2,3},{3,2},{4,5},{5,4},{6,7},{7,6},{8,9},{9,8},{10,11... | collective-permute-start | bytes 2408456 | tf_op jit(solution)/shard_map/ppermute | solution.py:91
  249.8 19.4 %collective-permute-start.32 = (f32[896,224]{0,1:T(8,128)S(1)}, f32[896,224]{0,1:T(8,128)S(1)}, u32[]{:S(2)}, u32[]{:S(2)}) collective-permute-start(f32[896,224]{0,1:T(8,128)S(1)} %pad_maximum_fusion.26), channel_id=1, source_target_pairs={{0,1},{1,0},{2,3},{3,2},{4,5},{5,4},{6,7},{7,6},{8,9},{9,8},{10,11... | collective-permute-start | bytes 2408456 | tf_op jit(solution)/shard_map/ppermute | solution.py:91
  277.7 16.2 %collective-permute-start.37 = (f32[896,224]{0,1:T(8,128)S(1)}, f32[896,224]{0,1:T(8,128)S(1)}, u32[]{:S(2)}, u32[]{:S(2)}) collective-permute-start(f32[896,224]{0,1:T(8,128)S(1)} %pad_maximum_fusion.27), channel_id=1, source_target_pairs={{0,1},{1,0},{2,3},{3,2},{4,5},{5,4},{6,7},{7,6},{8,9},{9,8},{10,11... | collective-permute-start | bytes 2408456 | tf_op jit(solution)/shard_map/ppermute | solution.py:91
  (91 other events, 875.8 us)
where the time goes:
time: 330 us; the launch traced here: 328 us
  waiting for transfers between devices  117 us (35%)
  local copies, waits for them, and re-layouts  64.2 us (19%)
  starting transfers between devices  61.7 us (19%)
  other arithmetic  58.3 us (18%)
  matrix products  16.7 us (5%)
  blocking collectives  8.5 us (3%)
    ppermute x27, waiting for transfers between devices, moved(): return lax.ppermute(value, 'snp', pairs)  88.1 us
    ppermute x27, starting transfers between devices, moved(): return lax.ppermute(value, 'snp', pairs)  47.8 us
    ppermute x8, waiting for transfers between devices, local(): last = lax.ppermute(payload, 'samp', across)  28.7 us
    unnamed x167, local copies, waits for them, and re-layouts  21.4 us
    dot_general x8, matrix products, finish(): jnp.einsum('ab,cb->ac', own_block, picked, preferred_element_type=jnp.flo...  16.7 us
    gather x8, local copies, waits for them, and re-layouts, finish(): picked = jnp.take(blocks, order, axis=0).reshape((BAND + 1) * step, -1)  15.1 us
    select_n x9, other arithmetic, finish(): picked = jnp.take(blocks, order, axis=0).reshape((BAND + 1) * step, -1)  15.1 us
    slice x7, local copies, waits for them, and re-layouts, local(): state['three_even'][second] = sent[-step:]  14.3 us
  transfers between devices with their start and end apart: 43, of which 17 were waited for; matrix products, arithmetic and copies ran while one was open for 24% of the time, Pallas kernels for 0%

commit v1 on v0

--- a/solution.py
+++ b/solution.py
@@ -30,9 +30,29 @@
     total = dosages.shape[1] * lax.axis_size("samp")
     count = lax.axis_size("snp")
     groups = lax.axis_size("samp")
-    sums, squares = local_moments(dosages)
-    sums, squares = lax.psum((sums, squares), "samp")
-    own_block = standardize(dosages, sums, squares, total)
+    me = lax.axis_index("samp")
+    flips = list(range(1, groups))
+
+    def choose(values):
+        ordered = []
+        for k in range(groups):
+            pick = values[0]
+            for i in flips:
+                pick = jnp.where(jnp.bitwise_xor(me, i) == k, values[i], pick)
+            ordered.append(pick)
+        return ordered
+
+    def added(values):
+        ordered = choose(values)
+        result = ordered[0]
+        for part in ordered[1:]:
+            result = result + part
+        return result
+
+    moments = jnp.stack(local_moments(dosages))
+    summed_moments = added(
+        [moments] + [lax.ppermute(moments, "samp", [(j, j ^ i) for j in range(groups)]) for i in flips])
+    own_block = standardize(dosages, summed_moments[0], summed_moments[1], total)
     rows = own_block.shape[0]
     step = rows // CHUNKS
     pieces = [own_block[c * step:(c + 1) * step] for c in range(CHUNKS)]
@@ -43,28 +63,29 @@
     odd_to_even = [(s, s - 1) for s in odd]
     even_to_odd = [(s, s + 1) for s in even if s + 1 < count]
 
-    me = lax.axis_index("samp")
-    order = jnp.bitwise_xor(me, jnp.arange(BAND + 1, dtype=me.dtype))
-    partner = [(j, j ^ 1) for j in range(groups)]
-    across = [(j, j ^ 2) for j in range(groups)]
-
-    names = ("two", "one_even", "one_odd", "three_even", "three_odd", "tiles", "first", "results")
+    names = ("two", "one_even", "one_odd", "three_even", "three_odd", "results")
     state = {name: [None] * CHUNKS for name in names}
 
     def finish(c):
-        blocks = jnp.stack([
+        blocks = jnp.concatenate([
             pieces[c],
             state["one_even"][c] + state["one_odd"][c],
             state["two"][c],
             state["three_even"][c] + state["three_odd"][c],
-        ])
-        picked = jnp.take(blocks, order, axis=0).reshape((BAND + 1) * step, -1)
-        state["tiles"][c] = jnp.einsum("ab,cb->ac", own_block, picked, preferred_element_type=jnp.float32)
+        ], axis=0)
+        gram = jnp.einsum("ab,cb->ac", own_block, blocks, preferred_element_type=jnp.float32)
+        tiles = [gram[:, k * step:(k + 1) * step] for k in range(BAND + 1)]
+        outgoing = []
+        for i in [0] + flips:
+            target = tiles[0]
+            for k in range(1, groups):
+                target = jnp.where(jnp.bitwise_xor(me, i) == k, tiles[k], target)
+            outgoing.append(target)
+        arrived = [outgoing[0]] + [
+            lax.ppermute(outgoing[i], "samp", [(j, j ^ i) for j in range(groups)]) for i in flips]
+        state["results"][c] = added(arrived)
 
-    def tile(c, k):
-        return state["tiles"][c][:, k * step:(k + 1) * step]
-
-    for t in range(CHUNKS + 4):
+    for t in range(CHUNKS + 3):
         new = t if t < CHUNKS else None
         second = t - 1 if 0 <= t - 1 < CHUNKS else None
         third = t - 2 if 0 <= t - 2 < CHUNKS else None
@@ -85,15 +106,7 @@
         if second is not None:
             state["one_odd"][second] = moved(state["two"][second], even_to_odd)
         if 0 <= t - 3 < CHUNKS:
-            c = t - 3
-            finish(c)
-            payload = jnp.concatenate([tile(c, 1), tile(c, 3)], axis=1)
-            state["first"][c] = lax.ppermute(payload, "samp", partner)
-        if 0 <= t - 4 < CHUNKS:
-            c = t - 4
-            payload = tile(c, 2) + state["first"][c][:, step:]
-            last = lax.ppermute(payload, "samp", across)
-            state["results"][c] = tile(c, 0) + state["first"][c][:, :step] + last
+            finish(t - 3)
         flat, tree = jax.tree.flatten(state)
         following = pieces[t + 1] if t + 1 < CHUNKS else own_block[:8]
         flat, following = lax.optimization_barrier((flat, following))

time: 330 us -> 317 us (0.961)
  waiting for transfers between devices: 117 us -> 204 us
  local copies, waits for them, and re-layouts: 64.2 us -> 11.4 us
  other arithmetic: 58.3 us -> 18.7 us
  blocking collectives: 8.5 us -> 0 us
    ppermute x16 -> x27, waiting for transfers between devices: 28.7 us -> 118 us  [the longest x24 115 us: finish(): lax.ppermute(outgoing[i], 'samp', [(j, j ^ i) for j in range(groups)])]
    unnamed x167 -> x41, local copies, waits for them, and re-layouts: 21.4 us -> 2.86 us
    gather x8 -> x0, local copies, waits for them, and re-layouts: 15.1 us -> none  [finish(): picked = jnp.take(blocks, order, axis=0).reshape((BAND + 1) * step, -1)]
    select_n x9 -> x16, other arithmetic: 15.1 us -> 2.98 us  [finish(): target = jnp.where(jnp.bitwise_xor(me, i) == k, tiles[k], target)]
    slice x7, local copies, waits for them, and re-layouts: 14.3 us -> 3.48 us  [local(): state['three_even'][second] = sent[-step:]]
    concatenate x7, other arithmetic: 12.9 us -> 2.48 us  [joined(): return parts[0] if len(parts) == 1 else jnp.concatenate(parts, axis=0)]
    psum x1 -> x0, blocking collectives: 8.5 us -> none  [local(): sums, squares = lax.psum((sums, squares), 'samp')]
    another operation x23 -> x1, other arithmetic: 8.42 us -> 0.01 us  [local(): moments = jnp.stack(local_moments(dosages))]
  transfers between devices with their start and end apart: 43 -> 54, of which waited for: 17 -> 33; matrix products, arithmetic and copies ran while one was open for 24% -> 3% of each run, Pallas kernels for 0% -> 0%
where the time goes in v1:
time: 317 us; the launch traced here: 316 us
  waiting for transfers between devices  204 us (64%)
  starting transfers between devices  63.8 us (20%)
  other arithmetic  18.7 us (6%)
  matrix products  16.8 us (5%)
  local copies, waits for them, and re-layouts  11.4 us (4%)
    ppermute x24, waiting for transfers between devices, finish(): lax.ppermute(outgoing[i], 'samp', [(j, j ^ i) for j in range(groups)])  115 us
    ppermute x27, waiting for transfers between devices, moved(): return lax.ppermute(value, 'snp', pairs)  86 us
    ppermute x27, starting transfers between devices, moved(): return lax.ppermute(value, 'snp', pairs)  42.9 us
    ppermute x24, starting transfers between devices, finish(): lax.ppermute(outgoing[i], 'samp', [(j, j ^ i) for j in range(groups)])  17.7 us
    dot_general x8, matrix products, finish(): jnp.einsum('ab,cb->ac', own_block, blocks, preferred_element_type=jnp.flo...  16.8 us
  transfers between devices with their start and end apart: 54, of which 33 were waited for; matrix products, arithmetic and copies ran while one was open for 3% of the time, Pallas kernels for 0%

profile of v1, /device:TPU:0, one launch (start us, length us, event | category | flops | bytes accessed | tf_op | source)
XLA Modules:
  0.0 316.0 jit_solution(8000641721275148696)
XLA Ops:
  0.0 4.0 %fusion.74 = (f32[896]{0:T(1024)S(1)}, f32[896]{0:T(1024)S(1)}) fusion(f32[896,2048]{1,0:T(8,128)} %param.1), kind=kLoop, calls=%fused_computation.135 | loop fusion | flops 5503232 | bytes 7347200 | tf_op jit(solution)/shard_map/reduce_sum | solution.py:21
  10.2 3.9 %multiply_convert_fusion = bf16[896,2048]{1,0:T(8,128)(2,1)S(1)} fusion(f32[896,2048]{1,0:T(8,128)} %param.1, f32[896]{0:T(1024)S(1)} %add_rsqrt_fusion, f32[896]{0:T(1024)S(1)} %get-tuple-element.269), kind=kLoop, calls=%fused_computation | loop fusion | flops 5505024 | bytes 11017216 | tf_op jit(solution)/shard_map/convert_element_type | solution.py:17
  17.1 11.2 %collective-permute-done.3 = bf16[112,2048]{1,0:T(8,128)(2,1)S(1)} collective-permute-done((bf16[112,2048]{1,0:T(8,128)(2,1)S(1)}, bf16[112,2048]{1,0:T(8,128)(2,1)S(1)}, u32[]{:S(2)}, u32[]{:S(2)}) %collective-permute-start.3) | collective-permute-done | bytes 458784 | tf_op jit(solution)/shard_map/ppermute | solution.py:11
  31.0 4.6 %collective-permute-start.6 = (bf16[112,2048]{1,0:T(8,128)(2,1)S(1)}, bf16[112,2048]{1,0:T(8,128)(2,1)S(1)}, u32[]{:S(2)}, u32[]{:S(2)}) collective-permute-start(bf16[112,2048]{1,0:T(8,128)(2,1)S(1)} %collective-permute-done.4), channel_id=1, source_target_pairs={{0,4},{8,12},{16,20},{24,28},{1,5},{9,13},{17,21},{25,29},{2,6},{1... | collective-permute-start | bytes 1376264 | tf_op jit(solution)/shard_map/ppermute | solution.py:11
  37.0 15.5 %collective-permute-done.5 = bf16[224,2048]{1,0:T(8,128)(2,1)S(1)} collective-permute-done((bf16[224,2048]{1,0:T(8,128)(2,1)S(1)}, bf16[224,2048]{1,0:T(8,128)(2,1)S(1)}, u32[]{:S(2)}, u32[]{:S(2)}) %collective-permute-start.5) | collective-permute-done | bytes 917536 | tf_op jit(solution)/shard_map/ppermute | solution.py:11
  56.2 4.6 %collective-permute-start.9 = (bf16[112,2048]{1,0:T(8,128)(2,1)S(1)}, bf16[112,2048]{1,0:T(8,128)(2,1)S(1)}, u32[]{:S(2)}, u32[]{:S(2)}) collective-permute-start(bf16[112,2048]{1,0:T(8,128)(2,1)S(1)} %collective-permute-done.7), channel_id=1, source_target_pairs={{0,4},{8,12},{16,20},{24,28},{1,5},{9,13},{17,21},{25,29},{2,6},{1... | collective-permute-start | bytes 1376264 | tf_op jit(solution)/shard_map/ppermute | solution.py:11
  60.8 14.6 %collective-permute-done.10 = bf16[224,2048]{1,0:T(8,128)(2,1)S(1)} collective-permute-done((bf16[224,2048]{1,0:T(8,128)(2,1)S(1)}, bf16[224,2048]{1,0:T(8,128)(2,1)S(1)}, u32[]{:S(2)}, u32[]{:S(2)}) %collective-permute-start.10) | collective-permute-done | bytes 917536 | tf_op jit(solution)/shard_map/ppermute | solution.py:11
  88.1 8.4 %collective-permute-done.13 = f32[896,112]{0,1:T(8,128)} collective-permute-done((f32[896,112]{0,1:T(8,128)}, f32[896,112]{0,1:T(8,128)}, u32[]{:S(2)}, u32[]{:S(2)}) %collective-permute-start.13) | collective-permute-done | bytes 401440 | tf_op jit(solution)/shard_map/ppermute | solution.py:85
  98.1 5.6 %collective-permute-done.14 = f32[896,112]{0,1:T(8,128)} collective-permute-done((f32[896,112]{0,1:T(8,128)}, f32[896,112]{0,1:T(8,128)}, u32[]{:S(2)}, u32[]{:S(2)}) %collective-permute-start.14) | collective-permute-done | bytes 401440 | tf_op jit(solution)/shard_map/ppermute | solution.py:85
  106.5 4.5 %collective-permute-done.11 = bf16[224,2048]{1,0:T(8,128)(2,1)} collective-permute-done((bf16[224,2048]{1,0:T(8,128)(2,1)}, bf16[224,2048]{1,0:T(8,128)(2,1)}, u32[]{:S(2)}, u32[]{:S(2)}) %collective-permute-start.11) | collective-permute-done | bytes 917536 | tf_op jit(solution)/shard_map/ppermute | solution.py:11
  120.9 8.1 %collective-permute-done.19 = f32[896,112]{0,1:T(8,128)S(1)} collective-permute-done((f32[896,112]{0,1:T(8,128)S(1)}, f32[896,112]{0,1:T(8,128)S(1)}, u32[]{:S(2)}, u32[]{:S(2)}) %collective-permute-start.19) | collective-permute-done | bytes 401440 | tf_op jit(solution)/shard_map/ppermute | solution.py:85
  130.7 5.4 %collective-permute-done.20 = f32[896,112]{0,1:T(8,128)S(1)} collective-permute-done((f32[896,112]{0,1:T(8,128)S(1)}, f32[896,112]{0,1:T(8,128)S(1)}, u32[]{:S(2)}, u32[]{:S(2)}) %collective-permute-start.20) | collective-permute-done | bytes 401440 | tf_op jit(solution)/shard_map/ppermute | solution.py:85
  136.4 3.9 %collective-permute-done.22 = bf16[224,2048]{1,0:T(8,128)(2,1)S(1)} collective-permute-done((bf16[224,2048]{1,0:T(8,128)(2,1)S(1)}, bf16[224,2048]{1,0:T(8,128)(2,1)S(1)}, u32[]{:S(2)}, u32[]{:S(2)}) %collective-permute-start.22) | collective-permute-done | bytes 917536 | tf_op jit(solution)/shard_map/ppermute | solution.py:11
  140.4 3.1 collective-permute-done.17
  151.9 8.1 %collective-permute-done.25 = f32[896,112]{0,1:T(8,128)S(1)} collective-permute-done((f32[896,112]{0,1:T(8,128)S(1)}, f32[896,112]{0,1:T(8,128)S(1)}, u32[]{:S(2)}, u32[]{:S(2)}) %collective-permute-start.25) | collective-permute-done | bytes 401440 | tf_op jit(solution)/shard_map/ppermute | solution.py:85
  161.6 5.6 %collective-permute-done.26 = f32[896,112]{0,1:T(8,128)S(1)} collective-permute-done((f32[896,112]{0,1:T(8,128)S(1)}, f32[896,112]{0,1:T(8,128)S(1)}, u32[]{:S(2)}, u32[]{:S(2)}) %collective-permute-start.26) | collective-permute-done | bytes 401440 | tf_op jit(solution)/shard_map/ppermute | solution.py:85
  167.4 4.6 %collective-permute-done.28 = bf16[224,2048]{1,0:T(8,128)(2,1)S(1)} collective-permute-done((bf16[224,2048]{1,0:T(8,128)(2,1)S(1)}, bf16[224,2048]{1,0:T(8,128)(2,1)S(1)}, u32[]{:S(2)}, u32[]{:S(2)}) %collective-permute-start.28) | collective-permute-done | bytes 917536 | tf_op jit(solution)/shard_map/ppermute | solution.py:11
  172.0 2.5 collective-permute-done.23
  182.9 8.1 %collective-permute-done.31 = f32[896,112]{0,1:T(8,128)S(1)} collective-permute-done((f32[896,112]{0,1:T(8,128)S(1)}, f32[896,112]{0,1:T(8,128)S(1)}, u32[]{:S(2)}, u32[]{:S(2)}) %collective-permute-start.31) | collective-permute-done | bytes 401440 | tf_op jit(solution)/shard_map/ppermute | solution.py:85
  192.5 5.6 %collective-permute-done.32 = f32[896,112]{0,1:T(8,128)S(1)} collective-permute-done((f32[896,112]{0,1:T(8,128)S(1)}, f32[896,112]{0,1:T(8,128)S(1)}, u32[]{:S(2)}, u32[]{:S(2)}) %collective-permute-start.32) | collective-permute-done | bytes 401440 | tf_op jit(solution)/shard_map/ppermute | solution.py:85
  198.3 5.2 %collective-permute-done.34 = bf16[224,2048]{1,0:T(8,128)(2,1)S(1)} collective-permute-done((bf16[224,2048]{1,0:T(8,128)(2,1)S(1)}, bf16[224,2048]{1,0:T(8,128)(2,1)S(1)}, u32[]{:S(2)}, u32[]{:S(2)}) %collective-permute-start.34) | collective-permute-done | bytes 917536 | tf_op jit(solution)/shard_map/ppermute | solution.py:11
  213.1 8.1 %collective-permute-done.37 = f32[896,112]{0,1:T(8,128)S(1)} collective-permute-done((f32[896,112]{0,1:T(8,128)S(1)}, f32[896,112]{0,1:T(8,128)S(1)}, u32[]{:S(2)}, u32[]{:S(2)}) %collective-permute-start.37) | collective-permute-done | bytes 401440 | tf_op jit(solution)/shard_map/ppermute | solution.py:85
  222.9 5.3 %collective-permute-done.38 = f32[896,112]{0,1:T(8,128)S(1)} collective-permute-done((f32[896,112]{0,1:T(8,128)S(1)}, f32[896,112]{0,1:T(8,128)S(1)}, u32[]{:S(2)}, u32[]{:S(2)}) %collective-permute-start.38) | collective-permute-done | bytes 401440 | tf_op jit(solution)/shard_map/ppermute | solution.py:85
  228.5 5.8 %collective-permute-done.40 = bf16[224,2048]{1,0:T(8,128)(2,1)S(1)} collective-permute-done((bf16[224,2048]{1,0:T(8,128)(2,1)S(1)}, bf16[224,2048]{1,0:T(8,128)(2,1)S(1)}, u32[]{:S(2)}, u32[]{:S(2)}) %collective-permute-start.40) | collective-permute-done | bytes 917536 | tf_op jit(solution)/shard_map/ppermute | solution.py:11
  243.3 6.5 %collective-permute-done.42 = f32[896,112]{0,1:T(8,128)S(1)} collective-permute-done((f32[896,112]{0,1:T(8,128)S(1)}, f32[896,112]{0,1:T(8,128)S(1)}, u32[]{:S(2)}, u32[]{:S(2)}) %collective-permute-start.42) | collective-permute-done | bytes 401440 | tf_op jit(solution)/shard_map/ppermute | solution.py:85
  251.1 5.7 %collective-permute-done.43 = f32[896,112]{0,1:T(8,128)S(1)} collective-permute-done((f32[896,112]{0,1:T(8,128)S(1)}, f32[896,112]{0,1:T(8,128)S(1)}, u32[]{:S(2)}, u32[]{:S(2)}) %collective-permute-start.43) | collective-permute-done | bytes 401440 | tf_op jit(solution)/shard_map/ppermute | solution.py:85
  257.1 9.3 %collective-permute-done.46 = bf16[112,2048]{1,0:T(8,128)(2,1)S(1)} collective-permute-done((bf16[112,2048]{1,0:T(8,128)(2,1)S(1)}, bf16[112,2048]{1,0:T(8,128)(2,1)S(1)}, u32[]{:S(2)}, u32[]{:S(2)}) %collective-permute-start.46) | collective-permute-done | bytes 458784 | tf_op jit(solution)/shard_map/ppermute | solution.py:11
  272.6 7.4 %collective-permute-done.47 = f32[896,112]{0,1:T(8,128)S(1)} collective-permute-done((f32[896,112]{0,1:T(8,128)S(1)}, f32[896,112]{0,1:T(8,128)S(1)}, u32[]{:S(2)}, u32[]{:S(2)}) %collective-permute-start.47) | collective-permute-done | bytes 401440 | tf_op jit(solution)/shard_map/ppermute | solution.py:85
  280.0 9.2 %collective-permute-done.48 = f32[896,112]{0,1:T(8,128)S(1)} collective-permute-done((f32[896,112]{0,1:T(8,128)S(1)}, f32[896,112]{0,1:T(8,128)S(1)}, u32[]{:S(2)}, u32[]{:S(2)}) %collective-permute-start.48) | collective-permute-done | bytes 401440 | tf_op jit(solution)/shard_map/ppermute | solution.py:85
  294.2 9.4 %collective-permute-done.51 = f32[896,112]{0,1:T(8,128)S(1)} collective-permute-done((f32[896,112]{0,1:T(8,128)S(1)}, f32[896,112]{0,1:T(8,128)S(1)}, u32[]{:S(2)}, u32[]{:S(2)}) %collective-permute-start.51) | collective-permute-done | bytes 401440 | tf_op jit(solution)/shard_map/ppermute | solution.py:85
  303.6 8.6 %collective-permute-done.52 = f32[896,112]{0,1:T(8,128)S(1)} collective-permute-done((f32[896,112]{0,1:T(8,128)S(1)}, f32[896,112]{0,1:T(8,128)S(1)}, u32[]{:S(2)}, u32[]{:S(2)}) %collective-permute-start.52) | collective-permute-done | bytes 401440 | tf_op jit(solution)/shard_map/ppermute | solution.py:85
  313.0 3.0 copy.2
  (197 shorter events, 99.2 us)
Async XLA Ops:
  29.7 22.8 %collective-permute-start.5 = (bf16[224,2048]{1,0:T(8,128)(2,1)S(1)}, bf16[224,2048]{1,0:T(8,128)(2,1)S(1)}, u32[]{:S(2)}, u32[]{:S(2)}) collective-permute-start(bf16[224,2048]{1,0:T(8,128)(2,1)S(1)} %pad_maximum_fusion.12), channel_id=1, source_target_pairs={{4,0},{12,8},{20,16},{28,24},{5,1},{13,9},{21,17},{29,25},{6,2},{1... | collective-permute-start | bytes 2752520 | tf_op jit(solution)/shard_map/ppermute | solution.py:11
  31.0 22.3 %collective-permute-start.6 = (bf16[112,2048]{1,0:T(8,128)(2,1)S(1)}, bf16[112,2048]{1,0:T(8,128)(2,1)S(1)}, u32[]{:S(2)}, u32[]{:S(2)}) collective-permute-start(bf16[112,2048]{1,0:T(8,128)(2,1)S(1)} %collective-permute-done.4), channel_id=1, source_target_pairs={{0,4},{8,12},{16,20},{24,28},{1,5},{9,13},{17,21},{25,29},{2,6},{1... | collective-permute-start | bytes 1376264 | tf_op jit(solution)/shard_map/ppermute | solution.py:11
  35.7 17.7 %collective-permute-start.7 = (bf16[112,2048]{1,0:T(8,128)(2,1)S(1)}, bf16[112,2048]{1,0:T(8,128)(2,1)S(1)}, u32[]{:S(2)}, u32[]{:S(2)}) collective-permute-start(bf16[112,2048]{1,0:T(8,128)(2,1)S(1)} %get-tuple-element.137), channel_id=1, source_target_pairs={{8,0},{12,4},{16,8},{20,12},{24,16},{28,20},{9,1},{13,5},{17,9},{2... | collective-permute-start | bytes 1376264 | tf_op jit(solution)/shard_map/ppermute | solution.py:11
  53.6 21.8 %collective-permute-start.10 = (bf16[224,2048]{1,0:T(8,128)(2,1)S(1)}, bf16[224,2048]{1,0:T(8,128)(2,1)S(1)}, u32[]{:S(2)}, u32[]{:S(2)}) collective-permute-start(bf16[224,2048]{1,0:T(8,128)(2,1)S(1)} %get-tuple-element.331), channel_id=1, source_target_pairs={{8,0},{12,4},{16,8},{20,12},{24,16},{28,20},{9,1},{13,5},{17,9},{2... | collective-permute-start | bytes 2752520 | tf_op jit(solution)/shard_map/ppermute | solution.py:11
  54.9 21.8 %collective-permute-start.8 = (bf16[224,2048]{1,0:T(8,128)(2,1)S(1)}, bf16[224,2048]{1,0:T(8,128)(2,1)S(1)}, u32[]{:S(2)}, u32[]{:S(2)}) collective-permute-start(bf16[224,2048]{1,0:T(8,128)(2,1)S(1)} %get-tuple-element.332), channel_id=1, source_target_pairs={{4,0},{12,8},{20,16},{28,24},{5,1},{13,9},{21,17},{29,25},{6,2},{1... | collective-permute-start | bytes 2752520 | tf_op jit(solution)/shard_map/ppermute | solution.py:11
  56.2 21.5 %collective-permute-start.9 = (bf16[112,2048]{1,0:T(8,128)(2,1)S(1)}, bf16[112,2048]{1,0:T(8,128)(2,1)S(1)}, u32[]{:S(2)}, u32[]{:S(2)}) collective-permute-start(bf16[112,2048]{1,0:T(8,128)(2,1)S(1)} %collective-permute-done.7), channel_id=1, source_target_pairs={{0,4},{8,12},{16,20},{24,28},{1,5},{9,13},{17,21},{25,29},{2,6},{1... | collective-permute-start | bytes 1376264 | tf_op jit(solution)/shard_map/ppermute | solution.py:11
  82.6 22.6 %collective-permute-start.16 = (bf16[224,2048]{1,0:T(8,128)(2,1)}, bf16[224,2048]{1,0:T(8,128)(2,1)}, u32[]{:S(2)}, u32[]{:S(2)}) collective-permute-start(bf16[224,2048]{1,0:T(8,128)(2,1)} %get-tuple-element.329), channel_id=1, source_target_pairs={{8,0},{12,4},{16,8},{20,12},{24,16},{28,20},{9,1},{13,5},{17,9},{2... | collective-permute-start | bytes 2752520 | tf_op jit(solution)/shard_map/ppermute | solution.py:11
  85.5 18.2 %collective-permute-start.14 = (f32[896,112]{0,1:T(8,128)}, f32[896,112]{0,1:T(8,128)}, u32[]{:S(2)}, u32[]{:S(2)}) collective-permute-start(f32[896,112]{0,1:T(8,128)} %select_select_fusion.22), channel_id=1, source_target_pairs={{0,2},{1,3},{2,0},{3,1},{4,6},{5,7},{6,4},{7,5},{8,10},{9,11},{10,... | collective-permute-start | bytes 1204232 | tf_op jit(solution)/shard_map/ppermute | solution.py:85
  86.8 24.2 %collective-permute-start.11 = (bf16[224,2048]{1,0:T(8,128)(2,1)}, bf16[224,2048]{1,0:T(8,128)(2,1)}, u32[]{:S(2)}, u32[]{:S(2)}) collective-permute-start(bf16[224,2048]{1,0:T(8,128)(2,1)} %get-tuple-element.330), channel_id=1, source_target_pairs={{4,0},{12,8},{20,16},{28,24},{5,1},{13,9},{21,17},{29,25},{6,2},{1... | collective-permute-start | bytes 2752520 | tf_op jit(solution)/shard_map/ppermute | solution.py:11
  96.6 15.9 %collective-permute-start.12 = (bf16[112,2048]{1,0:T(8,128)(2,1)}, bf16[112,2048]{1,0:T(8,128)(2,1)S(1)}, u32[]{:S(2)}, u32[]{:S(2)}) collective-permute-start(bf16[112,2048]{1,0:T(8,128)(2,1)} %copy-done.8), channel_id=1, source_target_pairs={{0,4},{8,12},{16,20},{24,28},{1,5},{9,13},{17,21},{25,29},{2,6},{1... | collective-permute-start | bytes 1376264 | tf_op jit(solution)/shard_map/ppermute | solution.py:11
  116.0 24.2 %collective-permute-start.22 = (bf16[224,2048]{1,0:T(8,128)(2,1)S(1)}, bf16[224,2048]{1,0:T(8,128)(2,1)S(1)}, u32[]{:S(2)}, u32[]{:S(2)}) collective-permute-start(bf16[224,2048]{1,0:T(8,128)(2,1)S(1)} %get-tuple-element.327), channel_id=1, source_target_pairs={{8,0},{12,4},{16,8},{20,12},{24,16},{28,20},{9,1},{13,5},{17,9},{2... | collective-permute-start | bytes 2752520 | tf_op jit(solution)/shard_map/ppermute | solution.py:11
  118.2 17.8 %collective-permute-start.20 = (f32[896,112]{0,1:T(8,128)S(1)}, f32[896,112]{0,1:T(8,128)S(1)}, u32[]{:S(2)}, u32[]{:S(2)}) collective-permute-start(f32[896,112]{0,1:T(8,128)S(1)} %select_select_fusion.19), channel_id=1, source_target_pairs={{0,2},{1,3},{2,0},{3,1},{4,6},{5,7},{6,4},{7,5},{8,10},{9,11},{10,... | collective-permute-start | bytes 1204232 | tf_op jit(solution)/shard_map/ppermute | solution.py:85
  119.6 23.9 %collective-permute-start.17 = (bf16[224,2048]{1,0:T(8,128)(2,1)S(1)}, bf16[224,2048]{1,0:T(8,128)(2,1)S(1)}, u32[]{:S(2)}, u32[]{:S(2)}) collective-permute-start(bf16[224,2048]{1,0:T(8,128)(2,1)S(1)} %get-tuple-element.328), channel_id=1, source_target_pairs={{4,0},{12,8},{20,16},{28,24},{5,1},{13,9},{21,17},{29,25},{6,2},{1... | collective-permute-start | bytes 2752520 | tf_op jit(solution)/shard_map/ppermute | solution.py:11
  129.0 14.5 %collective-permute-start.18 = (bf16[112,2048]{1,0:T(8,128)(2,1)S(1)}, bf16[112,2048]{1,0:T(8,128)(2,1)S(1)}, u32[]{:S(2)}, u32[]{:S(2)}) collective-permute-start(bf16[112,2048]{1,0:T(8,128)(2,1)S(1)} %get-tuple-element.195), channel_id=1, source_target_pairs={{0,4},{8,12},{16,20},{24,28},{1,5},{9,13},{17,21},{25,29},{2,6},{1... | collective-permute-start | bytes 1376264 | tf_op jit(solution)/shard_map/ppermute | solution.py:11
  147.1 24.9 %collective-permute-start.28 = (bf16[224,2048]{1,0:T(8,128)(2,1)S(1)}, bf16[224,2048]{1,0:T(8,128)(2,1)S(1)}, u32[]{:S(2)}, u32[]{:S(2)}) collective-permute-start(bf16[224,2048]{1,0:T(8,128)(2,1)S(1)} %get-tuple-element.325), channel_id=1, source_target_pairs={{8,0},{12,4},{16,8},{20,12},{24,16},{28,20},{9,1},{13,5},{17,9},{2... | collective-permute-start | bytes 2752520 | tf_op jit(solution)/shard_map/ppermute | solution.py:11
  149.3 17.8 %collective-permute-start.26 = (f32[896,112]{0,1:T(8,128)S(1)}, f32[896,112]{0,1:T(8,128)S(1)}, u32[]{:S(2)}, u32[]{:S(2)}) collective-permute-start(f32[896,112]{0,1:T(8,128)S(1)} %select_select_fusion.16), channel_id=1, source_target_pairs={{0,2},{1,3},{2,0},{3,1},{4,6},{5,7},{6,4},{7,5},{8,10},{9,11},{10,... | collective-permute-start | bytes 1204232 | tf_op jit(solution)/shard_map/ppermute | solution.py:85
  150.7 23.9 %collective-permute-start.23 = (bf16[224,2048]{1,0:T(8,128)(2,1)S(1)}, bf16[224,2048]{1,0:T(8,128)(2,1)S(1)}, u32[]{:S(2)}, u32[]{:S(2)}) collective-permute-start(bf16[224,2048]{1,0:T(8,128)(2,1)S(1)} %get-tuple-element.326), channel_id=1, source_target_pairs={{4,0},{12,8},{20,16},{28,24},{5,1},{13,9},{21,17},{29,25},{6,2},{1... | collective-permute-start | bytes 2752520 | tf_op jit(solution)/shard_map/ppermute | solution.py:11
  160.1 14.5 %collective-permute-start.24 = (bf16[112,2048]{1,0:T(8,128)(2,1)S(1)}, bf16[112,2048]{1,0:T(8,128)(2,1)S(1)}, u32[]{:S(2)}, u32[]{:S(2)}) collective-permute-start(bf16[112,2048]{1,0:T(8,128)(2,1)S(1)} %get-tuple-element.211), channel_id=1, source_target_pairs={{0,4},{8,12},{16,20},{24,28},{1,5},{9,13},{17,21},{25,29},{2,6},{1... | collective-permute-start | bytes 1376264 | tf_op jit(solution)/shard_map/ppermute | solution.py:11
  178.0 25.5 %collective-permute-start.34 = (bf16[224,2048]{1,0:T(8,128)(2,1)S(1)}, bf16[224,2048]{1,0:T(8,128)(2,1)S(1)}, u32[]{:S(2)}, u32[]{:S(2)}) collective-permute-start(bf16[224,2048]{1,0:T(8,128)(2,1)S(1)} %get-tuple-element.323), channel_id=1, source_target_pairs={{8,0},{12,4},{16,8},{20,12},{24,16},{28,20},{9,1},{13,5},{17,9},{2... | collective-permute-start | bytes 2752520 | tf_op jit(solution)/shard_map/ppermute | solution.py:11
  180.2 17.8 %collective-permute-start.32 = (f32[896,112]{0,1:T(8,128)S(1)}, f32[896,112]{0,1:T(8,128)S(1)}, u32[]{:S(2)}, u32[]{:S(2)}) collective-permute-start(f32[896,112]{0,1:T(8,128)S(1)} %select_select_fusion.13), channel_id=1, source_target_pairs={{0,2},{1,3},{2,0},{3,1},{4,6},{5,7},{6,4},{7,5},{8,10},{9,11},{10,... | collective-permute-start | bytes 1204232 | tf_op jit(solution)/shard_map/ppermute | solution.py:85
  181.6 23.9 %collective-permute-start.29 = (bf16[224,2048]{1,0:T(8,128)(2,1)S(1)}, bf16[224,2048]{1,0:T(8,128)(2,1)S(1)}, u32[]{:S(2)}, u32[]{:S(2)}) collective-permute-start(bf16[224,2048]{1,0:T(8,128)(2,1)S(1)} %get-tuple-element.324), channel_id=1, source_target_pairs={{4,0},{12,8},{20,16},{28,24},{5,1},{13,9},{21,17},{29,25},{6,2},{1... | collective-permute-start | bytes 2752520 | tf_op jit(solution)/shard_map/ppermute | solution.py:11
  191.0 14.5 %collective-permute-start.30 = (bf16[112,2048]{1,0:T(8,128)(2,1)S(1)}, bf16[112,2048]{1,0:T(8,128)(2,1)S(1)}, u32[]{:S(2)}, u32[]{:S(2)}) collective-permute-start(bf16[112,2048]{1,0:T(8,128)(2,1)S(1)} %get-tuple-element.227), channel_id=1, source_target_pairs={{0,4},{8,12},{16,20},{24,28},{1,5},{9,13},{17,21},{25,29},{2,6},{1... | collective-permute-start | bytes 1376264 | tf_op jit(solution)/shard_map/ppermute | solution.py:11
  208.2 26.1 %collective-permute-start.40 = (bf16[224,2048]{1,0:T(8,128)(2,1)S(1)}, bf16[224,2048]{1,0:T(8,128)(2,1)S(1)}, u32[]{:S(2)}, u32[]{:S(2)}) collective-permute-start(bf16[224,2048]{1,0:T(8,128)(2,1)S(1)} %get-tuple-element.321), channel_id=1, source_target_pairs={{8,0},{12,4},{16,8},{20,12},{24,16},{28,20},{9,1},{13,5},{17,9},{2... | collective-permute-start | bytes 2752520 | tf_op jit(solution)/shard_map/ppermute | solution.py:11
  210.4 17.8 %collective-permute-start.38 = (f32[896,112]{0,1:T(8,128)S(1)}, f32[896,112]{0,1:T(8,128)S(1)}, u32[]{:S(2)}, u32[]{:S(2)}) collective-permute-start(f32[896,112]{0,1:T(8,128)S(1)} %select_select_fusion.10), channel_id=1, source_target_pairs={{0,2},{1,3},{2,0},{3,1},{4,6},{5,7},{6,4},{7,5},{8,10},{9,11},{10,... | collective-permute-start | bytes 1204232 | tf_op jit(solution)/shard_map/ppermute | solution.py:85
  211.8 23.9 %collective-permute-start.35 = (bf16[224,2048]{1,0:T(8,128)(2,1)S(1)}, bf16[224,2048]{1,0:T(8,128)(2,1)S(1)}, u32[]{:S(2)}, u32[]{:S(2)}) collective-permute-start(bf16[224,2048]{1,0:T(8,128)(2,1)S(1)} %get-tuple-element.322), channel_id=1, source_target_pairs={{4,0},{12,8},{20,16},{28,24},{5,1},{13,9},{21,17},{29,25},{6,2},{1... | collective-permute-start | bytes 2752520 | tf_op jit(solution)/shard_map/ppermute | solution.py:11
  239.1 17.7 %collective-permute-start.43 = (f32[896,112]{0,1:T(8,128)S(1)}, f32[896,112]{0,1:T(8,128)S(1)}, u32[]{:S(2)}, u32[]{:S(2)}) collective-permute-start(f32[896,112]{0,1:T(8,128)S(1)} %select_select_fusion.7), channel_id=1, source_target_pairs={{0,2},{1,3},{2,0},{3,1},{4,6},{5,7},{6,4},{7,5},{8,10},{9,11},{10,... | collective-permute-start | bytes 1204232 | tf_op jit(solution)/shard_map/ppermute | solution.py:85
  240.5 16.6 %collective-permute-start.41 = (bf16[112,2048]{1,0:T(8,128)(2,1)S(1)}, bf16[112,2048]{1,0:T(8,128)(2,1)S(1)}, u32[]{:S(2)}, u32[]{:S(2)}) collective-permute-start(bf16[112,2048]{1,0:T(8,128)(2,1)S(1)} %get-tuple-element.256), channel_id=1, source_target_pairs={{0,4},{8,12},{16,20},{24,28},{1,5},{9,13},{17,21},{25,29},{2,6},{1... | collective-permute-start | bytes 1376264 | tf_op jit(solution)/shard_map/ppermute | solution.py:11
  242.0 15.1 %collective-permute-start.45 = (bf16[112,2048]{1,0:T(8,128)(2,1)S(1)}, bf16[112,2048]{1,0:T(8,128)(2,1)S(1)}, u32[]{:S(2)}, u32[]{:S(2)}) collective-permute-start(bf16[112,2048]{1,0:T(8,128)(2,1)S(1)} %get-tuple-element.256), channel_id=1, source_target_pairs={{4,0},{12,8},{20,16},{28,24},{5,1},{13,9},{21,17},{29,25},{6,2},{1... | collective-permute-start | bytes 1376264 | tf_op jit(solution)/shard_map/ppermute | solution.py:11
  249.8 16.6 %collective-permute-start.46 = (bf16[112,2048]{1,0:T(8,128)(2,1)S(1)}, bf16[112,2048]{1,0:T(8,128)(2,1)S(1)}, u32[]{:S(2)}, u32[]{:S(2)}) collective-permute-start(bf16[112,2048]{1,0:T(8,128)(2,1)S(1)} %collective-permute-done.36), channel_id=1, source_target_pairs={{8,0},{12,4},{16,8},{20,12},{24,16},{28,20},{9,1},{13,5},{17,9},{2... | collective-permute-start | bytes 1376264 | tf_op jit(solution)/shard_map/ppermute | solution.py:11
  271.2 18.0 %collective-permute-start.48 = (f32[896,112]{0,1:T(8,128)S(1)}, f32[896,112]{0,1:T(8,128)S(1)}, u32[]{:S(2)}, u32[]{:S(2)}) collective-permute-start(f32[896,112]{0,1:T(8,128)S(1)} %select_select_fusion.4), channel_id=1, source_target_pairs={{0,2},{1,3},{2,0},{3,1},{4,6},{5,7},{6,4},{7,5},{8,10},{9,11},{10,... | collective-permute-start | bytes 1204232 | tf_op jit(solution)/shard_map/ppermute | solution.py:85
  271.3 18.2 %collective-permute-start.50 = (bf16[112,2048]{1,0:T(8,128)(2,1)S(1)}, bf16[112,2048]{1,0:T(8,128)(2,1)S(1)}, u32[]{:S(2)}, u32[]{:S(2)}) collective-permute-start(bf16[112,2048]{1,0:T(8,128)(2,1)S(1)} %collective-permute-done.41), channel_id=1, source_target_pairs={{8,0},{12,4},{16,8},{20,12},{24,16},{28,20},{9,1},{13,5},{17,9},{2... | collective-permute-start | bytes 1376264 | tf_op jit(solution)/shard_map/ppermute | solution.py:11
  293.7 18.6 %collective-permute-start.52 = (f32[896,112]{0,1:T(8,128)S(1)}, f32[896,112]{0,1:T(8,128)S(1)}, u32[]{:S(2)}, u32[]{:S(2)}) collective-permute-start(f32[896,112]{0,1:T(8,128)S(1)} %select_select_fusion.1), channel_id=1, source_target_pairs={{0,2},{1,3},{2,0},{3,1},{4,6},{5,7},{6,4},{7,5},{8,10},{9,11},{10,... | collective-permute-start | bytes 1204232 | tf_op jit(solution)/shard_map/ppermute | solution.py:85
  (39 other events, 525.6 us)

commit v2 on v1

--- a/solution.py
+++ b/solution.py
@@ -63,7 +63,12 @@
     odd_to_even = [(s, s - 1) for s in odd]
     even_to_odd = [(s, s + 1) for s in even if s + 1 < count]
 
-    names = ("two", "one_even", "one_odd", "three_even", "three_odd", "results")
+    even_me = me % 2 == 0
+    low = me < 2
+    partner = [(j, j ^ 1) for j in range(groups)]
+    across = [(j, j ^ 2) for j in range(groups)]
+
+    names = ("two", "one_even", "one_odd", "three_even", "three_odd", "tiles", "first", "results")
     state = {name: [None] * CHUNKS for name in names}
 
     def finish(c):
@@ -75,15 +80,32 @@
         ], axis=0)
         gram = jnp.einsum("ab,cb->ac", own_block, blocks, preferred_element_type=jnp.float32)
         tiles = [gram[:, k * step:(k + 1) * step] for k in range(BAND + 1)]
-        outgoing = []
-        for i in [0] + flips:
-            target = tiles[0]
-            for k in range(1, groups):
-                target = jnp.where(jnp.bitwise_xor(me, i) == k, tiles[k], target)
-            outgoing.append(target)
-        arrived = [outgoing[0]] + [
-            lax.ppermute(outgoing[i], "samp", [(j, j ^ i) for j in range(groups)]) for i in flips]
-        state["results"][c] = added(arrived)
+        state["tiles"][c] = tiles
+        if c == CHUNKS - 1:
+            outgoing = []
+            for i in [0] + flips:
+                target = tiles[0]
+                for k in range(1, groups):
+                    target = jnp.where(jnp.bitwise_xor(me, i) == k, tiles[k], target)
+                outgoing.append(target)
+            arrived = [outgoing[0]] + [
+                lax.ppermute(outgoing[i], "samp", [(j, j ^ i) for j in range(groups)]) for i in flips]
+            state["results"][c] = added(arrived)
+        else:
+            payload = jnp.where(even_me, jnp.concatenate([tiles[1], tiles[3]], axis=1),
+                                jnp.concatenate([tiles[0], tiles[2]], axis=1))
+            state["first"][c] = lax.ppermute(payload, "samp", partner)
+
+    def pick(c, a, b, d, e):
+        t = state["tiles"][c]
+        return jnp.where(low, jnp.where(even_me, t[a], t[b]), jnp.where(even_me, t[d], t[e]))
+
+    def second_level(c):
+        got = state["first"][c]
+        mine = jnp.where(low, got[:, :step], got[:, step:])
+        onward = jnp.where(low, got[:, step:], got[:, :step])
+        last = lax.ppermute(pick(c, 2, 3, 0, 1) + onward, "samp", across)
+        state["results"][c] = pick(c, 0, 1, 2, 3) + mine + last
 
     for t in range(CHUNKS + 3):
         new = t if t < CHUNKS else None
@@ -107,6 +129,8 @@
             state["one_odd"][second] = moved(state["two"][second], even_to_odd)
         if 0 <= t - 3 < CHUNKS:
             finish(t - 3)
+        if 0 <= t - 4 < CHUNKS - 1:
+            second_level(t - 4)
         flat, tree = jax.tree.flatten(state)
         following = pieces[t + 1] if t + 1 < CHUNKS else own_block[:8]
         flat, following = lax.optimization_barrier((flat, following))

time: 317 us -> 272 us (0.86)
  waiting for transfers between devices: 204 us -> 159 us
  other arithmetic: 18.7 us -> 25.8 us
  starting transfers between devices: 63.8 us -> 57.3 us
    ppermute x24 -> x3, waiting for transfers between devices: 115 us -> 14.4 us  [finish(): lax.ppermute(outgoing[i], 'samp', [(j, j ^ i) for j in range(groups)])]
    ppermute x27, waiting for transfers between devices: 86 us -> 120 us  [moved(): return lax.ppermute(value, 'snp', pairs)]
    ppermute x0 -> x14, waiting for transfers between devices: none -> 21.8 us  [the longest x7 21.7 us: second_level(): last = lax.ppermute(pick(c, 2, 3, 0, 1) + onward, 'samp', across)]
    ppermute x24 -> x3, starting transfers between devices: 17.7 us -> 2.14 us  [finish(): lax.ppermute(outgoing[i], 'samp', [(j, j ^ i) for j in range(groups)])]
    add x0 -> x14, other arithmetic: none -> 9.11 us  [the longest x7 7.13 us: second_level(): state['results'][c] = pick(c, 0, 1, 2, 3) + mine + last]
    ppermute x0 -> x14, starting transfers between devices: none -> 7.62 us  [the longest x7 7.12 us: second_level(): last = lax.ppermute(pick(c, 2, 3, 0, 1) + onward, 'samp', across)]
  transfers between devices with their start and end apart: 54 -> 47, of which waited for: 33 -> 25; matrix products, arithmetic and copies ran while one was open for 3% -> 11% of each run, Pallas kernels for 0% -> 0%
where the time goes in v2:
time: 272 us; the launch traced here: 271 us
  waiting for transfers between devices  159 us (58%)
  starting transfers between devices  57.3 us (21%)
  other arithmetic  25.8 us (9%)
  matrix products  16.7 us (6%)
  local copies, waits for them, and re-layouts  10.9 us (4%)
    ppermute x27, waiting for transfers between devices, moved(): return lax.ppermute(value, 'snp', pairs)  120 us
    ppermute x27, starting transfers between devices, moved(): return lax.ppermute(value, 'snp', pairs)  44.4 us
    ppermute x7, waiting for transfers between devices, second_level(): last = lax.ppermute(pick(c, 2, 3, 0, 1) + onward, 'samp', across)  21.7 us
    dot_general x8, matrix products, finish(): jnp.einsum('ab,cb->ac', own_block, blocks, preferred_element_type=jnp.flo...  16.7 us
    ppermute x3, waiting for transfers between devices, finish(): lax.ppermute(outgoing[i], 'samp', [(j, j ^ i) for j in range(groups)])  14.4 us
    add x7, other arithmetic, second_level(): state['results'][c] = pick(c, 0, 1, 2, 3) + mine + last  7.13 us
    ppermute x7, starting transfers between devices, second_level(): last = lax.ppermute(pick(c, 2, 3, 0, 1) + onward, 'samp', across)  7.12 us
  transfers between devices with their start and end apart: 47, of which 25 were waited for; matrix products, arithmetic and copies ran while one was open for 11% of the time, Pallas kernels for 0%

profile of v2, /device:TPU:0, one launch (start us, length us, event | category | flops | bytes accessed | tf_op | source)
XLA Modules:
  0.0 270.9 jit_solution(7256924185575091208)
XLA Ops:
  0.0 4.0 %fusion.74 = (f32[896]{0:T(1024)S(1)}, f32[896]{0:T(1024)S(1)}) fusion(f32[896,2048]{1,0:T(8,128)} %param.1), kind=kLoop, calls=%fused_computation.142 | loop fusion | flops 5503232 | bytes 7347200 | tf_op jit(solution)/shard_map/reduce_sum | solution.py:21
  4.1 2.4 collective-permute-start
  7.9 2.3 collective-permute-done.1
  10.2 3.9 %multiply_convert_fusion = bf16[896,2048]{1,0:T(8,128)(2,1)S(1)} fusion(f32[896,2048]{1,0:T(8,128)} %param.1, f32[896]{0:T(1024)S(1)} %add_rsqrt_fusion, f32[896]{0:T(1024)S(1)} %get-tuple-element.325), kind=kLoop, calls=%fused_computation | loop fusion | flops 5505024 | bytes 11017216 | tf_op jit(solution)/shard_map/convert_element_type | solution.py:17
  18.5 11.2 %collective-permute-done.3 = bf16[112,2048]{1,0:T(8,128)(2,1)S(1)} collective-permute-done((bf16[112,2048]{1,0:T(8,128)(2,1)S(1)}, bf16[112,2048]{1,0:T(8,128)(2,1)S(1)}, u32[]{:S(2)}, u32[]{:S(2)}) %collective-permute-start.3) | collective-permute-done | bytes 458784 | tf_op jit(solution)/shard_map/ppermute | solution.py:11
  32.5 4.6 %collective-permute-start.6 = (bf16[112,2048]{1,0:T(8,128)(2,1)S(1)}, bf16[112,2048]{1,0:T(8,128)(2,1)S(1)}, u32[]{:S(2)}, u32[]{:S(2)}) collective-permute-start(bf16[112,2048]{1,0:T(8,128)(2,1)S(1)} %collective-permute-done.4), channel_id=1, source_target_pairs={{0,4},{8,12},{16,20},{24,28},{1,5},{9,13},{17,21},{25,29},{2,6},{1... | collective-permute-start | bytes 1376264 | tf_op jit(solution)/shard_map/ppermute | solution.py:11
  38.4 15.5 %collective-permute-done.5 = bf16[224,2048]{1,0:T(8,128)(2,1)S(1)} collective-permute-done((bf16[224,2048]{1,0:T(8,128)(2,1)S(1)}, bf16[224,2048]{1,0:T(8,128)(2,1)S(1)}, u32[]{:S(2)}, u32[]{:S(2)}) %collective-permute-start.5) | collective-permute-done | bytes 917536 | tf_op jit(solution)/shard_map/ppermute | solution.py:11
  59.8 5.6 %collective-permute-start.9 = (bf16[112,2048]{1,0:T(8,128)(2,1)}, bf16[112,2048]{1,0:T(8,128)(2,1)S(1)}, u32[]{:S(2)}, u32[]{:S(2)}) collective-permute-start(bf16[112,2048]{1,0:T(8,128)(2,1)} %copy-done.17), channel_id=1, source_target_pairs={{0,4},{8,12},{16,20},{24,28},{1,5},{9,13},{17,21},{25,29},{2,6},{1... | collective-permute-start | bytes 1376264 | tf_op jit(solution)/shard_map/ppermute | solution.py:11
  65.4 13.9 %collective-permute-done.10 = bf16[224,2048]{1,0:T(8,128)(2,1)} collective-permute-done((bf16[224,2048]{1,0:T(8,128)(2,1)}, bf16[224,2048]{1,0:T(8,128)(2,1)}, u32[]{:S(2)}, u32[]{:S(2)}) %collective-permute-start.10) | collective-permute-done | bytes 917536 | tf_op jit(solution)/shard_map/ppermute | solution.py:11
  82.0 1.9 collective-permute-start.13
  87.0 2.1 fusion
  89.4 15.6 %collective-permute-done.14 = bf16[224,2048]{1,0:T(8,128)(2,1)S(1)} collective-permute-done((bf16[224,2048]{1,0:T(8,128)(2,1)S(1)}, bf16[224,2048]{1,0:T(8,128)(2,1)S(1)}, u32[]{:S(2)}, u32[]{:S(2)}) %collective-permute-start.14) | collective-permute-done | bytes 917536 | tf_op jit(solution)/shard_map/ppermute | solution.py:11
  111.6 2.1 fusion.8
  115.2 13.5 %collective-permute-done.19 = bf16[224,2048]{1,0:T(8,128)(2,1)S(1)} collective-permute-done((bf16[224,2048]{1,0:T(8,128)(2,1)S(1)}, bf16[224,2048]{1,0:T(8,128)(2,1)S(1)}, u32[]{:S(2)}, u32[]{:S(2)}) %collective-permute-start.19) | collective-permute-done | bytes 917536 | tf_op jit(solution)/shard_map/ppermute | solution.py:11
  135.8 2.1 fusion.16
  139.1 12.5 %collective-permute-done.24 = bf16[224,2048]{1,0:T(8,128)(2,1)S(1)} collective-permute-done((bf16[224,2048]{1,0:T(8,128)(2,1)S(1)}, bf16[224,2048]{1,0:T(8,128)(2,1)S(1)}, u32[]{:S(2)}, u32[]{:S(2)}) %collective-permute-start.24) | collective-permute-done | bytes 917536 | tf_op jit(solution)/shard_map/ppermute | solution.py:11
  157.5 2.1 fusion.24
  161.1 11.5 %collective-permute-done.29 = bf16[224,2048]{1,0:T(8,128)(2,1)S(1)} collective-permute-done((bf16[224,2048]{1,0:T(8,128)(2,1)S(1)}, bf16[224,2048]{1,0:T(8,128)(2,1)S(1)}, u32[]{:S(2)}, u32[]{:S(2)}) %collective-permute-start.29) | collective-permute-done | bytes 917536 | tf_op jit(solution)/shard_map/ppermute | solution.py:11
  178.9 2.1 fusion.32
  182.3 12.4 %collective-permute-done.34 = bf16[224,2048]{1,0:T(8,128)(2,1)S(1)} collective-permute-done((bf16[224,2048]{1,0:T(8,128)(2,1)S(1)}, bf16[224,2048]{1,0:T(8,128)(2,1)S(1)}, u32[]{:S(2)}, u32[]{:S(2)}) %collective-permute-start.34) | collective-permute-done | bytes 917536 | tf_op jit(solution)/shard_map/ppermute | solution.py:11
  195.1 2.1 fusion.40
  202.8 6.7 %collective-permute-done.37 = f32[896,112]{0,1:T(8,128)S(1)} collective-permute-done((f32[896,112]{0,1:T(8,128)S(1)}, f32[896,112]{0,1:T(8,128)S(1)}, u32[]{:S(2)}, u32[]{:S(2)}) %collective-permute-start.37) | collective-permute-done | bytes 401440 | tf_op jit(solution)/shard_map/ppermute | solution.py:107
  210.4 3.9 %collective-permute-done.38 = bf16[112,2048]{1,0:T(8,128)(2,1)S(1)} collective-permute-done((bf16[112,2048]{1,0:T(8,128)(2,1)S(1)}, bf16[112,2048]{1,0:T(8,128)(2,1)S(1)}, u32[]{:S(2)}, u32[]{:S(2)}) %collective-permute-start.38) | collective-permute-done | bytes 458784 | tf_op jit(solution)/shard_map/ppermute | solution.py:11
  214.2 3.1 %collective-permute-done.39 = bf16[112,2048]{1,0:T(8,128)(2,1)S(1)} collective-permute-done((bf16[112,2048]{1,0:T(8,128)(2,1)S(1)}, bf16[112,2048]{1,0:T(8,128)(2,1)S(1)}, u32[]{:S(2)}, u32[]{:S(2)}) %collective-permute-start.39) | collective-permute-done | bytes 458784 | tf_op jit(solution)/shard_map/ppermute | solution.py:11
  217.6 2.1 fusion.48
  222.9 9.0 %collective-permute-done.41 = f32[896,112]{0,1:T(8,128)S(1)} collective-permute-done((f32[896,112]{0,1:T(8,128)S(1)}, f32[896,112]{0,1:T(8,128)S(1)}, u32[]{:S(2)}, u32[]{:S(2)}) %collective-permute-start.41) | collective-permute-done | bytes 401440 | tf_op jit(solution)/shard_map/ppermute | solution.py:107
  232.9 3.5 %collective-permute-done.42 = bf16[112,2048]{1,0:T(8,128)(2,1)S(1)} collective-permute-done((bf16[112,2048]{1,0:T(8,128)(2,1)S(1)}, bf16[112,2048]{1,0:T(8,128)(2,1)S(1)}, u32[]{:S(2)}, u32[]{:S(2)}) %collective-permute-start.42) | collective-permute-done | bytes 458784 | tf_op jit(solution)/shard_map/ppermute | solution.py:11
  238.3 2.1 fusion.56
  244.4 5.5 %collective-permute-done.43 = f32[896,112]{0,1:T(8,128)} collective-permute-done((f32[896,112]{0,1:T(8,128)}, f32[896,112]{0,1:T(8,128)}, u32[]{:S(2)}, u32[]{:S(2)}) %collective-permute-start.43) | collective-permute-done | bytes 401440 | tf_op jit(solution)/shard_map/ppermute | solution.py:107
  251.4 5.3 %collective-permute-done.44 = f32[896,112]{0,1:T(8,128)} collective-permute-done((f32[896,112]{0,1:T(8,128)}, f32[896,112]{0,1:T(8,128)}, u32[]{:S(2)}, u32[]{:S(2)}) %collective-permute-start.44) | collective-permute-done | bytes 401440 | tf_op jit(solution)/shard_map/ppermute | solution.py:92
  256.7 9.1 %collective-permute-done.45 = f32[896,112]{0,1:T(8,128)} collective-permute-done((f32[896,112]{0,1:T(8,128)}, f32[896,112]{0,1:T(8,128)}, u32[]{:S(2)}, u32[]{:S(2)}) %collective-permute-start.45) | collective-permute-done | bytes 401440 | tf_op jit(solution)/shard_map/ppermute | solution.py:92
  267.9 3.0 %copy.2 = f32[896,896]{1,0:T(8,128)} copy(f32[896,896]{0,1:T(8,128)S(1)} %broadcast_multiply_fusion) | data formatting | bytes 6422528 | tf_op jit(solution)/shard_map/div | solution.py:141
  (202 shorter events, 72.9 us)
Async XLA Ops:
  31.2 22.8 %collective-permute-start.5 = (bf16[224,2048]{1,0:T(8,128)(2,1)S(1)}, bf16[224,2048]{1,0:T(8,128)(2,1)S(1)}, u32[]{:S(2)}, u32[]{:S(2)}) collective-permute-start(bf16[224,2048]{1,0:T(8,128)(2,1)S(1)} %pad_maximum_fusion.12), channel_id=1, source_target_pairs={{4,0},{12,8},{20,16},{28,24},{5,1},{13,9},{21,17},{29,25},{6,2},{1... | collective-permute-start | bytes 2752520 | tf_op jit(solution)/shard_map/ppermute | solution.py:11
  32.5 22.5 %collective-permute-start.6 = (bf16[112,2048]{1,0:T(8,128)(2,1)S(1)}, bf16[112,2048]{1,0:T(8,128)(2,1)S(1)}, u32[]{:S(2)}, u32[]{:S(2)}) collective-permute-start(bf16[112,2048]{1,0:T(8,128)(2,1)S(1)} %collective-permute-done.4), channel_id=1, source_target_pairs={{0,4},{8,12},{16,20},{24,28},{1,5},{9,13},{17,21},{25,29},{2,6},{1... | collective-permute-start | bytes 1376264 | tf_op jit(solution)/shard_map/ppermute | solution.py:11
  37.1 17.9 %collective-permute-start.7 = (bf16[112,2048]{1,0:T(8,128)(2,1)S(1)}, bf16[112,2048]{1,0:T(8,128)(2,1)S(1)}, u32[]{:S(2)}, u32[]{:S(2)}) collective-permute-start(bf16[112,2048]{1,0:T(8,128)(2,1)S(1)} %get-tuple-element.165), channel_id=1, source_target_pairs={{8,0},{12,4},{16,8},{20,12},{24,16},{28,20},{9,1},{13,5},{17,9},{2... | collective-permute-start | bytes 1376264 | tf_op jit(solution)/shard_map/ppermute | solution.py:11
  57.2 22.1 %collective-permute-start.10 = (bf16[224,2048]{1,0:T(8,128)(2,1)}, bf16[224,2048]{1,0:T(8,128)(2,1)}, u32[]{:S(2)}, u32[]{:S(2)}) collective-permute-start(bf16[224,2048]{1,0:T(8,128)(2,1)} %get-tuple-element.401), channel_id=1, source_target_pairs={{8,0},{12,4},{16,8},{20,12},{24,16},{28,20},{9,1},{13,5},{17,9},{2... | collective-permute-start | bytes 2752520 | tf_op jit(solution)/shard_map/ppermute | solution.py:11
  58.5 22.2 %collective-permute-start.8 = (bf16[224,2048]{1,0:T(8,128)(2,1)}, bf16[224,2048]{1,0:T(8,128)(2,1)}, u32[]{:S(2)}, u32[]{:S(2)}) collective-permute-start(bf16[224,2048]{1,0:T(8,128)(2,1)} %get-tuple-element.402), channel_id=1, source_target_pairs={{4,0},{12,8},{20,16},{28,24},{5,1},{13,9},{21,17},{29,25},{6,2},{1... | collective-permute-start | bytes 2752520 | tf_op jit(solution)/shard_map/ppermute | solution.py:11
  59.8 22.1 %collective-permute-start.9 = (bf16[112,2048]{1,0:T(8,128)(2,1)}, bf16[112,2048]{1,0:T(8,128)(2,1)S(1)}, u32[]{:S(2)}, u32[]{:S(2)}) collective-permute-start(bf16[112,2048]{1,0:T(8,128)(2,1)} %copy-done.17), channel_id=1, source_target_pairs={{0,4},{8,12},{16,20},{24,28},{1,5},{9,13},{17,21},{25,29},{2,6},{1... | collective-permute-start | bytes 1376264 | tf_op jit(solution)/shard_map/ppermute | solution.py:11
  82.0 24.2 %collective-permute-start.13 = (bf16[112,2048]{1,0:T(8,128)(2,1)S(1)}, bf16[112,2048]{1,0:T(8,128)(2,1)S(1)}, u32[]{:S(2)}, u32[]{:S(2)}) collective-permute-start(bf16[112,2048]{1,0:T(8,128)(2,1)S(1)} %get-tuple-element.206), channel_id=1, source_target_pairs={{0,4},{8,12},{16,20},{24,28},{1,5},{9,13},{17,21},{25,29},{2,6},{1... | collective-permute-start | bytes 1376264 | tf_op jit(solution)/shard_map/ppermute | solution.py:11
  84.1 20.9 %collective-permute-start.14 = (bf16[224,2048]{1,0:T(8,128)(2,1)S(1)}, bf16[224,2048]{1,0:T(8,128)(2,1)S(1)}, u32[]{:S(2)}, u32[]{:S(2)}) collective-permute-start(bf16[224,2048]{1,0:T(8,128)(2,1)S(1)} %get-tuple-element.399), channel_id=1, source_target_pairs={{8,0},{12,4},{16,8},{20,12},{24,16},{28,20},{9,1},{13,5},{17,9},{2... | collective-permute-start | bytes 2752520 | tf_op jit(solution)/shard_map/ppermute | solution.py:11
  85.4 20.6 %collective-permute-start.12 = (bf16[224,2048]{1,0:T(8,128)(2,1)S(1)}, bf16[224,2048]{1,0:T(8,128)(2,1)S(1)}, u32[]{:S(2)}, u32[]{:S(2)}) collective-permute-start(bf16[224,2048]{1,0:T(8,128)(2,1)S(1)} %get-tuple-element.400), channel_id=1, source_target_pairs={{4,0},{12,8},{20,16},{28,24},{5,1},{13,9},{21,17},{29,25},{6,2},{1... | collective-permute-start | bytes 2752520 | tf_op jit(solution)/shard_map/ppermute | solution.py:11
  89.3 16.8 %collective-permute-start.11 = (f32[896,224]{0,1:T(8,128)S(1)}, f32[896,224]{0,1:T(8,128)S(1)}, u32[]{:S(2)}, u32[]{:S(2)}) collective-permute-start(f32[896,224]{0,1:T(8,128)S(1)} %maximum_select_fusion), channel_id=1, source_target_pairs={{0,1},{1,0},{2,3},{3,2},{4,5},{5,4},{6,7},{7,6},{8,9},{9,8},{10,11... | collective-permute-start | bytes 2408456 | tf_op jit(solution)/shard_map/ppermute | solution.py:97
  107.0 22.4 %collective-permute-start.17 = (bf16[112,2048]{1,0:T(8,128)(2,1)S(1)}, bf16[112,2048]{1,0:T(8,128)(2,1)S(1)}, u32[]{:S(2)}, u32[]{:S(2)}) collective-permute-start(bf16[112,2048]{1,0:T(8,128)(2,1)S(1)} %get-tuple-element.224), channel_id=1, source_target_pairs={{0,4},{8,12},{16,20},{24,28},{1,5},{9,13},{17,21},{25,29},{2,6},{1... | collective-permute-start | bytes 1376264 | tf_op jit(solution)/shard_map/ppermute | solution.py:11
  108.7 19.9 %collective-permute-start.19 = (bf16[224,2048]{1,0:T(8,128)(2,1)S(1)}, bf16[224,2048]{1,0:T(8,128)(2,1)S(1)}, u32[]{:S(2)}, u32[]{:S(2)}) collective-permute-start(bf16[224,2048]{1,0:T(8,128)(2,1)S(1)} %get-tuple-element.397), channel_id=1, source_target_pairs={{8,0},{12,4},{16,8},{20,12},{24,16},{28,20},{9,1},{13,5},{17,9},{2... | collective-permute-start | bytes 2752520 | tf_op jit(solution)/shard_map/ppermute | solution.py:11
  110.0 19.3 %collective-permute-start.16 = (bf16[224,2048]{1,0:T(8,128)(2,1)S(1)}, bf16[224,2048]{1,0:T(8,128)(2,1)S(1)}, u32[]{:S(2)}, u32[]{:S(2)}) collective-permute-start(bf16[224,2048]{1,0:T(8,128)(2,1)S(1)} %get-tuple-element.398), channel_id=1, source_target_pairs={{4,0},{12,8},{20,16},{28,24},{5,1},{13,9},{21,17},{29,25},{6,2},{1... | collective-permute-start | bytes 2752520 | tf_op jit(solution)/shard_map/ppermute | solution.py:11
  113.9 15.5 %collective-permute-start.15 = (f32[896,224]{0,1:T(8,128)S(1)}, f32[896,224]{0,1:T(8,128)S(1)}, u32[]{:S(2)}, u32[]{:S(2)}) collective-permute-start(f32[896,224]{0,1:T(8,128)S(1)} %maximum_select_fusion.1), channel_id=1, source_target_pairs={{0,1},{1,0},{2,3},{3,2},{4,5},{5,4},{6,7},{7,6},{8,9},{9,8},{10,11... | collective-permute-start | bytes 2408456 | tf_op jit(solution)/shard_map/ppermute | solution.py:97
  131.1 21.0 %collective-permute-start.22 = (bf16[112,2048]{1,0:T(8,128)(2,1)S(1)}, bf16[112,2048]{1,0:T(8,128)(2,1)S(1)}, u32[]{:S(2)}, u32[]{:S(2)}) collective-permute-start(bf16[112,2048]{1,0:T(8,128)(2,1)S(1)} %get-tuple-element.243), channel_id=1, source_target_pairs={{0,4},{8,12},{16,20},{24,28},{1,5},{9,13},{17,21},{25,29},{2,6},{1... | collective-permute-start | bytes 1376264 | tf_op jit(solution)/shard_map/ppermute | solution.py:11
  132.8 18.9 %collective-permute-start.24 = (bf16[224,2048]{1,0:T(8,128)(2,1)S(1)}, bf16[224,2048]{1,0:T(8,128)(2,1)S(1)}, u32[]{:S(2)}, u32[]{:S(2)}) collective-permute-start(bf16[224,2048]{1,0:T(8,128)(2,1)S(1)} %get-tuple-element.395), channel_id=1, source_target_pairs={{8,0},{12,4},{16,8},{20,12},{24,16},{28,20},{9,1},{13,5},{17,9},{2... | collective-permute-start | bytes 2752520 | tf_op jit(solution)/shard_map/ppermute | solution.py:11
  134.1 17.9 %collective-permute-start.21 = (bf16[224,2048]{1,0:T(8,128)(2,1)S(1)}, bf16[224,2048]{1,0:T(8,128)(2,1)S(1)}, u32[]{:S(2)}, u32[]{:S(2)}) collective-permute-start(bf16[224,2048]{1,0:T(8,128)(2,1)S(1)} %get-tuple-element.396), channel_id=1, source_target_pairs={{4,0},{12,8},{20,16},{28,24},{5,1},{13,9},{21,17},{29,25},{6,2},{1... | collective-permute-start | bytes 2752520 | tf_op jit(solution)/shard_map/ppermute | solution.py:11
  138.1 14.0 %collective-permute-start.20 = (f32[896,224]{0,1:T(8,128)S(1)}, f32[896,224]{0,1:T(8,128)S(1)}, u32[]{:S(2)}, u32[]{:S(2)}) collective-permute-start(f32[896,224]{0,1:T(8,128)S(1)} %maximum_select_fusion.2), channel_id=1, source_target_pairs={{0,1},{1,0},{2,3},{3,2},{4,5},{5,4},{6,7},{7,6},{8,9},{9,8},{10,11... | collective-permute-start | bytes 2408456 | tf_op jit(solution)/shard_map/ppermute | solution.py:97
  153.0 19.8 %collective-permute-start.27 = (bf16[112,2048]{1,0:T(8,128)(2,1)S(1)}, bf16[112,2048]{1,0:T(8,128)(2,1)S(1)}, u32[]{:S(2)}, u32[]{:S(2)}) collective-permute-start(bf16[112,2048]{1,0:T(8,128)(2,1)S(1)} %get-tuple-element.263), channel_id=1, source_target_pairs={{0,4},{8,12},{16,20},{24,28},{1,5},{9,13},{17,21},{25,29},{2,6},{1... | collective-permute-start | bytes 1376264 | tf_op jit(solution)/shard_map/ppermute | solution.py:11
  154.7 17.9 %collective-permute-start.29 = (bf16[224,2048]{1,0:T(8,128)(2,1)S(1)}, bf16[224,2048]{1,0:T(8,128)(2,1)S(1)}, u32[]{:S(2)}, u32[]{:S(2)}) collective-permute-start(bf16[224,2048]{1,0:T(8,128)(2,1)S(1)} %get-tuple-element.393), channel_id=1, source_target_pairs={{8,0},{12,4},{16,8},{20,12},{24,16},{28,20},{9,1},{13,5},{17,9},{2... | collective-permute-start | bytes 2752520 | tf_op jit(solution)/shard_map/ppermute | solution.py:11
  156.0 16.7 %collective-permute-start.26 = (bf16[224,2048]{1,0:T(8,128)(2,1)S(1)}, bf16[224,2048]{1,0:T(8,128)(2,1)S(1)}, u32[]{:S(2)}, u32[]{:S(2)}) collective-permute-start(bf16[224,2048]{1,0:T(8,128)(2,1)S(1)} %get-tuple-element.394), channel_id=1, source_target_pairs={{4,0},{12,8},{20,16},{28,24},{5,1},{13,9},{21,17},{29,25},{6,2},{1... | collective-permute-start | bytes 2752520 | tf_op jit(solution)/shard_map/ppermute | solution.py:11
  174.4 20.5 %collective-permute-start.32 = (bf16[112,2048]{1,0:T(8,128)(2,1)S(1)}, bf16[112,2048]{1,0:T(8,128)(2,1)S(1)}, u32[]{:S(2)}, u32[]{:S(2)}) collective-permute-start(bf16[112,2048]{1,0:T(8,128)(2,1)S(1)} %get-tuple-element.283), channel_id=1, source_target_pairs={{0,4},{8,12},{16,20},{24,28},{1,5},{9,13},{17,21},{25,29},{2,6},{1... | collective-permute-start | bytes 1376264 | tf_op jit(solution)/shard_map/ppermute | solution.py:11
  176.1 18.6 %collective-permute-start.34 = (bf16[224,2048]{1,0:T(8,128)(2,1)S(1)}, bf16[224,2048]{1,0:T(8,128)(2,1)S(1)}, u32[]{:S(2)}, u32[]{:S(2)}) collective-permute-start(bf16[224,2048]{1,0:T(8,128)(2,1)S(1)} %get-tuple-element.391), channel_id=1, source_target_pairs={{8,0},{12,4},{16,8},{20,12},{24,16},{28,20},{9,1},{13,5},{17,9},{2... | collective-permute-start | bytes 2752520 | tf_op jit(solution)/shard_map/ppermute | solution.py:11
  177.4 17.4 %collective-permute-start.31 = (bf16[224,2048]{1,0:T(8,128)(2,1)S(1)}, bf16[224,2048]{1,0:T(8,128)(2,1)S(1)}, u32[]{:S(2)}, u32[]{:S(2)}) collective-permute-start(bf16[224,2048]{1,0:T(8,128)(2,1)S(1)} %get-tuple-element.392), channel_id=1, source_target_pairs={{4,0},{12,8},{20,16},{28,24},{5,1},{13,9},{21,17},{29,25},{6,2},{1... | collective-permute-start | bytes 2752520 | tf_op jit(solution)/shard_map/ppermute | solution.py:11
  197.4 19.9 %collective-permute-start.35 = (f32[896,224]{0,1:T(8,128)S(1)}, f32[896,224]{0,1:T(8,128)S(1)}, u32[]{:S(2)}, u32[]{:S(2)}) collective-permute-start(f32[896,224]{0,1:T(8,128)S(1)} %maximum_select_fusion.5), channel_id=1, source_target_pairs={{0,1},{1,0},{2,3},{3,2},{4,5},{5,4},{6,7},{7,6},{8,9},{9,8},{10,11... | collective-permute-start | bytes 2408456 | tf_op jit(solution)/shard_map/ppermute | solution.py:97
  200.0 14.3 %collective-permute-start.38 = (bf16[112,2048]{1,0:T(8,128)(2,1)S(1)}, bf16[112,2048]{1,0:T(8,128)(2,1)S(1)}, u32[]{:S(2)}, u32[]{:S(2)}) collective-permute-start(bf16[112,2048]{1,0:T(8,128)(2,1)S(1)} %get-tuple-element.312), channel_id=1, source_target_pairs={{4,0},{12,8},{20,16},{28,24},{5,1},{13,9},{21,17},{29,25},{6,2},{1... | collective-permute-start | bytes 1376264 | tf_op jit(solution)/shard_map/ppermute | solution.py:11
  201.3 16.1 %collective-permute-start.39 = (bf16[112,2048]{1,0:T(8,128)(2,1)S(1)}, bf16[112,2048]{1,0:T(8,128)(2,1)S(1)}, u32[]{:S(2)}, u32[]{:S(2)}) collective-permute-start(bf16[112,2048]{1,0:T(8,128)(2,1)S(1)} %collective-permute-done.32), channel_id=1, source_target_pairs={{8,0},{12,4},{16,8},{20,12},{24,16},{28,20},{9,1},{13,5},{17,9},{2... | collective-permute-start | bytes 1376264 | tf_op jit(solution)/shard_map/ppermute | solution.py:11
  219.9 16.5 %collective-permute-start.40 = (f32[896,224]{0,1:T(8,128)S(1)}, f32[896,224]{0,1:T(8,128)S(1)}, u32[]{:S(2)}, u32[]{:S(2)}) collective-permute-start(f32[896,224]{0,1:T(8,128)S(1)} %maximum_select_fusion.6), channel_id=1, source_target_pairs={{0,1},{1,0},{2,3},{3,2},{4,5},{5,4},{6,7},{7,6},{8,9},{9,8},{10,11... | collective-permute-start | bytes 2408456 | tf_op jit(solution)/shard_map/ppermute | solution.py:97
  221.6 14.8 %collective-permute-start.42 = (bf16[112,2048]{1,0:T(8,128)(2,1)S(1)}, bf16[112,2048]{1,0:T(8,128)(2,1)S(1)}, u32[]{:S(2)}, u32[]{:S(2)}) collective-permute-start(bf16[112,2048]{1,0:T(8,128)(2,1)S(1)} %collective-permute-done.36), channel_id=1, source_target_pairs={{8,0},{12,4},{16,8},{20,12},{24,16},{28,20},{9,1},{13,5},{17,9},{2... | collective-permute-start | bytes 1376264 | tf_op jit(solution)/shard_map/ppermute | solution.py:11
  241.5 15.3 %collective-permute-start.44 = (f32[896,112]{0,1:T(8,128)}, f32[896,112]{0,1:T(8,128)}, u32[]{:S(2)}, u32[]{:S(2)}) collective-permute-start(f32[896,112]{0,1:T(8,128)} %get-tuple-element.336), channel_id=1, source_target_pairs={{0,3},{1,2},{2,1},{3,0},{4,7},{5,6},{6,5},{7,4},{8,11},{9,10},{10,... | collective-permute-start | bytes 1204232 | tf_op jit(solution)/shard_map/ppermute | solution.py:92
  242.7 14.0 %collective-permute-start.46 = (f32[896,112]{0,1:T(8,128)}, f32[896,112]{0,1:T(8,128)}, u32[]{:S(2)}, u32[]{:S(2)}) collective-permute-start(f32[896,112]{0,1:T(8,128)} %get-tuple-element.335), channel_id=1, source_target_pairs={{0,1},{1,0},{2,3},{3,2},{4,5},{5,4},{6,7},{7,6},{8,9},{9,8},{10,11... | collective-permute-start | bytes 1204232 | tf_op jit(solution)/shard_map/ppermute | solution.py:92
  243.8 22.1 %collective-permute-start.45 = (f32[896,112]{0,1:T(8,128)}, f32[896,112]{0,1:T(8,128)}, u32[]{:S(2)}, u32[]{:S(2)}) collective-permute-start(f32[896,112]{0,1:T(8,128)} %select_select_fusion.1), channel_id=1, source_target_pairs={{0,2},{1,3},{2,0},{3,1},{4,6},{5,7},{6,4},{7,5},{8,10},{9,11},{10,... | collective-permute-start | bytes 1204232 | tf_op jit(solution)/shard_map/ppermute | solution.py:92
  (38 other events, 606.2 us)

commit v3 on v2

--- a/solution.py
+++ b/solution.py
@@ -54,8 +54,10 @@
         [moments] + [lax.ppermute(moments, "samp", [(j, j ^ i) for j in range(groups)]) for i in flips])
     own_block = standardize(dosages, summed_moments[0], summed_moments[1], total)
     rows = own_block.shape[0]
-    step = rows // CHUNKS
-    pieces = [own_block[c * step:(c + 1) * step] for c in range(CHUNKS)]
+    edge = rows // (2 * CHUNKS - 2)
+    sizes = [edge] + [2 * edge] * (CHUNKS - 2) + [rows - edge * (2 * CHUNKS - 3)]
+    offsets = [sum(sizes[:c]) for c in range(CHUNKS)]
+    pieces = [own_block[offsets[c]:offsets[c] + sizes[c]] for c in range(CHUNKS)]
 
     odd = list(range(1, count, 2))
     even = list(range(0, count, 2))
@@ -79,6 +81,7 @@
             state["three_even"][c] + state["three_odd"][c],
         ], axis=0)
         gram = jnp.einsum("ab,cb->ac", own_block, blocks, preferred_element_type=jnp.float32)
+        step = sizes[c]
         tiles = [gram[:, k * step:(k + 1) * step] for k in range(BAND + 1)]
         state["tiles"][c] = tiles
         if c == CHUNKS - 1:
@@ -101,6 +104,7 @@
         return jnp.where(low, jnp.where(even_me, t[a], t[b]), jnp.where(even_me, t[d], t[e]))
 
     def second_level(c):
+        step = sizes[c]
         got = state["first"][c]
         mine = jnp.where(low, got[:, :step], got[:, step:])
         onward = jnp.where(low, got[:, step:], got[:, :step])
@@ -115,16 +119,16 @@
             sent = moved(joined([pieces[new] if new is not None else None,
                                  state["one_odd"][third] if third is not None else None]), z_down)
             if new is not None:
-                state["two"][new] = sent[:step]
+                state["two"][new] = sent[:sizes[new]]
             if third is not None:
-                state["three_odd"][third] = sent[-step:]
+                state["three_odd"][third] = sent[-sizes[third]:]
         if new is not None or second is not None:
             sent = moved(joined([pieces[new] if new is not None else None,
                                  state["two"][second] if second is not None else None]), odd_to_even)
             if new is not None:
-                state["one_even"][new] = sent[:step]
+                state["one_even"][new] = sent[:sizes[new]]
             if second is not None:
-                state["three_even"][second] = sent[-step:]
+                state["three_even"][second] = sent[-sizes[second]:]
         if second is not None:
             state["one_odd"][second] = moved(state["two"][second], even_to_odd)
         if 0 <= t - 3 < CHUNKS:

time: 272 us -> 276 us (1.015)
  starting transfers between devices: 57.3 us -> 62.6 us
  waiting for transfers between devices: 159 us -> 156 us
    ppermute x7, waiting for transfers between devices: 21.7 us -> 31.2 us  [second_level(): last = lax.ppermute(pick(c, 2, 3, 0, 1) + onward, 'samp', across)]
    ppermute x27, waiting for transfers between devices: 120 us -> 113 us  [moved(): return lax.ppermute(value, 'snp', pairs)]
    ppermute x3, waiting for transfers between devices: 14.4 us -> 8.62 us  [finish(): lax.ppermute(outgoing[i], 'samp', [(j, j ^ i) for j in range(groups)])]
    ppermute x27, starting transfers between devices: 44.4 us -> 49.3 us  [moved(): return lax.ppermute(value, 'snp', pairs)]
  transfers between devices with their start and end apart: 47 -> 47, of which waited for: 25 -> 25; matrix products, arithmetic and copies ran while one was open for 11% -> 10% of each run, Pallas kernels for 0% -> 0%
where the time goes in v3:
time: 276 us; the launch traced here: 275 us
  waiting for transfers between devices  156 us (57%)
  starting transfers between devices  62.6 us (23%)
  other arithmetic  25.2 us (9%)
  matrix products  18.9 us (7%)
  local copies, waits for them, and re-layouts  10.9 us (4%)
    ppermute x27, waiting for transfers between devices, moved(): return lax.ppermute(value, 'snp', pairs)  113 us
    ppermute x27, starting transfers between devices, moved(): return lax.ppermute(value, 'snp', pairs)  49.3 us
    ppermute x7, waiting for transfers between devices, second_level(): last = lax.ppermute(pick(c, 2, 3, 0, 1) + onward, 'samp', across)  31.2 us
    dot_general x8, matrix products, finish(): jnp.einsum('ab,cb->ac', own_block, blocks, preferred_element_type=jnp.flo...  18.9 us
    ppermute x3, waiting for transfers between devices, finish(): lax.ppermute(outgoing[i], 'samp', [(j, j ^ i) for j in range(groups)])  8.62 us
    ppermute x7, starting transfers between devices, second_level(): last = lax.ppermute(pick(c, 2, 3, 0, 1) + onward, 'samp', across)  7.55 us
  transfers between devices with their start and end apart: 47, of which 25 were waited for; matrix products, arithmetic and copies ran while one was open for 10% of the time, Pallas kernels for 0%

profile of v3, /device:TPU:0, one launch (start us, length us, event | category | flops | bytes accessed | tf_op | source)
XLA Modules:
  0.0 274.5 jit_solution(11381396782481176099)
XLA Ops:
  0.0 4.0 %fusion.74 = (f32[896]{0:T(1024)S(1)}, f32[896]{0:T(1024)S(1)}) fusion(f32[896,2048]{1,0:T(8,128)} %param.1), kind=kLoop, calls=%fused_computation.142 | loop fusion | flops 5503232 | bytes 7347200 | tf_op jit(solution)/shard_map/reduce_sum | solution.py:21
  4.1 2.4 collective-permute-start
  10.2 3.9 %multiply_convert_fusion = bf16[896,2048]{1,0:T(8,128)(2,1)S(1)} fusion(f32[896,2048]{1,0:T(8,128)} %param.1, f32[896]{0:T(1024)S(1)} %add_rsqrt_fusion, f32[896]{0:T(1024)S(1)} %get-tuple-element.325), kind=kLoop, calls=%fused_computation | loop fusion | flops 5505024 | bytes 11017216 | tf_op jit(solution)/shard_map/convert_element_type | solution.py:17
  17.9 6.6 %collective-permute-done.3 = bf16[64,2048]{1,0:T(8,128)(2,1)S(1)} collective-permute-done((bf16[64,2048]{1,0:T(8,128)(2,1)S(1)}, bf16[64,2048]{1,0:T(8,128)(2,1)S(1)}, u32[]{:S(2)}, u32[]{:S(2)}) %collective-permute-start.3) | collective-permute-done | bytes 262176 | tf_op jit(solution)/shard_map/ppermute | solution.py:11
  28.5 4.6 %collective-permute-start.6 = (bf16[64,2048]{1,0:T(8,128)(2,1)S(1)}, bf16[64,2048]{1,0:T(8,128)(2,1)S(1)}, u32[]{:S(2)}, u32[]{:S(2)}) collective-permute-start(bf16[64,2048]{1,0:T(8,128)(2,1)S(1)} %collective-permute-done.4), channel_id=1, source_target_pairs={{0,4},{8,12},{16,20},{24,28},{1,5},{9,13},{17,21},{25,29},{2,6},{1... | collective-permute-start | bytes 786440 | tf_op jit(solution)/shard_map/ppermute | solution.py:11
  33.2 12.7 %collective-permute-done.5 = bf16[192,2048]{1,0:T(8,128)(2,1)S(1)} collective-permute-done((bf16[192,2048]{1,0:T(8,128)(2,1)S(1)}, bf16[192,2048]{1,0:T(8,128)(2,1)S(1)}, u32[]{:S(2)}, u32[]{:S(2)}) %collective-permute-start.5) | collective-permute-done | bytes 786464 | tf_op jit(solution)/shard_map/ppermute | solution.py:11
  49.6 4.6 %collective-permute-start.9 = (bf16[128,2048]{1,0:T(8,128)(2,1)S(1)}, bf16[128,2048]{1,0:T(8,128)(2,1)S(1)}, u32[]{:S(2)}, u32[]{:S(2)}) collective-permute-start(bf16[128,2048]{1,0:T(8,128)(2,1)S(1)} %collective-permute-done.7), channel_id=1, source_target_pairs={{0,4},{8,12},{16,20},{24,28},{1,5},{9,13},{17,21},{25,29},{2,6},{1... | collective-permute-start | bytes 1572872 | tf_op jit(solution)/shard_map/ppermute | solution.py:11
  54.2 13.1 %collective-permute-done.10 = bf16[192,2048]{1,0:T(8,128)(2,1)S(1)} collective-permute-done((bf16[192,2048]{1,0:T(8,128)(2,1)S(1)}, bf16[192,2048]{1,0:T(8,128)(2,1)S(1)}, u32[]{:S(2)}, u32[]{:S(2)}) %collective-permute-start.10) | collective-permute-done | bytes 786464 | tf_op jit(solution)/shard_map/ppermute | solution.py:11
  68.1 3.4 %collective-permute-done.8 = bf16[256,2048]{1,0:T(8,128)(2,1)S(1)} collective-permute-done((bf16[256,2048]{1,0:T(8,128)(2,1)S(1)}, bf16[256,2048]{1,0:T(8,128)(2,1)S(1)}, u32[]{:S(2)}, u32[]{:S(2)}) %collective-permute-start.8) | collective-permute-done | bytes 1048608 | tf_op jit(solution)/shard_map/ppermute | solution.py:11
  81.2 3.4 %fusion.48 = f32[896,256]{0,1:T(8,128)S(1)} fusion(bf16[896,2048]{1,0:T(8,128)(2,1)} %copy-done, bf16[64,2048]{1,0:T(8,128)(2,1)S(1)} %add.150, bf16[64,2048]{1,0:T(8,128)(2,1)} %copy-done.21, bf16[64,2048]{1,0:T(8,128)(2,1)S(1)} %add.149, bf16[64,2048]{1,0:T(8,128)(2,1)} %copy-done.20), kind=kOutput, calls=%fused_computation.60 | convolution fusion | flops 943718400 | bytes 5636096 | tf_op jit(solution)/shard_map/ab,cb->ac/dot_general | solution.py:83
  84.8 14.2 %collective-permute-done.14 = bf16[256,2048]{1,0:T(8,128)(2,1)} collective-permute-done((bf16[256,2048]{1,0:T(8,128)(2,1)}, bf16[256,2048]{1,0:T(8,128)(2,1)}, u32[]{:S(2)}, u32[]{:S(2)}) %collective-permute-start.14) | collective-permute-done | bytes 1048608 | tf_op jit(solution)/shard_map/ppermute | solution.py:11
  107.3 2.4 fusion
  110.1 17.0 %collective-permute-done.19 = bf16[256,2048]{1,0:T(8,128)(2,1)S(1)} collective-permute-done((bf16[256,2048]{1,0:T(8,128)(2,1)S(1)}, bf16[256,2048]{1,0:T(8,128)(2,1)S(1)}, u32[]{:S(2)}, u32[]{:S(2)}) %collective-permute-start.19) | collective-permute-done | bytes 1048608 | tf_op jit(solution)/shard_map/ppermute | solution.py:11
  134.5 2.4 fusion.8
  137.3 15.8 %collective-permute-done.24 = bf16[256,2048]{1,0:T(8,128)(2,1)S(1)} collective-permute-done((bf16[256,2048]{1,0:T(8,128)(2,1)S(1)}, bf16[256,2048]{1,0:T(8,128)(2,1)S(1)}, u32[]{:S(2)}, u32[]{:S(2)}) %collective-permute-start.24) | collective-permute-done | bytes 1048608 | tf_op jit(solution)/shard_map/ppermute | solution.py:11
  163.4 14.2 %collective-permute-done.29 = bf16[256,2048]{1,0:T(8,128)(2,1)S(1)} collective-permute-done((bf16[256,2048]{1,0:T(8,128)(2,1)S(1)}, bf16[256,2048]{1,0:T(8,128)(2,1)S(1)}, u32[]{:S(2)}, u32[]{:S(2)}) %collective-permute-start.29) | collective-permute-done | bytes 1048608 | tf_op jit(solution)/shard_map/ppermute | solution.py:11
  177.8 3.1 %collective-permute-done.26 = bf16[256,2048]{1,0:T(8,128)(2,1)S(1)} collective-permute-done((bf16[256,2048]{1,0:T(8,128)(2,1)S(1)}, bf16[256,2048]{1,0:T(8,128)(2,1)S(1)}, u32[]{:S(2)}, u32[]{:S(2)}) %collective-permute-start.26) | collective-permute-done | bytes 1048608 | tf_op jit(solution)/shard_map/ppermute | solution.py:11
  184.1 2.4 fusion.24
  188.2 4.8 %collective-permute-start.32 = (bf16[128,2048]{1,0:T(8,128)(2,1)S(1)}, bf16[128,2048]{1,0:T(8,128)(2,1)S(1)}, u32[]{:S(2)}, u32[]{:S(2)}) collective-permute-start(bf16[128,2048]{1,0:T(8,128)(2,1)S(1)} %get-tuple-element.283), channel_id=1, source_target_pairs={{0,4},{8,12},{16,20},{24,28},{1,5},{9,13},{17,21},{25,29},{2,6},{1... | collective-permute-start | bytes 1572872 | tf_op jit(solution)/shard_map/ppermute | solution.py:11
  193.0 6.8 %collective-permute-done.33 = f32[896,128]{0,1:T(8,128)S(1)} collective-permute-done((f32[896,128]{0,1:T(8,128)S(1)}, f32[896,128]{0,1:T(8,128)S(1)}, u32[]{:S(2)}, u32[]{:S(2)}) %collective-permute-start.33) | collective-permute-done | bytes 458784 | tf_op jit(solution)/shard_map/ppermute | solution.py:111
  200.9 3.4 %collective-permute-done.32 = bf16[128,2048]{1,0:T(8,128)(2,1)S(1)} collective-permute-done((bf16[128,2048]{1,0:T(8,128)(2,1)S(1)}, bf16[128,2048]{1,0:T(8,128)(2,1)S(1)}, u32[]{:S(2)}, u32[]{:S(2)}) %collective-permute-start.32) | collective-permute-done | bytes 524320 | tf_op jit(solution)/shard_map/ppermute | solution.py:11
  204.6 2.4 fusion.32
  209.6 4.4 %collective-permute-start.36 = (bf16[64,2048]{1,0:T(8,128)(2,1)S(1)}, bf16[64,2048]{1,0:T(8,128)(2,1)S(1)}, u32[]{:S(2)}, u32[]{:S(2)}) collective-permute-start(bf16[64,2048]{1,0:T(8,128)(2,1)S(1)} %slice.404), channel_id=1, source_target_pairs={{0,4},{8,12},{16,20},{24,28},{1,5},{9,13},{17,21},{25,29},{2,6},{1... | collective-permute-start | bytes 786440 | tf_op jit(solution)/shard_map/ppermute | solution.py:11
  215.3 5.1 %collective-permute-done.37 = f32[896,128]{0,1:T(8,128)S(1)} collective-permute-done((f32[896,128]{0,1:T(8,128)S(1)}, f32[896,128]{0,1:T(8,128)S(1)}, u32[]{:S(2)}, u32[]{:S(2)}) %collective-permute-start.37) | collective-permute-done | bytes 458784 | tf_op jit(solution)/shard_map/ppermute | solution.py:111
  221.3 2.7 collective-permute-done.38
  224.0 2.8 %collective-permute-done.39 = bf16[128,2048]{1,0:T(8,128)(2,1)S(1)} collective-permute-done((bf16[128,2048]{1,0:T(8,128)(2,1)S(1)}, bf16[128,2048]{1,0:T(8,128)(2,1)S(1)}, u32[]{:S(2)}, u32[]{:S(2)}) %collective-permute-start.39) | collective-permute-done | bytes 524320 | tf_op jit(solution)/shard_map/ppermute | solution.py:11
  227.1 2.4 fusion.40
  232.5 10.4 %collective-permute-done.41 = f32[896,128]{0,1:T(8,128)S(1)} collective-permute-done((f32[896,128]{0,1:T(8,128)S(1)}, f32[896,128]{0,1:T(8,128)S(1)}, u32[]{:S(2)}, u32[]{:S(2)}) %collective-permute-start.41) | collective-permute-done | bytes 458784 | tf_op jit(solution)/shard_map/ppermute | solution.py:111
  251.1 3.9 %collective-permute-done.44 = f32[896,64]{0,1:T(8,128)} collective-permute-done((f32[896,64]{0,1:T(8,128)}, f32[896,64]{0,1:T(8,128)}, u32[]{:S(2)}, u32[]{:S(2)}) %collective-permute-start.44) | collective-permute-done | bytes 229408 | tf_op jit(solution)/shard_map/ppermute | solution.py:95
  255.0 4.7 %collective-permute-done.45 = f32[896,64]{0,1:T(8,128)} collective-permute-done((f32[896,64]{0,1:T(8,128)}, f32[896,64]{0,1:T(8,128)}, u32[]{:S(2)}, u32[]{:S(2)}) %collective-permute-start.45) | collective-permute-done | bytes 229408 | tf_op jit(solution)/shard_map/ppermute | solution.py:95
  261.1 8.5 %collective-permute-done.43 = f32[896,128]{0,1:T(8,128)} collective-permute-done((f32[896,128]{0,1:T(8,128)}, f32[896,128]{0,1:T(8,128)}, u32[]{:S(2)}, u32[]{:S(2)}) %collective-permute-start.43) | collective-permute-done | bytes 458784 | tf_op jit(solution)/shard_map/ppermute | solution.py:111
  271.6 3.0 %copy.2 = f32[896,896]{1,0:T(8,128)} copy(f32[896,896]{0,1:T(8,128)S(1)} %broadcast_multiply_fusion) | data formatting | bytes 6422528 | tf_op jit(solution)/shard_map/div | solution.py:145
  (210 shorter events, 77.8 us)
Async XLA Ops:
  25.9 19.9 %collective-permute-start.5 = (bf16[192,2048]{1,0:T(8,128)(2,1)S(1)}, bf16[192,2048]{1,0:T(8,128)(2,1)S(1)}, u32[]{:S(2)}, u32[]{:S(2)}) collective-permute-start(bf16[192,2048]{1,0:T(8,128)(2,1)S(1)} %pad_maximum_fusion.11), channel_id=1, source_target_pairs={{4,0},{12,8},{20,16},{28,24},{5,1},{13,9},{21,17},{29,25},{6,2},{1... | collective-permute-start | bytes 2359304 | tf_op jit(solution)/shard_map/ppermute | solution.py:11
  27.2 18.7 %collective-permute-start.7 = (bf16[128,2048]{1,0:T(8,128)(2,1)S(1)}, bf16[128,2048]{1,0:T(8,128)(2,1)S(1)}, u32[]{:S(2)}, u32[]{:S(2)}) collective-permute-start(bf16[128,2048]{1,0:T(8,128)(2,1)S(1)} %get-tuple-element.165), channel_id=1, source_target_pairs={{8,0},{12,4},{16,8},{20,12},{24,16},{28,20},{9,1},{13,5},{17,9},{2... | collective-permute-start | bytes 1572872 | tf_op jit(solution)/shard_map/ppermute | solution.py:11
  28.5 17.4 %collective-permute-start.6 = (bf16[64,2048]{1,0:T(8,128)(2,1)S(1)}, bf16[64,2048]{1,0:T(8,128)(2,1)S(1)}, u32[]{:S(2)}, u32[]{:S(2)}) collective-permute-start(bf16[64,2048]{1,0:T(8,128)(2,1)S(1)} %collective-permute-done.4), channel_id=1, source_target_pairs={{0,4},{8,12},{16,20},{24,28},{1,5},{9,13},{17,21},{25,29},{2,6},{1... | collective-permute-start | bytes 786440 | tf_op jit(solution)/shard_map/ppermute | solution.py:11
  46.9 24.6 %collective-permute-start.8 = (bf16[256,2048]{1,0:T(8,128)(2,1)S(1)}, bf16[256,2048]{1,0:T(8,128)(2,1)S(1)}, u32[]{:S(2)}, u32[]{:S(2)}) collective-permute-start(bf16[256,2048]{1,0:T(8,128)(2,1)S(1)} %pad_maximum_fusion.8), channel_id=1, source_target_pairs={{4,0},{12,8},{20,16},{28,24},{5,1},{13,9},{21,17},{29,25},{6,2},{1... | collective-permute-start | bytes 3145736 | tf_op jit(solution)/shard_map/ppermute | solution.py:11
  48.3 19.0 %collective-permute-start.10 = (bf16[192,2048]{1,0:T(8,128)(2,1)S(1)}, bf16[192,2048]{1,0:T(8,128)(2,1)S(1)}, u32[]{:S(2)}, u32[]{:S(2)}) collective-permute-start(bf16[192,2048]{1,0:T(8,128)(2,1)S(1)} %pad_maximum_fusion.12), channel_id=1, source_target_pairs={{8,0},{12,4},{16,8},{20,12},{24,16},{28,20},{9,1},{13,5},{17,9},{2... | collective-permute-start | bytes 2359304 | tf_op jit(solution)/shard_map/ppermute | solution.py:11
  49.6 23.0 %collective-permute-start.9 = (bf16[128,2048]{1,0:T(8,128)(2,1)S(1)}, bf16[128,2048]{1,0:T(8,128)(2,1)S(1)}, u32[]{:S(2)}, u32[]{:S(2)}) collective-permute-start(bf16[128,2048]{1,0:T(8,128)(2,1)S(1)} %collective-permute-done.7), channel_id=1, source_target_pairs={{0,4},{8,12},{16,20},{24,28},{1,5},{9,13},{17,21},{25,29},{2,6},{1... | collective-permute-start | bytes 1572872 | tf_op jit(solution)/shard_map/ppermute | solution.py:11
  75.0 24.0 %collective-permute-start.14 = (bf16[256,2048]{1,0:T(8,128)(2,1)}, bf16[256,2048]{1,0:T(8,128)(2,1)}, u32[]{:S(2)}, u32[]{:S(2)}) collective-permute-start(bf16[256,2048]{1,0:T(8,128)(2,1)} %get-tuple-element.389), channel_id=1, source_target_pairs={{8,0},{12,4},{16,8},{20,12},{24,16},{28,20},{9,1},{13,5},{17,9},{2... | collective-permute-start | bytes 3145736 | tf_op jit(solution)/shard_map/ppermute | solution.py:11
  76.3 25.3 %collective-permute-start.13 = (bf16[128,2048]{1,0:T(8,128)(2,1)}, bf16[128,2048]{1,0:T(8,128)(2,1)S(1)}, u32[]{:S(2)}, u32[]{:S(2)}) collective-permute-start(bf16[128,2048]{1,0:T(8,128)(2,1)} %copy-done.5), channel_id=1, source_target_pairs={{0,4},{8,12},{16,20},{24,28},{1,5},{9,13},{17,21},{25,29},{2,6},{1... | collective-permute-start | bytes 1572872 | tf_op jit(solution)/shard_map/ppermute | solution.py:11
  77.8 23.8 %collective-permute-start.12 = (bf16[256,2048]{1,0:T(8,128)(2,1)}, bf16[256,2048]{1,0:T(8,128)(2,1)S(1)}, u32[]{:S(2)}, u32[]{:S(2)}) collective-permute-start(bf16[256,2048]{1,0:T(8,128)(2,1)} %get-tuple-element.390), channel_id=1, source_target_pairs={{4,0},{12,8},{20,16},{28,24},{5,1},{13,9},{21,17},{29,25},{6,2},{1... | collective-permute-start | bytes 3145736 | tf_op jit(solution)/shard_map/ppermute | solution.py:11
  84.7 16.9 %collective-permute-start.11 = (f32[896,128]{0,1:T(8,128)S(1)}, f32[896,128]{0,1:T(8,128)S(1)}, u32[]{:S(2)}, u32[]{:S(2)}) collective-permute-start(f32[896,128]{0,1:T(8,128)S(1)} %maximum_select_fusion.6), channel_id=1, source_target_pairs={{0,1},{1,0},{2,3},{3,2},{4,5},{5,4},{6,7},{7,6},{8,9},{9,8},{10,11... | collective-permute-start | bytes 1376264 | tf_op jit(solution)/shard_map/ppermute | solution.py:100
  102.4 25.8 %collective-permute-start.17 = (bf16[128,2048]{1,0:T(8,128)(2,1)S(1)}, bf16[128,2048]{1,0:T(8,128)(2,1)S(1)}, u32[]{:S(2)}, u32[]{:S(2)}) collective-permute-start(bf16[128,2048]{1,0:T(8,128)(2,1)S(1)} %get-tuple-element.224), channel_id=1, source_target_pairs={{0,4},{8,12},{16,20},{24,28},{1,5},{9,13},{17,21},{25,29},{2,6},{1... | collective-permute-start | bytes 1572872 | tf_op jit(solution)/shard_map/ppermute | solution.py:11
  104.4 22.7 %collective-permute-start.19 = (bf16[256,2048]{1,0:T(8,128)(2,1)S(1)}, bf16[256,2048]{1,0:T(8,128)(2,1)S(1)}, u32[]{:S(2)}, u32[]{:S(2)}) collective-permute-start(bf16[256,2048]{1,0:T(8,128)(2,1)S(1)} %get-tuple-element.387), channel_id=1, source_target_pairs={{8,0},{12,4},{16,8},{20,12},{24,16},{28,20},{9,1},{13,5},{17,9},{2... | collective-permute-start | bytes 3145736 | tf_op jit(solution)/shard_map/ppermute | solution.py:11
  105.7 22.3 %collective-permute-start.16 = (bf16[256,2048]{1,0:T(8,128)(2,1)S(1)}, bf16[256,2048]{1,0:T(8,128)(2,1)S(1)}, u32[]{:S(2)}, u32[]{:S(2)}) collective-permute-start(bf16[256,2048]{1,0:T(8,128)(2,1)S(1)} %get-tuple-element.388), channel_id=1, source_target_pairs={{4,0},{12,8},{20,16},{28,24},{5,1},{13,9},{21,17},{29,25},{6,2},{1... | collective-permute-start | bytes 3145736 | tf_op jit(solution)/shard_map/ppermute | solution.py:11
  109.9 18.2 %collective-permute-start.15 = (f32[896,256]{0,1:T(8,128)S(1)}, f32[896,256]{0,1:T(8,128)S(1)}, u32[]{:S(2)}, u32[]{:S(2)}) collective-permute-start(f32[896,256]{0,1:T(8,128)S(1)} %maximum_select_fusion), channel_id=1, source_target_pairs={{0,1},{1,0},{2,3},{3,2},{4,5},{5,4},{6,7},{7,6},{8,9},{9,8},{10,11... | collective-permute-start | bytes 2752520 | tf_op jit(solution)/shard_map/ppermute | solution.py:100
  129.7 24.1 %collective-permute-start.22 = (bf16[128,2048]{1,0:T(8,128)(2,1)S(1)}, bf16[128,2048]{1,0:T(8,128)(2,1)S(1)}, u32[]{:S(2)}, u32[]{:S(2)}) collective-permute-start(bf16[128,2048]{1,0:T(8,128)(2,1)S(1)} %get-tuple-element.243), channel_id=1, source_target_pairs={{0,4},{8,12},{16,20},{24,28},{1,5},{9,13},{17,21},{25,29},{2,6},{1... | collective-permute-start | bytes 1572872 | tf_op jit(solution)/shard_map/ppermute | solution.py:11
  131.4 21.7 %collective-permute-start.24 = (bf16[256,2048]{1,0:T(8,128)(2,1)S(1)}, bf16[256,2048]{1,0:T(8,128)(2,1)S(1)}, u32[]{:S(2)}, u32[]{:S(2)}) collective-permute-start(bf16[256,2048]{1,0:T(8,128)(2,1)S(1)} %get-tuple-element.385), channel_id=1, source_target_pairs={{8,0},{12,4},{16,8},{20,12},{24,16},{28,20},{9,1},{13,5},{17,9},{2... | collective-permute-start | bytes 3145736 | tf_op jit(solution)/shard_map/ppermute | solution.py:11
  132.7 21.0 %collective-permute-start.21 = (bf16[256,2048]{1,0:T(8,128)(2,1)S(1)}, bf16[256,2048]{1,0:T(8,128)(2,1)S(1)}, u32[]{:S(2)}, u32[]{:S(2)}) collective-permute-start(bf16[256,2048]{1,0:T(8,128)(2,1)S(1)} %get-tuple-element.386), channel_id=1, source_target_pairs={{4,0},{12,8},{20,16},{28,24},{5,1},{13,9},{21,17},{29,25},{6,2},{1... | collective-permute-start | bytes 3145736 | tf_op jit(solution)/shard_map/ppermute | solution.py:11
  137.1 16.7 %collective-permute-start.20 = (f32[896,256]{0,1:T(8,128)S(1)}, f32[896,256]{0,1:T(8,128)S(1)}, u32[]{:S(2)}, u32[]{:S(2)}) collective-permute-start(f32[896,256]{0,1:T(8,128)S(1)} %maximum_select_fusion.1), channel_id=1, source_target_pairs={{0,1},{1,0},{2,3},{3,2},{4,5},{5,4},{6,7},{7,6},{8,9},{9,8},{10,11... | collective-permute-start | bytes 2752520 | tf_op jit(solution)/shard_map/ppermute | solution.py:100
  154.8 26.1 %collective-permute-start.27 = (bf16[128,2048]{1,0:T(8,128)(2,1)S(1)}, bf16[128,2048]{1,0:T(8,128)(2,1)S(1)}, u32[]{:S(2)}, u32[]{:S(2)}) collective-permute-start(bf16[128,2048]{1,0:T(8,128)(2,1)S(1)} %get-tuple-element.263), channel_id=1, source_target_pairs={{0,4},{8,12},{16,20},{24,28},{1,5},{9,13},{17,21},{25,29},{2,6},{1... | collective-permute-start | bytes 1572872 | tf_op jit(solution)/shard_map/ppermute | solution.py:11
  156.6 21.1 %collective-permute-start.29 = (bf16[256,2048]{1,0:T(8,128)(2,1)S(1)}, bf16[256,2048]{1,0:T(8,128)(2,1)S(1)}, u32[]{:S(2)}, u32[]{:S(2)}) collective-permute-start(bf16[256,2048]{1,0:T(8,128)(2,1)S(1)} %get-tuple-element.383), channel_id=1, source_target_pairs={{8,0},{12,4},{16,8},{20,12},{24,16},{28,20},{9,1},{13,5},{17,9},{2... | collective-permute-start | bytes 3145736 | tf_op jit(solution)/shard_map/ppermute | solution.py:11
  157.9 23.0 %collective-permute-start.26 = (bf16[256,2048]{1,0:T(8,128)(2,1)S(1)}, bf16[256,2048]{1,0:T(8,128)(2,1)S(1)}, u32[]{:S(2)}, u32[]{:S(2)}) collective-permute-start(bf16[256,2048]{1,0:T(8,128)(2,1)S(1)} %get-tuple-element.384), channel_id=1, source_target_pairs={{4,0},{12,8},{20,16},{28,24},{5,1},{13,9},{21,17},{29,25},{6,2},{1... | collective-permute-start | bytes 3145736 | tf_op jit(solution)/shard_map/ppermute | solution.py:11
  162.1 18.9 %collective-permute-start.25 = (f32[896,256]{0,1:T(8,128)S(1)}, f32[896,256]{0,1:T(8,128)S(1)}, u32[]{:S(2)}, u32[]{:S(2)}) collective-permute-start(f32[896,256]{0,1:T(8,128)S(1)} %maximum_select_fusion.2), channel_id=1, source_target_pairs={{0,1},{1,0},{2,3},{3,2},{4,5},{5,4},{6,7},{7,6},{8,9},{9,8},{10,11... | collective-permute-start | bytes 2752520 | tf_op jit(solution)/shard_map/ppermute | solution.py:100
  181.2 19.6 %collective-permute-start.31 = (bf16[192,2048]{1,0:T(8,128)(2,1)S(1)}, bf16[192,2048]{1,0:T(8,128)(2,1)S(1)}, u32[]{:S(2)}, u32[]{:S(2)}) collective-permute-start(bf16[192,2048]{1,0:T(8,128)(2,1)S(1)} %get-tuple-element.392), channel_id=1, source_target_pairs={{4,0},{12,8},{20,16},{28,24},{5,1},{13,9},{21,17},{29,25},{6,2},{1... | collective-permute-start | bytes 2359304 | tf_op jit(solution)/shard_map/ppermute | solution.py:11
  182.5 18.3 %collective-permute-start.34 = (bf16[192,2048]{1,0:T(8,128)(2,1)S(1)}, bf16[192,2048]{1,0:T(8,128)(2,1)S(1)}, u32[]{:S(2)}, u32[]{:S(2)}) collective-permute-start(bf16[192,2048]{1,0:T(8,128)(2,1)S(1)} %get-tuple-element.391), channel_id=1, source_target_pairs={{8,0},{12,4},{16,8},{20,12},{24,16},{28,20},{9,1},{13,5},{17,9},{2... | collective-permute-start | bytes 2359304 | tf_op jit(solution)/shard_map/ppermute | solution.py:11
  186.7 17.6 %collective-permute-start.30 = (f32[896,256]{0,1:T(8,128)S(1)}, f32[896,256]{0,1:T(8,128)S(1)}, u32[]{:S(2)}, u32[]{:S(2)}) collective-permute-start(f32[896,256]{0,1:T(8,128)S(1)} %maximum_select_fusion.3), channel_id=1, source_target_pairs={{0,1},{1,0},{2,3},{3,2},{4,5},{5,4},{6,7},{7,6},{8,9},{9,8},{10,11... | collective-permute-start | bytes 2752520 | tf_op jit(solution)/shard_map/ppermute | solution.py:100
  186.9 13.0 %collective-permute-start.33 = (f32[896,128]{0,1:T(8,128)S(1)}, f32[896,128]{0,1:T(8,128)S(1)}, u32[]{:S(2)}, u32[]{:S(2)}) collective-permute-start(f32[896,128]{0,1:T(8,128)S(1)} %select_add_fusion.3), channel_id=1, source_target_pairs={{0,2},{1,3},{2,0},{3,1},{4,6},{5,7},{6,4},{7,5},{8,10},{9,11},{10,... | collective-permute-start | bytes 1376264 | tf_op jit(solution)/shard_map/ppermute | solution.py:111
  188.2 16.1 %collective-permute-start.32 = (bf16[128,2048]{1,0:T(8,128)(2,1)S(1)}, bf16[128,2048]{1,0:T(8,128)(2,1)S(1)}, u32[]{:S(2)}, u32[]{:S(2)}) collective-permute-start(bf16[128,2048]{1,0:T(8,128)(2,1)S(1)} %get-tuple-element.283), channel_id=1, source_target_pairs={{0,4},{8,12},{16,20},{24,28},{1,5},{9,13},{17,21},{25,29},{2,6},{1... | collective-permute-start | bytes 1572872 | tf_op jit(solution)/shard_map/ppermute | solution.py:11
  207.2 19.6 %collective-permute-start.35 = (f32[896,256]{0,1:T(8,128)S(1)}, f32[896,256]{0,1:T(8,128)S(1)}, u32[]{:S(2)}, u32[]{:S(2)}) collective-permute-start(f32[896,256]{0,1:T(8,128)S(1)} %maximum_select_fusion.4), channel_id=1, source_target_pairs={{0,1},{1,0},{2,3},{3,2},{4,5},{5,4},{6,7},{7,6},{8,9},{9,8},{10,11... | collective-permute-start | bytes 2752520 | tf_op jit(solution)/shard_map/ppermute | solution.py:100
  207.4 13.0 %collective-permute-start.37 = (f32[896,128]{0,1:T(8,128)S(1)}, f32[896,128]{0,1:T(8,128)S(1)}, u32[]{:S(2)}, u32[]{:S(2)}) collective-permute-start(f32[896,128]{0,1:T(8,128)S(1)} %select_add_fusion.2), channel_id=1, source_target_pairs={{0,2},{1,3},{2,0},{3,1},{4,6},{5,7},{6,4},{7,5},{8,10},{9,11},{10,... | collective-permute-start | bytes 1376264 | tf_op jit(solution)/shard_map/ppermute | solution.py:111
  208.3 18.5 %collective-permute-start.39 = (bf16[128,2048]{1,0:T(8,128)(2,1)S(1)}, bf16[128,2048]{1,0:T(8,128)(2,1)S(1)}, u32[]{:S(2)}, u32[]{:S(2)}) collective-permute-start(bf16[128,2048]{1,0:T(8,128)(2,1)S(1)} %collective-permute-done.32), channel_id=1, source_target_pairs={{8,0},{12,4},{16,8},{20,12},{24,16},{28,20},{9,1},{13,5},{17,9},{2... | collective-permute-start | bytes 1572872 | tf_op jit(solution)/shard_map/ppermute | solution.py:11
  229.7 14.1 %collective-permute-start.40 = (f32[896,256]{0,1:T(8,128)S(1)}, f32[896,256]{0,1:T(8,128)S(1)}, u32[]{:S(2)}, u32[]{:S(2)}) collective-permute-start(f32[896,256]{0,1:T(8,128)S(1)} %maximum_select_fusion.5), channel_id=1, source_target_pairs={{0,1},{1,0},{2,3},{3,2},{4,5},{5,4},{6,7},{7,6},{8,9},{9,8},{10,11... | collective-permute-start | bytes 2752520 | tf_op jit(solution)/shard_map/ppermute | solution.py:100
  249.9 19.7 %collective-permute-start.43 = (f32[896,128]{0,1:T(8,128)}, f32[896,128]{0,1:T(8,128)}, u32[]{:S(2)}, u32[]{:S(2)}) collective-permute-start(f32[896,128]{0,1:T(8,128)} %select_add_fusion), channel_id=1, source_target_pairs={{0,2},{1,3},{2,0},{3,1},{4,6},{5,7},{6,4},{7,5},{8,10},{9,11},{10,... | collective-permute-start | bytes 1376264 | tf_op jit(solution)/shard_map/ppermute | solution.py:111
  (41 other events, 421.6 us)

commit v4 on v2

--- a/solution.py
+++ b/solution.py
@@ -49,13 +49,18 @@
             result = result + part
         return result
 
-    moments = jnp.stack(local_moments(dosages))
-    summed_moments = added(
-        [moments] + [lax.ppermute(moments, "samp", [(j, j ^ i) for j in range(groups)]) for i in flips])
-    own_block = standardize(dosages, summed_moments[0], summed_moments[1], total)
-    rows = own_block.shape[0]
+    def standard_rows(values):
+        moments = jnp.stack(local_moments(values))
+        summed = added(
+            [moments] + [lax.ppermute(moments, "samp", [(j, j ^ i) for j in range(groups)]) for i in flips])
+        return standardize(values, summed[0], summed[1], total)
+
+    rows = dosages.shape[0]
     step = rows // CHUNKS
-    pieces = [own_block[c * step:(c + 1) * step] for c in range(CHUNKS)]
+    first_piece = standard_rows(dosages[:step])
+    rest = standard_rows(dosages[step:])
+    own_block = jnp.concatenate([first_piece, rest], axis=0)
+    pieces = [first_piece] + [rest[(c - 1) * step:c * step] for c in range(1, CHUNKS)]
 
     odd = list(range(1, count, 2))
     even = list(range(0, count, 2))

time: 272 us -> 269 us (0.989)
  waiting for transfers between devices: 159 us -> 148 us
  other arithmetic: 25.8 us -> 30.1 us
  starting transfers between devices: 57.3 us -> 60.6 us
    ppermute x27, waiting for transfers between devices: 120 us -> 110 us  [moved(): return lax.ppermute(value, 'snp', pairs)]
  transfers between devices with their start and end apart: 47 -> 50, of which waited for: 25 -> 25; matrix products, arithmetic and copies ran while one was open for 11% -> 15% of each run, Pallas kernels for 0% -> 0%
where the time goes in v4:
time: 269 us; the launch traced here: 268 us
  waiting for transfers between devices  148 us (55%)
  starting transfers between devices  60.6 us (23%)
  other arithmetic  30.1 us (11%)
  matrix products  18 us (7%)
  local copies, waits for them, and re-layouts  10.5 us (4%)
    ppermute x27, waiting for transfers between devices, moved(): return lax.ppermute(value, 'snp', pairs)  110 us
    ppermute x27, starting transfers between devices, moved(): return lax.ppermute(value, 'snp', pairs)  43.2 us
    ppermute x7, waiting for transfers between devices, second_level(): last = lax.ppermute(pick(c, 2, 3, 0, 1) + onward, 'samp', across)  20.8 us
    dot_general x8, matrix products, finish(): jnp.einsum('ab,cb->ac', own_block, blocks, preferred_element_type=jnp.flo...  18 us
    ppermute x3, waiting for transfers between devices, finish(): lax.ppermute(outgoing[i], 'samp', [(j, j ^ i) for j in range(groups)])  14.5 us
    ppermute x7, starting transfers between devices, second_level(): last = lax.ppermute(pick(c, 2, 3, 0, 1) + onward, 'samp', across)  9.68 us
    add x7, other arithmetic, second_level(): state['results'][c] = pick(c, 0, 1, 2, 3) + mine + last  7.16 us
  transfers between devices with their start and end apart: 50, of which 25 were waited for; matrix products, arithmetic and copies ran while one was open for 15% of the time, Pallas kernels for 0%

profile of v4, /device:TPU:0, one launch (start us, length us, event | category | flops | bytes accessed | tf_op | source)
XLA Modules:
  0.0 268.4 jit_solution(14518621775542862157)
XLA Ops:
  0.0 3.7 %slice_reduce_fusion = (f32[784]{0:T(1024)S(1)}, f32[784]{0:T(1024)S(1)}) fusion(f32[896,2048]{1,0:T(8,128)} %param.1), kind=kLoop, calls=%fused_computation.2 | loop fusion | flops 4815328 | bytes 6428800 | tf_op jit(solution)/shard_map/reduce_sum | solution.py:21
  3.7 2.4 collective-permute-start.3
  11.3 1.9 collective-permute-done.1
  17.3 3.5 %multiply_convert_fusion = bf16[784,2048]{1,0:T(8,128)(2,1)S(1)} fusion(f32[896,2048]{1,0:T(8,128)} %param.1, f32[784]{0:T(1024)S(1)} %add_rsqrt_fusion, f32[784]{0:T(1024)S(1)} %get-tuple-element.327), kind=kLoop, calls=%fused_computation | loop fusion | flops 4816896 | bytes 9640064 | tf_op jit(solution)/shard_map/convert_element_type | solution.py:17
  22.5 5.4 %collective-permute-done.6 = bf16[112,2048]{1,0:T(8,128)(2,1)S(1)} collective-permute-done((bf16[112,2048]{1,0:T(8,128)(2,1)S(1)}, bf16[112,2048]{1,0:T(8,128)(2,1)S(1)}, u32[]{:S(2)}, u32[]{:S(2)}) %collective-permute-start.6) | collective-permute-done | bytes 458784 | tf_op jit(solution)/shard_map/ppermute | solution.py:11
  31.8 4.6 %collective-permute-start.9 = (bf16[112,2048]{1,0:T(8,128)(2,1)S(1)}, bf16[112,2048]{1,0:T(8,128)(2,1)S(1)}, u32[]{:S(2)}, u32[]{:S(2)}) collective-permute-start(bf16[112,2048]{1,0:T(8,128)(2,1)S(1)} %collective-permute-done.7), channel_id=1, source_target_pairs={{0,4},{8,12},{16,20},{24,28},{1,5},{9,13},{17,21},{25,29},{2,6},{1... | collective-permute-start | bytes 1376264 | tf_op jit(solution)/shard_map/ppermute | solution.py:11
  36.5 14.9 %collective-permute-done.8 = bf16[224,2048]{1,0:T(8,128)(2,1)S(1)} collective-permute-done((bf16[224,2048]{1,0:T(8,128)(2,1)S(1)}, bf16[224,2048]{1,0:T(8,128)(2,1)S(1)}, u32[]{:S(2)}, u32[]{:S(2)}) %collective-permute-start.8) | collective-permute-done | bytes 917536 | tf_op jit(solution)/shard_map/ppermute | solution.py:11
  55.3 4.6 %collective-permute-start.12 = (bf16[112,2048]{1,0:T(8,128)(2,1)S(1)}, bf16[112,2048]{1,0:T(8,128)(2,1)S(1)}, u32[]{:S(2)}, u32[]{:S(2)}) collective-permute-start(bf16[112,2048]{1,0:T(8,128)(2,1)S(1)} %collective-permute-done.10), channel_id=1, source_target_pairs={{0,4},{8,12},{16,20},{24,28},{1,5},{9,13},{17,21},{25,29},{2,6},{1... | collective-permute-start | bytes 1376264 | tf_op jit(solution)/shard_map/ppermute | solution.py:11
  59.9 14.0 %collective-permute-done.13 = bf16[224,2048]{1,0:T(8,128)(2,1)S(1)} collective-permute-done((bf16[224,2048]{1,0:T(8,128)(2,1)S(1)}, bf16[224,2048]{1,0:T(8,128)(2,1)S(1)}, u32[]{:S(2)}, u32[]{:S(2)}) %collective-permute-start.13) | collective-permute-done | bytes 917536 | tf_op jit(solution)/shard_map/ppermute | solution.py:11
  84.4 3.4 %fusion = f32[896,448]{0,1:T(8,128)S(1)} fusion(bf16[112,2048]{1,0:T(8,128)(2,1)S(1)} %add.174, bf16[112,2048]{1,0:T(8,128)(2,1)} %copy-done.29, bf16[112,2048]{1,0:T(8,128)(2,1)S(1)} %add.173, bf16[112,2048]{1,0:T(8,128)(2,1)} %copy-done.30, bf16[784,2048]{1,0:T(8,128)(2,1)S(1)} %multiply_convert_fusion), kind=kOutput, calls=%fused_computation.4 | convolution fusion | flops 1658847232 | bytes 6651904 | tf_op jit(solution)/shard_map/ab,cb->ac/dot_general | solution.py:86
  88.1 10.6 %collective-permute-done.17 = bf16[224,2048]{1,0:T(8,128)(2,1)} collective-permute-done((bf16[224,2048]{1,0:T(8,128)(2,1)}, bf16[224,2048]{1,0:T(8,128)(2,1)}, u32[]{:S(2)}, u32[]{:S(2)}) %collective-permute-start.17) | collective-permute-done | bytes 917536 | tf_op jit(solution)/shard_map/ppermute | solution.py:11
  101.3 3.3 %collective-permute-start.21 = (f32[896,112]{0,1:T(8,128)S(1)}, f32[896,112]{0,1:T(8,128)S(1)}, u32[]{:S(2)}, u32[]{:S(2)}) collective-permute-start(f32[896,112]{0,1:T(8,128)S(1)} %select_add_fusion.7), channel_id=1, source_target_pairs={{0,2},{1,3},{2,0},{3,1},{4,6},{5,7},{6,4},{7,5},{8,10},{9,11},{10,... | collective-permute-start | bytes 1204232 | tf_op jit(solution)/shard_map/ppermute | solution.py:112
  109.2 2.1 fusion.8
  112.6 14.0 %collective-permute-done.22 = bf16[224,2048]{1,0:T(8,128)(2,1)S(1)} collective-permute-done((bf16[224,2048]{1,0:T(8,128)(2,1)S(1)}, bf16[224,2048]{1,0:T(8,128)(2,1)S(1)}, u32[]{:S(2)}, u32[]{:S(2)}) %collective-permute-start.22) | collective-permute-done | bytes 917536 | tf_op jit(solution)/shard_map/ppermute | solution.py:11
  132.8 2.1 fusion.16
  136.4 12.8 %collective-permute-done.27 = bf16[224,2048]{1,0:T(8,128)(2,1)S(1)} collective-permute-done((bf16[224,2048]{1,0:T(8,128)(2,1)S(1)}, bf16[224,2048]{1,0:T(8,128)(2,1)S(1)}, u32[]{:S(2)}, u32[]{:S(2)}) %collective-permute-start.27) | collective-permute-done | bytes 917536 | tf_op jit(solution)/shard_map/ppermute | solution.py:11
  155.7 2.1 fusion.24
  159.1 12.0 %collective-permute-done.32 = bf16[224,2048]{1,0:T(8,128)(2,1)S(1)} collective-permute-done((bf16[224,2048]{1,0:T(8,128)(2,1)S(1)}, bf16[224,2048]{1,0:T(8,128)(2,1)S(1)}, u32[]{:S(2)}, u32[]{:S(2)}) %collective-permute-start.32) | collective-permute-done | bytes 917536 | tf_op jit(solution)/shard_map/ppermute | solution.py:11
  177.0 2.1 fusion.32
  180.4 11.8 %collective-permute-done.37 = bf16[224,2048]{1,0:T(8,128)(2,1)S(1)} collective-permute-done((bf16[224,2048]{1,0:T(8,128)(2,1)S(1)}, bf16[224,2048]{1,0:T(8,128)(2,1)S(1)}, u32[]{:S(2)}, u32[]{:S(2)}) %collective-permute-start.37) | collective-permute-done | bytes 917536 | tf_op jit(solution)/shard_map/ppermute | solution.py:11
  192.6 2.1 fusion.40
  200.9 6.0 %collective-permute-done.40 = f32[896,112]{0,1:T(8,128)S(1)} collective-permute-done((f32[896,112]{0,1:T(8,128)S(1)}, f32[896,112]{0,1:T(8,128)S(1)}, u32[]{:S(2)}, u32[]{:S(2)}) %collective-permute-start.40) | collective-permute-done | bytes 401440 | tf_op jit(solution)/shard_map/ppermute | solution.py:112
  208.2 4.1 %collective-permute-done.41 = bf16[112,2048]{1,0:T(8,128)(2,1)S(1)} collective-permute-done((bf16[112,2048]{1,0:T(8,128)(2,1)S(1)}, bf16[112,2048]{1,0:T(8,128)(2,1)S(1)}, u32[]{:S(2)}, u32[]{:S(2)}) %collective-permute-start.41) | collective-permute-done | bytes 458784 | tf_op jit(solution)/shard_map/ppermute | solution.py:11
  212.4 3.1 %collective-permute-done.42 = bf16[112,2048]{1,0:T(8,128)(2,1)S(1)} collective-permute-done((bf16[112,2048]{1,0:T(8,128)(2,1)S(1)}, bf16[112,2048]{1,0:T(8,128)(2,1)S(1)}, u32[]{:S(2)}, u32[]{:S(2)}) %collective-permute-start.42) | collective-permute-done | bytes 458784 | tf_op jit(solution)/shard_map/ppermute | solution.py:11
  215.7 2.1 fusion.48
  220.4 9.7 %collective-permute-done.44 = f32[896,112]{0,1:T(8,128)S(1)} collective-permute-done((f32[896,112]{0,1:T(8,128)S(1)}, f32[896,112]{0,1:T(8,128)S(1)}, u32[]{:S(2)}, u32[]{:S(2)}) %collective-permute-start.44) | collective-permute-done | bytes 401440 | tf_op jit(solution)/shard_map/ppermute | solution.py:112
  231.0 2.9 %collective-permute-done.45 = bf16[112,2048]{1,0:T(8,128)(2,1)S(1)} collective-permute-done((bf16[112,2048]{1,0:T(8,128)(2,1)S(1)}, bf16[112,2048]{1,0:T(8,128)(2,1)S(1)}, u32[]{:S(2)}, u32[]{:S(2)}) %collective-permute-start.45) | collective-permute-done | bytes 458784 | tf_op jit(solution)/shard_map/ppermute | solution.py:11
  236.5 2.1 fusion.56
  242.5 4.9 %collective-permute-done.46 = f32[896,112]{0,1:T(8,128)} collective-permute-done((f32[896,112]{0,1:T(8,128)}, f32[896,112]{0,1:T(8,128)}, u32[]{:S(2)}, u32[]{:S(2)}) %collective-permute-start.46) | collective-permute-done | bytes 401440 | tf_op jit(solution)/shard_map/ppermute | solution.py:112
  248.9 6.0 %collective-permute-done.47 = f32[896,112]{0,1:T(8,128)} collective-permute-done((f32[896,112]{0,1:T(8,128)}, f32[896,112]{0,1:T(8,128)}, u32[]{:S(2)}, u32[]{:S(2)}) %collective-permute-start.47) | collective-permute-done | bytes 401440 | tf_op jit(solution)/shard_map/ppermute | solution.py:97
  254.9 8.5 %collective-permute-done.48 = f32[896,112]{0,1:T(8,128)} collective-permute-done((f32[896,112]{0,1:T(8,128)}, f32[896,112]{0,1:T(8,128)}, u32[]{:S(2)}, u32[]{:S(2)}) %collective-permute-start.48) | collective-permute-done | bytes 401440 | tf_op jit(solution)/shard_map/ppermute | solution.py:97
  265.4 3.0 %copy.2 = f32[896,896]{1,0:T(8,128)} copy(f32[896,896]{0,1:T(8,128)S(1)} %broadcast_multiply_fusion) | data formatting | bytes 6422528 | tf_op jit(solution)/shard_map/div | solution.py:146
  (234 shorter events, 81.3 us)
Async XLA Ops:
  3.7 13.5 %collective-permute-start.3 = (f32[2,784]{1,0:T(2,128)S(1)}, f32[2,784]{1,0:T(2,128)S(1)}, u32[]{:S(2)}, u32[]{:S(2)}) collective-permute-start(f32[2,784]{1,0:T(2,128)S(1)} %pad_maximum_fusion.14), channel_id=1, source_target_pairs={{0,3},{1,2},{2,1},{3,0},{4,7},{5,6},{6,5},{7,4},{8,11},{9,10},{10,... | collective-permute-start | bytes 18824 | tf_op jit(solution)/shard_map/ppermute | solution.py:55
  29.2 22.2 %collective-permute-start.8 = (bf16[224,2048]{1,0:T(8,128)(2,1)S(1)}, bf16[224,2048]{1,0:T(8,128)(2,1)S(1)}, u32[]{:S(2)}, u32[]{:S(2)}) collective-permute-start(bf16[224,2048]{1,0:T(8,128)(2,1)S(1)} %pad_maximum_fusion.13), channel_id=1, source_target_pairs={{4,0},{12,8},{20,16},{28,24},{5,1},{13,9},{21,17},{29,25},{6,2},{1... | collective-permute-start | bytes 2752520 | tf_op jit(solution)/shard_map/ppermute | solution.py:11
  30.5 21.9 %collective-permute-start.10 = (bf16[112,2048]{1,0:T(8,128)(2,1)S(1)}, bf16[112,2048]{1,0:T(8,128)(2,1)S(1)}, u32[]{:S(2)}, u32[]{:S(2)}) collective-permute-start(bf16[112,2048]{1,0:T(8,128)(2,1)S(1)} %get-tuple-element.165), channel_id=1, source_target_pairs={{8,0},{12,4},{16,8},{20,12},{24,16},{28,20},{9,1},{13,5},{17,9},{2... | collective-permute-start | bytes 1376264 | tf_op jit(solution)/shard_map/ppermute | solution.py:11
  31.8 20.6 %collective-permute-start.9 = (bf16[112,2048]{1,0:T(8,128)(2,1)S(1)}, bf16[112,2048]{1,0:T(8,128)(2,1)S(1)}, u32[]{:S(2)}, u32[]{:S(2)}) collective-permute-start(bf16[112,2048]{1,0:T(8,128)(2,1)S(1)} %collective-permute-done.7), channel_id=1, source_target_pairs={{0,4},{8,12},{16,20},{24,28},{1,5},{9,13},{17,21},{25,29},{2,6},{1... | collective-permute-start | bytes 1376264 | tf_op jit(solution)/shard_map/ppermute | solution.py:11
  52.7 21.2 %collective-permute-start.13 = (bf16[224,2048]{1,0:T(8,128)(2,1)S(1)}, bf16[224,2048]{1,0:T(8,128)(2,1)S(1)}, u32[]{:S(2)}, u32[]{:S(2)}) collective-permute-start(bf16[224,2048]{1,0:T(8,128)(2,1)S(1)} %get-tuple-element.402), channel_id=1, source_target_pairs={{8,0},{12,4},{16,8},{20,12},{24,16},{28,20},{9,1},{13,5},{17,9},{2... | collective-permute-start | bytes 2752520 | tf_op jit(solution)/shard_map/ppermute | solution.py:11
  54.0 21.2 %collective-permute-start.11 = (bf16[224,2048]{1,0:T(8,128)(2,1)S(1)}, bf16[224,2048]{1,0:T(8,128)(2,1)S(1)}, u32[]{:S(2)}, u32[]{:S(2)}) collective-permute-start(bf16[224,2048]{1,0:T(8,128)(2,1)S(1)} %get-tuple-element.403), channel_id=1, source_target_pairs={{4,0},{12,8},{20,16},{28,24},{5,1},{13,9},{21,17},{29,25},{6,2},{1... | collective-permute-start | bytes 2752520 | tf_op jit(solution)/shard_map/ppermute | solution.py:11
  55.3 21.0 %collective-permute-start.12 = (bf16[112,2048]{1,0:T(8,128)(2,1)S(1)}, bf16[112,2048]{1,0:T(8,128)(2,1)S(1)}, u32[]{:S(2)}, u32[]{:S(2)}) collective-permute-start(bf16[112,2048]{1,0:T(8,128)(2,1)S(1)} %collective-permute-done.10), channel_id=1, source_target_pairs={{0,4},{8,12},{16,20},{24,28},{1,5},{9,13},{17,21},{25,29},{2,6},{1... | collective-permute-start | bytes 1376264 | tf_op jit(solution)/shard_map/ppermute | solution.py:11
  77.8 21.0 %collective-permute-start.17 = (bf16[224,2048]{1,0:T(8,128)(2,1)}, bf16[224,2048]{1,0:T(8,128)(2,1)}, u32[]{:S(2)}, u32[]{:S(2)}) collective-permute-start(bf16[224,2048]{1,0:T(8,128)(2,1)} %get-tuple-element.400), channel_id=1, source_target_pairs={{8,0},{12,4},{16,8},{20,12},{24,16},{28,20},{9,1},{13,5},{17,9},{2... | collective-permute-start | bytes 2752520 | tf_op jit(solution)/shard_map/ppermute | solution.py:11
  79.1 21.9 %collective-permute-start.16 = (bf16[112,2048]{1,0:T(8,128)(2,1)}, bf16[112,2048]{1,0:T(8,128)(2,1)S(1)}, u32[]{:S(2)}, u32[]{:S(2)}) collective-permute-start(bf16[112,2048]{1,0:T(8,128)(2,1)} %copy-done.13), channel_id=1, source_target_pairs={{0,4},{8,12},{16,20},{24,28},{1,5},{9,13},{17,21},{25,29},{2,6},{1... | collective-permute-start | bytes 1376264 | tf_op jit(solution)/shard_map/ppermute | solution.py:11
  80.6 20.4 %collective-permute-start.15 = (bf16[224,2048]{1,0:T(8,128)(2,1)}, bf16[224,2048]{1,0:T(8,128)(2,1)S(1)}, u32[]{:S(2)}, u32[]{:S(2)}) collective-permute-start(bf16[224,2048]{1,0:T(8,128)(2,1)} %get-tuple-element.401), channel_id=1, source_target_pairs={{4,0},{12,8},{20,16},{28,24},{5,1},{13,9},{21,17},{29,25},{6,2},{1... | collective-permute-start | bytes 2752520 | tf_op jit(solution)/shard_map/ppermute | solution.py:11
  104.5 22.7 %collective-permute-start.20 = (bf16[112,2048]{1,0:T(8,128)(2,1)S(1)}, bf16[112,2048]{1,0:T(8,128)(2,1)S(1)}, u32[]{:S(2)}, u32[]{:S(2)}) collective-permute-start(bf16[112,2048]{1,0:T(8,128)(2,1)S(1)} %get-tuple-element.224), channel_id=1, source_target_pairs={{0,4},{8,12},{16,20},{24,28},{1,5},{9,13},{17,21},{25,29},{2,6},{1... | collective-permute-start | bytes 1376264 | tf_op jit(solution)/shard_map/ppermute | solution.py:11
  106.4 20.2 %collective-permute-start.22 = (bf16[224,2048]{1,0:T(8,128)(2,1)S(1)}, bf16[224,2048]{1,0:T(8,128)(2,1)S(1)}, u32[]{:S(2)}, u32[]{:S(2)}) collective-permute-start(bf16[224,2048]{1,0:T(8,128)(2,1)S(1)} %get-tuple-element.398), channel_id=1, source_target_pairs={{8,0},{12,4},{16,8},{20,12},{24,16},{28,20},{9,1},{13,5},{17,9},{2... | collective-permute-start | bytes 2752520 | tf_op jit(solution)/shard_map/ppermute | solution.py:11
  107.7 19.5 %collective-permute-start.19 = (bf16[224,2048]{1,0:T(8,128)(2,1)S(1)}, bf16[224,2048]{1,0:T(8,128)(2,1)S(1)}, u32[]{:S(2)}, u32[]{:S(2)}) collective-permute-start(bf16[224,2048]{1,0:T(8,128)(2,1)S(1)} %get-tuple-element.399), channel_id=1, source_target_pairs={{4,0},{12,8},{20,16},{28,24},{5,1},{13,9},{21,17},{29,25},{6,2},{1... | collective-permute-start | bytes 2752520 | tf_op jit(solution)/shard_map/ppermute | solution.py:11
  111.6 15.7 %collective-permute-start.18 = (f32[896,224]{0,1:T(8,128)S(1)}, f32[896,224]{0,1:T(8,128)S(1)}, u32[]{:S(2)}, u32[]{:S(2)}) collective-permute-start(f32[896,224]{0,1:T(8,128)S(1)} %maximum_select_fusion.1), channel_id=1, source_target_pairs={{0,1},{1,0},{2,3},{3,2},{4,5},{5,4},{6,7},{7,6},{8,9},{9,8},{10,11... | collective-permute-start | bytes 2408456 | tf_op jit(solution)/shard_map/ppermute | solution.py:102
  128.0 21.6 %collective-permute-start.25 = (bf16[112,2048]{1,0:T(8,128)(2,1)S(1)}, bf16[112,2048]{1,0:T(8,128)(2,1)S(1)}, u32[]{:S(2)}, u32[]{:S(2)}) collective-permute-start(bf16[112,2048]{1,0:T(8,128)(2,1)S(1)} %get-tuple-element.243), channel_id=1, source_target_pairs={{0,4},{8,12},{16,20},{24,28},{1,5},{9,13},{17,21},{25,29},{2,6},{1... | collective-permute-start | bytes 1376264 | tf_op jit(solution)/shard_map/ppermute | solution.py:11
  129.7 19.5 %collective-permute-start.27 = (bf16[224,2048]{1,0:T(8,128)(2,1)S(1)}, bf16[224,2048]{1,0:T(8,128)(2,1)S(1)}, u32[]{:S(2)}, u32[]{:S(2)}) collective-permute-start(bf16[224,2048]{1,0:T(8,128)(2,1)S(1)} %get-tuple-element.396), channel_id=1, source_target_pairs={{8,0},{12,4},{16,8},{20,12},{24,16},{28,20},{9,1},{13,5},{17,9},{2... | collective-permute-start | bytes 2752520 | tf_op jit(solution)/shard_map/ppermute | solution.py:11
  131.0 18.5 %collective-permute-start.24 = (bf16[224,2048]{1,0:T(8,128)(2,1)S(1)}, bf16[224,2048]{1,0:T(8,128)(2,1)S(1)}, u32[]{:S(2)}, u32[]{:S(2)}) collective-permute-start(bf16[224,2048]{1,0:T(8,128)(2,1)S(1)} %get-tuple-element.397), channel_id=1, source_target_pairs={{4,0},{12,8},{20,16},{28,24},{5,1},{13,9},{21,17},{29,25},{6,2},{1... | collective-permute-start | bytes 2752520 | tf_op jit(solution)/shard_map/ppermute | solution.py:11
  135.1 14.5 %collective-permute-start.23 = (f32[896,224]{0,1:T(8,128)S(1)}, f32[896,224]{0,1:T(8,128)S(1)}, u32[]{:S(2)}, u32[]{:S(2)}) collective-permute-start(f32[896,224]{0,1:T(8,128)S(1)} %maximum_select_fusion.2), channel_id=1, source_target_pairs={{0,1},{1,0},{2,3},{3,2},{4,5},{5,4},{6,7},{7,6},{8,9},{9,8},{10,11... | collective-permute-start | bytes 2408456 | tf_op jit(solution)/shard_map/ppermute | solution.py:102
  151.1 20.1 %collective-permute-start.30 = (bf16[112,2048]{1,0:T(8,128)(2,1)S(1)}, bf16[112,2048]{1,0:T(8,128)(2,1)S(1)}, u32[]{:S(2)}, u32[]{:S(2)}) collective-permute-start(bf16[112,2048]{1,0:T(8,128)(2,1)S(1)} %get-tuple-element.263), channel_id=1, source_target_pairs={{0,4},{8,12},{16,20},{24,28},{1,5},{9,13},{17,21},{25,29},{2,6},{1... | collective-permute-start | bytes 1376264 | tf_op jit(solution)/shard_map/ppermute | solution.py:11
  152.8 18.2 %collective-permute-start.32 = (bf16[224,2048]{1,0:T(8,128)(2,1)S(1)}, bf16[224,2048]{1,0:T(8,128)(2,1)S(1)}, u32[]{:S(2)}, u32[]{:S(2)}) collective-permute-start(bf16[224,2048]{1,0:T(8,128)(2,1)S(1)} %get-tuple-element.394), channel_id=1, source_target_pairs={{8,0},{12,4},{16,8},{20,12},{24,16},{28,20},{9,1},{13,5},{17,9},{2... | collective-permute-start | bytes 2752520 | tf_op jit(solution)/shard_map/ppermute | solution.py:11
  154.1 17.0 %collective-permute-start.29 = (bf16[224,2048]{1,0:T(8,128)(2,1)S(1)}, bf16[224,2048]{1,0:T(8,128)(2,1)S(1)}, u32[]{:S(2)}, u32[]{:S(2)}) collective-permute-start(bf16[224,2048]{1,0:T(8,128)(2,1)S(1)} %get-tuple-element.395), channel_id=1, source_target_pairs={{4,0},{12,8},{20,16},{28,24},{5,1},{13,9},{21,17},{29,25},{6,2},{1... | collective-permute-start | bytes 2752520 | tf_op jit(solution)/shard_map/ppermute | solution.py:11
  172.5 19.8 %collective-permute-start.35 = (bf16[112,2048]{1,0:T(8,128)(2,1)S(1)}, bf16[112,2048]{1,0:T(8,128)(2,1)S(1)}, u32[]{:S(2)}, u32[]{:S(2)}) collective-permute-start(bf16[112,2048]{1,0:T(8,128)(2,1)S(1)} %get-tuple-element.283), channel_id=1, source_target_pairs={{0,4},{8,12},{16,20},{24,28},{1,5},{9,13},{17,21},{25,29},{2,6},{1... | collective-permute-start | bytes 1376264 | tf_op jit(solution)/shard_map/ppermute | solution.py:11
  174.2 18.0 %collective-permute-start.37 = (bf16[224,2048]{1,0:T(8,128)(2,1)S(1)}, bf16[224,2048]{1,0:T(8,128)(2,1)S(1)}, u32[]{:S(2)}, u32[]{:S(2)}) collective-permute-start(bf16[224,2048]{1,0:T(8,128)(2,1)S(1)} %get-tuple-element.392), channel_id=1, source_target_pairs={{8,0},{12,4},{16,8},{20,12},{24,16},{28,20},{9,1},{13,5},{17,9},{2... | collective-permute-start | bytes 2752520 | tf_op jit(solution)/shard_map/ppermute | solution.py:11
  175.5 16.8 %collective-permute-start.34 = (bf16[224,2048]{1,0:T(8,128)(2,1)S(1)}, bf16[224,2048]{1,0:T(8,128)(2,1)S(1)}, u32[]{:S(2)}, u32[]{:S(2)}) collective-permute-start(bf16[224,2048]{1,0:T(8,128)(2,1)S(1)} %get-tuple-element.393), channel_id=1, source_target_pairs={{4,0},{12,8},{20,16},{28,24},{5,1},{13,9},{21,17},{29,25},{6,2},{1... | collective-permute-start | bytes 2752520 | tf_op jit(solution)/shard_map/ppermute | solution.py:11
  194.9 20.6 %collective-permute-start.38 = (f32[896,224]{0,1:T(8,128)S(1)}, f32[896,224]{0,1:T(8,128)S(1)}, u32[]{:S(2)}, u32[]{:S(2)}) collective-permute-start(f32[896,224]{0,1:T(8,128)S(1)} %maximum_select_fusion.5), channel_id=1, source_target_pairs={{0,1},{1,0},{2,3},{3,2},{4,5},{5,4},{6,7},{7,6},{8,9},{9,8},{10,11... | collective-permute-start | bytes 2408456 | tf_op jit(solution)/shard_map/ppermute | solution.py:102
  198.1 14.3 %collective-permute-start.41 = (bf16[112,2048]{1,0:T(8,128)(2,1)S(1)}, bf16[112,2048]{1,0:T(8,128)(2,1)S(1)}, u32[]{:S(2)}, u32[]{:S(2)}) collective-permute-start(bf16[112,2048]{1,0:T(8,128)(2,1)S(1)} %get-tuple-element.312), channel_id=1, source_target_pairs={{4,0},{12,8},{20,16},{28,24},{5,1},{13,9},{21,17},{29,25},{6,2},{1... | collective-permute-start | bytes 1376264 | tf_op jit(solution)/shard_map/ppermute | solution.py:11
  199.4 16.1 %collective-permute-start.42 = (bf16[112,2048]{1,0:T(8,128)(2,1)S(1)}, bf16[112,2048]{1,0:T(8,128)(2,1)S(1)}, u32[]{:S(2)}, u32[]{:S(2)}) collective-permute-start(bf16[112,2048]{1,0:T(8,128)(2,1)S(1)} %collective-permute-done.35), channel_id=1, source_target_pairs={{8,0},{12,4},{16,8},{20,12},{24,16},{28,20},{9,1},{13,5},{17,9},{2... | collective-permute-start | bytes 1376264 | tf_op jit(solution)/shard_map/ppermute | solution.py:11
  218.1 15.9 %collective-permute-start.43 = (f32[896,224]{0,1:T(8,128)S(1)}, f32[896,224]{0,1:T(8,128)S(1)}, u32[]{:S(2)}, u32[]{:S(2)}) collective-permute-start(f32[896,224]{0,1:T(8,128)S(1)} %maximum_select_fusion.6), channel_id=1, source_target_pairs={{0,1},{1,0},{2,3},{3,2},{4,5},{5,4},{6,7},{7,6},{8,9},{9,8},{10,11... | collective-permute-start | bytes 2408456 | tf_op jit(solution)/shard_map/ppermute | solution.py:102
  219.1 14.8 %collective-permute-start.45 = (bf16[112,2048]{1,0:T(8,128)(2,1)S(1)}, bf16[112,2048]{1,0:T(8,128)(2,1)S(1)}, u32[]{:S(2)}, u32[]{:S(2)}) collective-permute-start(bf16[112,2048]{1,0:T(8,128)(2,1)S(1)} %collective-permute-done.39), channel_id=1, source_target_pairs={{8,0},{12,4},{16,8},{20,12},{24,16},{28,20},{9,1},{13,5},{17,9},{2... | collective-permute-start | bytes 1376264 | tf_op jit(solution)/shard_map/ppermute | solution.py:11
  239.6 15.3 %collective-permute-start.47 = (f32[896,112]{0,1:T(8,128)}, f32[896,112]{0,1:T(8,128)}, u32[]{:S(2)}, u32[]{:S(2)}) collective-permute-start(f32[896,112]{0,1:T(8,128)} %get-tuple-element.337), channel_id=1, source_target_pairs={{0,3},{1,2},{2,1},{3,0},{4,7},{5,6},{6,5},{7,4},{8,11},{9,10},{10,... | collective-permute-start | bytes 1204232 | tf_op jit(solution)/shard_map/ppermute | solution.py:97
  240.4 14.5 %collective-permute-start.49 = (f32[896,112]{0,1:T(8,128)}, f32[896,112]{0,1:T(8,128)}, u32[]{:S(2)}, u32[]{:S(2)}) collective-permute-start(f32[896,112]{0,1:T(8,128)} %get-tuple-element.336), channel_id=1, source_target_pairs={{0,1},{1,0},{2,3},{3,2},{4,5},{5,4},{6,7},{7,6},{8,9},{9,8},{10,11... | collective-permute-start | bytes 1204232 | tf_op jit(solution)/shard_map/ppermute | solution.py:97
  241.2 22.1 %collective-permute-start.48 = (f32[896,112]{0,1:T(8,128)}, f32[896,112]{0,1:T(8,128)}, u32[]{:S(2)}, u32[]{:S(2)}) collective-permute-start(f32[896,112]{0,1:T(8,128)} %select_select_fusion.1), channel_id=1, source_target_pairs={{0,2},{1,3},{2,0},{3,1},{4,6},{5,7},{6,4},{7,5},{8,10},{9,11},{10,... | collective-permute-start | bytes 1204232 | tf_op jit(solution)/shard_map/ppermute | solution.py:97
  (51 other events, 821.6 us)

commit v5 on v4

--- a/solution.py
+++ b/solution.py
@@ -58,7 +58,8 @@
     rows = dosages.shape[0]
     step = rows // CHUNKS
     first_piece = standard_rows(dosages[:step])
-    rest = standard_rows(dosages[step:])
+    first_piece, later = lax.optimization_barrier((first_piece, dosages[step:]))
+    rest = standard_rows(later)
     own_block = jnp.concatenate([first_piece, rest], axis=0)
     pieces = [first_piece] + [rest[(c - 1) * step:c * step] for c in range(1, CHUNKS)]
 

time: 269 us -> 274 us (1.019)
  waiting for transfers between devices: 148 us -> 157 us
  other arithmetic: 30.1 us -> 24.4 us
  local copies, waits for them, and re-layouts: 10.5 us -> 14.1 us
    ppermute x27, waiting for transfers between devices: 110 us -> 121 us  [moved(): return lax.ppermute(value, 'snp', pairs)]
    slice x0 -> x1, local copies, waits for them, and re-layouts: none -> 3.61 us  [local(): first_piece, later = lax.optimization_barrier((first_piece, dosages[step:]))]
    convert_element_type x2, other arithmetic: 4.85 us -> 2.01 us  [standardize(): ((values - mean[:, None]) * lax.rsqrt(variance + 1e-05)[:, None]).astype(...]
    reduce_sum x2, other arithmetic: 5.02 us -> 2.24 us  [local_moments(): return (jnp.sum(values, axis=1), jnp.sum(values * values, axis=1))]
  transfers between devices with their start and end apart: 50 -> 50, of which waited for: 25 -> 24; matrix products, arithmetic and copies ran while one was open for 15% -> 14% of each run, Pallas kernels for 0% -> 0%
where the time goes in v5:
time: 274 us; the launch traced here: 273 us
  waiting for transfers between devices  157 us (57%)
  starting transfers between devices  58.1 us (21%)
  other arithmetic  24.4 us (9%)
  matrix products  18 us (7%)
  local copies, waits for them, and re-layouts  14.1 us (5%)
    ppermute x27, waiting for transfers between devices, moved(): return lax.ppermute(value, 'snp', pairs)  121 us
    ppermute x27, starting transfers between devices, moved(): return lax.ppermute(value, 'snp', pairs)  43 us
    ppermute x7, waiting for transfers between devices, second_level(): last = lax.ppermute(pick(c, 2, 3, 0, 1) + onward, 'samp', across)  22 us
    dot_general x8, matrix products, finish(): jnp.einsum('ab,cb->ac', own_block, blocks, preferred_element_type=jnp.flo...  18 us
    ppermute x3, waiting for transfers between devices, finish(): lax.ppermute(outgoing[i], 'samp', [(j, j ^ i) for j in range(groups)])  14.1 us
    add x7, other arithmetic, second_level(): state['results'][c] = pick(c, 0, 1, 2, 3) + mine + last  7.15 us
    ppermute x7, starting transfers between devices, second_level(): last = lax.ppermute(pick(c, 2, 3, 0, 1) + onward, 'samp', across)  7.12 us
  transfers between devices with their start and end apart: 50, of which 24 were waited for; matrix products, arithmetic and copies ran while one was open for 14% of the time, Pallas kernels for 0%

profile of v5, /device:TPU:0, one launch (start us, length us, event | category | flops | bytes accessed | tf_op | source)
XLA Modules:
  0.0 273.4 jit_solution(4927211506021425136)
XLA Ops:
  1.4 2.4 collective-permute-start
  4.5 3.6 %slice.278 = f32[784,2048]{1,0:T(8,128)S(1)} slice(f32[896,2048]{1,0:T(8,128)} %param.1), slice={[112:896], [0:2048]} | slice | bytes 12845056 | tf_op jit(solution)/shard_map/slice | solution.py:61
  16.4 1.6 fusion.77
  18.0 9.4 %collective-permute-done.6 = bf16[112,2048]{1,0:T(8,128)(2,1)S(1)} collective-permute-done((bf16[112,2048]{1,0:T(8,128)(2,1)S(1)}, bf16[112,2048]{1,0:T(8,128)(2,1)S(1)}, u32[]{:S(2)}, u32[]{:S(2)}) %collective-permute-start.6) | collective-permute-done | bytes 458784 | tf_op jit(solution)/shard_map/ppermute | solution.py:11
  31.4 4.6 %collective-permute-start.9 = (bf16[112,2048]{1,0:T(8,128)(2,1)S(1)}, bf16[112,2048]{1,0:T(8,128)(2,1)S(1)}, u32[]{:S(2)}, u32[]{:S(2)}) collective-permute-start(bf16[112,2048]{1,0:T(8,128)(2,1)S(1)} %collective-permute-done.7), channel_id=1, source_target_pairs={{0,4},{8,12},{16,20},{24,28},{1,5},{9,13},{17,21},{25,29},{2,6},{1... | collective-permute-start | bytes 1376264 | tf_op jit(solution)/shard_map/ppermute | solution.py:11
  36.1 16.6 %collective-permute-done.8 = bf16[224,2048]{1,0:T(8,128)(2,1)S(1)} collective-permute-done((bf16[224,2048]{1,0:T(8,128)(2,1)S(1)}, bf16[224,2048]{1,0:T(8,128)(2,1)S(1)}, u32[]{:S(2)}, u32[]{:S(2)}) %collective-permute-start.8) | collective-permute-done | bytes 917536 | tf_op jit(solution)/shard_map/ppermute | solution.py:11
  56.6 4.6 %collective-permute-start.12 = (bf16[112,2048]{1,0:T(8,128)(2,1)S(1)}, bf16[112,2048]{1,0:T(8,128)(2,1)S(1)}, u32[]{:S(2)}, u32[]{:S(2)}) collective-permute-start(bf16[112,2048]{1,0:T(8,128)(2,1)S(1)} %collective-permute-done.10), channel_id=1, source_target_pairs={{0,4},{8,12},{16,20},{24,28},{1,5},{9,13},{17,21},{25,29},{2,6},{1... | collective-permute-start | bytes 1376264 | tf_op jit(solution)/shard_map/ppermute | solution.py:11
  61.3 15.7 %collective-permute-done.13 = bf16[224,2048]{1,0:T(8,128)(2,1)S(1)} collective-permute-done((bf16[224,2048]{1,0:T(8,128)(2,1)S(1)}, bf16[224,2048]{1,0:T(8,128)(2,1)S(1)}, u32[]{:S(2)}, u32[]{:S(2)}) %collective-permute-start.13) | collective-permute-done | bytes 917536 | tf_op jit(solution)/shard_map/ppermute | solution.py:11
  87.5 3.4 %fusion = f32[896,448]{0,1:T(8,128)S(1)} fusion(bf16[112,2048]{1,0:T(8,128)(2,1)S(1)} %add.174, bf16[112,2048]{1,0:T(8,128)(2,1)} %copy-done.29, bf16[112,2048]{1,0:T(8,128)(2,1)S(1)} %add.173, bf16[112,2048]{1,0:T(8,128)(2,1)} %copy-done.30, bf16[784,2048]{1,0:T(8,128)(2,1)S(1)} %multiply_convert_fusion), kind=kOutput, calls=%fused_computation.3 | convolution fusion | flops 1658847232 | bytes 6651904 | tf_op jit(solution)/shard_map/ab,cb->ac/dot_general | solution.py:87
  91.2 12.4 %collective-permute-done.17 = bf16[224,2048]{1,0:T(8,128)(2,1)} collective-permute-done((bf16[224,2048]{1,0:T(8,128)(2,1)}, bf16[224,2048]{1,0:T(8,128)(2,1)}, u32[]{:S(2)}, u32[]{:S(2)}) %collective-permute-start.17) | collective-permute-done | bytes 917536 | tf_op jit(solution)/shard_map/ppermute | solution.py:11
  106.9 1.6 collective-permute-start.20
  111.7 2.1 fusion.8
  115.2 14.7 %collective-permute-done.22 = bf16[224,2048]{1,0:T(8,128)(2,1)S(1)} collective-permute-done((bf16[224,2048]{1,0:T(8,128)(2,1)S(1)}, bf16[224,2048]{1,0:T(8,128)(2,1)S(1)}, u32[]{:S(2)}, u32[]{:S(2)}) %collective-permute-start.22) | collective-permute-done | bytes 917536 | tf_op jit(solution)/shard_map/ppermute | solution.py:11
  136.9 2.1 fusion.16
  140.3 13.8 %collective-permute-done.27 = bf16[224,2048]{1,0:T(8,128)(2,1)S(1)} collective-permute-done((bf16[224,2048]{1,0:T(8,128)(2,1)S(1)}, bf16[224,2048]{1,0:T(8,128)(2,1)S(1)}, u32[]{:S(2)}, u32[]{:S(2)}) %collective-permute-start.27) | collective-permute-done | bytes 917536 | tf_op jit(solution)/shard_map/ppermute | solution.py:11
  160.0 2.1 fusion.24
  163.6 12.7 %collective-permute-done.32 = bf16[224,2048]{1,0:T(8,128)(2,1)S(1)} collective-permute-done((bf16[224,2048]{1,0:T(8,128)(2,1)S(1)}, bf16[224,2048]{1,0:T(8,128)(2,1)S(1)}, u32[]{:S(2)}, u32[]{:S(2)}) %collective-permute-start.32) | collective-permute-done | bytes 917536 | tf_op jit(solution)/shard_map/ppermute | solution.py:11
  182.7 2.1 fusion.32
  186.0 11.8 %collective-permute-done.37 = bf16[224,2048]{1,0:T(8,128)(2,1)S(1)} collective-permute-done((bf16[224,2048]{1,0:T(8,128)(2,1)S(1)}, bf16[224,2048]{1,0:T(8,128)(2,1)S(1)}, u32[]{:S(2)}, u32[]{:S(2)}) %collective-permute-start.37) | collective-permute-done | bytes 917536 | tf_op jit(solution)/shard_map/ppermute | solution.py:11
  198.3 2.1 fusion.40
  205.6 6.9 %collective-permute-done.40 = f32[896,112]{0,1:T(8,128)S(1)} collective-permute-done((f32[896,112]{0,1:T(8,128)S(1)}, f32[896,112]{0,1:T(8,128)S(1)}, u32[]{:S(2)}, u32[]{:S(2)}) %collective-permute-start.40) | collective-permute-done | bytes 401440 | tf_op jit(solution)/shard_map/ppermute | solution.py:113
  213.5 3.7 %collective-permute-done.41 = bf16[112,2048]{1,0:T(8,128)(2,1)S(1)} collective-permute-done((bf16[112,2048]{1,0:T(8,128)(2,1)S(1)}, bf16[112,2048]{1,0:T(8,128)(2,1)S(1)}, u32[]{:S(2)}, u32[]{:S(2)}) %collective-permute-start.41) | collective-permute-done | bytes 458784 | tf_op jit(solution)/shard_map/ppermute | solution.py:11
  217.2 3.1 %collective-permute-done.42 = bf16[112,2048]{1,0:T(8,128)(2,1)S(1)} collective-permute-done((bf16[112,2048]{1,0:T(8,128)(2,1)S(1)}, bf16[112,2048]{1,0:T(8,128)(2,1)S(1)}, u32[]{:S(2)}, u32[]{:S(2)}) %collective-permute-start.42) | collective-permute-done | bytes 458784 | tf_op jit(solution)/shard_map/ppermute | solution.py:11
  220.6 2.1 fusion.48
  223.2 1.6 collective-permute-start.44
  226.0 8.9 %collective-permute-done.44 = f32[896,112]{0,1:T(8,128)S(1)} collective-permute-done((f32[896,112]{0,1:T(8,128)S(1)}, f32[896,112]{0,1:T(8,128)S(1)}, u32[]{:S(2)}, u32[]{:S(2)}) %collective-permute-start.44) | collective-permute-done | bytes 401440 | tf_op jit(solution)/shard_map/ppermute | solution.py:113
  235.9 3.4 %collective-permute-done.45 = bf16[112,2048]{1,0:T(8,128)(2,1)S(1)} collective-permute-done((bf16[112,2048]{1,0:T(8,128)(2,1)S(1)}, bf16[112,2048]{1,0:T(8,128)(2,1)S(1)}, u32[]{:S(2)}, u32[]{:S(2)}) %collective-permute-start.45) | collective-permute-done | bytes 458784 | tf_op jit(solution)/shard_map/ppermute | solution.py:11
  241.1 2.1 fusion.56
  247.1 5.7 %collective-permute-done.46 = f32[896,112]{0,1:T(8,128)} collective-permute-done((f32[896,112]{0,1:T(8,128)}, f32[896,112]{0,1:T(8,128)}, u32[]{:S(2)}, u32[]{:S(2)}) %collective-permute-start.46) | collective-permute-done | bytes 401440 | tf_op jit(solution)/shard_map/ppermute | solution.py:113
  254.3 5.2 %collective-permute-done.47 = f32[896,112]{0,1:T(8,128)} collective-permute-done((f32[896,112]{0,1:T(8,128)}, f32[896,112]{0,1:T(8,128)}, u32[]{:S(2)}, u32[]{:S(2)}) %collective-permute-start.47) | collective-permute-done | bytes 401440 | tf_op jit(solution)/shard_map/ppermute | solution.py:98
  259.5 8.9 %collective-permute-done.48 = f32[896,112]{0,1:T(8,128)} collective-permute-done((f32[896,112]{0,1:T(8,128)}, f32[896,112]{0,1:T(8,128)}, u32[]{:S(2)}, u32[]{:S(2)}) %collective-permute-start.48) | collective-permute-done | bytes 401440 | tf_op jit(solution)/shard_map/ppermute | solution.py:98
  270.5 3.0 %copy.2 = f32[896,896]{1,0:T(8,128)} copy(f32[896,896]{0,1:T(8,128)S(1)} %broadcast_multiply_fusion) | data formatting | bytes 6422528 | tf_op jit(solution)/shard_map/div | solution.py:147
  (235 shorter events, 77.9 us)
Async XLA Ops:
  12.6 14.8 %collective-permute-start.6 = (bf16[112,2048]{1,0:T(8,128)(2,1)S(1)}, bf16[112,2048]{1,0:T(8,128)(2,1)S(1)}, u32[]{:S(2)}, u32[]{:S(2)}) collective-permute-start(bf16[112,2048]{1,0:T(8,128)(2,1)S(1)} %multiply_convert_fusion.1), channel_id=1, source_target_pairs={{4,0},{12,8},{20,16},{28,24},{5,1},{13,9},{21,17},{29,25},{6,2},{1... | collective-permute-start | bytes 1376264 | tf_op jit(solution)/shard_map/ppermute | solution.py:11
  13.9 14.8 %collective-permute-start.7 = (bf16[112,2048]{1,0:T(8,128)(2,1)S(1)}, bf16[112,2048]{1,0:T(8,128)(2,1)S(1)}, u32[]{:S(2)}, u32[]{:S(2)}) collective-permute-start(bf16[112,2048]{1,0:T(8,128)(2,1)S(1)} %multiply_convert_fusion.1), channel_id=1, source_target_pairs={{8,0},{12,4},{16,8},{20,12},{24,16},{28,20},{9,1},{13,5},{17,9},{2... | collective-permute-start | bytes 1376264 | tf_op jit(solution)/shard_map/ppermute | solution.py:11
  28.8 23.9 %collective-permute-start.8 = (bf16[224,2048]{1,0:T(8,128)(2,1)S(1)}, bf16[224,2048]{1,0:T(8,128)(2,1)S(1)}, u32[]{:S(2)}, u32[]{:S(2)}) collective-permute-start(bf16[224,2048]{1,0:T(8,128)(2,1)S(1)} %pad_maximum_fusion.13), channel_id=1, source_target_pairs={{4,0},{12,8},{20,16},{28,24},{5,1},{13,9},{21,17},{29,25},{6,2},{1... | collective-permute-start | bytes 2752520 | tf_op jit(solution)/shard_map/ppermute | solution.py:11
  30.1 23.6 %collective-permute-start.10 = (bf16[112,2048]{1,0:T(8,128)(2,1)S(1)}, bf16[112,2048]{1,0:T(8,128)(2,1)S(1)}, u32[]{:S(2)}, u32[]{:S(2)}) collective-permute-start(bf16[112,2048]{1,0:T(8,128)(2,1)S(1)} %get-tuple-element.169), channel_id=1, source_target_pairs={{8,0},{12,4},{16,8},{20,12},{24,16},{28,20},{9,1},{13,5},{17,9},{2... | collective-permute-start | bytes 1376264 | tf_op jit(solution)/shard_map/ppermute | solution.py:11
  31.4 22.3 %collective-permute-start.9 = (bf16[112,2048]{1,0:T(8,128)(2,1)S(1)}, bf16[112,2048]{1,0:T(8,128)(2,1)S(1)}, u32[]{:S(2)}, u32[]{:S(2)}) collective-permute-start(bf16[112,2048]{1,0:T(8,128)(2,1)S(1)} %collective-permute-done.7), channel_id=1, source_target_pairs={{0,4},{8,12},{16,20},{24,28},{1,5},{9,13},{17,21},{25,29},{2,6},{1... | collective-permute-start | bytes 1376264 | tf_op jit(solution)/shard_map/ppermute | solution.py:11
  54.0 23.0 %collective-permute-start.13 = (bf16[224,2048]{1,0:T(8,128)(2,1)S(1)}, bf16[224,2048]{1,0:T(8,128)(2,1)S(1)}, u32[]{:S(2)}, u32[]{:S(2)}) collective-permute-start(bf16[224,2048]{1,0:T(8,128)(2,1)S(1)} %get-tuple-element.406), channel_id=1, source_target_pairs={{8,0},{12,4},{16,8},{20,12},{24,16},{28,20},{9,1},{13,5},{17,9},{2... | collective-permute-start | bytes 2752520 | tf_op jit(solution)/shard_map/ppermute | solution.py:11
  55.3 23.0 %collective-permute-start.11 = (bf16[224,2048]{1,0:T(8,128)(2,1)S(1)}, bf16[224,2048]{1,0:T(8,128)(2,1)S(1)}, u32[]{:S(2)}, u32[]{:S(2)}) collective-permute-start(bf16[224,2048]{1,0:T(8,128)(2,1)S(1)} %get-tuple-element.407), channel_id=1, source_target_pairs={{4,0},{12,8},{20,16},{28,24},{5,1},{13,9},{21,17},{29,25},{6,2},{1... | collective-permute-start | bytes 2752520 | tf_op jit(solution)/shard_map/ppermute | solution.py:11
  56.6 22.8 %collective-permute-start.12 = (bf16[112,2048]{1,0:T(8,128)(2,1)S(1)}, bf16[112,2048]{1,0:T(8,128)(2,1)S(1)}, u32[]{:S(2)}, u32[]{:S(2)}) collective-permute-start(bf16[112,2048]{1,0:T(8,128)(2,1)S(1)} %collective-permute-done.10), channel_id=1, source_target_pairs={{0,4},{8,12},{16,20},{24,28},{1,5},{9,13},{17,21},{25,29},{2,6},{1... | collective-permute-start | bytes 1376264 | tf_op jit(solution)/shard_map/ppermute | solution.py:11
  80.8 22.7 %collective-permute-start.17 = (bf16[224,2048]{1,0:T(8,128)(2,1)}, bf16[224,2048]{1,0:T(8,128)(2,1)}, u32[]{:S(2)}, u32[]{:S(2)}) collective-permute-start(bf16[224,2048]{1,0:T(8,128)(2,1)} %get-tuple-element.404), channel_id=1, source_target_pairs={{8,0},{12,4},{16,8},{20,12},{24,16},{28,20},{9,1},{13,5},{17,9},{2... | collective-permute-start | bytes 2752520 | tf_op jit(solution)/shard_map/ppermute | solution.py:11
  82.2 23.7 %collective-permute-start.16 = (bf16[112,2048]{1,0:T(8,128)(2,1)}, bf16[112,2048]{1,0:T(8,128)(2,1)S(1)}, u32[]{:S(2)}, u32[]{:S(2)}) collective-permute-start(bf16[112,2048]{1,0:T(8,128)(2,1)} %copy-done.13), channel_id=1, source_target_pairs={{0,4},{8,12},{16,20},{24,28},{1,5},{9,13},{17,21},{25,29},{2,6},{1... | collective-permute-start | bytes 1376264 | tf_op jit(solution)/shard_map/ppermute | solution.py:11
  83.6 22.1 %collective-permute-start.15 = (bf16[224,2048]{1,0:T(8,128)(2,1)}, bf16[224,2048]{1,0:T(8,128)(2,1)S(1)}, u32[]{:S(2)}, u32[]{:S(2)}) collective-permute-start(bf16[224,2048]{1,0:T(8,128)(2,1)} %get-tuple-element.405), channel_id=1, source_target_pairs={{4,0},{12,8},{20,16},{28,24},{5,1},{13,9},{21,17},{29,25},{6,2},{1... | collective-permute-start | bytes 2752520 | tf_op jit(solution)/shard_map/ppermute | solution.py:11
  91.1 14.8 %collective-permute-start.14 = (f32[896,224]{0,1:T(8,128)S(1)}, f32[896,224]{0,1:T(8,128)S(1)}, u32[]{:S(2)}, u32[]{:S(2)}) collective-permute-start(f32[896,224]{0,1:T(8,128)S(1)} %maximum_select_fusion), channel_id=1, source_target_pairs={{0,1},{1,0},{2,3},{3,2},{4,5},{5,4},{6,7},{7,6},{8,9},{9,8},{10,11... | collective-permute-start | bytes 2408456 | tf_op jit(solution)/shard_map/ppermute | solution.py:103
  106.9 23.7 %collective-permute-start.20 = (bf16[112,2048]{1,0:T(8,128)(2,1)S(1)}, bf16[112,2048]{1,0:T(8,128)(2,1)S(1)}, u32[]{:S(2)}, u32[]{:S(2)}) collective-permute-start(bf16[112,2048]{1,0:T(8,128)(2,1)S(1)} %get-tuple-element.228), channel_id=1, source_target_pairs={{0,4},{8,12},{16,20},{24,28},{1,5},{9,13},{17,21},{25,29},{2,6},{1... | collective-permute-start | bytes 1376264 | tf_op jit(solution)/shard_map/ppermute | solution.py:11
  108.8 21.2 %collective-permute-start.22 = (bf16[224,2048]{1,0:T(8,128)(2,1)S(1)}, bf16[224,2048]{1,0:T(8,128)(2,1)S(1)}, u32[]{:S(2)}, u32[]{:S(2)}) collective-permute-start(bf16[224,2048]{1,0:T(8,128)(2,1)S(1)} %get-tuple-element.402), channel_id=1, source_target_pairs={{8,0},{12,4},{16,8},{20,12},{24,16},{28,20},{9,1},{13,5},{17,9},{2... | collective-permute-start | bytes 2752520 | tf_op jit(solution)/shard_map/ppermute | solution.py:11
  110.1 20.5 %collective-permute-start.19 = (bf16[224,2048]{1,0:T(8,128)(2,1)S(1)}, bf16[224,2048]{1,0:T(8,128)(2,1)S(1)}, u32[]{:S(2)}, u32[]{:S(2)}) collective-permute-start(bf16[224,2048]{1,0:T(8,128)(2,1)S(1)} %get-tuple-element.403), channel_id=1, source_target_pairs={{4,0},{12,8},{20,16},{28,24},{5,1},{13,9},{21,17},{29,25},{6,2},{1... | collective-permute-start | bytes 2752520 | tf_op jit(solution)/shard_map/ppermute | solution.py:11
  114.0 16.6 %collective-permute-start.18 = (f32[896,224]{0,1:T(8,128)S(1)}, f32[896,224]{0,1:T(8,128)S(1)}, u32[]{:S(2)}, u32[]{:S(2)}) collective-permute-start(f32[896,224]{0,1:T(8,128)S(1)} %maximum_select_fusion.1), channel_id=1, source_target_pairs={{0,1},{1,0},{2,3},{3,2},{4,5},{5,4},{6,7},{7,6},{8,9},{9,8},{10,11... | collective-permute-start | bytes 2408456 | tf_op jit(solution)/shard_map/ppermute | solution.py:103
  132.2 22.3 %collective-permute-start.25 = (bf16[112,2048]{1,0:T(8,128)(2,1)S(1)}, bf16[112,2048]{1,0:T(8,128)(2,1)S(1)}, u32[]{:S(2)}, u32[]{:S(2)}) collective-permute-start(bf16[112,2048]{1,0:T(8,128)(2,1)S(1)} %get-tuple-element.247), channel_id=1, source_target_pairs={{0,4},{8,12},{16,20},{24,28},{1,5},{9,13},{17,21},{25,29},{2,6},{1... | collective-permute-start | bytes 1376264 | tf_op jit(solution)/shard_map/ppermute | solution.py:11
  133.9 20.2 %collective-permute-start.27 = (bf16[224,2048]{1,0:T(8,128)(2,1)S(1)}, bf16[224,2048]{1,0:T(8,128)(2,1)S(1)}, u32[]{:S(2)}, u32[]{:S(2)}) collective-permute-start(bf16[224,2048]{1,0:T(8,128)(2,1)S(1)} %get-tuple-element.400), channel_id=1, source_target_pairs={{8,0},{12,4},{16,8},{20,12},{24,16},{28,20},{9,1},{13,5},{17,9},{2... | collective-permute-start | bytes 2752520 | tf_op jit(solution)/shard_map/ppermute | solution.py:11
  135.2 19.2 %collective-permute-start.24 = (bf16[224,2048]{1,0:T(8,128)(2,1)S(1)}, bf16[224,2048]{1,0:T(8,128)(2,1)S(1)}, u32[]{:S(2)}, u32[]{:S(2)}) collective-permute-start(bf16[224,2048]{1,0:T(8,128)(2,1)S(1)} %get-tuple-element.401), channel_id=1, source_target_pairs={{4,0},{12,8},{20,16},{28,24},{5,1},{13,9},{21,17},{29,25},{6,2},{1... | collective-permute-start | bytes 2752520 | tf_op jit(solution)/shard_map/ppermute | solution.py:11
  139.3 15.2 %collective-permute-start.23 = (f32[896,224]{0,1:T(8,128)S(1)}, f32[896,224]{0,1:T(8,128)S(1)}, u32[]{:S(2)}, u32[]{:S(2)}) collective-permute-start(f32[896,224]{0,1:T(8,128)S(1)} %maximum_select_fusion.2), channel_id=1, source_target_pairs={{0,1},{1,0},{2,3},{3,2},{4,5},{5,4},{6,7},{7,6},{8,9},{9,8},{10,11... | collective-permute-start | bytes 2408456 | tf_op jit(solution)/shard_map/ppermute | solution.py:103
  155.4 21.1 %collective-permute-start.30 = (bf16[112,2048]{1,0:T(8,128)(2,1)S(1)}, bf16[112,2048]{1,0:T(8,128)(2,1)S(1)}, u32[]{:S(2)}, u32[]{:S(2)}) collective-permute-start(bf16[112,2048]{1,0:T(8,128)(2,1)S(1)} %get-tuple-element.267), channel_id=1, source_target_pairs={{0,4},{8,12},{16,20},{24,28},{1,5},{9,13},{17,21},{25,29},{2,6},{1... | collective-permute-start | bytes 1376264 | tf_op jit(solution)/shard_map/ppermute | solution.py:11
  157.1 19.1 %collective-permute-start.32 = (bf16[224,2048]{1,0:T(8,128)(2,1)S(1)}, bf16[224,2048]{1,0:T(8,128)(2,1)S(1)}, u32[]{:S(2)}, u32[]{:S(2)}) collective-permute-start(bf16[224,2048]{1,0:T(8,128)(2,1)S(1)} %get-tuple-element.398), channel_id=1, source_target_pairs={{8,0},{12,4},{16,8},{20,12},{24,16},{28,20},{9,1},{13,5},{17,9},{2... | collective-permute-start | bytes 2752520 | tf_op jit(solution)/shard_map/ppermute | solution.py:11
  158.4 17.9 %collective-permute-start.29 = (bf16[224,2048]{1,0:T(8,128)(2,1)S(1)}, bf16[224,2048]{1,0:T(8,128)(2,1)S(1)}, u32[]{:S(2)}, u32[]{:S(2)}) collective-permute-start(bf16[224,2048]{1,0:T(8,128)(2,1)S(1)} %get-tuple-element.399), channel_id=1, source_target_pairs={{4,0},{12,8},{20,16},{28,24},{5,1},{13,9},{21,17},{29,25},{6,2},{1... | collective-permute-start | bytes 2752520 | tf_op jit(solution)/shard_map/ppermute | solution.py:11
  178.2 19.9 %collective-permute-start.35 = (bf16[112,2048]{1,0:T(8,128)(2,1)S(1)}, bf16[112,2048]{1,0:T(8,128)(2,1)S(1)}, u32[]{:S(2)}, u32[]{:S(2)}) collective-permute-start(bf16[112,2048]{1,0:T(8,128)(2,1)S(1)} %get-tuple-element.287), channel_id=1, source_target_pairs={{0,4},{8,12},{16,20},{24,28},{1,5},{9,13},{17,21},{25,29},{2,6},{1... | collective-permute-start | bytes 1376264 | tf_op jit(solution)/shard_map/ppermute | solution.py:11
  179.8 18.0 %collective-permute-start.37 = (bf16[224,2048]{1,0:T(8,128)(2,1)S(1)}, bf16[224,2048]{1,0:T(8,128)(2,1)S(1)}, u32[]{:S(2)}, u32[]{:S(2)}) collective-permute-start(bf16[224,2048]{1,0:T(8,128)(2,1)S(1)} %get-tuple-element.396), channel_id=1, source_target_pairs={{8,0},{12,4},{16,8},{20,12},{24,16},{28,20},{9,1},{13,5},{17,9},{2... | collective-permute-start | bytes 2752520 | tf_op jit(solution)/shard_map/ppermute | solution.py:11
  181.1 16.8 %collective-permute-start.34 = (bf16[224,2048]{1,0:T(8,128)(2,1)S(1)}, bf16[224,2048]{1,0:T(8,128)(2,1)S(1)}, u32[]{:S(2)}, u32[]{:S(2)}) collective-permute-start(bf16[224,2048]{1,0:T(8,128)(2,1)S(1)} %get-tuple-element.397), channel_id=1, source_target_pairs={{4,0},{12,8},{20,16},{28,24},{5,1},{13,9},{21,17},{29,25},{6,2},{1... | collective-permute-start | bytes 2752520 | tf_op jit(solution)/shard_map/ppermute | solution.py:11
  200.6 19.8 %collective-permute-start.38 = (f32[896,224]{0,1:T(8,128)S(1)}, f32[896,224]{0,1:T(8,128)S(1)}, u32[]{:S(2)}, u32[]{:S(2)}) collective-permute-start(f32[896,224]{0,1:T(8,128)S(1)} %maximum_select_fusion.5), channel_id=1, source_target_pairs={{0,1},{1,0},{2,3},{3,2},{4,5},{5,4},{6,7},{7,6},{8,9},{9,8},{10,11... | collective-permute-start | bytes 2408456 | tf_op jit(solution)/shard_map/ppermute | solution.py:103
  204.1 16.2 %collective-permute-start.42 = (bf16[112,2048]{1,0:T(8,128)(2,1)S(1)}, bf16[112,2048]{1,0:T(8,128)(2,1)S(1)}, u32[]{:S(2)}, u32[]{:S(2)}) collective-permute-start(bf16[112,2048]{1,0:T(8,128)(2,1)S(1)} %collective-permute-done.35), channel_id=1, source_target_pairs={{8,0},{12,4},{16,8},{20,12},{24,16},{28,20},{9,1},{13,5},{17,9},{2... | collective-permute-start | bytes 1376264 | tf_op jit(solution)/shard_map/ppermute | solution.py:11
  222.9 16.4 %collective-permute-start.43 = (f32[896,224]{0,1:T(8,128)S(1)}, f32[896,224]{0,1:T(8,128)S(1)}, u32[]{:S(2)}, u32[]{:S(2)}) collective-permute-start(f32[896,224]{0,1:T(8,128)S(1)} %maximum_select_fusion.6), channel_id=1, source_target_pairs={{0,1},{1,0},{2,3},{3,2},{4,5},{5,4},{6,7},{7,6},{8,9},{9,8},{10,11... | collective-permute-start | bytes 2408456 | tf_op jit(solution)/shard_map/ppermute | solution.py:103
  224.8 14.5 %collective-permute-start.45 = (bf16[112,2048]{1,0:T(8,128)(2,1)S(1)}, bf16[112,2048]{1,0:T(8,128)(2,1)S(1)}, u32[]{:S(2)}, u32[]{:S(2)}) collective-permute-start(bf16[112,2048]{1,0:T(8,128)(2,1)S(1)} %collective-permute-done.39), channel_id=1, source_target_pairs={{8,0},{12,4},{16,8},{20,12},{24,16},{28,20},{9,1},{13,5},{17,9},{2... | collective-permute-start | bytes 1376264 | tf_op jit(solution)/shard_map/ppermute | solution.py:11
  244.1 15.3 %collective-permute-start.47 = (f32[896,112]{0,1:T(8,128)}, f32[896,112]{0,1:T(8,128)}, u32[]{:S(2)}, u32[]{:S(2)}) collective-permute-start(f32[896,112]{0,1:T(8,128)} %get-tuple-element.341), channel_id=1, source_target_pairs={{0,3},{1,2},{2,1},{3,0},{4,7},{5,6},{6,5},{7,4},{8,11},{9,10},{10,... | collective-permute-start | bytes 1204232 | tf_op jit(solution)/shard_map/ppermute | solution.py:98
  246.6 21.8 %collective-permute-start.48 = (f32[896,112]{0,1:T(8,128)}, f32[896,112]{0,1:T(8,128)}, u32[]{:S(2)}, u32[]{:S(2)}) collective-permute-start(f32[896,112]{0,1:T(8,128)} %select_select_fusion.1), channel_id=1, source_target_pairs={{0,2},{1,3},{2,0},{3,1},{4,6},{5,7},{6,4},{7,5},{8,10},{9,11},{10,... | collective-permute-start | bytes 1204232 | tf_op jit(solution)/shard_map/ppermute | solution.py:98
  (51 other events, 829.7 us)

commit v6 on v4

--- a/solution.py
+++ b/solution.py
@@ -58,7 +58,8 @@
     rows = dosages.shape[0]
     step = rows // CHUNKS
     first_piece = standard_rows(dosages[:step])
-    rest = standard_rows(dosages[step:])
+    first_piece, later = lax.optimization_barrier((first_piece, dosages))
+    rest = standard_rows(later[step:])
     own_block = jnp.concatenate([first_piece, rest], axis=0)
     pieces = [first_piece] + [rest[(c - 1) * step:c * step] for c in range(1, CHUNKS)]
 

time: 269 us -> 273 us (1.015)
  waiting for transfers between devices: 148 us -> 156 us
    ppermute x27, waiting for transfers between devices: 110 us -> 118 us  [moved(): return lax.ppermute(value, 'snp', pairs)]
  transfers between devices with their start and end apart: 50 -> 50, of which waited for: 25 -> 25; matrix products, arithmetic and copies ran while one was open for 15% -> 13% of each run, Pallas kernels for 0% -> 0%
where the time goes in v6:
time: 273 us; the launch traced here: 272 us
  waiting for transfers between devices  156 us (57%)
  starting transfers between devices  58.4 us (21%)
  other arithmetic  27.8 us (10%)
  matrix products  18 us (7%)
  local copies, waits for them, and re-layouts  10.5 us (4%)
    ppermute x27, waiting for transfers between devices, moved(): return lax.ppermute(value, 'snp', pairs)  118 us
    ppermute x27, starting transfers between devices, moved(): return lax.ppermute(value, 'snp', pairs)  43.1 us
    ppermute x7, waiting for transfers between devices, second_level(): last = lax.ppermute(pick(c, 2, 3, 0, 1) + onward, 'samp', across)  20.9 us
    dot_general x8, matrix products, finish(): jnp.einsum('ab,cb->ac', own_block, blocks, preferred_element_type=jnp.flo...  18 us
    ppermute x3, waiting for transfers between devices, finish(): lax.ppermute(outgoing[i], 'samp', [(j, j ^ i) for j in range(groups)])  14.4 us
    ppermute x7, starting transfers between devices, second_level(): last = lax.ppermute(pick(c, 2, 3, 0, 1) + onward, 'samp', across)  7.61 us
    add x7, other arithmetic, second_level(): state['results'][c] = pick(c, 0, 1, 2, 3) + mine + last  7.16 us
    reduce_sum x2, other arithmetic, local_moments(): return (jnp.sum(values, axis=1), jnp.sum(values * values, axis=1))  5.47 us
  transfers between devices with their start and end apart: 50, of which 25 were waited for; matrix products, arithmetic and copies ran while one was open for 13% of the time, Pallas kernels for 0%

profile of v6, /device:TPU:0, one launch (start us, length us, event | category | flops | bytes accessed | tf_op | source)
XLA Modules:
  0.0 272.5 jit_solution(9017907095508887888)
XLA Ops:
  1.4 2.4 collective-permute-start
  5.1 2.3 collective-permute-done.1
  9.0 4.1 %slice_reduce_fusion = (f32[784]{0:T(1024)S(1)}, f32[784]{0:T(1024)S(1)}) fusion(f32[896,2048]{1,0:T(8,128)} %param.1), kind=kLoop, calls=%fused_computation.2 | loop fusion | flops 4815328 | bytes 6428800 | tf_op jit(solution)/shard_map/reduce_sum | solution.py:21
  18.5 1.6 fusion.76
  20.1 9.3 %collective-permute-done.6 = bf16[112,2048]{1,0:T(8,128)(2,1)S(1)} collective-permute-done((bf16[112,2048]{1,0:T(8,128)(2,1)S(1)}, bf16[112,2048]{1,0:T(8,128)(2,1)S(1)}, u32[]{:S(2)}, u32[]{:S(2)}) %collective-permute-start.6) | collective-permute-done | bytes 458784 | tf_op jit(solution)/shard_map/ppermute | solution.py:11
  33.3 4.6 %collective-permute-start.9 = (bf16[112,2048]{1,0:T(8,128)(2,1)S(1)}, bf16[112,2048]{1,0:T(8,128)(2,1)S(1)}, u32[]{:S(2)}, u32[]{:S(2)}) collective-permute-start(bf16[112,2048]{1,0:T(8,128)(2,1)S(1)} %collective-permute-done.7), channel_id=1, source_target_pairs={{0,4},{8,12},{16,20},{24,28},{1,5},{9,13},{17,21},{25,29},{2,6},{1... | collective-permute-start | bytes 1376264 | tf_op jit(solution)/shard_map/ppermute | solution.py:11
  38.0 16.1 %collective-permute-done.8 = bf16[224,2048]{1,0:T(8,128)(2,1)S(1)} collective-permute-done((bf16[224,2048]{1,0:T(8,128)(2,1)S(1)}, bf16[224,2048]{1,0:T(8,128)(2,1)S(1)}, u32[]{:S(2)}, u32[]{:S(2)}) %collective-permute-start.8) | collective-permute-done | bytes 917536 | tf_op jit(solution)/shard_map/ppermute | solution.py:11
  57.9 4.6 %collective-permute-start.12 = (bf16[112,2048]{1,0:T(8,128)(2,1)S(1)}, bf16[112,2048]{1,0:T(8,128)(2,1)S(1)}, u32[]{:S(2)}, u32[]{:S(2)}) collective-permute-start(bf16[112,2048]{1,0:T(8,128)(2,1)S(1)} %collective-permute-done.10), channel_id=1, source_target_pairs={{0,4},{8,12},{16,20},{24,28},{1,5},{9,13},{17,21},{25,29},{2,6},{1... | collective-permute-start | bytes 1376264 | tf_op jit(solution)/shard_map/ppermute | solution.py:11
  62.6 15.1 %collective-permute-done.13 = bf16[224,2048]{1,0:T(8,128)(2,1)S(1)} collective-permute-done((bf16[224,2048]{1,0:T(8,128)(2,1)S(1)}, bf16[224,2048]{1,0:T(8,128)(2,1)S(1)}, u32[]{:S(2)}, u32[]{:S(2)}) %collective-permute-start.13) | collective-permute-done | bytes 917536 | tf_op jit(solution)/shard_map/ppermute | solution.py:11
  88.2 3.4 %fusion = f32[896,448]{0,1:T(8,128)S(1)} fusion(bf16[112,2048]{1,0:T(8,128)(2,1)S(1)} %add.174, bf16[112,2048]{1,0:T(8,128)(2,1)} %copy-done.30, bf16[112,2048]{1,0:T(8,128)(2,1)S(1)} %add.173, bf16[112,2048]{1,0:T(8,128)(2,1)} %copy-done.31, bf16[784,2048]{1,0:T(8,128)(2,1)S(1)} %multiply_convert_fusion), kind=kOutput, calls=%fused_computation.4 | convolution fusion | flops 1658847232 | bytes 6651904 | tf_op jit(solution)/shard_map/ab,cb->ac/dot_general | solution.py:87
  91.9 11.8 %collective-permute-done.17 = bf16[224,2048]{1,0:T(8,128)(2,1)} collective-permute-done((bf16[224,2048]{1,0:T(8,128)(2,1)}, bf16[224,2048]{1,0:T(8,128)(2,1)}, u32[]{:S(2)}, u32[]{:S(2)}) %collective-permute-start.17) | collective-permute-done | bytes 917536 | tf_op jit(solution)/shard_map/ppermute | solution.py:11
  107.4 1.6 collective-permute-start.20
  112.1 2.1 fusion.8
  115.5 14.5 %collective-permute-done.22 = bf16[224,2048]{1,0:T(8,128)(2,1)S(1)} collective-permute-done((bf16[224,2048]{1,0:T(8,128)(2,1)S(1)}, bf16[224,2048]{1,0:T(8,128)(2,1)S(1)}, u32[]{:S(2)}, u32[]{:S(2)}) %collective-permute-start.22) | collective-permute-done | bytes 917536 | tf_op jit(solution)/shard_map/ppermute | solution.py:11
  136.6 2.1 fusion.16
  140.0 13.3 %collective-permute-done.27 = bf16[224,2048]{1,0:T(8,128)(2,1)S(1)} collective-permute-done((bf16[224,2048]{1,0:T(8,128)(2,1)S(1)}, bf16[224,2048]{1,0:T(8,128)(2,1)S(1)}, u32[]{:S(2)}, u32[]{:S(2)}) %collective-permute-start.27) | collective-permute-done | bytes 917536 | tf_op jit(solution)/shard_map/ppermute | solution.py:11
  159.6 2.1 fusion.24
  163.0 12.5 %collective-permute-done.32 = bf16[224,2048]{1,0:T(8,128)(2,1)S(1)} collective-permute-done((bf16[224,2048]{1,0:T(8,128)(2,1)S(1)}, bf16[224,2048]{1,0:T(8,128)(2,1)S(1)}, u32[]{:S(2)}, u32[]{:S(2)}) %collective-permute-start.32) | collective-permute-done | bytes 917536 | tf_op jit(solution)/shard_map/ppermute | solution.py:11
  181.3 2.1 fusion.32
  184.7 11.5 %collective-permute-done.37 = bf16[224,2048]{1,0:T(8,128)(2,1)S(1)} collective-permute-done((bf16[224,2048]{1,0:T(8,128)(2,1)S(1)}, bf16[224,2048]{1,0:T(8,128)(2,1)S(1)}, u32[]{:S(2)}, u32[]{:S(2)}) %collective-permute-start.37) | collective-permute-done | bytes 917536 | tf_op jit(solution)/shard_map/ppermute | solution.py:11
  196.7 2.1 fusion.40
  204.8 6.2 %collective-permute-done.40 = f32[896,112]{0,1:T(8,128)S(1)} collective-permute-done((f32[896,112]{0,1:T(8,128)S(1)}, f32[896,112]{0,1:T(8,128)S(1)}, u32[]{:S(2)}, u32[]{:S(2)}) %collective-permute-start.40) | collective-permute-done | bytes 401440 | tf_op jit(solution)/shard_map/ppermute | solution.py:113
  212.1 4.1 %collective-permute-done.41 = bf16[112,2048]{1,0:T(8,128)(2,1)S(1)} collective-permute-done((bf16[112,2048]{1,0:T(8,128)(2,1)S(1)}, bf16[112,2048]{1,0:T(8,128)(2,1)S(1)}, u32[]{:S(2)}, u32[]{:S(2)}) %collective-permute-start.41) | collective-permute-done | bytes 458784 | tf_op jit(solution)/shard_map/ppermute | solution.py:11
  216.3 3.1 %collective-permute-done.42 = bf16[112,2048]{1,0:T(8,128)(2,1)S(1)} collective-permute-done((bf16[112,2048]{1,0:T(8,128)(2,1)S(1)}, bf16[112,2048]{1,0:T(8,128)(2,1)S(1)}, u32[]{:S(2)}, u32[]{:S(2)}) %collective-permute-start.42) | collective-permute-done | bytes 458784 | tf_op jit(solution)/shard_map/ppermute | solution.py:11
  219.6 2.1 fusion.48
  224.5 9.5 %collective-permute-done.44 = f32[896,112]{0,1:T(8,128)S(1)} collective-permute-done((f32[896,112]{0,1:T(8,128)S(1)}, f32[896,112]{0,1:T(8,128)S(1)}, u32[]{:S(2)}, u32[]{:S(2)}) %collective-permute-start.44) | collective-permute-done | bytes 401440 | tf_op jit(solution)/shard_map/ppermute | solution.py:113
  235.0 3.0 %collective-permute-done.45 = bf16[112,2048]{1,0:T(8,128)(2,1)S(1)} collective-permute-done((bf16[112,2048]{1,0:T(8,128)(2,1)S(1)}, bf16[112,2048]{1,0:T(8,128)(2,1)S(1)}, u32[]{:S(2)}, u32[]{:S(2)}) %collective-permute-start.45) | collective-permute-done | bytes 458784 | tf_op jit(solution)/shard_map/ppermute | solution.py:11
  240.4 2.1 fusion.56
  246.4 5.1 %collective-permute-done.46 = f32[896,112]{0,1:T(8,128)} collective-permute-done((f32[896,112]{0,1:T(8,128)}, f32[896,112]{0,1:T(8,128)}, u32[]{:S(2)}, u32[]{:S(2)}) %collective-permute-start.46) | collective-permute-done | bytes 401440 | tf_op jit(solution)/shard_map/ppermute | solution.py:113
  253.0 5.8 %collective-permute-done.47 = f32[896,112]{0,1:T(8,128)} collective-permute-done((f32[896,112]{0,1:T(8,128)}, f32[896,112]{0,1:T(8,128)}, u32[]{:S(2)}, u32[]{:S(2)}) %collective-permute-start.47) | collective-permute-done | bytes 401440 | tf_op jit(solution)/shard_map/ppermute | solution.py:98
  258.8 8.6 %collective-permute-done.48 = f32[896,112]{0,1:T(8,128)} collective-permute-done((f32[896,112]{0,1:T(8,128)}, f32[896,112]{0,1:T(8,128)}, u32[]{:S(2)}, u32[]{:S(2)}) %collective-permute-start.48) | collective-permute-done | bytes 401440 | tf_op jit(solution)/shard_map/ppermute | solution.py:98
  269.5 3.0 %copy.2 = f32[896,896]{1,0:T(8,128)} copy(f32[896,896]{0,1:T(8,128)S(1)} %broadcast_multiply_fusion) | data formatting | bytes 6422528 | tf_op jit(solution)/shard_map/div | solution.py:147
  (236 shorter events, 79.2 us)
Async XLA Ops:
  15.0 14.3 %collective-permute-start.6 = (bf16[112,2048]{1,0:T(8,128)(2,1)S(1)}, bf16[112,2048]{1,0:T(8,128)(2,1)S(1)}, u32[]{:S(2)}, u32[]{:S(2)}) collective-permute-start(bf16[112,2048]{1,0:T(8,128)(2,1)S(1)} %multiply_convert_fusion.1), channel_id=1, source_target_pairs={{4,0},{12,8},{20,16},{28,24},{5,1},{13,9},{21,17},{29,25},{6,2},{1... | collective-permute-start | bytes 1376264 | tf_op jit(solution)/shard_map/ppermute | solution.py:11
  16.3 14.3 %collective-permute-start.7 = (bf16[112,2048]{1,0:T(8,128)(2,1)S(1)}, bf16[112,2048]{1,0:T(8,128)(2,1)S(1)}, u32[]{:S(2)}, u32[]{:S(2)}) collective-permute-start(bf16[112,2048]{1,0:T(8,128)(2,1)S(1)} %multiply_convert_fusion.1), channel_id=1, source_target_pairs={{8,0},{12,4},{16,8},{20,12},{24,16},{28,20},{9,1},{13,5},{17,9},{2... | collective-permute-start | bytes 1376264 | tf_op jit(solution)/shard_map/ppermute | solution.py:11
  30.7 23.3 %collective-permute-start.8 = (bf16[224,2048]{1,0:T(8,128)(2,1)S(1)}, bf16[224,2048]{1,0:T(8,128)(2,1)S(1)}, u32[]{:S(2)}, u32[]{:S(2)}) collective-permute-start(bf16[224,2048]{1,0:T(8,128)(2,1)S(1)} %pad_maximum_fusion.13), channel_id=1, source_target_pairs={{4,0},{12,8},{20,16},{28,24},{5,1},{13,9},{21,17},{29,25},{6,2},{1... | collective-permute-start | bytes 2752520 | tf_op jit(solution)/shard_map/ppermute | solution.py:11
  32.0 23.0 %collective-permute-start.10 = (bf16[112,2048]{1,0:T(8,128)(2,1)S(1)}, bf16[112,2048]{1,0:T(8,128)(2,1)S(1)}, u32[]{:S(2)}, u32[]{:S(2)}) collective-permute-start(bf16[112,2048]{1,0:T(8,128)(2,1)S(1)} %get-tuple-element.169), channel_id=1, source_target_pairs={{8,0},{12,4},{16,8},{20,12},{24,16},{28,20},{9,1},{13,5},{17,9},{2... | collective-permute-start | bytes 1376264 | tf_op jit(solution)/shard_map/ppermute | solution.py:11
  33.3 21.7 %collective-permute-start.9 = (bf16[112,2048]{1,0:T(8,128)(2,1)S(1)}, bf16[112,2048]{1,0:T(8,128)(2,1)S(1)}, u32[]{:S(2)}, u32[]{:S(2)}) collective-permute-start(bf16[112,2048]{1,0:T(8,128)(2,1)S(1)} %collective-permute-done.7), channel_id=1, source_target_pairs={{0,4},{8,12},{16,20},{24,28},{1,5},{9,13},{17,21},{25,29},{2,6},{1... | collective-permute-start | bytes 1376264 | tf_op jit(solution)/shard_map/ppermute | solution.py:11
  55.3 22.4 %collective-permute-start.13 = (bf16[224,2048]{1,0:T(8,128)(2,1)S(1)}, bf16[224,2048]{1,0:T(8,128)(2,1)S(1)}, u32[]{:S(2)}, u32[]{:S(2)}) collective-permute-start(bf16[224,2048]{1,0:T(8,128)(2,1)S(1)} %get-tuple-element.406), channel_id=1, source_target_pairs={{8,0},{12,4},{16,8},{20,12},{24,16},{28,20},{9,1},{13,5},{17,9},{2... | collective-permute-start | bytes 2752520 | tf_op jit(solution)/shard_map/ppermute | solution.py:11
  56.6 22.4 %collective-permute-start.11 = (bf16[224,2048]{1,0:T(8,128)(2,1)S(1)}, bf16[224,2048]{1,0:T(8,128)(2,1)S(1)}, u32[]{:S(2)}, u32[]{:S(2)}) collective-permute-start(bf16[224,2048]{1,0:T(8,128)(2,1)S(1)} %get-tuple-element.407), channel_id=1, source_target_pairs={{4,0},{12,8},{20,16},{28,24},{5,1},{13,9},{21,17},{29,25},{6,2},{1... | collective-permute-start | bytes 2752520 | tf_op jit(solution)/shard_map/ppermute | solution.py:11
  57.9 22.2 %collective-permute-start.12 = (bf16[112,2048]{1,0:T(8,128)(2,1)S(1)}, bf16[112,2048]{1,0:T(8,128)(2,1)S(1)}, u32[]{:S(2)}, u32[]{:S(2)}) collective-permute-start(bf16[112,2048]{1,0:T(8,128)(2,1)S(1)} %collective-permute-done.10), channel_id=1, source_target_pairs={{0,4},{8,12},{16,20},{24,28},{1,5},{9,13},{17,21},{25,29},{2,6},{1... | collective-permute-start | bytes 1376264 | tf_op jit(solution)/shard_map/ppermute | solution.py:11
  81.6 22.1 %collective-permute-start.17 = (bf16[224,2048]{1,0:T(8,128)(2,1)}, bf16[224,2048]{1,0:T(8,128)(2,1)}, u32[]{:S(2)}, u32[]{:S(2)}) collective-permute-start(bf16[224,2048]{1,0:T(8,128)(2,1)} %get-tuple-element.404), channel_id=1, source_target_pairs={{8,0},{12,4},{16,8},{20,12},{24,16},{28,20},{9,1},{13,5},{17,9},{2... | collective-permute-start | bytes 2752520 | tf_op jit(solution)/shard_map/ppermute | solution.py:11
  82.9 23.1 %collective-permute-start.16 = (bf16[112,2048]{1,0:T(8,128)(2,1)}, bf16[112,2048]{1,0:T(8,128)(2,1)S(1)}, u32[]{:S(2)}, u32[]{:S(2)}) collective-permute-start(bf16[112,2048]{1,0:T(8,128)(2,1)} %copy-done.14), channel_id=1, source_target_pairs={{0,4},{8,12},{16,20},{24,28},{1,5},{9,13},{17,21},{25,29},{2,6},{1... | collective-permute-start | bytes 1376264 | tf_op jit(solution)/shard_map/ppermute | solution.py:11
  84.3 21.5 %collective-permute-start.15 = (bf16[224,2048]{1,0:T(8,128)(2,1)}, bf16[224,2048]{1,0:T(8,128)(2,1)S(1)}, u32[]{:S(2)}, u32[]{:S(2)}) collective-permute-start(bf16[224,2048]{1,0:T(8,128)(2,1)} %get-tuple-element.405), channel_id=1, source_target_pairs={{4,0},{12,8},{20,16},{28,24},{5,1},{13,9},{21,17},{29,25},{6,2},{1... | collective-permute-start | bytes 2752520 | tf_op jit(solution)/shard_map/ppermute | solution.py:11
  107.4 23.3 %collective-permute-start.20 = (bf16[112,2048]{1,0:T(8,128)(2,1)S(1)}, bf16[112,2048]{1,0:T(8,128)(2,1)S(1)}, u32[]{:S(2)}, u32[]{:S(2)}) collective-permute-start(bf16[112,2048]{1,0:T(8,128)(2,1)S(1)} %get-tuple-element.228), channel_id=1, source_target_pairs={{0,4},{8,12},{16,20},{24,28},{1,5},{9,13},{17,21},{25,29},{2,6},{1... | collective-permute-start | bytes 1376264 | tf_op jit(solution)/shard_map/ppermute | solution.py:11
  109.2 20.8 %collective-permute-start.22 = (bf16[224,2048]{1,0:T(8,128)(2,1)S(1)}, bf16[224,2048]{1,0:T(8,128)(2,1)S(1)}, u32[]{:S(2)}, u32[]{:S(2)}) collective-permute-start(bf16[224,2048]{1,0:T(8,128)(2,1)S(1)} %get-tuple-element.402), channel_id=1, source_target_pairs={{8,0},{12,4},{16,8},{20,12},{24,16},{28,20},{9,1},{13,5},{17,9},{2... | collective-permute-start | bytes 2752520 | tf_op jit(solution)/shard_map/ppermute | solution.py:11
  110.5 20.1 %collective-permute-start.19 = (bf16[224,2048]{1,0:T(8,128)(2,1)S(1)}, bf16[224,2048]{1,0:T(8,128)(2,1)S(1)}, u32[]{:S(2)}, u32[]{:S(2)}) collective-permute-start(bf16[224,2048]{1,0:T(8,128)(2,1)S(1)} %get-tuple-element.403), channel_id=1, source_target_pairs={{4,0},{12,8},{20,16},{28,24},{5,1},{13,9},{21,17},{29,25},{6,2},{1... | collective-permute-start | bytes 2752520 | tf_op jit(solution)/shard_map/ppermute | solution.py:11
  114.4 16.2 %collective-permute-start.18 = (f32[896,224]{0,1:T(8,128)S(1)}, f32[896,224]{0,1:T(8,128)S(1)}, u32[]{:S(2)}, u32[]{:S(2)}) collective-permute-start(f32[896,224]{0,1:T(8,128)S(1)} %maximum_select_fusion.1), channel_id=1, source_target_pairs={{0,1},{1,0},{2,3},{3,2},{4,5},{5,4},{6,7},{7,6},{8,9},{9,8},{10,11... | collective-permute-start | bytes 2408456 | tf_op jit(solution)/shard_map/ppermute | solution.py:103
  131.8 21.8 %collective-permute-start.25 = (bf16[112,2048]{1,0:T(8,128)(2,1)S(1)}, bf16[112,2048]{1,0:T(8,128)(2,1)S(1)}, u32[]{:S(2)}, u32[]{:S(2)}) collective-permute-start(bf16[112,2048]{1,0:T(8,128)(2,1)S(1)} %get-tuple-element.247), channel_id=1, source_target_pairs={{0,4},{8,12},{16,20},{24,28},{1,5},{9,13},{17,21},{25,29},{2,6},{1... | collective-permute-start | bytes 1376264 | tf_op jit(solution)/shard_map/ppermute | solution.py:11
  133.5 19.8 %collective-permute-start.27 = (bf16[224,2048]{1,0:T(8,128)(2,1)S(1)}, bf16[224,2048]{1,0:T(8,128)(2,1)S(1)}, u32[]{:S(2)}, u32[]{:S(2)}) collective-permute-start(bf16[224,2048]{1,0:T(8,128)(2,1)S(1)} %get-tuple-element.400), channel_id=1, source_target_pairs={{8,0},{12,4},{16,8},{20,12},{24,16},{28,20},{9,1},{13,5},{17,9},{2... | collective-permute-start | bytes 2752520 | tf_op jit(solution)/shard_map/ppermute | solution.py:11
  134.8 18.7 %collective-permute-start.24 = (bf16[224,2048]{1,0:T(8,128)(2,1)S(1)}, bf16[224,2048]{1,0:T(8,128)(2,1)S(1)}, u32[]{:S(2)}, u32[]{:S(2)}) collective-permute-start(bf16[224,2048]{1,0:T(8,128)(2,1)S(1)} %get-tuple-element.401), channel_id=1, source_target_pairs={{4,0},{12,8},{20,16},{28,24},{5,1},{13,9},{21,17},{29,25},{6,2},{1... | collective-permute-start | bytes 2752520 | tf_op jit(solution)/shard_map/ppermute | solution.py:11
  138.9 14.7 %collective-permute-start.23 = (f32[896,224]{0,1:T(8,128)S(1)}, f32[896,224]{0,1:T(8,128)S(1)}, u32[]{:S(2)}, u32[]{:S(2)}) collective-permute-start(f32[896,224]{0,1:T(8,128)S(1)} %maximum_select_fusion.2), channel_id=1, source_target_pairs={{0,1},{1,0},{2,3},{3,2},{4,5},{5,4},{6,7},{7,6},{8,9},{9,8},{10,11... | collective-permute-start | bytes 2408456 | tf_op jit(solution)/shard_map/ppermute | solution.py:103
  155.0 20.7 %collective-permute-start.30 = (bf16[112,2048]{1,0:T(8,128)(2,1)S(1)}, bf16[112,2048]{1,0:T(8,128)(2,1)S(1)}, u32[]{:S(2)}, u32[]{:S(2)}) collective-permute-start(bf16[112,2048]{1,0:T(8,128)(2,1)S(1)} %get-tuple-element.267), channel_id=1, source_target_pairs={{0,4},{8,12},{16,20},{24,28},{1,5},{9,13},{17,21},{25,29},{2,6},{1... | collective-permute-start | bytes 1376264 | tf_op jit(solution)/shard_map/ppermute | solution.py:11
  156.8 18.7 %collective-permute-start.32 = (bf16[224,2048]{1,0:T(8,128)(2,1)S(1)}, bf16[224,2048]{1,0:T(8,128)(2,1)S(1)}, u32[]{:S(2)}, u32[]{:S(2)}) collective-permute-start(bf16[224,2048]{1,0:T(8,128)(2,1)S(1)} %get-tuple-element.398), channel_id=1, source_target_pairs={{8,0},{12,4},{16,8},{20,12},{24,16},{28,20},{9,1},{13,5},{17,9},{2... | collective-permute-start | bytes 2752520 | tf_op jit(solution)/shard_map/ppermute | solution.py:11
  158.1 17.5 %collective-permute-start.29 = (bf16[224,2048]{1,0:T(8,128)(2,1)S(1)}, bf16[224,2048]{1,0:T(8,128)(2,1)S(1)}, u32[]{:S(2)}, u32[]{:S(2)}) collective-permute-start(bf16[224,2048]{1,0:T(8,128)(2,1)S(1)} %get-tuple-element.399), channel_id=1, source_target_pairs={{4,0},{12,8},{20,16},{28,24},{5,1},{13,9},{21,17},{29,25},{6,2},{1... | collective-permute-start | bytes 2752520 | tf_op jit(solution)/shard_map/ppermute | solution.py:11
  176.8 19.6 %collective-permute-start.35 = (bf16[112,2048]{1,0:T(8,128)(2,1)S(1)}, bf16[112,2048]{1,0:T(8,128)(2,1)S(1)}, u32[]{:S(2)}, u32[]{:S(2)}) collective-permute-start(bf16[112,2048]{1,0:T(8,128)(2,1)S(1)} %get-tuple-element.287), channel_id=1, source_target_pairs={{0,4},{8,12},{16,20},{24,28},{1,5},{9,13},{17,21},{25,29},{2,6},{1... | collective-permute-start | bytes 1376264 | tf_op jit(solution)/shard_map/ppermute | solution.py:11
  178.5 17.8 %collective-permute-start.37 = (bf16[224,2048]{1,0:T(8,128)(2,1)S(1)}, bf16[224,2048]{1,0:T(8,128)(2,1)S(1)}, u32[]{:S(2)}, u32[]{:S(2)}) collective-permute-start(bf16[224,2048]{1,0:T(8,128)(2,1)S(1)} %get-tuple-element.396), channel_id=1, source_target_pairs={{8,0},{12,4},{16,8},{20,12},{24,16},{28,20},{9,1},{13,5},{17,9},{2... | collective-permute-start | bytes 2752520 | tf_op jit(solution)/shard_map/ppermute | solution.py:11
  179.8 16.6 %collective-permute-start.34 = (bf16[224,2048]{1,0:T(8,128)(2,1)S(1)}, bf16[224,2048]{1,0:T(8,128)(2,1)S(1)}, u32[]{:S(2)}, u32[]{:S(2)}) collective-permute-start(bf16[224,2048]{1,0:T(8,128)(2,1)S(1)} %get-tuple-element.397), channel_id=1, source_target_pairs={{4,0},{12,8},{20,16},{28,24},{5,1},{13,9},{21,17},{29,25},{6,2},{1... | collective-permute-start | bytes 2752520 | tf_op jit(solution)/shard_map/ppermute | solution.py:11
  199.0 20.4 %collective-permute-start.38 = (f32[896,224]{0,1:T(8,128)S(1)}, f32[896,224]{0,1:T(8,128)S(1)}, u32[]{:S(2)}, u32[]{:S(2)}) collective-permute-start(f32[896,224]{0,1:T(8,128)S(1)} %maximum_select_fusion.5), channel_id=1, source_target_pairs={{0,1},{1,0},{2,3},{3,2},{4,5},{5,4},{6,7},{7,6},{8,9},{9,8},{10,11... | collective-permute-start | bytes 2408456 | tf_op jit(solution)/shard_map/ppermute | solution.py:103
  203.3 16.1 %collective-permute-start.42 = (bf16[112,2048]{1,0:T(8,128)(2,1)S(1)}, bf16[112,2048]{1,0:T(8,128)(2,1)S(1)}, u32[]{:S(2)}, u32[]{:S(2)}) collective-permute-start(bf16[112,2048]{1,0:T(8,128)(2,1)S(1)} %collective-permute-done.35), channel_id=1, source_target_pairs={{8,0},{12,4},{16,8},{20,12},{24,16},{28,20},{9,1},{13,5},{17,9},{2... | collective-permute-start | bytes 1376264 | tf_op jit(solution)/shard_map/ppermute | solution.py:11
  222.0 16.0 %collective-permute-start.43 = (f32[896,224]{0,1:T(8,128)S(1)}, f32[896,224]{0,1:T(8,128)S(1)}, u32[]{:S(2)}, u32[]{:S(2)}) collective-permute-start(f32[896,224]{0,1:T(8,128)S(1)} %maximum_select_fusion.6), channel_id=1, source_target_pairs={{0,1},{1,0},{2,3},{3,2},{4,5},{5,4},{6,7},{7,6},{8,9},{9,8},{10,11... | collective-permute-start | bytes 2408456 | tf_op jit(solution)/shard_map/ppermute | solution.py:103
  223.2 14.8 %collective-permute-start.45 = (bf16[112,2048]{1,0:T(8,128)(2,1)S(1)}, bf16[112,2048]{1,0:T(8,128)(2,1)S(1)}, u32[]{:S(2)}, u32[]{:S(2)}) collective-permute-start(bf16[112,2048]{1,0:T(8,128)(2,1)S(1)} %collective-permute-done.39), channel_id=1, source_target_pairs={{8,0},{12,4},{16,8},{20,12},{24,16},{28,20},{9,1},{13,5},{17,9},{2... | collective-permute-start | bytes 1376264 | tf_op jit(solution)/shard_map/ppermute | solution.py:11
  243.5 15.3 %collective-permute-start.47 = (f32[896,112]{0,1:T(8,128)}, f32[896,112]{0,1:T(8,128)}, u32[]{:S(2)}, u32[]{:S(2)}) collective-permute-start(f32[896,112]{0,1:T(8,128)} %get-tuple-element.341), channel_id=1, source_target_pairs={{0,3},{1,2},{2,1},{3,0},{4,7},{5,6},{6,5},{7,4},{8,11},{9,10},{10,... | collective-permute-start | bytes 1204232 | tf_op jit(solution)/shard_map/ppermute | solution.py:98
  244.3 14.5 %collective-permute-start.49 = (f32[896,112]{0,1:T(8,128)}, f32[896,112]{0,1:T(8,128)}, u32[]{:S(2)}, u32[]{:S(2)}) collective-permute-start(f32[896,112]{0,1:T(8,128)} %get-tuple-element.340), channel_id=1, source_target_pairs={{0,1},{1,0},{2,3},{3,2},{4,5},{5,4},{6,7},{7,6},{8,9},{9,8},{10,11... | collective-permute-start | bytes 1204232 | tf_op jit(solution)/shard_map/ppermute | solution.py:98
  245.3 22.1 %collective-permute-start.48 = (f32[896,112]{0,1:T(8,128)}, f32[896,112]{0,1:T(8,128)}, u32[]{:S(2)}, u32[]{:S(2)}) collective-permute-start(f32[896,112]{0,1:T(8,128)} %select_select_fusion.1), channel_id=1, source_target_pairs={{0,2},{1,3},{2,0},{3,1},{4,6},{5,7},{6,4},{7,5},{8,10},{9,11},{10,... | collective-permute-start | bytes 1204232 | tf_op jit(solution)/shard_map/ppermute | solution.py:98
  (52 other events, 831.5 us)

commit v7 on v4

--- a/solution.py
+++ b/solution.py
@@ -65,23 +65,23 @@
     odd = list(range(1, count, 2))
     even = list(range(0, count, 2))
     z_down = [(s, s - 2) for s in range(2, count)]
-    odd_to_even = [(s, s - 1) for s in odd]
-    even_to_odd = [(s, s + 1) for s in even if s + 1 < count]
+    swap = [(s, s - 1) for s in odd] + [(s, s + 1) for s in even if s + 1 < count]
+    even_snp = lax.axis_index("snp") % 2 == 0
 
     even_me = me % 2 == 0
     low = me < 2
     partner = [(j, j ^ 1) for j in range(groups)]
     across = [(j, j ^ 2) for j in range(groups)]
 
-    names = ("two", "one_even", "one_odd", "three_even", "three_odd", "tiles", "first", "results")
+    names = ("two", "one", "three_even", "three_odd", "tiles", "first", "results")
     state = {name: [None] * CHUNKS for name in names}
 
     def finish(c):
         blocks = jnp.concatenate([
             pieces[c],
-            state["one_even"][c] + state["one_odd"][c],
+            state["one"][c],
             state["two"][c],
-            state["three_even"][c] + state["three_odd"][c],
+            jnp.where(even_snp, state["three_even"][c], state["three_odd"][c]),
         ], axis=0)
         gram = jnp.einsum("ab,cb->ac", own_block, blocks, preferred_element_type=jnp.float32)
         tiles = [gram[:, k * step:(k + 1) * step] for k in range(BAND + 1)]
@@ -118,20 +118,19 @@
         third = t - 2 if 0 <= t - 2 < CHUNKS else None
         if new is not None or third is not None:
             sent = moved(joined([pieces[new] if new is not None else None,
-                                 state["one_odd"][third] if third is not None else None]), z_down)
+                                 state["one"][third] if third is not None else None]), z_down)
             if new is not None:
                 state["two"][new] = sent[:step]
             if third is not None:
                 state["three_odd"][third] = sent[-step:]
         if new is not None or second is not None:
             sent = moved(joined([pieces[new] if new is not None else None,
-                                 state["two"][second] if second is not None else None]), odd_to_even)
+                                 state["two"][second] if second is not None else None]), swap)
             if new is not None:
-                state["one_even"][new] = sent[:step]
+                state["one"][new] = sent[:step]
             if second is not None:
                 state["three_even"][second] = sent[-step:]
-        if second is not None:
-            state["one_odd"][second] = moved(state["two"][second], even_to_odd)
+                state["one"][second] = jnp.where(even_snp, state["one"][second], sent[-step:])
         if 0 <= t - 3 < CHUNKS:
             finish(t - 3)
         if 0 <= t - 4 < CHUNKS - 1:

time: 269 us -> 260 us (0.967)
  starting transfers between devices: 60.6 us -> 36.6 us
  waiting for transfers between devices: 148 us -> 161 us
  other arithmetic: 30.1 us -> 33.8 us
    ppermute x27 -> x19, starting transfers between devices: 43.2 us -> 19.8 us  [moved(): return lax.ppermute(value, 'snp', pairs)]
    ppermute x27 -> x19, waiting for transfers between devices: 110 us -> 119 us  [moved(): return lax.ppermute(value, 'snp', pairs)]
    slice x0 -> x7, other arithmetic: none -> 4.29 us  [local(): sent[-step:]]
    add x16 -> x0, other arithmetic: 4.07 us -> none  [the longest x8 2.04 us: finish(): state['three_even'][c] + state['three_odd'][c]]
    concatenate x7, other arithmetic: 2.63 us -> 5.67 us  [joined(): return parts[0] if len(parts) == 1 else jnp.concatenate(parts, axis=0)]
    ppermute x7, waiting for transfers between devices: 20.8 us -> 23.9 us  [second_level(): last = lax.ppermute(pick(c, 2, 3, 0, 1) + onward, 'samp', across)]
  transfers between devices with their start and end apart: 50 -> 42, of which waited for: 25 -> 23; matrix products, arithmetic and copies ran while one was open for 15% -> 15% of each run, Pallas kernels for 0% -> 0%
where the time goes in v7:
time: 260 us; the launch traced here: 259 us
  waiting for transfers between devices  161 us (62%)
  starting transfers between devices  36.6 us (14%)
  other arithmetic  33.8 us (13%)
  matrix products  17.7 us (7%)
  local copies, waits for them, and re-layouts  9.02 us (3%)
    ppermute x19, waiting for transfers between devices, moved(): return lax.ppermute(value, 'snp', pairs)  119 us
    ppermute x7, waiting for transfers between devices, second_level(): last = lax.ppermute(pick(c, 2, 3, 0, 1) + onward, 'samp', across)  23.9 us
    ppermute x19, starting transfers between devices, moved(): return lax.ppermute(value, 'snp', pairs)  19.8 us
    dot_general x8, matrix products, finish(): jnp.einsum('ab,cb->ac', own_block, blocks, preferred_element_type=jnp.flo...  17.7 us
    ppermute x3, waiting for transfers between devices, finish(): lax.ppermute(outgoing[i], 'samp', [(j, j ^ i) for j in range(groups)])  14.3 us
    ppermute x7, starting transfers between devices, second_level(): last = lax.ppermute(pick(c, 2, 3, 0, 1) + onward, 'samp', across)  9.09 us
    add x7, other arithmetic, second_level(): state['results'][c] = pick(c, 0, 1, 2, 3) + mine + last  7.09 us
    concatenate x7, other arithmetic, joined(): return parts[0] if len(parts) == 1 else jnp.concatenate(parts, axis=0)  5.67 us
  transfers between devices with their start and end apart: 42, of which 23 were waited for; matrix products, arithmetic and copies ran while one was open for 15% of the time, Pallas kernels for 0%

profile of v7, /device:TPU:0, one launch (start us, length us, event | category | flops | bytes accessed | tf_op | source)
XLA Modules:
  0.0 258.8 jit_solution(7044274289503192388)
XLA Ops:
  0.0 3.6 %slice_reduce_fusion = (f32[784]{0:T(1024)S(1)}, f32[784]{0:T(1024)S(1)}) fusion(f32[896,2048]{1,0:T(8,128)} %param.1), kind=kLoop, calls=%fused_computation.2 | loop fusion | flops 4815328 | bytes 6428800 | tf_op jit(solution)/shard_map/reduce_sum | solution.py:21
  3.7 2.4 collective-permute-start.3
  17.6 3.5 %multiply_convert_fusion = bf16[784,2048]{1,0:T(8,128)(2,1)S(1)} fusion(f32[896,2048]{1,0:T(8,128)} %param.1, f32[784]{0:T(1024)S(1)} %add_rsqrt_fusion, f32[784]{0:T(1024)S(1)} %get-tuple-element.295), kind=kLoop, calls=%fused_computation | loop fusion | flops 4816896 | bytes 9640064 | tf_op jit(solution)/shard_map/convert_element_type | solution.py:17
  22.9 3.1 %collective-permute-done.6 = bf16[112,2048]{1,0:T(8,128)(2,1)S(1)} collective-permute-done((bf16[112,2048]{1,0:T(8,128)(2,1)S(1)}, bf16[112,2048]{1,0:T(8,128)(2,1)S(1)}, u32[]{:S(2)}, u32[]{:S(2)}) %collective-permute-start.6) | collective-permute-done | bytes 458784 | tf_op jit(solution)/shard_map/ppermute | solution.py:11
  26.0 3.1 %collective-permute-done.7 = bf16[112,2048]{1,0:T(8,128)(2,1)S(1)} collective-permute-done((bf16[112,2048]{1,0:T(8,128)(2,1)S(1)}, bf16[112,2048]{1,0:T(8,128)(2,1)S(1)}, u32[]{:S(2)}, u32[]{:S(2)}) %collective-permute-start.7) | collective-permute-done | bytes 458784 | tf_op jit(solution)/shard_map/ppermute | solution.py:11
  33.8 18.5 %collective-permute-done.8 = bf16[224,2048]{1,0:T(8,128)(2,1)} collective-permute-done((bf16[224,2048]{1,0:T(8,128)(2,1)}, bf16[224,2048]{1,0:T(8,128)(2,1)}, u32[]{:S(2)}, u32[]{:S(2)}) %collective-permute-start.8) | collective-permute-done | bytes 917536 | tf_op jit(solution)/shard_map/ppermute | solution.py:11
  52.3 2.3 fusion.96
  55.4 2.5 pad_maximum_fusion.1
  59.6 19.5 %collective-permute-done.11 = bf16[224,2048]{1,0:T(8,128)(2,1)} collective-permute-done((bf16[224,2048]{1,0:T(8,128)(2,1)}, bf16[224,2048]{1,0:T(8,128)(2,1)}, u32[]{:S(2)}, u32[]{:S(2)}) %collective-permute-start.11) | collective-permute-done | bytes 917536 | tf_op jit(solution)/shard_map/ppermute | solution.py:11
  83.9 2.1 fusion
  86.3 16.0 %collective-permute-done.14 = bf16[224,2048]{1,0:T(8,128)(2,1)S(1)} collective-permute-done((bf16[224,2048]{1,0:T(8,128)(2,1)S(1)}, bf16[224,2048]{1,0:T(8,128)(2,1)S(1)}, u32[]{:S(2)}, u32[]{:S(2)}) %collective-permute-start.14) | collective-permute-done | bytes 917536 | tf_op jit(solution)/shard_map/ppermute | solution.py:11
  102.7 3.1 %collective-permute-start.17 = (f32[896,112]{0,1:T(8,128)S(1)}, f32[896,112]{0,1:T(8,128)S(1)}, u32[]{:S(2)}, u32[]{:S(2)}) collective-permute-start(f32[896,112]{0,1:T(8,128)S(1)} %select_add_fusion.7), channel_id=1, source_target_pairs={{0,2},{1,3},{2,0},{3,1},{4,6},{5,7},{6,4},{7,5},{8,10},{9,11},{10,... | collective-permute-start | bytes 1204232 | tf_op jit(solution)/shard_map/ppermute | solution.py:112
  108.5 3.1 %fusion.8 = f32[896,448]{0,1:T(8,128)S(1)} fusion(bf16[112,2048]{1,0:T(8,128)(2,1)S(1)} %broadcast_select_fusion.11, bf16[112,2048]{1,0:T(8,128)(2,1)S(1)} %copy-done.21, bf16[112,2048]{1,0:T(8,128)(2,1)S(1)} %get-tuple-element.168, bf16[112,2048]{1,0:T(8,128)(2,1)} %get-tuple-element.149, bf16[784,2048]{1,0:T(8,128)(2,1)S(1)} %multiply_convert_fusion, ...), kind=kOutput, calls=%fused_computation.12 | convolution fusion | flops 1658847232 | bytes 7110656 | tf_op jit(solution)/shard_map/ab,cb->ac/dot_general | solution.py:86
  112.9 13.0 %collective-permute-done.18 = bf16[224,2048]{1,0:T(8,128)(2,1)S(1)} collective-permute-done((bf16[224,2048]{1,0:T(8,128)(2,1)S(1)}, bf16[224,2048]{1,0:T(8,128)(2,1)S(1)}, u32[]{:S(2)}, u32[]{:S(2)}) %collective-permute-start.18) | collective-permute-done | bytes 917536 | tf_op jit(solution)/shard_map/ppermute | solution.py:11
  130.4 2.1 fusion.16
  135.2 12.7 %collective-permute-done.22 = bf16[224,2048]{1,0:T(8,128)(2,1)S(1)} collective-permute-done((bf16[224,2048]{1,0:T(8,128)(2,1)S(1)}, bf16[224,2048]{1,0:T(8,128)(2,1)S(1)}, u32[]{:S(2)}, u32[]{:S(2)}) %collective-permute-start.22) | collective-permute-done | bytes 917536 | tf_op jit(solution)/shard_map/ppermute | solution.py:11
  150.8 2.1 fusion.24
  153.2 3.0 %collective-permute-done.25 = f32[896,112]{0,1:T(8,128)S(1)} collective-permute-done((f32[896,112]{0,1:T(8,128)S(1)}, f32[896,112]{0,1:T(8,128)S(1)}, u32[]{:S(2)}, u32[]{:S(2)}) %collective-permute-start.25) | collective-permute-done | bytes 401440 | tf_op jit(solution)/shard_map/ppermute | solution.py:112
  157.2 11.1 %collective-permute-done.26 = bf16[224,2048]{1,0:T(8,128)(2,1)S(1)} collective-permute-done((bf16[224,2048]{1,0:T(8,128)(2,1)S(1)}, bf16[224,2048]{1,0:T(8,128)(2,1)S(1)}, u32[]{:S(2)}, u32[]{:S(2)}) %collective-permute-start.26) | collective-permute-done | bytes 917536 | tf_op jit(solution)/shard_map/ppermute | solution.py:11
  171.4 2.1 fusion.32
  173.8 2.7 %collective-permute-done.29 = f32[896,112]{0,1:T(8,128)S(1)} collective-permute-done((f32[896,112]{0,1:T(8,128)S(1)}, f32[896,112]{0,1:T(8,128)S(1)}, u32[]{:S(2)}, u32[]{:S(2)}) %collective-permute-start.29) | collective-permute-done | bytes 401440 | tf_op jit(solution)/shard_map/ppermute | solution.py:112
  177.5 8.5 %collective-permute-done.30 = bf16[224,2048]{1,0:T(8,128)(2,1)S(1)} collective-permute-done((bf16[224,2048]{1,0:T(8,128)(2,1)S(1)}, bf16[224,2048]{1,0:T(8,128)(2,1)S(1)}, u32[]{:S(2)}, u32[]{:S(2)}) %collective-permute-start.30) | collective-permute-done | bytes 917536 | tf_op jit(solution)/shard_map/ppermute | solution.py:11
  188.8 2.1 fusion.40
  196.2 9.9 %collective-permute-done.34 = bf16[112,2048]{1,0:T(8,128)(2,1)S(1)} collective-permute-done((bf16[112,2048]{1,0:T(8,128)(2,1)S(1)}, bf16[112,2048]{1,0:T(8,128)(2,1)S(1)}, u32[]{:S(2)}, u32[]{:S(2)}) %collective-permute-start.34) | collective-permute-done | bytes 458784 | tf_op jit(solution)/shard_map/ppermute | solution.py:11
  206.1 2.1 fusion.48
  211.1 9.3 %collective-permute-done.36 = f32[896,112]{0,1:T(8,128)S(1)} collective-permute-done((f32[896,112]{0,1:T(8,128)S(1)}, f32[896,112]{0,1:T(8,128)S(1)}, u32[]{:S(2)}, u32[]{:S(2)}) %collective-permute-start.36) | collective-permute-done | bytes 401440 | tf_op jit(solution)/shard_map/ppermute | solution.py:112
  221.4 3.1 %collective-permute-done.37 = bf16[112,2048]{1,0:T(8,128)(2,1)S(1)} collective-permute-done((bf16[112,2048]{1,0:T(8,128)(2,1)S(1)}, bf16[112,2048]{1,0:T(8,128)(2,1)S(1)}, u32[]{:S(2)}, u32[]{:S(2)}) %collective-permute-start.37) | collective-permute-done | bytes 458784 | tf_op jit(solution)/shard_map/ppermute | solution.py:11
  226.6 2.1 fusion.56
  232.6 5.4 %collective-permute-done.38 = f32[896,112]{0,1:T(8,128)} collective-permute-done((f32[896,112]{0,1:T(8,128)}, f32[896,112]{0,1:T(8,128)}, u32[]{:S(2)}, u32[]{:S(2)}) %collective-permute-start.38) | collective-permute-done | bytes 401440 | tf_op jit(solution)/shard_map/ppermute | solution.py:112
  239.5 5.6 %collective-permute-done.39 = f32[896,112]{0,1:T(8,128)} collective-permute-done((f32[896,112]{0,1:T(8,128)}, f32[896,112]{0,1:T(8,128)}, u32[]{:S(2)}, u32[]{:S(2)}) %collective-permute-start.39) | collective-permute-done | bytes 401440 | tf_op jit(solution)/shard_map/ppermute | solution.py:97
  245.1 8.6 %collective-permute-done.40 = f32[896,112]{0,1:T(8,128)} collective-permute-done((f32[896,112]{0,1:T(8,128)}, f32[896,112]{0,1:T(8,128)}, u32[]{:S(2)}, u32[]{:S(2)}) %collective-permute-start.40) | collective-permute-done | bytes 401440 | tf_op jit(solution)/shard_map/ppermute | solution.py:97
  255.8 3.0 %copy.2 = f32[896,896]{1,0:T(8,128)} copy(f32[896,896]{0,1:T(8,128)S(1)} %broadcast_multiply_fusion) | data formatting | bytes 6422528 | tf_op jit(solution)/shard_map/div | solution.py:145
  (195 shorter events, 66.3 us)
Async XLA Ops:
  3.7 13.8 %collective-permute-start.3 = (f32[2,784]{1,0:T(2,128)S(1)}, f32[2,784]{1,0:T(2,128)S(1)}, u32[]{:S(2)}, u32[]{:S(2)}) collective-permute-start(f32[2,784]{1,0:T(2,128)S(1)} %pad_maximum_fusion.14), channel_id=1, source_target_pairs={{0,3},{1,2},{2,1},{3,0},{4,7},{5,6},{6,5},{7,4},{8,11},{9,10},{10,... | collective-permute-start | bytes 18824 | tf_op jit(solution)/shard_map/ppermute | solution.py:55
  6.1 11.4 %collective-permute-start.4 = (f32[2,784]{1,0:T(2,128)S(1)}, f32[2,784]{1,0:T(2,128)S(1)}, u32[]{:S(2)}, u32[]{:S(2)}) collective-permute-start(f32[2,784]{1,0:T(2,128)S(1)} %pad_maximum_fusion.14), channel_id=1, source_target_pairs={{0,2},{1,3},{2,0},{3,1},{4,6},{5,7},{6,4},{7,5},{8,10},{9,11},{10,... | collective-permute-start | bytes 18824 | tf_op jit(solution)/shard_map/ppermute | solution.py:55
  14.6 11.4 %collective-permute-start.6 = (bf16[112,2048]{1,0:T(8,128)(2,1)S(1)}, bf16[112,2048]{1,0:T(8,128)(2,1)S(1)}, u32[]{:S(2)}, u32[]{:S(2)}) collective-permute-start(bf16[112,2048]{1,0:T(8,128)(2,1)S(1)} %multiply_convert_fusion.1), channel_id=1, source_target_pairs={{4,0},{12,8},{20,16},{28,24},{0,4},{8,12},{16,20},{24,28},{5,1},{1... | collective-permute-start | bytes 1376264 | tf_op jit(solution)/shard_map/ppermute | solution.py:11
  16.2 13.0 %collective-permute-start.7 = (bf16[112,2048]{1,0:T(8,128)(2,1)S(1)}, bf16[112,2048]{1,0:T(8,128)(2,1)S(1)}, u32[]{:S(2)}, u32[]{:S(2)}) collective-permute-start(bf16[112,2048]{1,0:T(8,128)(2,1)S(1)} %multiply_convert_fusion.1), channel_id=1, source_target_pairs={{8,0},{12,4},{16,8},{20,12},{24,16},{28,20},{9,1},{13,5},{17,9},{2... | collective-permute-start | bytes 1376264 | tf_op jit(solution)/shard_map/ppermute | solution.py:11
  32.0 20.3 %collective-permute-start.8 = (bf16[224,2048]{1,0:T(8,128)(2,1)}, bf16[224,2048]{1,0:T(8,128)(2,1)}, u32[]{:S(2)}, u32[]{:S(2)}) collective-permute-start(bf16[224,2048]{1,0:T(8,128)(2,1)} %pad_maximum_fusion.13), channel_id=1, source_target_pairs={{4,0},{12,8},{20,16},{28,24},{0,4},{8,12},{16,20},{24,28},{5,1},{1... | collective-permute-start | bytes 2752520 | tf_op jit(solution)/shard_map/ppermute | solution.py:11
  32.5 22.1 %collective-permute-start.9 = (bf16[112,2048]{1,0:T(8,128)(2,1)}, bf16[112,2048]{1,0:T(8,128)(2,1)S(1)}, u32[]{:S(2)}, u32[]{:S(2)}) collective-permute-start(bf16[112,2048]{1,0:T(8,128)(2,1)} %get-tuple-element.149), channel_id=1, source_target_pairs={{8,0},{12,4},{16,8},{20,12},{24,16},{28,20},{9,1},{13,5},{17,9},{2... | collective-permute-start | bytes 1376264 | tf_op jit(solution)/shard_map/ppermute | solution.py:11
  57.9 21.3 %collective-permute-start.11 = (bf16[224,2048]{1,0:T(8,128)(2,1)}, bf16[224,2048]{1,0:T(8,128)(2,1)}, u32[]{:S(2)}, u32[]{:S(2)}) collective-permute-start(bf16[224,2048]{1,0:T(8,128)(2,1)} %get-tuple-element.377), channel_id=1, source_target_pairs={{8,0},{12,4},{16,8},{20,12},{24,16},{28,20},{9,1},{13,5},{17,9},{2... | collective-permute-start | bytes 2752520 | tf_op jit(solution)/shard_map/ppermute | solution.py:11
  59.2 21.2 %collective-permute-start.10 = (bf16[224,2048]{1,0:T(8,128)(2,1)}, bf16[224,2048]{1,0:T(8,128)(2,1)}, u32[]{:S(2)}, u32[]{:S(2)}) collective-permute-start(bf16[224,2048]{1,0:T(8,128)(2,1)} %get-tuple-element.378), channel_id=1, source_target_pairs={{4,0},{12,8},{20,16},{28,24},{0,4},{8,12},{16,20},{24,28},{5,1},{1... | collective-permute-start | bytes 2752520 | tf_op jit(solution)/shard_map/ppermute | solution.py:11
  82.2 20.2 %collective-permute-start.13 = (bf16[224,2048]{1,0:T(8,128)(2,1)S(1)}, bf16[224,2048]{1,0:T(8,128)(2,1)S(1)}, u32[]{:S(2)}, u32[]{:S(2)}) collective-permute-start(bf16[224,2048]{1,0:T(8,128)(2,1)S(1)} %get-tuple-element.376), channel_id=1, source_target_pairs={{4,0},{12,8},{20,16},{28,24},{0,4},{8,12},{16,20},{24,28},{5,1},{1... | collective-permute-start | bytes 2752520 | tf_op jit(solution)/shard_map/ppermute | solution.py:11
  82.5 19.8 %collective-permute-start.14 = (bf16[224,2048]{1,0:T(8,128)(2,1)S(1)}, bf16[224,2048]{1,0:T(8,128)(2,1)S(1)}, u32[]{:S(2)}, u32[]{:S(2)}) collective-permute-start(bf16[224,2048]{1,0:T(8,128)(2,1)S(1)} %get-tuple-element.375), channel_id=1, source_target_pairs={{8,0},{12,4},{16,8},{20,12},{24,16},{28,20},{9,1},{13,5},{17,9},{2... | collective-permute-start | bytes 2752520 | tf_op jit(solution)/shard_map/ppermute | solution.py:11
  86.2 16.3 %collective-permute-start.12 = (f32[896,224]{0,1:T(8,128)S(1)}, f32[896,224]{0,1:T(8,128)S(1)}, u32[]{:S(2)}, u32[]{:S(2)}) collective-permute-start(f32[896,224]{0,1:T(8,128)S(1)} %maximum_select_fusion), channel_id=1, source_target_pairs={{0,1},{1,0},{2,3},{3,2},{4,5},{5,4},{6,7},{7,6},{8,9},{9,8},{10,11... | collective-permute-start | bytes 2408456 | tf_op jit(solution)/shard_map/ppermute | solution.py:102
  106.1 19.9 %collective-permute-start.16 = (bf16[224,2048]{1,0:T(8,128)(2,1)S(1)}, bf16[224,2048]{1,0:T(8,128)(2,1)S(1)}, u32[]{:S(2)}, u32[]{:S(2)}) collective-permute-start(bf16[224,2048]{1,0:T(8,128)(2,1)S(1)} %get-tuple-element.374), channel_id=1, source_target_pairs={{4,0},{12,8},{20,16},{28,24},{0,4},{8,12},{16,20},{24,28},{5,1},{1... | collective-permute-start | bytes 2752520 | tf_op jit(solution)/shard_map/ppermute | solution.py:11
  107.2 18.7 %collective-permute-start.18 = (bf16[224,2048]{1,0:T(8,128)(2,1)S(1)}, bf16[224,2048]{1,0:T(8,128)(2,1)S(1)}, u32[]{:S(2)}, u32[]{:S(2)}) collective-permute-start(bf16[224,2048]{1,0:T(8,128)(2,1)S(1)} %get-tuple-element.373), channel_id=1, source_target_pairs={{8,0},{12,4},{16,8},{20,12},{24,16},{28,20},{9,1},{13,5},{17,9},{2... | collective-permute-start | bytes 2752520 | tf_op jit(solution)/shard_map/ppermute | solution.py:11
  111.9 14.3 %collective-permute-start.15 = (f32[896,224]{0,1:T(8,128)S(1)}, f32[896,224]{0,1:T(8,128)S(1)}, u32[]{:S(2)}, u32[]{:S(2)}) collective-permute-start(f32[896,224]{0,1:T(8,128)S(1)} %maximum_select_fusion.1), channel_id=1, source_target_pairs={{0,1},{1,0},{2,3},{3,2},{4,5},{5,4},{6,7},{7,6},{8,9},{9,8},{10,11... | collective-permute-start | bytes 2408456 | tf_op jit(solution)/shard_map/ppermute | solution.py:102
  127.5 20.5 %collective-permute-start.20 = (bf16[224,2048]{1,0:T(8,128)(2,1)S(1)}, bf16[224,2048]{1,0:T(8,128)(2,1)S(1)}, u32[]{:S(2)}, u32[]{:S(2)}) collective-permute-start(bf16[224,2048]{1,0:T(8,128)(2,1)S(1)} %get-tuple-element.372), channel_id=1, source_target_pairs={{4,0},{12,8},{20,16},{28,24},{0,4},{8,12},{16,20},{24,28},{5,1},{1... | collective-permute-start | bytes 2752520 | tf_op jit(solution)/shard_map/ppermute | solution.py:11
  128.9 19.1 %collective-permute-start.22 = (bf16[224,2048]{1,0:T(8,128)(2,1)S(1)}, bf16[224,2048]{1,0:T(8,128)(2,1)S(1)}, u32[]{:S(2)}, u32[]{:S(2)}) collective-permute-start(bf16[224,2048]{1,0:T(8,128)(2,1)S(1)} %get-tuple-element.371), channel_id=1, source_target_pairs={{8,0},{12,4},{16,8},{20,12},{24,16},{28,20},{9,1},{13,5},{17,9},{2... | collective-permute-start | bytes 2752520 | tf_op jit(solution)/shard_map/ppermute | solution.py:11
  132.7 15.4 %collective-permute-start.19 = (f32[896,224]{0,1:T(8,128)S(1)}, f32[896,224]{0,1:T(8,128)S(1)}, u32[]{:S(2)}, u32[]{:S(2)}) collective-permute-start(f32[896,224]{0,1:T(8,128)S(1)} %maximum_select_fusion.2), channel_id=1, source_target_pairs={{0,1},{1,0},{2,3},{3,2},{4,5},{5,4},{6,7},{7,6},{8,9},{9,8},{10,11... | collective-permute-start | bytes 2408456 | tf_op jit(solution)/shard_map/ppermute | solution.py:102
  149.4 19.0 %collective-permute-start.24 = (bf16[224,2048]{1,0:T(8,128)(2,1)S(1)}, bf16[224,2048]{1,0:T(8,128)(2,1)S(1)}, u32[]{:S(2)}, u32[]{:S(2)}) collective-permute-start(bf16[224,2048]{1,0:T(8,128)(2,1)S(1)} %get-tuple-element.370), channel_id=1, source_target_pairs={{4,0},{12,8},{20,16},{28,24},{0,4},{8,12},{16,20},{24,28},{5,1},{1... | collective-permute-start | bytes 2752520 | tf_op jit(solution)/shard_map/ppermute | solution.py:11
  149.5 18.8 %collective-permute-start.26 = (bf16[224,2048]{1,0:T(8,128)(2,1)S(1)}, bf16[224,2048]{1,0:T(8,128)(2,1)S(1)}, u32[]{:S(2)}, u32[]{:S(2)}) collective-permute-start(bf16[224,2048]{1,0:T(8,128)(2,1)S(1)} %get-tuple-element.369), channel_id=1, source_target_pairs={{8,0},{12,4},{16,8},{20,12},{24,16},{28,20},{9,1},{13,5},{17,9},{2... | collective-permute-start | bytes 2752520 | tf_op jit(solution)/shard_map/ppermute | solution.py:11
  153.2 15.3 %collective-permute-start.23 = (f32[896,224]{0,1:T(8,128)S(1)}, f32[896,224]{0,1:T(8,128)S(1)}, u32[]{:S(2)}, u32[]{:S(2)}) collective-permute-start(f32[896,224]{0,1:T(8,128)S(1)} %maximum_select_fusion.3), channel_id=1, source_target_pairs={{0,1},{1,0},{2,3},{3,2},{4,5},{5,4},{6,7},{7,6},{8,9},{9,8},{10,11... | collective-permute-start | bytes 2408456 | tf_op jit(solution)/shard_map/ppermute | solution.py:102
  170.0 16.5 %collective-permute-start.28 = (bf16[224,2048]{1,0:T(8,128)(2,1)S(1)}, bf16[224,2048]{1,0:T(8,128)(2,1)S(1)}, u32[]{:S(2)}, u32[]{:S(2)}) collective-permute-start(bf16[224,2048]{1,0:T(8,128)(2,1)S(1)} %get-tuple-element.368), channel_id=1, source_target_pairs={{4,0},{12,8},{20,16},{28,24},{0,4},{8,12},{16,20},{24,28},{5,1},{1... | collective-permute-start | bytes 2752520 | tf_op jit(solution)/shard_map/ppermute | solution.py:11
  170.1 15.9 %collective-permute-start.30 = (bf16[224,2048]{1,0:T(8,128)(2,1)S(1)}, bf16[224,2048]{1,0:T(8,128)(2,1)S(1)}, u32[]{:S(2)}, u32[]{:S(2)}) collective-permute-start(bf16[224,2048]{1,0:T(8,128)(2,1)S(1)} %get-tuple-element.367), channel_id=1, source_target_pairs={{8,0},{12,4},{16,8},{20,12},{24,16},{28,20},{9,1},{13,5},{17,9},{2... | collective-permute-start | bytes 2752520 | tf_op jit(solution)/shard_map/ppermute | solution.py:11
  173.8 12.8 %collective-permute-start.27 = (f32[896,224]{0,1:T(8,128)S(1)}, f32[896,224]{0,1:T(8,128)S(1)}, u32[]{:S(2)}, u32[]{:S(2)}) collective-permute-start(f32[896,224]{0,1:T(8,128)S(1)} %maximum_select_fusion.4), channel_id=1, source_target_pairs={{0,1},{1,0},{2,3},{3,2},{4,5},{5,4},{6,7},{7,6},{8,9},{9,8},{10,11... | collective-permute-start | bytes 2408456 | tf_op jit(solution)/shard_map/ppermute | solution.py:102
  191.2 14.9 %collective-permute-start.31 = (f32[896,224]{0,1:T(8,128)S(1)}, f32[896,224]{0,1:T(8,128)S(1)}, u32[]{:S(2)}, u32[]{:S(2)}) collective-permute-start(f32[896,224]{0,1:T(8,128)S(1)} %maximum_select_fusion.5), channel_id=1, source_target_pairs={{0,1},{1,0},{2,3},{3,2},{4,5},{5,4},{6,7},{7,6},{8,9},{9,8},{10,11... | collective-permute-start | bytes 2408456 | tf_op jit(solution)/shard_map/ppermute | solution.py:102
  191.2 14.8 %collective-permute-start.34 = (bf16[112,2048]{1,0:T(8,128)(2,1)S(1)}, bf16[112,2048]{1,0:T(8,128)(2,1)S(1)}, u32[]{:S(2)}, u32[]{:S(2)}) collective-permute-start(bf16[112,2048]{1,0:T(8,128)(2,1)S(1)} %get-tuple-element.252), channel_id=1, source_target_pairs={{8,0},{12,4},{16,8},{20,12},{24,16},{28,20},{9,1},{13,5},{17,9},{2... | collective-permute-start | bytes 1376264 | tf_op jit(solution)/shard_map/ppermute | solution.py:11
  208.4 16.0 %collective-permute-start.35 = (f32[896,224]{0,1:T(8,128)S(1)}, f32[896,224]{0,1:T(8,128)S(1)}, u32[]{:S(2)}, u32[]{:S(2)}) collective-permute-start(f32[896,224]{0,1:T(8,128)S(1)} %maximum_select_fusion.6), channel_id=1, source_target_pairs={{0,1},{1,0},{2,3},{3,2},{4,5},{5,4},{6,7},{7,6},{8,9},{9,8},{10,11... | collective-permute-start | bytes 2408456 | tf_op jit(solution)/shard_map/ppermute | solution.py:102
  208.7 11.8 %collective-permute-start.36 = (f32[896,112]{0,1:T(8,128)S(1)}, f32[896,112]{0,1:T(8,128)S(1)}, u32[]{:S(2)}, u32[]{:S(2)}) collective-permute-start(f32[896,112]{0,1:T(8,128)S(1)} %select_add_fusion.2), channel_id=1, source_target_pairs={{0,2},{1,3},{2,0},{3,1},{4,6},{5,7},{6,4},{7,5},{8,10},{9,11},{10,... | collective-permute-start | bytes 1204232 | tf_op jit(solution)/shard_map/ppermute | solution.py:112
  209.8 14.7 %collective-permute-start.37 = (bf16[112,2048]{1,0:T(8,128)(2,1)S(1)}, bf16[112,2048]{1,0:T(8,128)(2,1)S(1)}, u32[]{:S(2)}, u32[]{:S(2)}) collective-permute-start(bf16[112,2048]{1,0:T(8,128)(2,1)S(1)} %broadcast_select_fusion.2), channel_id=1, source_target_pairs={{8,0},{12,4},{16,8},{20,12},{24,16},{28,20},{9,1},{13,5},{17,9},{2... | collective-permute-start | bytes 1376264 | tf_op jit(solution)/shard_map/ppermute | solution.py:11
  225.5 12.5 %collective-permute-start.38 = (f32[896,112]{0,1:T(8,128)}, f32[896,112]{0,1:T(8,128)}, u32[]{:S(2)}, u32[]{:S(2)}) collective-permute-start(f32[896,112]{0,1:T(8,128)} %select_add_fusion.1), channel_id=1, source_target_pairs={{0,2},{1,3},{2,0},{3,1},{4,6},{5,7},{6,4},{7,5},{8,10},{9,11},{10,... | collective-permute-start | bytes 1204232 | tf_op jit(solution)/shard_map/ppermute | solution.py:112
  229.6 15.5 %collective-permute-start.39 = (f32[896,112]{0,1:T(8,128)}, f32[896,112]{0,1:T(8,128)}, u32[]{:S(2)}, u32[]{:S(2)}) collective-permute-start(f32[896,112]{0,1:T(8,128)} %get-tuple-element.305), channel_id=1, source_target_pairs={{0,3},{1,2},{2,1},{3,0},{4,7},{5,6},{6,5},{7,4},{8,11},{9,10},{10,... | collective-permute-start | bytes 1204232 | tf_op jit(solution)/shard_map/ppermute | solution.py:97
  230.5 14.7 %collective-permute-start.41 = (f32[896,112]{0,1:T(8,128)}, f32[896,112]{0,1:T(8,128)}, u32[]{:S(2)}, u32[]{:S(2)}) collective-permute-start(f32[896,112]{0,1:T(8,128)} %get-tuple-element.304), channel_id=1, source_target_pairs={{0,1},{1,0},{2,3},{3,2},{4,5},{5,4},{6,7},{7,6},{8,9},{9,8},{10,11... | collective-permute-start | bytes 1204232 | tf_op jit(solution)/shard_map/ppermute | solution.py:97
  231.7 22.1 %collective-permute-start.40 = (f32[896,112]{0,1:T(8,128)}, f32[896,112]{0,1:T(8,128)}, u32[]{:S(2)}, u32[]{:S(2)}) collective-permute-start(f32[896,112]{0,1:T(8,128)} %select_select_fusion.1), channel_id=1, source_target_pairs={{0,2},{1,3},{2,0},{3,1},{4,6},{5,7},{6,4},{7,5},{8,10},{9,11},{10,... | collective-permute-start | bytes 1204232 | tf_op jit(solution)/shard_map/ppermute | solution.py:97
  (35 other events, 450.6 us)

commit v8 on v7

--- a/solution.py
+++ b/solution.py
@@ -73,15 +73,15 @@
     partner = [(j, j ^ 1) for j in range(groups)]
     across = [(j, j ^ 2) for j in range(groups)]
 
-    names = ("two", "one", "three_even", "three_odd", "tiles", "first", "results")
-    state = {name: [None] * CHUNKS for name in names}
+    names = ("two", "swapped", "one", "three", "tiles", "first", "results")
+    state = {name: [None] * (CHUNKS + 1) for name in names}
 
     def finish(c):
         blocks = jnp.concatenate([
             pieces[c],
             state["one"][c],
             state["two"][c],
-            jnp.where(even_snp, state["three_even"][c], state["three_odd"][c]),
+            state["three"][c],
         ], axis=0)
         gram = jnp.einsum("ab,cb->ac", own_block, blocks, preferred_element_type=jnp.float32)
         tiles = [gram[:, k * step:(k + 1) * step] for k in range(BAND + 1)]
@@ -122,15 +122,15 @@
             if new is not None:
                 state["two"][new] = sent[:step]
             if third is not None:
-                state["three_odd"][third] = sent[-step:]
+                state["three"][third] = sent[-step:]
         if new is not None or second is not None:
-            sent = moved(joined([pieces[new] if new is not None else None,
-                                 state["two"][second] if second is not None else None]), swap)
-            if new is not None:
-                state["one"][new] = sent[:step]
-            if second is not None:
-                state["three_even"][second] = sent[-step:]
-                state["one"][second] = jnp.where(even_snp, state["one"][second], sent[-step:])
+            if new is not None and second is not None:
+                payload = jnp.where(even_snp, state["two"][second], pieces[new])
+            else:
+                payload = pieces[new] if new is not None else state["two"][second]
+            state["swapped"][t] = moved(payload, swap)
+        if second is not None:
+            state["one"][second] = jnp.where(even_snp, state["swapped"][second], state["swapped"][t])
         if 0 <= t - 3 < CHUNKS:
             finish(t - 3)
         if 0 <= t - 4 < CHUNKS - 1:
@@ -141,7 +141,7 @@
         state = {k: list(v) for k, v in jax.tree.unflatten(tree, flat).items()}
         if t + 1 < CHUNKS:
             pieces[t + 1] = following
-    summed = jnp.concatenate(state["results"], axis=1)
+    summed = jnp.concatenate(state["results"][:CHUNKS], axis=1)
     return summed / total
 
 

time: 260 us -> 240 us (0.923)
  waiting for transfers between devices: 161 us -> 140 us
  starting transfers between devices: 36.6 us -> 44.9 us
  other arithmetic: 33.8 us -> 28.5 us
    ppermute x19, waiting for transfers between devices: 119 us -> 97.6 us  [moved(): return lax.ppermute(value, 'snp', pairs)]
    ppermute x7, starting transfers between devices: 9.09 us -> 13.5 us  [second_level(): last = lax.ppermute(pick(c, 2, 3, 0, 1) + onward, 'samp', across)]
    slice x7 -> x0, other arithmetic: 4.29 us -> none  [local(): sent[-step:]]
    concatenate x7 -> x6, other arithmetic: 5.67 us -> 1.48 us  [joined(): return parts[0] if len(parts) == 1 else jnp.concatenate(parts, axis=0)]
    ppermute x19, starting transfers between devices: 19.8 us -> 23.7 us  [moved(): return lax.ppermute(value, 'snp', pairs)]
    select_n x9 -> x15, other arithmetic: 0.46 us -> 3.62 us  [the longest x8 2.43 us: local(): jnp.where(even_snp, state['swapped'][second], state['swapped'][t])]
  transfers between devices with their start and end apart: 42 -> 42, of which waited for: 23 -> 30; matrix products, arithmetic and copies ran while one was open for 15% -> 16% of each run, Pallas kernels for 0% -> 0%
where the time goes in v8:
time: 240 us; the launch traced here: 239 us
  waiting for transfers between devices  140 us (58%)
  starting transfers between devices  44.9 us (19%)
  other arithmetic  28.5 us (12%)
  matrix products  16.7 us (7%)
  local copies, waits for them, and re-layouts  8.07 us (3%)
    ppermute x19, waiting for transfers between devices, moved(): return lax.ppermute(value, 'snp', pairs)  97.6 us
    ppermute x7, waiting for transfers between devices, second_level(): last = lax.ppermute(pick(c, 2, 3, 0, 1) + onward, 'samp', across)  25.2 us
    ppermute x19, starting transfers between devices, moved(): return lax.ppermute(value, 'snp', pairs)  23.7 us
    dot_general x8, matrix products, finish(): jnp.einsum('ab,cb->ac', own_block, blocks, preferred_element_type=jnp.flo...  16.7 us
    ppermute x3, waiting for transfers between devices, finish(): lax.ppermute(outgoing[i], 'samp', [(j, j ^ i) for j in range(groups)])  14.4 us
    ppermute x7, starting transfers between devices, second_level(): last = lax.ppermute(pick(c, 2, 3, 0, 1) + onward, 'samp', across)  13.5 us
    add x7, other arithmetic, second_level(): state['results'][c] = pick(c, 0, 1, 2, 3) + mine + last  7.12 us
    ppermute x6, starting transfers between devices, standard_rows(): lax.ppermute(moments, 'samp', [(j, j ^ i) for j in range(groups)])  5.12 us
  transfers between devices with their start and end apart: 42, of which 30 were waited for; matrix products, arithmetic and copies ran while one was open for 16% of the time, Pallas kernels for 0%

profile of v8, /device:TPU:0, one launch (start us, length us, event | category | flops | bytes accessed | tf_op | source)
XLA Modules:
  0.0 239.3 jit_solution(3794529979914910674)
XLA Ops:
  0.0 3.6 %slice_reduce_fusion = (f32[784]{0:T(1024)S(1)}, f32[784]{0:T(1024)S(1)}) fusion(f32[896,2048]{1,0:T(8,128)} %param.1), kind=kLoop, calls=%fused_computation.2 | loop fusion | flops 4815328 | bytes 6428800 | tf_op jit(solution)/shard_map/reduce_sum | solution.py:21
  3.7 2.4 %collective-permute-start.3 = (f32[2,784]{1,0:T(2,128)S(1)}, f32[2,784]{1,0:T(2,128)S(1)}, u32[]{:S(2)}, u32[]{:S(2)}) collective-permute-start(f32[2,784]{1,0:T(2,128)S(1)} %pad_maximum_fusion.7), channel_id=1, source_target_pairs={{0,3},{1,2},{2,1},{3,0},{4,7},{5,6},{6,5},{7,4},{8,11},{9,10},{10,... | collective-permute-start | bytes 18824 | tf_op jit(solution)/shard_map/ppermute | solution.py:55
  17.6 3.5 %multiply_convert_fusion = bf16[784,2048]{1,0:T(8,128)(2,1)S(1)} fusion(f32[896,2048]{1,0:T(8,128)} %param.1, f32[784]{0:T(1024)S(1)} %add_rsqrt_fusion, f32[784]{0:T(1024)S(1)} %get-tuple-element.263), kind=kLoop, calls=%fused_computation | loop fusion | flops 4816896 | bytes 9640064 | tf_op jit(solution)/shard_map/convert_element_type | solution.py:17
  22.8 3.3 %collective-permute-done.6 = bf16[112,2048]{1,0:T(8,128)(2,1)S(1)} collective-permute-done((bf16[112,2048]{1,0:T(8,128)(2,1)S(1)}, bf16[112,2048]{1,0:T(8,128)(2,1)S(1)}, u32[]{:S(2)}, u32[]{:S(2)}) %collective-permute-start.6) | collective-permute-done | bytes 458784 | tf_op jit(solution)/shard_map/ppermute | solution.py:11
  26.0 3.1 %collective-permute-done.7 = bf16[112,2048]{1,0:T(8,128)(2,1)S(1)} collective-permute-done((bf16[112,2048]{1,0:T(8,128)(2,1)S(1)}, bf16[112,2048]{1,0:T(8,128)(2,1)S(1)}, u32[]{:S(2)}, u32[]{:S(2)}) %collective-permute-start.7) | collective-permute-done | bytes 458784 | tf_op jit(solution)/shard_map/ppermute | solution.py:11
  31.1 8.4 %collective-permute-done.8 = bf16[112,2048]{1,0:T(8,128)(2,1)S(1)} collective-permute-done((bf16[112,2048]{1,0:T(8,128)(2,1)S(1)}, bf16[112,2048]{1,0:T(8,128)(2,1)S(1)}, u32[]{:S(2)}, u32[]{:S(2)}) %collective-permute-start.8) | collective-permute-done | bytes 458784 | tf_op jit(solution)/shard_map/ppermute | solution.py:11
  47.2 5.3 %collective-permute-done.10 = bf16[112,2048]{1,0:T(8,128)(2,1)} collective-permute-done((bf16[112,2048]{1,0:T(8,128)(2,1)}, bf16[112,2048]{1,0:T(8,128)(2,1)}, u32[]{:S(2)}, u32[]{:S(2)}) %collective-permute-start.10) | collective-permute-done | bytes 458784 | tf_op jit(solution)/shard_map/ppermute | solution.py:11
  53.6 13.0 %collective-permute-done.11 = bf16[224,2048]{1,0:T(8,128)(2,1)} collective-permute-done((bf16[224,2048]{1,0:T(8,128)(2,1)}, bf16[224,2048]{1,0:T(8,128)(2,1)}, u32[]{:S(2)}, u32[]{:S(2)}) %collective-permute-start.11) | collective-permute-done | bytes 917536 | tf_op jit(solution)/shard_map/ppermute | solution.py:11
  69.8 2.1 fusion
  72.2 5.6 %collective-permute-done.13 = bf16[112,2048]{1,0:T(8,128)(2,1)S(1)} collective-permute-done((bf16[112,2048]{1,0:T(8,128)(2,1)S(1)}, bf16[112,2048]{1,0:T(8,128)(2,1)S(1)}, u32[]{:S(2)}, u32[]{:S(2)}) %collective-permute-start.13) | collective-permute-done | bytes 458784 | tf_op jit(solution)/shard_map/ppermute | solution.py:11
  78.8 9.2 %collective-permute-done.14 = bf16[224,2048]{1,0:T(8,128)(2,1)S(1)} collective-permute-done((bf16[224,2048]{1,0:T(8,128)(2,1)S(1)}, bf16[224,2048]{1,0:T(8,128)(2,1)S(1)}, u32[]{:S(2)}, u32[]{:S(2)}) %collective-permute-start.14) | collective-permute-done | bytes 917536 | tf_op jit(solution)/shard_map/ppermute | solution.py:11
  92.9 2.1 fusion.8
  95.3 2.4 collective-permute-done.17
  100.4 8.1 %collective-permute-done.18 = bf16[224,2048]{1,0:T(8,128)(2,1)S(1)} collective-permute-done((bf16[224,2048]{1,0:T(8,128)(2,1)S(1)}, bf16[224,2048]{1,0:T(8,128)(2,1)S(1)}, u32[]{:S(2)}, u32[]{:S(2)}) %collective-permute-start.18) | collective-permute-done | bytes 917536 | tf_op jit(solution)/shard_map/ppermute | solution.py:11
  116.0 2.4 %collective-permute-done.21 = f32[896,112]{0,1:T(8,128)S(1)} collective-permute-done((f32[896,112]{0,1:T(8,128)S(1)}, f32[896,112]{0,1:T(8,128)S(1)}, u32[]{:S(2)}, u32[]{:S(2)}) %collective-permute-start.21) | collective-permute-done | bytes 401440 | tf_op jit(solution)/shard_map/ppermute | solution.py:112
  121.1 8.0 %collective-permute-done.22 = bf16[224,2048]{1,0:T(8,128)(2,1)S(1)} collective-permute-done((bf16[224,2048]{1,0:T(8,128)(2,1)S(1)}, bf16[224,2048]{1,0:T(8,128)(2,1)S(1)}, u32[]{:S(2)}, u32[]{:S(2)}) %collective-permute-start.22) | collective-permute-done | bytes 917536 | tf_op jit(solution)/shard_map/ppermute | solution.py:11
  136.4 2.4 collective-permute-done.25
  141.5 6.7 %collective-permute-done.26 = bf16[224,2048]{1,0:T(8,128)(2,1)S(1)} collective-permute-done((bf16[224,2048]{1,0:T(8,128)(2,1)S(1)}, bf16[224,2048]{1,0:T(8,128)(2,1)S(1)}, u32[]{:S(2)}, u32[]{:S(2)}) %collective-permute-start.26) | collective-permute-done | bytes 917536 | tf_op jit(solution)/shard_map/ppermute | solution.py:11
  149.9 3.5 %collective-permute-start.29 = (f32[896,112]{0,1:T(8,128)S(1)}, f32[896,112]{0,1:T(8,128)S(1)}, u32[]{:S(2)}, u32[]{:S(2)}) collective-permute-start(f32[896,112]{0,1:T(8,128)S(1)} %select_add_fusion.4), channel_id=1, source_target_pairs={{0,2},{1,3},{2,0},{3,1},{4,6},{5,7},{6,4},{7,5},{8,10},{9,11},{10,... | collective-permute-start | bytes 1204232 | tf_op jit(solution)/shard_map/ppermute | solution.py:112
  156.9 2.3 collective-permute-done.29
  162.0 4.0 %collective-permute-done.30 = bf16[224,2048]{1,0:T(8,128)(2,1)S(1)} collective-permute-done((bf16[224,2048]{1,0:T(8,128)(2,1)S(1)}, bf16[224,2048]{1,0:T(8,128)(2,1)S(1)}, u32[]{:S(2)}, u32[]{:S(2)}) %collective-permute-start.30) | collective-permute-done | bytes 917536 | tf_op jit(solution)/shard_map/ppermute | solution.py:11
  166.2 2.5 %collective-permute-start.33 = (f32[896,112]{0,1:T(8,128)S(1)}, f32[896,112]{0,1:T(8,128)S(1)}, u32[]{:S(2)}, u32[]{:S(2)}) collective-permute-start(f32[896,112]{0,1:T(8,128)S(1)} %select_add_fusion.3), channel_id=1, source_target_pairs={{0,2},{1,3},{2,0},{3,1},{4,6},{5,7},{6,4},{7,5},{8,10},{9,11},{10,... | collective-permute-start | bytes 1204232 | tf_op jit(solution)/shard_map/ppermute | solution.py:112
  169.9 2.1 fusion.40
  177.2 9.9 %collective-permute-done.34 = bf16[112,2048]{1,0:T(8,128)(2,1)S(1)} collective-permute-done((bf16[112,2048]{1,0:T(8,128)(2,1)S(1)}, bf16[112,2048]{1,0:T(8,128)(2,1)S(1)}, u32[]{:S(2)}, u32[]{:S(2)}) %collective-permute-start.34) | collective-permute-done | bytes 458784 | tf_op jit(solution)/shard_map/ppermute | solution.py:11
  187.1 2.1 fusion.48
  191.4 10.1 %collective-permute-done.36 = f32[896,112]{0,1:T(8,128)S(1)} collective-permute-done((f32[896,112]{0,1:T(8,128)S(1)}, f32[896,112]{0,1:T(8,128)S(1)}, u32[]{:S(2)}, u32[]{:S(2)}) %collective-permute-start.36) | collective-permute-done | bytes 401440 | tf_op jit(solution)/shard_map/ppermute | solution.py:112
  202.4 2.5 %collective-permute-done.37 = bf16[112,2048]{1,0:T(8,128)(2,1)S(1)} collective-permute-done((bf16[112,2048]{1,0:T(8,128)(2,1)S(1)}, bf16[112,2048]{1,0:T(8,128)(2,1)S(1)}, u32[]{:S(2)}, u32[]{:S(2)}) %collective-permute-start.37) | collective-permute-done | bytes 458784 | tf_op jit(solution)/shard_map/ppermute | solution.py:11
  207.4 2.1 fusion.56
  213.4 5.0 %collective-permute-done.38 = f32[896,112]{0,1:T(8,128)} collective-permute-done((f32[896,112]{0,1:T(8,128)}, f32[896,112]{0,1:T(8,128)}, u32[]{:S(2)}, u32[]{:S(2)}) %collective-permute-start.38) | collective-permute-done | bytes 401440 | tf_op jit(solution)/shard_map/ppermute | solution.py:112
  219.9 6.1 %collective-permute-done.39 = f32[896,112]{0,1:T(8,128)} collective-permute-done((f32[896,112]{0,1:T(8,128)}, f32[896,112]{0,1:T(8,128)}, u32[]{:S(2)}, u32[]{:S(2)}) %collective-permute-start.39) | collective-permute-done | bytes 401440 | tf_op jit(solution)/shard_map/ppermute | solution.py:97
  226.1 8.2 %collective-permute-done.40 = f32[896,112]{0,1:T(8,128)} collective-permute-done((f32[896,112]{0,1:T(8,128)}, f32[896,112]{0,1:T(8,128)}, u32[]{:S(2)}, u32[]{:S(2)}) %collective-permute-start.40) | collective-permute-done | bytes 401440 | tf_op jit(solution)/shard_map/ppermute | solution.py:97
  236.3 3.0 %copy.2 = f32[896,896]{1,0:T(8,128)} copy(f32[896,896]{0,1:T(8,128)S(1)} %broadcast_multiply_fusion) | data formatting | bytes 6422528 | tf_op jit(solution)/shard_map/div | solution.py:145
  (197 shorter events, 83.6 us)
Async XLA Ops:
  3.7 13.8 %collective-permute-start.3 = (f32[2,784]{1,0:T(2,128)S(1)}, f32[2,784]{1,0:T(2,128)S(1)}, u32[]{:S(2)}, u32[]{:S(2)}) collective-permute-start(f32[2,784]{1,0:T(2,128)S(1)} %pad_maximum_fusion.7), channel_id=1, source_target_pairs={{0,3},{1,2},{2,1},{3,0},{4,7},{5,6},{6,5},{7,4},{8,11},{9,10},{10,... | collective-permute-start | bytes 18824 | tf_op jit(solution)/shard_map/ppermute | solution.py:55
  6.1 11.4 %collective-permute-start.4 = (f32[2,784]{1,0:T(2,128)S(1)}, f32[2,784]{1,0:T(2,128)S(1)}, u32[]{:S(2)}, u32[]{:S(2)}) collective-permute-start(f32[2,784]{1,0:T(2,128)S(1)} %pad_maximum_fusion.7), channel_id=1, source_target_pairs={{0,2},{1,3},{2,0},{3,1},{4,6},{5,7},{6,4},{7,5},{8,10},{9,11},{10,... | collective-permute-start | bytes 18824 | tf_op jit(solution)/shard_map/ppermute | solution.py:55
  14.6 11.4 %collective-permute-start.6 = (bf16[112,2048]{1,0:T(8,128)(2,1)S(1)}, bf16[112,2048]{1,0:T(8,128)(2,1)S(1)}, u32[]{:S(2)}, u32[]{:S(2)}) collective-permute-start(bf16[112,2048]{1,0:T(8,128)(2,1)S(1)} %multiply_convert_fusion.1), channel_id=1, source_target_pairs={{4,0},{12,8},{20,16},{28,24},{0,4},{8,12},{16,20},{24,28},{5,1},{1... | collective-permute-start | bytes 1376264 | tf_op jit(solution)/shard_map/ppermute | solution.py:11
  16.2 13.0 %collective-permute-start.7 = (bf16[112,2048]{1,0:T(8,128)(2,1)S(1)}, bf16[112,2048]{1,0:T(8,128)(2,1)S(1)}, u32[]{:S(2)}, u32[]{:S(2)}) collective-permute-start(bf16[112,2048]{1,0:T(8,128)(2,1)S(1)} %multiply_convert_fusion.1), channel_id=1, source_target_pairs={{8,0},{12,4},{16,8},{20,12},{24,16},{28,20},{9,1},{13,5},{17,9},{2... | collective-permute-start | bytes 1376264 | tf_op jit(solution)/shard_map/ppermute | solution.py:11
  29.2 10.2 %collective-permute-start.8 = (bf16[112,2048]{1,0:T(8,128)(2,1)S(1)}, bf16[112,2048]{1,0:T(8,128)(2,1)S(1)}, u32[]{:S(2)}, u32[]{:S(2)}) collective-permute-start(bf16[112,2048]{1,0:T(8,128)(2,1)S(1)} %broadcast_select_fusion.14), channel_id=1, source_target_pairs={{4,0},{12,8},{20,16},{28,24},{0,4},{8,12},{16,20},{24,28},{5,1},{1... | collective-permute-start | bytes 1376264 | tf_op jit(solution)/shard_map/ppermute | solution.py:11
  29.8 11.8 %collective-permute-start.9 = (bf16[112,2048]{1,0:T(8,128)(2,1)S(1)}, bf16[112,2048]{1,0:T(8,128)(2,1)S(1)}, u32[]{:S(2)}, u32[]{:S(2)}) collective-permute-start(bf16[112,2048]{1,0:T(8,128)(2,1)S(1)} %get-tuple-element.134), channel_id=1, source_target_pairs={{8,0},{12,4},{16,8},{20,12},{24,16},{28,20},{9,1},{13,5},{17,9},{2... | collective-permute-start | bytes 1376264 | tf_op jit(solution)/shard_map/ppermute | solution.py:11
  43.2 9.3 %collective-permute-start.10 = (bf16[112,2048]{1,0:T(8,128)(2,1)}, bf16[112,2048]{1,0:T(8,128)(2,1)}, u32[]{:S(2)}, u32[]{:S(2)}) collective-permute-start(bf16[112,2048]{1,0:T(8,128)(2,1)} %broadcast_select_fusion.12), channel_id=1, source_target_pairs={{4,0},{12,8},{20,16},{28,24},{0,4},{8,12},{16,20},{24,28},{5,1},{1... | collective-permute-start | bytes 1376264 | tf_op jit(solution)/shard_map/ppermute | solution.py:11
  45.8 20.7 %collective-permute-start.11 = (bf16[224,2048]{1,0:T(8,128)(2,1)}, bf16[224,2048]{1,0:T(8,128)(2,1)}, u32[]{:S(2)}, u32[]{:S(2)}) collective-permute-start(bf16[224,2048]{1,0:T(8,128)(2,1)} %pad_maximum_fusion.1), channel_id=1, source_target_pairs={{8,0},{12,4},{16,8},{20,12},{24,16},{28,20},{9,1},{13,5},{17,9},{2... | collective-permute-start | bytes 2752520 | tf_op jit(solution)/shard_map/ppermute | solution.py:11
  67.8 20.2 %collective-permute-start.14 = (bf16[224,2048]{1,0:T(8,128)(2,1)S(1)}, bf16[224,2048]{1,0:T(8,128)(2,1)S(1)}, u32[]{:S(2)}, u32[]{:S(2)}) collective-permute-start(bf16[224,2048]{1,0:T(8,128)(2,1)S(1)} %pad_maximum_fusion.2), channel_id=1, source_target_pairs={{8,0},{12,4},{16,8},{20,12},{24,16},{28,20},{9,1},{13,5},{17,9},{2... | collective-permute-start | bytes 2752520 | tf_op jit(solution)/shard_map/ppermute | solution.py:11
  69.2 8.5 %collective-permute-start.13 = (bf16[112,2048]{1,0:T(8,128)(2,1)S(1)}, bf16[112,2048]{1,0:T(8,128)(2,1)S(1)}, u32[]{:S(2)}, u32[]{:S(2)}) collective-permute-start(bf16[112,2048]{1,0:T(8,128)(2,1)S(1)} %broadcast_select_fusion.10), channel_id=1, source_target_pairs={{4,0},{12,8},{20,16},{28,24},{0,4},{8,12},{16,20},{24,28},{5,1},{1... | collective-permute-start | bytes 1376264 | tf_op jit(solution)/shard_map/ppermute | solution.py:11
  72.1 16.0 %collective-permute-start.12 = (f32[896,224]{0,1:T(8,128)S(1)}, f32[896,224]{0,1:T(8,128)S(1)}, u32[]{:S(2)}, u32[]{:S(2)}) collective-permute-start(f32[896,224]{0,1:T(8,128)S(1)} %maximum_select_fusion), channel_id=1, source_target_pairs={{0,1},{1,0},{2,3},{3,2},{4,5},{5,4},{6,7},{7,6},{8,9},{9,8},{10,11... | collective-permute-start | bytes 2408456 | tf_op jit(solution)/shard_map/ppermute | solution.py:102
  88.2 20.3 %collective-permute-start.18 = (bf16[224,2048]{1,0:T(8,128)(2,1)S(1)}, bf16[224,2048]{1,0:T(8,128)(2,1)S(1)}, u32[]{:S(2)}, u32[]{:S(2)}) collective-permute-start(bf16[224,2048]{1,0:T(8,128)(2,1)S(1)} %pad_maximum_fusion.3), channel_id=1, source_target_pairs={{8,0},{12,4},{16,8},{20,12},{24,16},{28,20},{9,1},{13,5},{17,9},{2... | collective-permute-start | bytes 2752520 | tf_op jit(solution)/shard_map/ppermute | solution.py:11
  91.8 8.5 %collective-permute-start.16 = (bf16[112,2048]{1,0:T(8,128)(2,1)S(1)}, bf16[112,2048]{1,0:T(8,128)(2,1)S(1)}, u32[]{:S(2)}, u32[]{:S(2)}) collective-permute-start(bf16[112,2048]{1,0:T(8,128)(2,1)S(1)} %broadcast_select_fusion.8), channel_id=1, source_target_pairs={{4,0},{12,8},{20,16},{28,24},{0,4},{8,12},{16,20},{24,28},{5,1},{1... | collective-permute-start | bytes 1376264 | tf_op jit(solution)/shard_map/ppermute | solution.py:11
  95.3 13.4 %collective-permute-start.15 = (f32[896,224]{0,1:T(8,128)S(1)}, f32[896,224]{0,1:T(8,128)S(1)}, u32[]{:S(2)}, u32[]{:S(2)}) collective-permute-start(f32[896,224]{0,1:T(8,128)S(1)} %maximum_select_fusion.1), channel_id=1, source_target_pairs={{0,1},{1,0},{2,3},{3,2},{4,5},{5,4},{6,7},{7,6},{8,9},{9,8},{10,11... | collective-permute-start | bytes 2408456 | tf_op jit(solution)/shard_map/ppermute | solution.py:102
  108.7 20.4 %collective-permute-start.22 = (bf16[224,2048]{1,0:T(8,128)(2,1)S(1)}, bf16[224,2048]{1,0:T(8,128)(2,1)S(1)}, u32[]{:S(2)}, u32[]{:S(2)}) collective-permute-start(bf16[224,2048]{1,0:T(8,128)(2,1)S(1)} %pad_maximum_fusion.4), channel_id=1, source_target_pairs={{8,0},{12,4},{16,8},{20,12},{24,16},{28,20},{9,1},{13,5},{17,9},{2... | collective-permute-start | bytes 2752520 | tf_op jit(solution)/shard_map/ppermute | solution.py:11
  112.5 8.5 %collective-permute-start.20 = (bf16[112,2048]{1,0:T(8,128)(2,1)S(1)}, bf16[112,2048]{1,0:T(8,128)(2,1)S(1)}, u32[]{:S(2)}, u32[]{:S(2)}) collective-permute-start(bf16[112,2048]{1,0:T(8,128)(2,1)S(1)} %broadcast_select_fusion.6), channel_id=1, source_target_pairs={{4,0},{12,8},{20,16},{28,24},{0,4},{8,12},{16,20},{24,28},{5,1},{1... | collective-permute-start | bytes 1376264 | tf_op jit(solution)/shard_map/ppermute | solution.py:11
  116.0 13.3 %collective-permute-start.19 = (f32[896,224]{0,1:T(8,128)S(1)}, f32[896,224]{0,1:T(8,128)S(1)}, u32[]{:S(2)}, u32[]{:S(2)}) collective-permute-start(f32[896,224]{0,1:T(8,128)S(1)} %maximum_select_fusion.2), channel_id=1, source_target_pairs={{0,1},{1,0},{2,3},{3,2},{4,5},{5,4},{6,7},{7,6},{8,9},{9,8},{10,11... | collective-permute-start | bytes 2408456 | tf_op jit(solution)/shard_map/ppermute | solution.py:102
  129.4 18.8 %collective-permute-start.26 = (bf16[224,2048]{1,0:T(8,128)(2,1)S(1)}, bf16[224,2048]{1,0:T(8,128)(2,1)S(1)}, u32[]{:S(2)}, u32[]{:S(2)}) collective-permute-start(bf16[224,2048]{1,0:T(8,128)(2,1)S(1)} %pad_maximum_fusion.5), channel_id=1, source_target_pairs={{8,0},{12,4},{16,8},{20,12},{24,16},{28,20},{9,1},{13,5},{17,9},{2... | collective-permute-start | bytes 2752520 | tf_op jit(solution)/shard_map/ppermute | solution.py:11
  132.9 8.5 %collective-permute-start.24 = (bf16[112,2048]{1,0:T(8,128)(2,1)S(1)}, bf16[112,2048]{1,0:T(8,128)(2,1)S(1)}, u32[]{:S(2)}, u32[]{:S(2)}) collective-permute-start(bf16[112,2048]{1,0:T(8,128)(2,1)S(1)} %broadcast_select_fusion.4), channel_id=1, source_target_pairs={{4,0},{12,8},{20,16},{28,24},{0,4},{8,12},{16,20},{24,28},{5,1},{1... | collective-permute-start | bytes 1376264 | tf_op jit(solution)/shard_map/ppermute | solution.py:11
  136.3 12.0 %collective-permute-start.23 = (f32[896,224]{0,1:T(8,128)S(1)}, f32[896,224]{0,1:T(8,128)S(1)}, u32[]{:S(2)}, u32[]{:S(2)}) collective-permute-start(f32[896,224]{0,1:T(8,128)S(1)} %maximum_select_fusion.3), channel_id=1, source_target_pairs={{0,1},{1,0},{2,3},{3,2},{4,5},{5,4},{6,7},{7,6},{8,9},{9,8},{10,11... | collective-permute-start | bytes 2408456 | tf_op jit(solution)/shard_map/ppermute | solution.py:102
  148.4 17.5 %collective-permute-start.30 = (bf16[224,2048]{1,0:T(8,128)(2,1)S(1)}, bf16[224,2048]{1,0:T(8,128)(2,1)S(1)}, u32[]{:S(2)}, u32[]{:S(2)}) collective-permute-start(bf16[224,2048]{1,0:T(8,128)(2,1)S(1)} %pad_maximum_fusion.6), channel_id=1, source_target_pairs={{8,0},{12,4},{16,8},{20,12},{24,16},{28,20},{9,1},{13,5},{17,9},{2... | collective-permute-start | bytes 2752520 | tf_op jit(solution)/shard_map/ppermute | solution.py:11
  149.9 9.3 %collective-permute-start.29 = (f32[896,112]{0,1:T(8,128)S(1)}, f32[896,112]{0,1:T(8,128)S(1)}, u32[]{:S(2)}, u32[]{:S(2)}) collective-permute-start(f32[896,112]{0,1:T(8,128)S(1)} %select_add_fusion.4), channel_id=1, source_target_pairs={{0,2},{1,3},{2,0},{3,1},{4,6},{5,7},{6,4},{7,5},{8,10},{9,11},{10,... | collective-permute-start | bytes 1204232 | tf_op jit(solution)/shard_map/ppermute | solution.py:112
  156.8 9.2 %collective-permute-start.27 = (f32[896,224]{0,1:T(8,128)S(1)}, f32[896,224]{0,1:T(8,128)S(1)}, u32[]{:S(2)}, u32[]{:S(2)}) collective-permute-start(f32[896,224]{0,1:T(8,128)S(1)} %maximum_select_fusion.4), channel_id=1, source_target_pairs={{0,1},{1,0},{2,3},{3,2},{4,5},{5,4},{6,7},{7,6},{8,9},{9,8},{10,11... | collective-permute-start | bytes 2408456 | tf_op jit(solution)/shard_map/ppermute | solution.py:102
  172.2 14.9 %collective-permute-start.31 = (f32[896,224]{0,1:T(8,128)S(1)}, f32[896,224]{0,1:T(8,128)S(1)}, u32[]{:S(2)}, u32[]{:S(2)}) collective-permute-start(f32[896,224]{0,1:T(8,128)S(1)} %maximum_select_fusion.5), channel_id=1, source_target_pairs={{0,1},{1,0},{2,3},{3,2},{4,5},{5,4},{6,7},{7,6},{8,9},{9,8},{10,11... | collective-permute-start | bytes 2408456 | tf_op jit(solution)/shard_map/ppermute | solution.py:102
  172.3 14.8 %collective-permute-start.34 = (bf16[112,2048]{1,0:T(8,128)(2,1)S(1)}, bf16[112,2048]{1,0:T(8,128)(2,1)S(1)}, u32[]{:S(2)}, u32[]{:S(2)}) collective-permute-start(bf16[112,2048]{1,0:T(8,128)(2,1)S(1)} %broadcast_select_fusion.1), channel_id=1, source_target_pairs={{8,0},{12,4},{16,8},{20,12},{24,16},{28,20},{9,1},{13,5},{17,9},{2... | collective-permute-start | bytes 1376264 | tf_op jit(solution)/shard_map/ppermute | solution.py:11
  189.5 15.4 %collective-permute-start.35 = (f32[896,224]{0,1:T(8,128)S(1)}, f32[896,224]{0,1:T(8,128)S(1)}, u32[]{:S(2)}, u32[]{:S(2)}) collective-permute-start(f32[896,224]{0,1:T(8,128)S(1)} %maximum_select_fusion.6), channel_id=1, source_target_pairs={{0,1},{1,0},{2,3},{3,2},{4,5},{5,4},{6,7},{7,6},{8,9},{9,8},{10,11... | collective-permute-start | bytes 2408456 | tf_op jit(solution)/shard_map/ppermute | solution.py:102
  189.7 11.8 %collective-permute-start.36 = (f32[896,112]{0,1:T(8,128)S(1)}, f32[896,112]{0,1:T(8,128)S(1)}, u32[]{:S(2)}, u32[]{:S(2)}) collective-permute-start(f32[896,112]{0,1:T(8,128)S(1)} %select_add_fusion.2), channel_id=1, source_target_pairs={{0,2},{1,3},{2,0},{3,1},{4,6},{5,7},{6,4},{7,5},{8,10},{9,11},{10,... | collective-permute-start | bytes 1204232 | tf_op jit(solution)/shard_map/ppermute | solution.py:112
  189.9 15.0 %collective-permute-start.37 = (bf16[112,2048]{1,0:T(8,128)(2,1)S(1)}, bf16[112,2048]{1,0:T(8,128)(2,1)S(1)}, u32[]{:S(2)}, u32[]{:S(2)}) collective-permute-start(bf16[112,2048]{1,0:T(8,128)(2,1)S(1)} %broadcast_select_fusion), channel_id=1, source_target_pairs={{8,0},{12,4},{16,8},{20,12},{24,16},{28,20},{9,1},{13,5},{17,9},{2... | collective-permute-start | bytes 1376264 | tf_op jit(solution)/shard_map/ppermute | solution.py:11
  205.9 12.5 %collective-permute-start.38 = (f32[896,112]{0,1:T(8,128)}, f32[896,112]{0,1:T(8,128)}, u32[]{:S(2)}, u32[]{:S(2)}) collective-permute-start(f32[896,112]{0,1:T(8,128)} %select_add_fusion.1), channel_id=1, source_target_pairs={{0,2},{1,3},{2,0},{3,1},{4,6},{5,7},{6,4},{7,5},{8,10},{9,11},{10,... | collective-permute-start | bytes 1204232 | tf_op jit(solution)/shard_map/ppermute | solution.py:112
  210.5 15.6 %collective-permute-start.39 = (f32[896,112]{0,1:T(8,128)}, f32[896,112]{0,1:T(8,128)}, u32[]{:S(2)}, u32[]{:S(2)}) collective-permute-start(f32[896,112]{0,1:T(8,128)} %get-tuple-element.273), channel_id=1, source_target_pairs={{0,3},{1,2},{2,1},{3,0},{4,7},{5,6},{6,5},{7,4},{8,11},{9,10},{10,... | collective-permute-start | bytes 1204232 | tf_op jit(solution)/shard_map/ppermute | solution.py:97
  211.3 14.8 %collective-permute-start.41 = (f32[896,112]{0,1:T(8,128)}, f32[896,112]{0,1:T(8,128)}, u32[]{:S(2)}, u32[]{:S(2)}) collective-permute-start(f32[896,112]{0,1:T(8,128)} %get-tuple-element.272), channel_id=1, source_target_pairs={{0,1},{1,0},{2,3},{3,2},{4,5},{5,4},{6,7},{7,6},{8,9},{9,8},{10,11... | collective-permute-start | bytes 1204232 | tf_op jit(solution)/shard_map/ppermute | solution.py:97
  212.0 22.3 %collective-permute-start.40 = (f32[896,112]{0,1:T(8,128)}, f32[896,112]{0,1:T(8,128)}, u32[]{:S(2)}, u32[]{:S(2)}) collective-permute-start(f32[896,112]{0,1:T(8,128)} %select_select_fusion.1), channel_id=1, source_target_pairs={{0,2},{1,3},{2,0},{3,1},{4,6},{5,7},{6,4},{7,5},{8,10},{9,11},{10,... | collective-permute-start | bytes 1204232 | tf_op jit(solution)/shard_map/ppermute | solution.py:97
  (37 other events, 594.5 us)

commit v9 on v8

--- a/solution.py
+++ b/solution.py
@@ -86,20 +86,11 @@
         gram = jnp.einsum("ab,cb->ac", own_block, blocks, preferred_element_type=jnp.float32)
         tiles = [gram[:, k * step:(k + 1) * step] for k in range(BAND + 1)]
         state["tiles"][c] = tiles
+        payload = jnp.where(even_me, jnp.concatenate([tiles[1], tiles[3]], axis=1),
+                            jnp.concatenate([tiles[0], tiles[2]], axis=1))
+        state["first"][c] = lax.ppermute(payload, "samp", partner)
         if c == CHUNKS - 1:
-            outgoing = []
-            for i in [0] + flips:
-                target = tiles[0]
-                for k in range(1, groups):
-                    target = jnp.where(jnp.bitwise_xor(me, i) == k, tiles[k], target)
-                outgoing.append(target)
-            arrived = [outgoing[0]] + [
-                lax.ppermute(outgoing[i], "samp", [(j, j ^ i) for j in range(groups)]) for i in flips]
-            state["results"][c] = added(arrived)
-        else:
-            payload = jnp.where(even_me, jnp.concatenate([tiles[1], tiles[3]], axis=1),
-                                jnp.concatenate([tiles[0], tiles[2]], axis=1))
-            state["first"][c] = lax.ppermute(payload, "samp", partner)
+            second_level(c)
 
     def pick(c, a, b, d, e):
         t = state["tiles"][c]

time: 240 us -> 232 us (0.967)
  other arithmetic: 28.5 us -> 18.5 us
    ppermute x3 -> x0, waiting for transfers between devices: 14.4 us -> none  [finish(): lax.ppermute(outgoing[i], 'samp', [(j, j ^ i) for j in range(groups)])]
    ppermute x7 -> x8, waiting for transfers between devices: 25.2 us -> 36.7 us  [second_level(): last = lax.ppermute(pick(c, 2, 3, 0, 1) + onward, 'samp', across)]
    add x7 -> x8, other arithmetic: 7.12 us -> 1.42 us  [second_level(): state['results'][c] = pick(c, 0, 1, 2, 3) + mine + last]
    ppermute x19, waiting for transfers between devices: 97.6 us -> 102 us  [moved(): return lax.ppermute(value, 'snp', pairs)]
    ppermute x7 -> x8, starting transfers between devices: 13.5 us -> 15.6 us  [second_level(): last = lax.ppermute(pick(c, 2, 3, 0, 1) + onward, 'samp', across)]
  transfers between devices with their start and end apart: 42 -> 41, of which waited for: 30 -> 30; matrix products, arithmetic and copies ran while one was open for 16% -> 12% of each run, Pallas kernels for 0% -> 0%
where the time goes in v9:
time: 232 us; the launch traced here: 231 us
  waiting for transfers between devices  142 us (61%)
  starting transfers between devices  44.6 us (19%)
  other arithmetic  18.5 us (8%)
  matrix products  16.7 us (7%)
  local copies, waits for them, and re-layouts  7.9 us (3%)
    ppermute x19, waiting for transfers between devices, moved(): return lax.ppermute(value, 'snp', pairs)  102 us
    ppermute x8, waiting for transfers between devices, second_level(): last = lax.ppermute(pick(c, 2, 3, 0, 1) + onward, 'samp', across)  36.7 us
    ppermute x19, starting transfers between devices, moved(): return lax.ppermute(value, 'snp', pairs)  23.4 us
    dot_general x8, matrix products, finish(): jnp.einsum('ab,cb->ac', own_block, blocks, preferred_element_type=jnp.flo...  16.7 us
    ppermute x8, starting transfers between devices, second_level(): last = lax.ppermute(pick(c, 2, 3, 0, 1) + onward, 'samp', across)  15.6 us
    ppermute x6, starting transfers between devices, standard_rows(): lax.ppermute(moments, 'samp', [(j, j ^ i) for j in range(groups)])  5.12 us
    reduce_sum x2, other arithmetic, local_moments(): return (jnp.sum(values, axis=1), jnp.sum(values * values, axis=1))  5.01 us
    convert_element_type x2, other arithmetic, standardize(): ((values - mean[:, None]) * lax.rsqrt(variance + 1e-05)[:, None]).astype(...  4.83 us
  transfers between devices with their start and end apart: 41, of which 30 were waited for; matrix products, arithmetic and copies ran while one was open for 12% of the time, Pallas kernels for 0%

profile of v9, /device:TPU:0, one launch (start us, length us, event | category | flops | bytes accessed | tf_op | source)
XLA Modules:
  0.0 231.0 jit_solution(12006526941166497020)
XLA Ops:
  0.0 3.6 %slice_reduce_fusion = (f32[784]{0:T(1024)S(1)}, f32[784]{0:T(1024)S(1)}) fusion(f32[896,2048]{1,0:T(8,128)} %param.1), kind=kLoop, calls=%fused_computation.2 | loop fusion | flops 4815328 | bytes 6428800 | tf_op jit(solution)/shard_map/reduce_sum | solution.py:21
  3.7 2.4 %collective-permute-start.3 = (f32[2,784]{1,0:T(2,128)S(1)}, f32[2,784]{1,0:T(2,128)S(1)}, u32[]{:S(2)}, u32[]{:S(2)}) collective-permute-start(f32[2,784]{1,0:T(2,128)S(1)} %pad_maximum_fusion.7), channel_id=1, source_target_pairs={{0,3},{1,2},{2,1},{3,0},{4,7},{5,6},{6,5},{7,4},{8,11},{9,10},{10,... | collective-permute-start | bytes 18824 | tf_op jit(solution)/shard_map/ppermute | solution.py:55
  17.6 3.5 %multiply_convert_fusion = bf16[784,2048]{1,0:T(8,128)(2,1)S(1)} fusion(f32[896,2048]{1,0:T(8,128)} %param.1, f32[784]{0:T(1024)S(1)} %add_rsqrt_fusion, f32[784]{0:T(1024)S(1)} %get-tuple-element.263), kind=kLoop, calls=%fused_computation | loop fusion | flops 4816896 | bytes 9640064 | tf_op jit(solution)/shard_map/convert_element_type | solution.py:17
  22.6 3.4 %collective-permute-done.6 = bf16[112,2048]{1,0:T(8,128)(2,1)S(1)} collective-permute-done((bf16[112,2048]{1,0:T(8,128)(2,1)S(1)}, bf16[112,2048]{1,0:T(8,128)(2,1)S(1)}, u32[]{:S(2)}, u32[]{:S(2)}) %collective-permute-start.6) | collective-permute-done | bytes 458784 | tf_op jit(solution)/shard_map/ppermute | solution.py:11
  26.0 3.1 %collective-permute-done.7 = bf16[112,2048]{1,0:T(8,128)(2,1)S(1)} collective-permute-done((bf16[112,2048]{1,0:T(8,128)(2,1)S(1)}, bf16[112,2048]{1,0:T(8,128)(2,1)S(1)}, u32[]{:S(2)}, u32[]{:S(2)}) %collective-permute-start.7) | collective-permute-done | bytes 458784 | tf_op jit(solution)/shard_map/ppermute | solution.py:11
  31.1 8.4 %collective-permute-done.8 = bf16[112,2048]{1,0:T(8,128)(2,1)S(1)} collective-permute-done((bf16[112,2048]{1,0:T(8,128)(2,1)S(1)}, bf16[112,2048]{1,0:T(8,128)(2,1)S(1)}, u32[]{:S(2)}, u32[]{:S(2)}) %collective-permute-start.8) | collective-permute-done | bytes 458784 | tf_op jit(solution)/shard_map/ppermute | solution.py:11
  47.1 5.4 %collective-permute-done.10 = bf16[112,2048]{1,0:T(8,128)(2,1)} collective-permute-done((bf16[112,2048]{1,0:T(8,128)(2,1)}, bf16[112,2048]{1,0:T(8,128)(2,1)}, u32[]{:S(2)}, u32[]{:S(2)}) %collective-permute-start.10) | collective-permute-done | bytes 458784 | tf_op jit(solution)/shard_map/ppermute | solution.py:11
  53.5 12.9 %collective-permute-done.11 = bf16[224,2048]{1,0:T(8,128)(2,1)} collective-permute-done((bf16[224,2048]{1,0:T(8,128)(2,1)}, bf16[224,2048]{1,0:T(8,128)(2,1)}, u32[]{:S(2)}, u32[]{:S(2)}) %collective-permute-start.11) | collective-permute-done | bytes 917536 | tf_op jit(solution)/shard_map/ppermute | solution.py:11
  72.1 5.6 %collective-permute-done.13 = bf16[112,2048]{1,0:T(8,128)(2,1)S(1)} collective-permute-done((bf16[112,2048]{1,0:T(8,128)(2,1)S(1)}, bf16[112,2048]{1,0:T(8,128)(2,1)S(1)}, u32[]{:S(2)}, u32[]{:S(2)}) %collective-permute-start.13) | collective-permute-done | bytes 458784 | tf_op jit(solution)/shard_map/ppermute | solution.py:11
  78.7 9.2 %collective-permute-done.14 = bf16[224,2048]{1,0:T(8,128)(2,1)S(1)} collective-permute-done((bf16[224,2048]{1,0:T(8,128)(2,1)S(1)}, bf16[224,2048]{1,0:T(8,128)(2,1)S(1)}, u32[]{:S(2)}, u32[]{:S(2)}) %collective-permute-start.14) | collective-permute-done | bytes 917536 | tf_op jit(solution)/shard_map/ppermute | solution.py:11
  92.8 2.1 fusion.8
  95.2 2.4 %collective-permute-done.17 = f32[896,112]{0,1:T(8,128)S(1)} collective-permute-done((f32[896,112]{0,1:T(8,128)S(1)}, f32[896,112]{0,1:T(8,128)S(1)}, u32[]{:S(2)}, u32[]{:S(2)}) %collective-permute-start.17) | collective-permute-done | bytes 401440 | tf_op jit(solution)/shard_map/ppermute | solution.py:103
  97.8 2.5 %collective-permute-done.16 = bf16[112,2048]{1,0:T(8,128)(2,1)S(1)} collective-permute-done((bf16[112,2048]{1,0:T(8,128)(2,1)S(1)}, bf16[112,2048]{1,0:T(8,128)(2,1)S(1)}, u32[]{:S(2)}, u32[]{:S(2)}) %collective-permute-start.16) | collective-permute-done | bytes 458784 | tf_op jit(solution)/shard_map/ppermute | solution.py:11
  100.3 8.1 %collective-permute-done.18 = bf16[224,2048]{1,0:T(8,128)(2,1)S(1)} collective-permute-done((bf16[224,2048]{1,0:T(8,128)(2,1)S(1)}, bf16[224,2048]{1,0:T(8,128)(2,1)S(1)}, u32[]{:S(2)}, u32[]{:S(2)}) %collective-permute-start.18) | collective-permute-done | bytes 917536 | tf_op jit(solution)/shard_map/ppermute | solution.py:11
  115.9 2.4 %collective-permute-done.21 = f32[896,112]{0,1:T(8,128)S(1)} collective-permute-done((f32[896,112]{0,1:T(8,128)S(1)}, f32[896,112]{0,1:T(8,128)S(1)}, u32[]{:S(2)}, u32[]{:S(2)}) %collective-permute-start.21) | collective-permute-done | bytes 401440 | tf_op jit(solution)/shard_map/ppermute | solution.py:103
  118.5 2.5 %collective-permute-done.20 = bf16[112,2048]{1,0:T(8,128)(2,1)S(1)} collective-permute-done((bf16[112,2048]{1,0:T(8,128)(2,1)S(1)}, bf16[112,2048]{1,0:T(8,128)(2,1)S(1)}, u32[]{:S(2)}, u32[]{:S(2)}) %collective-permute-start.20) | collective-permute-done | bytes 458784 | tf_op jit(solution)/shard_map/ppermute | solution.py:11
  121.0 8.1 %collective-permute-done.22 = bf16[224,2048]{1,0:T(8,128)(2,1)S(1)} collective-permute-done((bf16[224,2048]{1,0:T(8,128)(2,1)S(1)}, bf16[224,2048]{1,0:T(8,128)(2,1)S(1)}, u32[]{:S(2)}, u32[]{:S(2)}) %collective-permute-start.22) | collective-permute-done | bytes 917536 | tf_op jit(solution)/shard_map/ppermute | solution.py:11
  136.3 2.4 %collective-permute-done.25 = f32[896,112]{0,1:T(8,128)S(1)} collective-permute-done((f32[896,112]{0,1:T(8,128)S(1)}, f32[896,112]{0,1:T(8,128)S(1)}, u32[]{:S(2)}, u32[]{:S(2)}) %collective-permute-start.25) | collective-permute-done | bytes 401440 | tf_op jit(solution)/shard_map/ppermute | solution.py:103
  138.9 2.5 %collective-permute-done.24 = bf16[112,2048]{1,0:T(8,128)(2,1)S(1)} collective-permute-done((bf16[112,2048]{1,0:T(8,128)(2,1)S(1)}, bf16[112,2048]{1,0:T(8,128)(2,1)S(1)}, u32[]{:S(2)}, u32[]{:S(2)}) %collective-permute-start.24) | collective-permute-done | bytes 458784 | tf_op jit(solution)/shard_map/ppermute | solution.py:11
  141.4 6.8 %collective-permute-done.26 = bf16[224,2048]{1,0:T(8,128)(2,1)S(1)} collective-permute-done((bf16[224,2048]{1,0:T(8,128)(2,1)S(1)}, bf16[224,2048]{1,0:T(8,128)(2,1)S(1)}, u32[]{:S(2)}, u32[]{:S(2)}) %collective-permute-start.26) | collective-permute-done | bytes 917536 | tf_op jit(solution)/shard_map/ppermute | solution.py:11
  149.8 3.5 %collective-permute-start.29 = (f32[896,112]{0,1:T(8,128)S(1)}, f32[896,112]{0,1:T(8,128)S(1)}, u32[]{:S(2)}, u32[]{:S(2)}) collective-permute-start(f32[896,112]{0,1:T(8,128)S(1)} %select_add_fusion.4), channel_id=1, source_target_pairs={{0,2},{1,3},{2,0},{3,1},{4,6},{5,7},{6,4},{7,5},{8,10},{9,11},{10,... | collective-permute-start | bytes 1204232 | tf_op jit(solution)/shard_map/ppermute | solution.py:103
  156.8 2.3 %collective-permute-done.29 = f32[896,112]{0,1:T(8,128)S(1)} collective-permute-done((f32[896,112]{0,1:T(8,128)S(1)}, f32[896,112]{0,1:T(8,128)S(1)}, u32[]{:S(2)}, u32[]{:S(2)}) %collective-permute-start.29) | collective-permute-done | bytes 401440 | tf_op jit(solution)/shard_map/ppermute | solution.py:103
  159.3 2.6 %collective-permute-done.28 = bf16[112,2048]{1,0:T(8,128)(2,1)S(1)} collective-permute-done((bf16[112,2048]{1,0:T(8,128)(2,1)S(1)}, bf16[112,2048]{1,0:T(8,128)(2,1)S(1)}, u32[]{:S(2)}, u32[]{:S(2)}) %collective-permute-start.28) | collective-permute-done | bytes 458784 | tf_op jit(solution)/shard_map/ppermute | solution.py:11
  161.9 4.0 %collective-permute-done.30 = bf16[224,2048]{1,0:T(8,128)(2,1)S(1)} collective-permute-done((bf16[224,2048]{1,0:T(8,128)(2,1)S(1)}, bf16[224,2048]{1,0:T(8,128)(2,1)S(1)}, u32[]{:S(2)}, u32[]{:S(2)}) %collective-permute-start.30) | collective-permute-done | bytes 917536 | tf_op jit(solution)/shard_map/ppermute | solution.py:11
  166.1 2.5 %collective-permute-start.33 = (f32[896,112]{0,1:T(8,128)S(1)}, f32[896,112]{0,1:T(8,128)S(1)}, u32[]{:S(2)}, u32[]{:S(2)}) collective-permute-start(f32[896,112]{0,1:T(8,128)S(1)} %select_add_fusion.3), channel_id=1, source_target_pairs={{0,2},{1,3},{2,0},{3,1},{4,6},{5,7},{6,4},{7,5},{8,10},{9,11},{10,... | collective-permute-start | bytes 1204232 | tf_op jit(solution)/shard_map/ppermute | solution.py:103
  174.6 2.4 %collective-permute-done.32 = bf16[112,2048]{1,0:T(8,128)(2,1)S(1)} collective-permute-done((bf16[112,2048]{1,0:T(8,128)(2,1)S(1)}, bf16[112,2048]{1,0:T(8,128)(2,1)S(1)}, u32[]{:S(2)}, u32[]{:S(2)}) %collective-permute-start.32) | collective-permute-done | bytes 458784 | tf_op jit(solution)/shard_map/ppermute | solution.py:11
  177.1 9.9 %collective-permute-done.34 = bf16[112,2048]{1,0:T(8,128)(2,1)S(1)} collective-permute-done((bf16[112,2048]{1,0:T(8,128)(2,1)S(1)}, bf16[112,2048]{1,0:T(8,128)(2,1)S(1)}, u32[]{:S(2)}, u32[]{:S(2)}) %collective-permute-start.34) | collective-permute-done | bytes 458784 | tf_op jit(solution)/shard_map/ppermute | solution.py:11
  191.0 10.3 %collective-permute-done.36 = f32[896,112]{0,1:T(8,128)S(1)} collective-permute-done((f32[896,112]{0,1:T(8,128)S(1)}, f32[896,112]{0,1:T(8,128)S(1)}, u32[]{:S(2)}, u32[]{:S(2)}) %collective-permute-start.36) | collective-permute-done | bytes 401440 | tf_op jit(solution)/shard_map/ppermute | solution.py:103
  201.5 3.0 %collective-permute-done.37 = bf16[112,2048]{1,0:T(8,128)(2,1)S(1)} collective-permute-done((bf16[112,2048]{1,0:T(8,128)(2,1)S(1)}, bf16[112,2048]{1,0:T(8,128)(2,1)S(1)}, u32[]{:S(2)}, u32[]{:S(2)}) %collective-permute-start.37) | collective-permute-done | bytes 458784 | tf_op jit(solution)/shard_map/ppermute | solution.py:11
  211.1 8.1 %collective-permute-done.39 = f32[896,112]{0,1:T(8,128)S(1)} collective-permute-done((f32[896,112]{0,1:T(8,128)S(1)}, f32[896,112]{0,1:T(8,128)S(1)}, u32[]{:S(2)}, u32[]{:S(2)}) %collective-permute-start.39) | collective-permute-done | bytes 401440 | tf_op jit(solution)/shard_map/ppermute | solution.py:103
  219.4 8.0 %collective-permute-done.40 = f32[896,112]{0,1:T(8,128)S(1)} collective-permute-done((f32[896,112]{0,1:T(8,128)S(1)}, f32[896,112]{0,1:T(8,128)S(1)}, u32[]{:S(2)}, u32[]{:S(2)}) %collective-permute-start.40) | collective-permute-done | bytes 401440 | tf_op jit(solution)/shard_map/ppermute | solution.py:103
  228.0 3.0 %copy.2 = f32[896,896]{1,0:T(8,128)} copy(f32[896,896]{0,1:T(8,128)S(1)} %broadcast_multiply_fusion) | data formatting | bytes 6422528 | tf_op jit(solution)/shard_map/div | solution.py:136
  (178 shorter events, 73.3 us)
Async XLA Ops:
  3.7 13.8 %collective-permute-start.3 = (f32[2,784]{1,0:T(2,128)S(1)}, f32[2,784]{1,0:T(2,128)S(1)}, u32[]{:S(2)}, u32[]{:S(2)}) collective-permute-start(f32[2,784]{1,0:T(2,128)S(1)} %pad_maximum_fusion.7), channel_id=1, source_target_pairs={{0,3},{1,2},{2,1},{3,0},{4,7},{5,6},{6,5},{7,4},{8,11},{9,10},{10,... | collective-permute-start | bytes 18824 | tf_op jit(solution)/shard_map/ppermute | solution.py:55
  6.1 11.4 %collective-permute-start.4 = (f32[2,784]{1,0:T(2,128)S(1)}, f32[2,784]{1,0:T(2,128)S(1)}, u32[]{:S(2)}, u32[]{:S(2)}) collective-permute-start(f32[2,784]{1,0:T(2,128)S(1)} %pad_maximum_fusion.7), channel_id=1, source_target_pairs={{0,2},{1,3},{2,0},{3,1},{4,6},{5,7},{6,4},{7,5},{8,10},{9,11},{10,... | collective-permute-start | bytes 18824 | tf_op jit(solution)/shard_map/ppermute | solution.py:55
  14.6 11.4 %collective-permute-start.6 = (bf16[112,2048]{1,0:T(8,128)(2,1)S(1)}, bf16[112,2048]{1,0:T(8,128)(2,1)S(1)}, u32[]{:S(2)}, u32[]{:S(2)}) collective-permute-start(bf16[112,2048]{1,0:T(8,128)(2,1)S(1)} %multiply_convert_fusion.1), channel_id=1, source_target_pairs={{4,0},{12,8},{20,16},{28,24},{0,4},{8,12},{16,20},{24,28},{5,1},{1... | collective-permute-start | bytes 1376264 | tf_op jit(solution)/shard_map/ppermute | solution.py:11
  16.2 13.0 %collective-permute-start.7 = (bf16[112,2048]{1,0:T(8,128)(2,1)S(1)}, bf16[112,2048]{1,0:T(8,128)(2,1)S(1)}, u32[]{:S(2)}, u32[]{:S(2)}) collective-permute-start(bf16[112,2048]{1,0:T(8,128)(2,1)S(1)} %multiply_convert_fusion.1), channel_id=1, source_target_pairs={{8,0},{12,4},{16,8},{20,12},{24,16},{28,20},{9,1},{13,5},{17,9},{2... | collective-permute-start | bytes 1376264 | tf_op jit(solution)/shard_map/ppermute | solution.py:11
  29.2 10.2 %collective-permute-start.8 = (bf16[112,2048]{1,0:T(8,128)(2,1)S(1)}, bf16[112,2048]{1,0:T(8,128)(2,1)S(1)}, u32[]{:S(2)}, u32[]{:S(2)}) collective-permute-start(bf16[112,2048]{1,0:T(8,128)(2,1)S(1)} %broadcast_select_fusion.14), channel_id=1, source_target_pairs={{4,0},{12,8},{20,16},{28,24},{0,4},{8,12},{16,20},{24,28},{5,1},{1... | collective-permute-start | bytes 1376264 | tf_op jit(solution)/shard_map/ppermute | solution.py:11
  29.8 11.8 %collective-permute-start.9 = (bf16[112,2048]{1,0:T(8,128)(2,1)S(1)}, bf16[112,2048]{1,0:T(8,128)(2,1)S(1)}, u32[]{:S(2)}, u32[]{:S(2)}) collective-permute-start(bf16[112,2048]{1,0:T(8,128)(2,1)S(1)} %get-tuple-element.134), channel_id=1, source_target_pairs={{8,0},{12,4},{16,8},{20,12},{24,16},{28,20},{9,1},{13,5},{17,9},{2... | collective-permute-start | bytes 1376264 | tf_op jit(solution)/shard_map/ppermute | solution.py:11
  43.2 9.3 %collective-permute-start.10 = (bf16[112,2048]{1,0:T(8,128)(2,1)}, bf16[112,2048]{1,0:T(8,128)(2,1)}, u32[]{:S(2)}, u32[]{:S(2)}) collective-permute-start(bf16[112,2048]{1,0:T(8,128)(2,1)} %broadcast_select_fusion.12), channel_id=1, source_target_pairs={{4,0},{12,8},{20,16},{28,24},{0,4},{8,12},{16,20},{24,28},{5,1},{1... | collective-permute-start | bytes 1376264 | tf_op jit(solution)/shard_map/ppermute | solution.py:11
  45.7 20.7 %collective-permute-start.11 = (bf16[224,2048]{1,0:T(8,128)(2,1)}, bf16[224,2048]{1,0:T(8,128)(2,1)}, u32[]{:S(2)}, u32[]{:S(2)}) collective-permute-start(bf16[224,2048]{1,0:T(8,128)(2,1)} %pad_maximum_fusion.1), channel_id=1, source_target_pairs={{8,0},{12,4},{16,8},{20,12},{24,16},{28,20},{9,1},{13,5},{17,9},{2... | collective-permute-start | bytes 2752520 | tf_op jit(solution)/shard_map/ppermute | solution.py:11
  67.7 20.2 %collective-permute-start.14 = (bf16[224,2048]{1,0:T(8,128)(2,1)S(1)}, bf16[224,2048]{1,0:T(8,128)(2,1)S(1)}, u32[]{:S(2)}, u32[]{:S(2)}) collective-permute-start(bf16[224,2048]{1,0:T(8,128)(2,1)S(1)} %pad_maximum_fusion.2), channel_id=1, source_target_pairs={{8,0},{12,4},{16,8},{20,12},{24,16},{28,20},{9,1},{13,5},{17,9},{2... | collective-permute-start | bytes 2752520 | tf_op jit(solution)/shard_map/ppermute | solution.py:11
  69.1 8.5 %collective-permute-start.13 = (bf16[112,2048]{1,0:T(8,128)(2,1)S(1)}, bf16[112,2048]{1,0:T(8,128)(2,1)S(1)}, u32[]{:S(2)}, u32[]{:S(2)}) collective-permute-start(bf16[112,2048]{1,0:T(8,128)(2,1)S(1)} %broadcast_select_fusion.10), channel_id=1, source_target_pairs={{4,0},{12,8},{20,16},{28,24},{0,4},{8,12},{16,20},{24,28},{5,1},{1... | collective-permute-start | bytes 1376264 | tf_op jit(solution)/shard_map/ppermute | solution.py:11
  72.0 16.0 %collective-permute-start.12 = (f32[896,224]{0,1:T(8,128)S(1)}, f32[896,224]{0,1:T(8,128)S(1)}, u32[]{:S(2)}, u32[]{:S(2)}) collective-permute-start(f32[896,224]{0,1:T(8,128)S(1)} %maximum_select_fusion), channel_id=1, source_target_pairs={{0,1},{1,0},{2,3},{3,2},{4,5},{5,4},{6,7},{7,6},{8,9},{9,8},{10,11... | collective-permute-start | bytes 2408456 | tf_op jit(solution)/shard_map/ppermute | solution.py:91
  88.1 20.3 %collective-permute-start.18 = (bf16[224,2048]{1,0:T(8,128)(2,1)S(1)}, bf16[224,2048]{1,0:T(8,128)(2,1)S(1)}, u32[]{:S(2)}, u32[]{:S(2)}) collective-permute-start(bf16[224,2048]{1,0:T(8,128)(2,1)S(1)} %pad_maximum_fusion.3), channel_id=1, source_target_pairs={{8,0},{12,4},{16,8},{20,12},{24,16},{28,20},{9,1},{13,5},{17,9},{2... | collective-permute-start | bytes 2752520 | tf_op jit(solution)/shard_map/ppermute | solution.py:11
  91.7 8.5 %collective-permute-start.16 = (bf16[112,2048]{1,0:T(8,128)(2,1)S(1)}, bf16[112,2048]{1,0:T(8,128)(2,1)S(1)}, u32[]{:S(2)}, u32[]{:S(2)}) collective-permute-start(bf16[112,2048]{1,0:T(8,128)(2,1)S(1)} %broadcast_select_fusion.8), channel_id=1, source_target_pairs={{4,0},{12,8},{20,16},{28,24},{0,4},{8,12},{16,20},{24,28},{5,1},{1... | collective-permute-start | bytes 1376264 | tf_op jit(solution)/shard_map/ppermute | solution.py:11
  95.1 13.4 %collective-permute-start.15 = (f32[896,224]{0,1:T(8,128)S(1)}, f32[896,224]{0,1:T(8,128)S(1)}, u32[]{:S(2)}, u32[]{:S(2)}) collective-permute-start(f32[896,224]{0,1:T(8,128)S(1)} %maximum_select_fusion.1), channel_id=1, source_target_pairs={{0,1},{1,0},{2,3},{3,2},{4,5},{5,4},{6,7},{7,6},{8,9},{9,8},{10,11... | collective-permute-start | bytes 2408456 | tf_op jit(solution)/shard_map/ppermute | solution.py:91
  108.6 20.5 %collective-permute-start.22 = (bf16[224,2048]{1,0:T(8,128)(2,1)S(1)}, bf16[224,2048]{1,0:T(8,128)(2,1)S(1)}, u32[]{:S(2)}, u32[]{:S(2)}) collective-permute-start(bf16[224,2048]{1,0:T(8,128)(2,1)S(1)} %pad_maximum_fusion.4), channel_id=1, source_target_pairs={{8,0},{12,4},{16,8},{20,12},{24,16},{28,20},{9,1},{13,5},{17,9},{2... | collective-permute-start | bytes 2752520 | tf_op jit(solution)/shard_map/ppermute | solution.py:11
  112.4 8.5 %collective-permute-start.20 = (bf16[112,2048]{1,0:T(8,128)(2,1)S(1)}, bf16[112,2048]{1,0:T(8,128)(2,1)S(1)}, u32[]{:S(2)}, u32[]{:S(2)}) collective-permute-start(bf16[112,2048]{1,0:T(8,128)(2,1)S(1)} %broadcast_select_fusion.6), channel_id=1, source_target_pairs={{4,0},{12,8},{20,16},{28,24},{0,4},{8,12},{16,20},{24,28},{5,1},{1... | collective-permute-start | bytes 1376264 | tf_op jit(solution)/shard_map/ppermute | solution.py:11
  115.8 13.4 %collective-permute-start.19 = (f32[896,224]{0,1:T(8,128)S(1)}, f32[896,224]{0,1:T(8,128)S(1)}, u32[]{:S(2)}, u32[]{:S(2)}) collective-permute-start(f32[896,224]{0,1:T(8,128)S(1)} %maximum_select_fusion.2), channel_id=1, source_target_pairs={{0,1},{1,0},{2,3},{3,2},{4,5},{5,4},{6,7},{7,6},{8,9},{9,8},{10,11... | collective-permute-start | bytes 2408456 | tf_op jit(solution)/shard_map/ppermute | solution.py:91
  129.3 18.9 %collective-permute-start.26 = (bf16[224,2048]{1,0:T(8,128)(2,1)S(1)}, bf16[224,2048]{1,0:T(8,128)(2,1)S(1)}, u32[]{:S(2)}, u32[]{:S(2)}) collective-permute-start(bf16[224,2048]{1,0:T(8,128)(2,1)S(1)} %pad_maximum_fusion.5), channel_id=1, source_target_pairs={{8,0},{12,4},{16,8},{20,12},{24,16},{28,20},{9,1},{13,5},{17,9},{2... | collective-permute-start | bytes 2752520 | tf_op jit(solution)/shard_map/ppermute | solution.py:11
  132.8 8.5 %collective-permute-start.24 = (bf16[112,2048]{1,0:T(8,128)(2,1)S(1)}, bf16[112,2048]{1,0:T(8,128)(2,1)S(1)}, u32[]{:S(2)}, u32[]{:S(2)}) collective-permute-start(bf16[112,2048]{1,0:T(8,128)(2,1)S(1)} %broadcast_select_fusion.4), channel_id=1, source_target_pairs={{4,0},{12,8},{20,16},{28,24},{0,4},{8,12},{16,20},{24,28},{5,1},{1... | collective-permute-start | bytes 1376264 | tf_op jit(solution)/shard_map/ppermute | solution.py:11
  136.2 12.0 %collective-permute-start.23 = (f32[896,224]{0,1:T(8,128)S(1)}, f32[896,224]{0,1:T(8,128)S(1)}, u32[]{:S(2)}, u32[]{:S(2)}) collective-permute-start(f32[896,224]{0,1:T(8,128)S(1)} %maximum_select_fusion.3), channel_id=1, source_target_pairs={{0,1},{1,0},{2,3},{3,2},{4,5},{5,4},{6,7},{7,6},{8,9},{9,8},{10,11... | collective-permute-start | bytes 2408456 | tf_op jit(solution)/shard_map/ppermute | solution.py:91
  148.3 17.5 %collective-permute-start.30 = (bf16[224,2048]{1,0:T(8,128)(2,1)S(1)}, bf16[224,2048]{1,0:T(8,128)(2,1)S(1)}, u32[]{:S(2)}, u32[]{:S(2)}) collective-permute-start(bf16[224,2048]{1,0:T(8,128)(2,1)S(1)} %pad_maximum_fusion.6), channel_id=1, source_target_pairs={{8,0},{12,4},{16,8},{20,12},{24,16},{28,20},{9,1},{13,5},{17,9},{2... | collective-permute-start | bytes 2752520 | tf_op jit(solution)/shard_map/ppermute | solution.py:11
  149.8 9.3 %collective-permute-start.29 = (f32[896,112]{0,1:T(8,128)S(1)}, f32[896,112]{0,1:T(8,128)S(1)}, u32[]{:S(2)}, u32[]{:S(2)}) collective-permute-start(f32[896,112]{0,1:T(8,128)S(1)} %select_add_fusion.4), channel_id=1, source_target_pairs={{0,2},{1,3},{2,0},{3,1},{4,6},{5,7},{6,4},{7,5},{8,10},{9,11},{10,... | collective-permute-start | bytes 1204232 | tf_op jit(solution)/shard_map/ppermute | solution.py:103
  153.3 8.5 %collective-permute-start.28 = (bf16[112,2048]{1,0:T(8,128)(2,1)S(1)}, bf16[112,2048]{1,0:T(8,128)(2,1)S(1)}, u32[]{:S(2)}, u32[]{:S(2)}) collective-permute-start(bf16[112,2048]{1,0:T(8,128)(2,1)S(1)} %broadcast_select_fusion.2), channel_id=1, source_target_pairs={{4,0},{12,8},{20,16},{28,24},{0,4},{8,12},{16,20},{24,28},{5,1},{1... | collective-permute-start | bytes 1376264 | tf_op jit(solution)/shard_map/ppermute | solution.py:11
  156.7 9.3 %collective-permute-start.27 = (f32[896,224]{0,1:T(8,128)S(1)}, f32[896,224]{0,1:T(8,128)S(1)}, u32[]{:S(2)}, u32[]{:S(2)}) collective-permute-start(f32[896,224]{0,1:T(8,128)S(1)} %maximum_select_fusion.4), channel_id=1, source_target_pairs={{0,1},{1,0},{2,3},{3,2},{4,5},{5,4},{6,7},{7,6},{8,9},{9,8},{10,11... | collective-permute-start | bytes 2408456 | tf_op jit(solution)/shard_map/ppermute | solution.py:91
  168.6 8.5 %collective-permute-start.32 = (bf16[112,2048]{1,0:T(8,128)(2,1)S(1)}, bf16[112,2048]{1,0:T(8,128)(2,1)S(1)}, u32[]{:S(2)}, u32[]{:S(2)}) collective-permute-start(bf16[112,2048]{1,0:T(8,128)(2,1)S(1)} %get-tuple-element.239), channel_id=1, source_target_pairs={{4,0},{12,8},{20,16},{28,24},{0,4},{8,12},{16,20},{24,28},{5,1},{1... | collective-permute-start | bytes 1376264 | tf_op jit(solution)/shard_map/ppermute | solution.py:11
  172.1 14.9 %collective-permute-start.31 = (f32[896,224]{0,1:T(8,128)S(1)}, f32[896,224]{0,1:T(8,128)S(1)}, u32[]{:S(2)}, u32[]{:S(2)}) collective-permute-start(f32[896,224]{0,1:T(8,128)S(1)} %maximum_select_fusion.5), channel_id=1, source_target_pairs={{0,1},{1,0},{2,3},{3,2},{4,5},{5,4},{6,7},{7,6},{8,9},{9,8},{10,11... | collective-permute-start | bytes 2408456 | tf_op jit(solution)/shard_map/ppermute | solution.py:91
  172.2 14.8 %collective-permute-start.34 = (bf16[112,2048]{1,0:T(8,128)(2,1)S(1)}, bf16[112,2048]{1,0:T(8,128)(2,1)S(1)}, u32[]{:S(2)}, u32[]{:S(2)}) collective-permute-start(bf16[112,2048]{1,0:T(8,128)(2,1)S(1)} %broadcast_select_fusion.1), channel_id=1, source_target_pairs={{8,0},{12,4},{16,8},{20,12},{24,16},{28,20},{9,1},{13,5},{17,9},{2... | collective-permute-start | bytes 1376264 | tf_op jit(solution)/shard_map/ppermute | solution.py:11
  189.3 15.1 %collective-permute-start.35 = (f32[896,224]{0,1:T(8,128)S(1)}, f32[896,224]{0,1:T(8,128)S(1)}, u32[]{:S(2)}, u32[]{:S(2)}) collective-permute-start(f32[896,224]{0,1:T(8,128)S(1)} %maximum_select_fusion.6), channel_id=1, source_target_pairs={{0,1},{1,0},{2,3},{3,2},{4,5},{5,4},{6,7},{7,6},{8,9},{9,8},{10,11... | collective-permute-start | bytes 2408456 | tf_op jit(solution)/shard_map/ppermute | solution.py:91
  189.6 11.8 %collective-permute-start.36 = (f32[896,112]{0,1:T(8,128)S(1)}, f32[896,112]{0,1:T(8,128)S(1)}, u32[]{:S(2)}, u32[]{:S(2)}) collective-permute-start(f32[896,112]{0,1:T(8,128)S(1)} %select_add_fusion.2), channel_id=1, source_target_pairs={{0,2},{1,3},{2,0},{3,1},{4,6},{5,7},{6,4},{7,5},{8,10},{9,11},{10,... | collective-permute-start | bytes 1204232 | tf_op jit(solution)/shard_map/ppermute | solution.py:103
  189.7 14.7 %collective-permute-start.37 = (bf16[112,2048]{1,0:T(8,128)(2,1)S(1)}, bf16[112,2048]{1,0:T(8,128)(2,1)S(1)}, u32[]{:S(2)}, u32[]{:S(2)}) collective-permute-start(bf16[112,2048]{1,0:T(8,128)(2,1)S(1)} %broadcast_select_fusion), channel_id=1, source_target_pairs={{8,0},{12,4},{16,8},{20,12},{24,16},{28,20},{9,1},{13,5},{17,9},{2... | collective-permute-start | bytes 1376264 | tf_op jit(solution)/shard_map/ppermute | solution.py:11
  207.0 12.1 %collective-permute-start.39 = (f32[896,112]{0,1:T(8,128)S(1)}, f32[896,112]{0,1:T(8,128)S(1)}, u32[]{:S(2)}, u32[]{:S(2)}) collective-permute-start(f32[896,112]{0,1:T(8,128)S(1)} %select_add_fusion.1), channel_id=1, source_target_pairs={{0,2},{1,3},{2,0},{3,1},{4,6},{5,7},{6,4},{7,5},{8,10},{9,11},{10,... | collective-permute-start | bytes 1204232 | tf_op jit(solution)/shard_map/ppermute | solution.py:103
  209.3 18.1 %collective-permute-start.40 = (f32[896,112]{0,1:T(8,128)S(1)}, f32[896,112]{0,1:T(8,128)S(1)}, u32[]{:S(2)}, u32[]{:S(2)}) collective-permute-start(f32[896,112]{0,1:T(8,128)S(1)} %select_add_fusion), channel_id=1, source_target_pairs={{0,2},{1,3},{2,0},{3,1},{4,6},{5,7},{6,4},{7,5},{8,10},{9,11},{10,... | collective-permute-start | bytes 1204232 | tf_op jit(solution)/shard_map/ppermute | solution.py:103
  (27 other events, 286.3 us)

commit v10 on v9

--- a/solution.py
+++ b/solution.py
@@ -57,10 +57,13 @@
 
     rows = dosages.shape[0]
     step = rows // CHUNKS
-    first_piece = standard_rows(dosages[:step])
-    rest = standard_rows(dosages[step:])
+    sizes = [step + 16] + [step] * (CHUNKS - 2) + [step - 16]
+    offsets = [sum(sizes[:c]) for c in range(CHUNKS)]
+    first_piece = standard_rows(dosages[:sizes[0]])
+    rest = standard_rows(dosages[sizes[0]:])
     own_block = jnp.concatenate([first_piece, rest], axis=0)
-    pieces = [first_piece] + [rest[(c - 1) * step:c * step] for c in range(1, CHUNKS)]
+    pieces = [first_piece] + [
+        rest[offsets[c] - sizes[0]:offsets[c] - sizes[0] + sizes[c]] for c in range(1, CHUNKS)]
 
     odd = list(range(1, count, 2))
     even = list(range(0, count, 2))
@@ -84,7 +87,8 @@
             state["three"][c],
         ], axis=0)
         gram = jnp.einsum("ab,cb->ac", own_block, blocks, preferred_element_type=jnp.float32)
-        tiles = [gram[:, k * step:(k + 1) * step] for k in range(BAND + 1)]
+        size = sizes[c]
+        tiles = [gram[:, k * size:(k + 1) * size] for k in range(BAND + 1)]
         state["tiles"][c] = tiles
         payload = jnp.where(even_me, jnp.concatenate([tiles[1], tiles[3]], axis=1),
                             jnp.concatenate([tiles[0], tiles[2]], axis=1))
@@ -98,8 +102,9 @@
 
     def second_level(c):
         got = state["first"][c]
-        mine = jnp.where(low, got[:, :step], got[:, step:])
-        onward = jnp.where(low, got[:, step:], got[:, :step])
+        size = sizes[c]
+        mine = jnp.where(low, got[:, :size], got[:, size:])
+        onward = jnp.where(low, got[:, size:], got[:, :size])
         last = lax.ppermute(pick(c, 2, 3, 0, 1) + onward, "samp", across)
         state["results"][c] = pick(c, 0, 1, 2, 3) + mine + last
 
@@ -111,17 +116,20 @@
             sent = moved(joined([pieces[new] if new is not None else None,
                                  state["one"][third] if third is not None else None]), z_down)
             if new is not None:
-                state["two"][new] = sent[:step]
+                state["two"][new] = sent[:sizes[new]]
             if third is not None:
-                state["three"][third] = sent[-step:]
+                state["three"][third] = sent[-sizes[third]:]
         if new is not None or second is not None:
             if new is not None and second is not None:
-                payload = jnp.where(even_snp, state["two"][second], pieces[new])
+                height = max(sizes[new], sizes[second])
+                padded = [jnp.pad(x, ((0, height - x.shape[0]), (0, 0))) for x in (state["two"][second], pieces[new])]
+                payload = jnp.where(even_snp, padded[0], padded[1])
             else:
                 payload = pieces[new] if new is not None else state["two"][second]
             state["swapped"][t] = moved(payload, swap)
         if second is not None:
-            state["one"][second] = jnp.where(even_snp, state["swapped"][second], state["swapped"][t])
+            size = sizes[second]
+            state["one"][second] = jnp.where(even_snp, state["swapped"][second][:size], state["swapped"][t][:size])
         if 0 <= t - 3 < CHUNKS:
             finish(t - 3)
         if 0 <= t - 4 < CHUNKS - 1:

time: 232 us -> 230 us (level)
  waiting for transfers between devices: 142 us -> 137 us
    ppermute x19, waiting for transfers between devices: 102 us -> 94.6 us  [moved(): return lax.ppermute(value, 'snp', pairs)]
    ppermute x8, waiting for transfers between devices: 36.7 us -> 39.6 us  [second_level(): last = lax.ppermute(pick(c, 2, 3, 0, 1) + onward, 'samp', across)]
    ppermute x8, starting transfers between devices: 15.6 us -> 18.1 us  [second_level(): last = lax.ppermute(pick(c, 2, 3, 0, 1) + onward, 'samp', across)]
    slice x15 -> x18, local copies, waits for them, and re-layouts: 3.83 us -> 4.65 us  [the longest x6 1.36 us: local(): state['two'][new] = sent[:sizes[new]]]
  transfers between devices with their start and end apart: 41 -> 41, of which waited for: 30 -> 27; matrix products, arithmetic and copies ran while one was open for 12% -> 12% of each run, Pallas kernels for 0% -> 0%
where the time goes in v10:
time: 230 us
  waiting for transfers between devices  137 us (60%)
  starting transfers between devices  46.5 us (20%)
  other arithmetic  18.7 us (8%)
  matrix products  16.8 us (7%)
  local copies, waits for them, and re-layouts  9.47 us (4%)
    ppermute x19, waiting for transfers between devices, moved(): return lax.ppermute(value, 'snp', pairs)  94.6 us
    ppermute x8, waiting for transfers between devices, second_level(): last = lax.ppermute(pick(c, 2, 3, 0, 1) + onward, 'samp', across)  39.6 us
    ppermute x19, starting transfers between devices, moved(): return lax.ppermute(value, 'snp', pairs)  22.7 us
    ppermute x8, starting transfers between devices, second_level(): last = lax.ppermute(pick(c, 2, 3, 0, 1) + onward, 'samp', across)  18.1 us
    dot_general x8, matrix products, finish(): jnp.einsum('ab,cb->ac', own_block, blocks, preferred_element_type=jnp.flo...  16.8 us
    ppermute x6, starting transfers between devices, standard_rows(): lax.ppermute(moments, 'samp', [(j, j ^ i) for j in range(groups)])  5.12 us
    reduce_sum x2, other arithmetic, local_moments(): return (jnp.sum(values, axis=1), jnp.sum(values * values, axis=1))  5.07 us
    convert_element_type x2, other arithmetic, standardize(): ((values - mean[:, None]) * lax.rsqrt(variance + 1e-05)[:, None]).astype(...  4.84 us
  transfers between devices with their start and end apart: 41, of which 27 were waited for; matrix products, arithmetic and copies ran while one was open for 12% of the time, Pallas kernels for 0%

profile of v10, /device:TPU:0, one launch (start us, length us, event | category | flops | bytes accessed | tf_op | source)
XLA Modules:
  0.0 229.8 jit_solution(12294136412628512743)
XLA Ops:
  0.0 3.7 %slice_reduce_fusion = (f32[768]{0:T(1024)S(1)}, f32[768]{0:T(1024)S(1)}) fusion(f32[896,2048]{1,0:T(8,128)} %param.1), kind=kLoop, calls=%fused_computation.2 | loop fusion | flops 4717056 | bytes 6297600 | tf_op jit(solution)/shard_map/reduce_sum | solution.py:21
  3.7 2.4 %collective-permute-start.3 = (f32[2,768]{1,0:T(2,128)S(1)}, f32[2,768]{1,0:T(2,128)S(1)}, u32[]{:S(2)}, u32[]{:S(2)}) collective-permute-start(f32[2,768]{1,0:T(2,128)S(1)} %pad_maximum_fusion.7), channel_id=1, source_target_pairs={{0,3},{1,2},{2,1},{3,0},{4,7},{5,6},{6,5},{7,4},{8,11},{9,10},{10,... | collective-permute-start | bytes 18440 | tf_op jit(solution)/shard_map/ppermute | solution.py:55
  17.7 3.4 %multiply_convert_fusion = bf16[768,2048]{1,0:T(8,128)(2,1)S(1)} fusion(f32[896,2048]{1,0:T(8,128)} %param.1, f32[768]{0:T(1024)S(1)} %add_rsqrt_fusion, f32[768]{0:T(1024)S(1)} %get-tuple-element.263), kind=kLoop, calls=%fused_computation | loop fusion | flops 4718592 | bytes 9443328 | tf_op jit(solution)/shard_map/convert_element_type | solution.py:17
  22.5 5.1 %collective-permute-done.6 = bf16[128,2048]{1,0:T(8,128)(2,1)S(1)} collective-permute-done((bf16[128,2048]{1,0:T(8,128)(2,1)S(1)}, bf16[128,2048]{1,0:T(8,128)(2,1)S(1)}, u32[]{:S(2)}, u32[]{:S(2)}) %collective-permute-start.6) | collective-permute-done | bytes 524320 | tf_op jit(solution)/shard_map/ppermute | solution.py:11
  27.5 3.1 %collective-permute-done.7 = bf16[128,2048]{1,0:T(8,128)(2,1)S(1)} collective-permute-done((bf16[128,2048]{1,0:T(8,128)(2,1)S(1)}, bf16[128,2048]{1,0:T(8,128)(2,1)S(1)}, u32[]{:S(2)}, u32[]{:S(2)}) %collective-permute-start.7) | collective-permute-done | bytes 524320 | tf_op jit(solution)/shard_map/ppermute | solution.py:11
  32.7 9.8 %collective-permute-done.8 = bf16[128,2048]{1,0:T(8,128)(2,1)S(1)} collective-permute-done((bf16[128,2048]{1,0:T(8,128)(2,1)S(1)}, bf16[128,2048]{1,0:T(8,128)(2,1)S(1)}, u32[]{:S(2)}, u32[]{:S(2)}) %collective-permute-start.8) | collective-permute-done | bytes 524320 | tf_op jit(solution)/shard_map/ppermute | solution.py:11
  48.0 8.9 %collective-permute-done.10 = bf16[112,2048]{1,0:T(8,128)(2,1)} collective-permute-done((bf16[112,2048]{1,0:T(8,128)(2,1)}, bf16[112,2048]{1,0:T(8,128)(2,1)}, u32[]{:S(2)}, u32[]{:S(2)}) %collective-permute-start.10) | collective-permute-done | bytes 458784 | tf_op jit(solution)/shard_map/ppermute | solution.py:11
  57.9 9.9 %collective-permute-done.11 = bf16[240,2048]{1,0:T(8,128)(2,1)} collective-permute-done((bf16[240,2048]{1,0:T(8,128)(2,1)}, bf16[240,2048]{1,0:T(8,128)(2,1)}, u32[]{:S(2)}, u32[]{:S(2)}) %collective-permute-start.11) | collective-permute-done | bytes 983072 | tf_op jit(solution)/shard_map/ppermute | solution.py:11
  71.9 2.4 %fusion = f32[896,512]{0,1:T(8,128)S(1)} fusion(bf16[128,2048]{1,0:T(8,128)(2,1)S(1)} %slice.327, bf16[128,2048]{1,0:T(8,128)(2,1)S(1)} %copy-done.12, bf16[128,2048]{1,0:T(8,128)(2,1)S(1)} %copy-done.7, bf16[128,2048]{1,0:T(8,128)(2,1)S(1)} %copy-done.14, bf16[768,2048]{1,0:T(8,128)(2,1)S(1)} %multiply_convert_fusion), kind=kOutput, calls=%fused_computation.4 | convolution fusion | flops 1894776832 | bytes 7077888 | tf_op jit(solution)/shard_map/ab,cb->ac/dot_general | solution.py:89
  74.6 5.3 %collective-permute-done.13 = bf16[112,2048]{1,0:T(8,128)(2,1)S(1)} collective-permute-done((bf16[112,2048]{1,0:T(8,128)(2,1)S(1)}, bf16[112,2048]{1,0:T(8,128)(2,1)S(1)}, u32[]{:S(2)}, u32[]{:S(2)}) %collective-permute-start.13) | collective-permute-done | bytes 458784 | tf_op jit(solution)/shard_map/ppermute | solution.py:11
  81.0 9.2 %collective-permute-done.14 = bf16[224,2048]{1,0:T(8,128)(2,1)S(1)} collective-permute-done((bf16[224,2048]{1,0:T(8,128)(2,1)S(1)}, bf16[224,2048]{1,0:T(8,128)(2,1)S(1)}, u32[]{:S(2)}, u32[]{:S(2)}) %collective-permute-start.14) | collective-permute-done | bytes 917536 | tf_op jit(solution)/shard_map/ppermute | solution.py:11
  92.0 2.3 %collective-permute-start.17 = (f32[896,128]{0,1:T(8,128)S(1)}, f32[896,128]{0,1:T(8,128)S(1)}, u32[]{:S(2)}, u32[]{:S(2)}) collective-permute-start(f32[896,128]{0,1:T(8,128)S(1)} %select_add_fusion), channel_id=1, source_target_pairs={{0,2},{1,3},{2,0},{3,1},{4,6},{5,7},{6,4},{7,5},{8,10},{9,11},{10,... | collective-permute-start | bytes 1376264 | tf_op jit(solution)/shard_map/ppermute | solution.py:108
  95.7 2.1 fusion.8
  98.1 4.8 %collective-permute-done.16 = bf16[112,2048]{1,0:T(8,128)(2,1)S(1)} collective-permute-done((bf16[112,2048]{1,0:T(8,128)(2,1)S(1)}, bf16[112,2048]{1,0:T(8,128)(2,1)S(1)}, u32[]{:S(2)}, u32[]{:S(2)}) %collective-permute-start.16) | collective-permute-done | bytes 458784 | tf_op jit(solution)/shard_map/ppermute | solution.py:11
  103.2 7.5 %collective-permute-done.18 = bf16[224,2048]{1,0:T(8,128)(2,1)S(1)} collective-permute-done((bf16[224,2048]{1,0:T(8,128)(2,1)S(1)}, bf16[224,2048]{1,0:T(8,128)(2,1)S(1)}, u32[]{:S(2)}, u32[]{:S(2)}) %collective-permute-start.18) | collective-permute-done | bytes 917536 | tf_op jit(solution)/shard_map/ppermute | solution.py:11
  112.7 2.3 %collective-permute-start.21 = (f32[896,112]{0,1:T(8,128)S(1)}, f32[896,112]{0,1:T(8,128)S(1)}, u32[]{:S(2)}, u32[]{:S(2)}) collective-permute-start(f32[896,112]{0,1:T(8,128)S(1)} %select_add_fusion.6), channel_id=1, source_target_pairs={{0,2},{1,3},{2,0},{3,1},{4,6},{5,7},{6,4},{7,5},{8,10},{9,11},{10,... | collective-permute-start | bytes 1204232 | tf_op jit(solution)/shard_map/ppermute | solution.py:108
  121.0 2.6 %collective-permute-done.20 = bf16[112,2048]{1,0:T(8,128)(2,1)S(1)} collective-permute-done((bf16[112,2048]{1,0:T(8,128)(2,1)S(1)}, bf16[112,2048]{1,0:T(8,128)(2,1)S(1)}, u32[]{:S(2)}, u32[]{:S(2)}) %collective-permute-start.20) | collective-permute-done | bytes 458784 | tf_op jit(solution)/shard_map/ppermute | solution.py:11
  123.7 7.7 %collective-permute-done.22 = bf16[224,2048]{1,0:T(8,128)(2,1)S(1)} collective-permute-done((bf16[224,2048]{1,0:T(8,128)(2,1)S(1)}, bf16[224,2048]{1,0:T(8,128)(2,1)S(1)}, u32[]{:S(2)}, u32[]{:S(2)}) %collective-permute-start.22) | collective-permute-done | bytes 917536 | tf_op jit(solution)/shard_map/ppermute | solution.py:11
  133.0 2.3 %collective-permute-start.25 = (f32[896,112]{0,1:T(8,128)S(1)}, f32[896,112]{0,1:T(8,128)S(1)}, u32[]{:S(2)}, u32[]{:S(2)}) collective-permute-start(f32[896,112]{0,1:T(8,128)S(1)} %select_add_fusion.5), channel_id=1, source_target_pairs={{0,2},{1,3},{2,0},{3,1},{4,6},{5,7},{6,4},{7,5},{8,10},{9,11},{10,... | collective-permute-start | bytes 1204232 | tf_op jit(solution)/shard_map/ppermute | solution.py:108
  141.4 2.6 %collective-permute-done.24 = bf16[112,2048]{1,0:T(8,128)(2,1)S(1)} collective-permute-done((bf16[112,2048]{1,0:T(8,128)(2,1)S(1)}, bf16[112,2048]{1,0:T(8,128)(2,1)S(1)}, u32[]{:S(2)}, u32[]{:S(2)}) %collective-permute-start.24) | collective-permute-done | bytes 458784 | tf_op jit(solution)/shard_map/ppermute | solution.py:11
  144.0 6.9 %collective-permute-done.26 = bf16[224,2048]{1,0:T(8,128)(2,1)S(1)} collective-permute-done((bf16[224,2048]{1,0:T(8,128)(2,1)S(1)}, bf16[224,2048]{1,0:T(8,128)(2,1)S(1)}, u32[]{:S(2)}, u32[]{:S(2)}) %collective-permute-start.26) | collective-permute-done | bytes 917536 | tf_op jit(solution)/shard_map/ppermute | solution.py:11
  152.5 3.3 %collective-permute-start.29 = (f32[896,112]{0,1:T(8,128)S(1)}, f32[896,112]{0,1:T(8,128)S(1)}, u32[]{:S(2)}, u32[]{:S(2)}) collective-permute-start(f32[896,112]{0,1:T(8,128)S(1)} %select_add_fusion.4), channel_id=1, source_target_pairs={{0,2},{1,3},{2,0},{3,1},{4,6},{5,7},{6,4},{7,5},{8,10},{9,11},{10,... | collective-permute-start | bytes 1204232 | tf_op jit(solution)/shard_map/ppermute | solution.py:108
  161.8 2.7 %collective-permute-done.28 = bf16[112,2048]{1,0:T(8,128)(2,1)S(1)} collective-permute-done((bf16[112,2048]{1,0:T(8,128)(2,1)S(1)}, bf16[112,2048]{1,0:T(8,128)(2,1)S(1)}, u32[]{:S(2)}, u32[]{:S(2)}) %collective-permute-start.28) | collective-permute-done | bytes 458784 | tf_op jit(solution)/shard_map/ppermute | solution.py:11
  164.5 2.7 %collective-permute-done.30 = bf16[208,2048]{1,0:T(8,128)(2,1)S(1)} collective-permute-done((bf16[208,2048]{1,0:T(8,128)(2,1)S(1)}, bf16[208,2048]{1,0:T(8,128)(2,1)S(1)}, u32[]{:S(2)}, u32[]{:S(2)}) %collective-permute-start.30) | collective-permute-done | bytes 852000 | tf_op jit(solution)/shard_map/ppermute | solution.py:11
  170.4 3.9 %collective-permute-start.33 = (f32[896,112]{0,1:T(8,128)S(1)}, f32[896,112]{0,1:T(8,128)S(1)}, u32[]{:S(2)}, u32[]{:S(2)}) collective-permute-start(f32[896,112]{0,1:T(8,128)S(1)} %select_add_fusion.3), channel_id=1, source_target_pairs={{0,2},{1,3},{2,0},{3,1},{4,6},{5,7},{6,4},{7,5},{8,10},{9,11},{10,... | collective-permute-start | bytes 1204232 | tf_op jit(solution)/shard_map/ppermute | solution.py:108
  175.8 8.4 %collective-permute-done.33 = f32[896,112]{0,1:T(8,128)S(1)} collective-permute-done((f32[896,112]{0,1:T(8,128)S(1)}, f32[896,112]{0,1:T(8,128)S(1)}, u32[]{:S(2)}, u32[]{:S(2)}) %collective-permute-start.33) | collective-permute-done | bytes 401440 | tf_op jit(solution)/shard_map/ppermute | solution.py:108
  184.3 4.4 %collective-permute-done.34 = bf16[112,2048]{1,0:T(8,128)(2,1)S(1)} collective-permute-done((bf16[112,2048]{1,0:T(8,128)(2,1)S(1)}, bf16[112,2048]{1,0:T(8,128)(2,1)S(1)}, u32[]{:S(2)}, u32[]{:S(2)}) %collective-permute-start.34) | collective-permute-done | bytes 458784 | tf_op jit(solution)/shard_map/ppermute | solution.py:11
  188.7 2.1 fusion.48
  193.0 10.1 %collective-permute-done.36 = f32[896,112]{0,1:T(8,128)S(1)} collective-permute-done((f32[896,112]{0,1:T(8,128)S(1)}, f32[896,112]{0,1:T(8,128)S(1)}, u32[]{:S(2)}, u32[]{:S(2)}) %collective-permute-start.36) | collective-permute-done | bytes 401440 | tf_op jit(solution)/shard_map/ppermute | solution.py:108
  210.9 8.3 %collective-permute-done.39 = f32[896,112]{0,1:T(8,128)S(1)} collective-permute-done((f32[896,112]{0,1:T(8,128)S(1)}, f32[896,112]{0,1:T(8,128)S(1)}, u32[]{:S(2)}, u32[]{:S(2)}) %collective-permute-start.39) | collective-permute-done | bytes 401440 | tf_op jit(solution)/shard_map/ppermute | solution.py:108
  219.4 6.8 %collective-permute-done.40 = f32[896,96]{0,1:T(8,128)S(1)} collective-permute-done((f32[896,96]{0,1:T(8,128)S(1)}, f32[896,96]{0,1:T(8,128)S(1)}, u32[]{:S(2)}, u32[]{:S(2)}) %collective-permute-start.40) | collective-permute-done | bytes 344096 | tf_op jit(solution)/shard_map/ppermute | solution.py:108
  226.8 3.0 %copy.2 = f32[896,896]{1,0:T(8,128)} copy(f32[896,896]{0,1:T(8,128)S(1)} %broadcast_multiply_fusion) | data formatting | bytes 6422528 | tf_op jit(solution)/shard_map/div | solution.py:144
  (179 shorter events, 69.1 us)
Async XLA Ops:
  3.7 13.9 %collective-permute-start.3 = (f32[2,768]{1,0:T(2,128)S(1)}, f32[2,768]{1,0:T(2,128)S(1)}, u32[]{:S(2)}, u32[]{:S(2)}) collective-permute-start(f32[2,768]{1,0:T(2,128)S(1)} %pad_maximum_fusion.7), channel_id=1, source_target_pairs={{0,3},{1,2},{2,1},{3,0},{4,7},{5,6},{6,5},{7,4},{8,11},{9,10},{10,... | collective-permute-start | bytes 18440 | tf_op jit(solution)/shard_map/ppermute | solution.py:55
  6.2 11.5 %collective-permute-start.4 = (f32[2,768]{1,0:T(2,128)S(1)}, f32[2,768]{1,0:T(2,128)S(1)}, u32[]{:S(2)}, u32[]{:S(2)}) collective-permute-start(f32[2,768]{1,0:T(2,128)S(1)} %pad_maximum_fusion.7), channel_id=1, source_target_pairs={{0,2},{1,3},{2,0},{3,1},{4,6},{5,7},{6,4},{7,5},{8,10},{9,11},{10,... | collective-permute-start | bytes 18440 | tf_op jit(solution)/shard_map/ppermute | solution.py:55
  14.7 12.8 %collective-permute-start.6 = (bf16[128,2048]{1,0:T(8,128)(2,1)S(1)}, bf16[128,2048]{1,0:T(8,128)(2,1)S(1)}, u32[]{:S(2)}, u32[]{:S(2)}) collective-permute-start(bf16[128,2048]{1,0:T(8,128)(2,1)S(1)} %multiply_convert_fusion.1), channel_id=1, source_target_pairs={{4,0},{12,8},{20,16},{28,24},{0,4},{8,12},{16,20},{24,28},{5,1},{1... | collective-permute-start | bytes 1572872 | tf_op jit(solution)/shard_map/ppermute | solution.py:11
  16.3 14.4 %collective-permute-start.7 = (bf16[128,2048]{1,0:T(8,128)(2,1)S(1)}, bf16[128,2048]{1,0:T(8,128)(2,1)S(1)}, u32[]{:S(2)}, u32[]{:S(2)}) collective-permute-start(bf16[128,2048]{1,0:T(8,128)(2,1)S(1)} %multiply_convert_fusion.1), channel_id=1, source_target_pairs={{8,0},{12,4},{16,8},{20,12},{24,16},{28,20},{9,1},{13,5},{17,9},{2... | collective-permute-start | bytes 1572872 | tf_op jit(solution)/shard_map/ppermute | solution.py:11
  30.8 11.6 %collective-permute-start.8 = (bf16[128,2048]{1,0:T(8,128)(2,1)S(1)}, bf16[128,2048]{1,0:T(8,128)(2,1)S(1)}, u32[]{:S(2)}, u32[]{:S(2)}) collective-permute-start(bf16[128,2048]{1,0:T(8,128)(2,1)S(1)} %pad_select_fusion), channel_id=1, source_target_pairs={{4,0},{12,8},{20,16},{28,24},{0,4},{8,12},{16,20},{24,28},{5,1},{1... | collective-permute-start | bytes 1572872 | tf_op jit(solution)/shard_map/ppermute | solution.py:11
  31.4 11.9 %collective-permute-start.9 = (bf16[112,2048]{1,0:T(8,128)(2,1)S(1)}, bf16[112,2048]{1,0:T(8,128)(2,1)S(1)}, u32[]{:S(2)}, u32[]{:S(2)}) collective-permute-start(bf16[112,2048]{1,0:T(8,128)(2,1)S(1)} %get-tuple-element.134), channel_id=1, source_target_pairs={{8,0},{12,4},{16,8},{20,12},{24,16},{28,20},{9,1},{13,5},{17,9},{2... | collective-permute-start | bytes 1376264 | tf_op jit(solution)/shard_map/ppermute | solution.py:11
  45.1 22.7 %collective-permute-start.11 = (bf16[240,2048]{1,0:T(8,128)(2,1)}, bf16[240,2048]{1,0:T(8,128)(2,1)}, u32[]{:S(2)}, u32[]{:S(2)}) collective-permute-start(bf16[240,2048]{1,0:T(8,128)(2,1)} %pad_maximum_fusion.1), channel_id=1, source_target_pairs={{8,0},{12,4},{16,8},{20,12},{24,16},{28,20},{9,1},{13,5},{17,9},{2... | collective-permute-start | bytes 2949128 | tf_op jit(solution)/shard_map/ppermute | solution.py:11
  47.2 9.6 %collective-permute-start.10 = (bf16[112,2048]{1,0:T(8,128)(2,1)}, bf16[112,2048]{1,0:T(8,128)(2,1)}, u32[]{:S(2)}, u32[]{:S(2)}) collective-permute-start(bf16[112,2048]{1,0:T(8,128)(2,1)} %broadcast_select_fusion.10), channel_id=1, source_target_pairs={{4,0},{12,8},{20,16},{28,24},{0,4},{8,12},{16,20},{24,28},{5,1},{1... | collective-permute-start | bytes 1376264 | tf_op jit(solution)/shard_map/ppermute | solution.py:11
  70.0 20.2 %collective-permute-start.14 = (bf16[224,2048]{1,0:T(8,128)(2,1)S(1)}, bf16[224,2048]{1,0:T(8,128)(2,1)S(1)}, u32[]{:S(2)}, u32[]{:S(2)}) collective-permute-start(bf16[224,2048]{1,0:T(8,128)(2,1)S(1)} %pad_maximum_fusion.2), channel_id=1, source_target_pairs={{8,0},{12,4},{16,8},{20,12},{24,16},{28,20},{9,1},{13,5},{17,9},{2... | collective-permute-start | bytes 2752520 | tf_op jit(solution)/shard_map/ppermute | solution.py:11
  71.3 8.5 %collective-permute-start.13 = (bf16[112,2048]{1,0:T(8,128)(2,1)S(1)}, bf16[112,2048]{1,0:T(8,128)(2,1)S(1)}, u32[]{:S(2)}, u32[]{:S(2)}) collective-permute-start(bf16[112,2048]{1,0:T(8,128)(2,1)S(1)} %broadcast_select_fusion.9), channel_id=1, source_target_pairs={{4,0},{12,8},{20,16},{28,24},{0,4},{8,12},{16,20},{24,28},{5,1},{1... | collective-permute-start | bytes 1376264 | tf_op jit(solution)/shard_map/ppermute | solution.py:11
  74.5 15.7 %collective-permute-start.12 = (f32[896,256]{0,1:T(8,128)S(1)}, f32[896,256]{0,1:T(8,128)S(1)}, u32[]{:S(2)}, u32[]{:S(2)}) collective-permute-start(f32[896,256]{0,1:T(8,128)S(1)} %maximum_select_fusion), channel_id=1, source_target_pairs={{0,1},{1,0},{2,3},{3,2},{4,5},{5,4},{6,7},{7,6},{8,9},{9,8},{10,11... | collective-permute-start | bytes 2752520 | tf_op jit(solution)/shard_map/ppermute | solution.py:95
  90.4 20.3 %collective-permute-start.18 = (bf16[224,2048]{1,0:T(8,128)(2,1)S(1)}, bf16[224,2048]{1,0:T(8,128)(2,1)S(1)}, u32[]{:S(2)}, u32[]{:S(2)}) collective-permute-start(bf16[224,2048]{1,0:T(8,128)(2,1)S(1)} %pad_maximum_fusion.3), channel_id=1, source_target_pairs={{8,0},{12,4},{16,8},{20,12},{24,16},{28,20},{9,1},{13,5},{17,9},{2... | collective-permute-start | bytes 2752520 | tf_op jit(solution)/shard_map/ppermute | solution.py:11
  92.0 11.0 %collective-permute-start.17 = (f32[896,128]{0,1:T(8,128)S(1)}, f32[896,128]{0,1:T(8,128)S(1)}, u32[]{:S(2)}, u32[]{:S(2)}) collective-permute-start(f32[896,128]{0,1:T(8,128)S(1)} %select_add_fusion), channel_id=1, source_target_pairs={{0,2},{1,3},{2,0},{3,1},{4,6},{5,7},{6,4},{7,5},{8,10},{9,11},{10,... | collective-permute-start | bytes 1376264 | tf_op jit(solution)/shard_map/ppermute | solution.py:108
  94.4 8.5 %collective-permute-start.16 = (bf16[112,2048]{1,0:T(8,128)(2,1)S(1)}, bf16[112,2048]{1,0:T(8,128)(2,1)S(1)}, u32[]{:S(2)}, u32[]{:S(2)}) collective-permute-start(bf16[112,2048]{1,0:T(8,128)(2,1)S(1)} %broadcast_select_fusion.7), channel_id=1, source_target_pairs={{4,0},{12,8},{20,16},{28,24},{0,4},{8,12},{16,20},{24,28},{5,1},{1... | collective-permute-start | bytes 1376264 | tf_op jit(solution)/shard_map/ppermute | solution.py:11
  98.0 12.8 %collective-permute-start.15 = (f32[896,224]{0,1:T(8,128)S(1)}, f32[896,224]{0,1:T(8,128)S(1)}, u32[]{:S(2)}, u32[]{:S(2)}) collective-permute-start(f32[896,224]{0,1:T(8,128)S(1)} %maximum_select_fusion.1), channel_id=1, source_target_pairs={{0,1},{1,0},{2,3},{3,2},{4,5},{5,4},{6,7},{7,6},{8,9},{9,8},{10,11... | collective-permute-start | bytes 2408456 | tf_op jit(solution)/shard_map/ppermute | solution.py:95
  110.9 20.5 %collective-permute-start.22 = (bf16[224,2048]{1,0:T(8,128)(2,1)S(1)}, bf16[224,2048]{1,0:T(8,128)(2,1)S(1)}, u32[]{:S(2)}, u32[]{:S(2)}) collective-permute-start(bf16[224,2048]{1,0:T(8,128)(2,1)S(1)} %pad_maximum_fusion.4), channel_id=1, source_target_pairs={{8,0},{12,4},{16,8},{20,12},{24,16},{28,20},{9,1},{13,5},{17,9},{2... | collective-permute-start | bytes 2752520 | tf_op jit(solution)/shard_map/ppermute | solution.py:11
  115.1 8.5 %collective-permute-start.20 = (bf16[112,2048]{1,0:T(8,128)(2,1)S(1)}, bf16[112,2048]{1,0:T(8,128)(2,1)S(1)}, u32[]{:S(2)}, u32[]{:S(2)}) collective-permute-start(bf16[112,2048]{1,0:T(8,128)(2,1)S(1)} %broadcast_select_fusion.5), channel_id=1, source_target_pairs={{4,0},{12,8},{20,16},{28,24},{0,4},{8,12},{16,20},{24,28},{5,1},{1... | collective-permute-start | bytes 1376264 | tf_op jit(solution)/shard_map/ppermute | solution.py:11
  118.7 12.7 %collective-permute-start.19 = (f32[896,224]{0,1:T(8,128)S(1)}, f32[896,224]{0,1:T(8,128)S(1)}, u32[]{:S(2)}, u32[]{:S(2)}) collective-permute-start(f32[896,224]{0,1:T(8,128)S(1)} %maximum_select_fusion.2), channel_id=1, source_target_pairs={{0,1},{1,0},{2,3},{3,2},{4,5},{5,4},{6,7},{7,6},{8,9},{9,8},{10,11... | collective-permute-start | bytes 2408456 | tf_op jit(solution)/shard_map/ppermute | solution.py:95
  131.5 19.4 %collective-permute-start.26 = (bf16[224,2048]{1,0:T(8,128)(2,1)S(1)}, bf16[224,2048]{1,0:T(8,128)(2,1)S(1)}, u32[]{:S(2)}, u32[]{:S(2)}) collective-permute-start(bf16[224,2048]{1,0:T(8,128)(2,1)S(1)} %pad_maximum_fusion.5), channel_id=1, source_target_pairs={{8,0},{12,4},{16,8},{20,12},{24,16},{28,20},{9,1},{13,5},{17,9},{2... | collective-permute-start | bytes 2752520 | tf_op jit(solution)/shard_map/ppermute | solution.py:11
  135.4 8.5 %collective-permute-start.24 = (bf16[112,2048]{1,0:T(8,128)(2,1)S(1)}, bf16[112,2048]{1,0:T(8,128)(2,1)S(1)}, u32[]{:S(2)}, u32[]{:S(2)}) collective-permute-start(bf16[112,2048]{1,0:T(8,128)(2,1)S(1)} %broadcast_select_fusion.3), channel_id=1, source_target_pairs={{4,0},{12,8},{20,16},{28,24},{0,4},{8,12},{16,20},{24,28},{5,1},{1... | collective-permute-start | bytes 1376264 | tf_op jit(solution)/shard_map/ppermute | solution.py:11
  139.0 12.0 %collective-permute-start.23 = (f32[896,224]{0,1:T(8,128)S(1)}, f32[896,224]{0,1:T(8,128)S(1)}, u32[]{:S(2)}, u32[]{:S(2)}) collective-permute-start(f32[896,224]{0,1:T(8,128)S(1)} %maximum_select_fusion.3), channel_id=1, source_target_pairs={{0,1},{1,0},{2,3},{3,2},{4,5},{5,4},{6,7},{7,6},{8,9},{9,8},{10,11... | collective-permute-start | bytes 2408456 | tf_op jit(solution)/shard_map/ppermute | solution.py:95
  151.1 16.2 %collective-permute-start.30 = (bf16[208,2048]{1,0:T(8,128)(2,1)S(1)}, bf16[208,2048]{1,0:T(8,128)(2,1)S(1)}, u32[]{:S(2)}, u32[]{:S(2)}) collective-permute-start(bf16[208,2048]{1,0:T(8,128)(2,1)S(1)} %pad_maximum_fusion.6), channel_id=1, source_target_pairs={{8,0},{12,4},{16,8},{20,12},{24,16},{28,20},{9,1},{13,5},{17,9},{2... | collective-permute-start | bytes 2555912 | tf_op jit(solution)/shard_map/ppermute | solution.py:11
  152.5 9.1 %collective-permute-start.29 = (f32[896,112]{0,1:T(8,128)S(1)}, f32[896,112]{0,1:T(8,128)S(1)}, u32[]{:S(2)}, u32[]{:S(2)}) collective-permute-start(f32[896,112]{0,1:T(8,128)S(1)} %select_add_fusion.4), channel_id=1, source_target_pairs={{0,2},{1,3},{2,0},{3,1},{4,6},{5,7},{6,4},{7,5},{8,10},{9,11},{10,... | collective-permute-start | bytes 1204232 | tf_op jit(solution)/shard_map/ppermute | solution.py:108
  155.9 8.5 %collective-permute-start.28 = (bf16[112,2048]{1,0:T(8,128)(2,1)S(1)}, bf16[112,2048]{1,0:T(8,128)(2,1)S(1)}, u32[]{:S(2)}, u32[]{:S(2)}) collective-permute-start(bf16[112,2048]{1,0:T(8,128)(2,1)S(1)} %pad_select_fusion.1), channel_id=1, source_target_pairs={{4,0},{12,8},{20,16},{28,24},{0,4},{8,12},{16,20},{24,28},{5,1},{1... | collective-permute-start | bytes 1376264 | tf_op jit(solution)/shard_map/ppermute | solution.py:11
  170.1 18.6 %collective-permute-start.31 = (f32[896,224]{0,1:T(8,128)S(1)}, f32[896,224]{0,1:T(8,128)S(1)}, u32[]{:S(2)}, u32[]{:S(2)}) collective-permute-start(f32[896,224]{0,1:T(8,128)S(1)} %maximum_select_fusion.5), channel_id=1, source_target_pairs={{0,1},{1,0},{2,3},{3,2},{4,5},{5,4},{6,7},{7,6},{8,9},{9,8},{10,11... | collective-permute-start | bytes 2408456 | tf_op jit(solution)/shard_map/ppermute | solution.py:95
  170.4 13.8 %collective-permute-start.33 = (f32[896,112]{0,1:T(8,128)S(1)}, f32[896,112]{0,1:T(8,128)S(1)}, u32[]{:S(2)}, u32[]{:S(2)}) collective-permute-start(f32[896,112]{0,1:T(8,128)S(1)} %select_add_fusion.3), channel_id=1, source_target_pairs={{0,2},{1,3},{2,0},{3,1},{4,6},{5,7},{6,4},{7,5},{8,10},{9,11},{10,... | collective-permute-start | bytes 1204232 | tf_op jit(solution)/shard_map/ppermute | solution.py:108
  174.2 14.5 %collective-permute-start.34 = (bf16[112,2048]{1,0:T(8,128)(2,1)S(1)}, bf16[112,2048]{1,0:T(8,128)(2,1)S(1)}, u32[]{:S(2)}, u32[]{:S(2)}) collective-permute-start(bf16[112,2048]{1,0:T(8,128)(2,1)S(1)} %broadcast_select_fusion.1), channel_id=1, source_target_pairs={{8,0},{12,4},{16,8},{20,12},{24,16},{28,20},{9,1},{13,5},{17,9},{2... | collective-permute-start | bytes 1376264 | tf_op jit(solution)/shard_map/ppermute | solution.py:11
  191.1 13.7 %collective-permute-start.35 = (f32[896,224]{0,1:T(8,128)S(1)}, f32[896,224]{0,1:T(8,128)S(1)}, u32[]{:S(2)}, u32[]{:S(2)}) collective-permute-start(f32[896,224]{0,1:T(8,128)S(1)} %maximum_select_fusion.6), channel_id=1, source_target_pairs={{0,1},{1,0},{2,3},{3,2},{4,5},{5,4},{6,7},{7,6},{8,9},{9,8},{10,11... | collective-permute-start | bytes 2408456 | tf_op jit(solution)/shard_map/ppermute | solution.py:95
  191.3 11.8 %collective-permute-start.36 = (f32[896,112]{0,1:T(8,128)S(1)}, f32[896,112]{0,1:T(8,128)S(1)}, u32[]{:S(2)}, u32[]{:S(2)}) collective-permute-start(f32[896,112]{0,1:T(8,128)S(1)} %select_add_fusion.2), channel_id=1, source_target_pairs={{0,2},{1,3},{2,0},{3,1},{4,6},{5,7},{6,4},{7,5},{8,10},{9,11},{10,... | collective-permute-start | bytes 1204232 | tf_op jit(solution)/shard_map/ppermute | solution.py:108
  191.7 13.1 %collective-permute-start.37 = (bf16[96,2048]{1,0:T(8,128)(2,1)S(1)}, bf16[96,2048]{1,0:T(8,128)(2,1)S(1)}, u32[]{:S(2)}, u32[]{:S(2)}) collective-permute-start(bf16[96,2048]{1,0:T(8,128)(2,1)S(1)} %slice_select_fusion.1), channel_id=1, source_target_pairs={{8,0},{12,4},{16,8},{20,12},{24,16},{28,20},{9,1},{13,5},{17,9},{2... | collective-permute-start | bytes 1179656 | tf_op jit(solution)/shard_map/ppermute | solution.py:11
  207.0 12.1 %collective-permute-start.39 = (f32[896,112]{0,1:T(8,128)S(1)}, f32[896,112]{0,1:T(8,128)S(1)}, u32[]{:S(2)}, u32[]{:S(2)}) collective-permute-start(f32[896,112]{0,1:T(8,128)S(1)} %select_add_fusion.1), channel_id=1, source_target_pairs={{0,2},{1,3},{2,0},{3,1},{4,6},{5,7},{6,4},{7,5},{8,10},{9,11},{10,... | collective-permute-start | bytes 1204232 | tf_op jit(solution)/shard_map/ppermute | solution.py:108
  209.1 17.1 %collective-permute-start.40 = (f32[896,96]{0,1:T(8,128)S(1)}, f32[896,96]{0,1:T(8,128)S(1)}, u32[]{:S(2)}, u32[]{:S(2)}) collective-permute-start(f32[896,96]{0,1:T(8,128)S(1)} %select_add_fusion.7), channel_id=1, source_target_pairs={{0,2},{1,3},{2,0},{3,1},{4,6},{5,7},{6,4},{7,5},{8,10},{9,11},{10,... | collective-permute-start | bytes 1032200 | tf_op jit(solution)/shard_map/ppermute | solution.py:108
  (26 other events, 279.9 us)

commit v11 on v10

--- a/solution.py
+++ b/solution.py
@@ -69,6 +69,7 @@
     even = list(range(0, count, 2))
     z_down = [(s, s - 2) for s in range(2, count)]
     swap = [(s, s - 1) for s in odd] + [(s, s + 1) for s in even if s + 1 < count]
+    one_down = [(s, s - 1) for s in range(1, count)]
     even_snp = lax.axis_index("snp") % 2 == 0
 
     even_me = me % 2 == 0
@@ -93,7 +94,7 @@
         payload = jnp.where(even_me, jnp.concatenate([tiles[1], tiles[3]], axis=1),
                             jnp.concatenate([tiles[0], tiles[2]], axis=1))
         state["first"][c] = lax.ppermute(payload, "samp", partner)
-        if c == CHUNKS - 1:
+        if c >= CHUNKS - 2:
             second_level(c)
 
     def pick(c, a, b, d, e):
@@ -108,10 +109,11 @@
         last = lax.ppermute(pick(c, 2, 3, 0, 1) + onward, "samp", across)
         state["results"][c] = pick(c, 0, 1, 2, 3) + mine + last
 
-    for t in range(CHUNKS + 3):
+    ready = [c + 3 for c in range(CHUNKS - 1)] + [CHUNKS + 1]
+    for t in range(CHUNKS + 2):
         new = t if t < CHUNKS else None
         second = t - 1 if 0 <= t - 1 < CHUNKS else None
-        third = t - 2 if 0 <= t - 2 < CHUNKS else None
+        third = t - 2 if 0 <= t - 2 < CHUNKS - 1 else None
         if new is not None or third is not None:
             sent = moved(joined([pieces[new] if new is not None else None,
                                  state["one"][third] if third is not None else None]), z_down)
@@ -130,9 +132,11 @@
         if second is not None:
             size = sizes[second]
             state["one"][second] = jnp.where(even_snp, state["swapped"][second][:size], state["swapped"][t][:size])
-        if 0 <= t - 3 < CHUNKS:
-            finish(t - 3)
-        if 0 <= t - 4 < CHUNKS - 1:
+        if second == CHUNKS - 1:
+            state["three"][second] = moved(state["two"][second], one_down)
+        for c in [c for c in range(CHUNKS) if ready[c] == t]:
+            finish(c)
+        if 0 <= t - 4 < CHUNKS - 2:
             second_level(t - 4)
         flat, tree = jax.tree.flatten(state)
         following = pieces[t + 1] if t + 1 < CHUNKS else own_block[:8]

time: 230 us -> 230 us (level)
    ppermute x8, waiting for transfers between devices: 39.6 us -> 35.9 us  [second_level(): last = lax.ppermute(pick(c, 2, 3, 0, 1) + onward, 'samp', across)]
    ppermute x19, waiting for transfers between devices: 94.6 us -> 98.1 us  [moved(): return lax.ppermute(value, 'snp', pairs)]
  transfers between devices with their start and end apart: 41 -> 41, of which waited for: 27 -> 26; matrix products, arithmetic and copies ran while one was open for 12% -> 13% of each run, Pallas kernels for 0% -> 0%
where the time goes in v11:
time: 230 us; the launch traced here: 229 us
  waiting for transfers between devices  137 us (60%)
  starting transfers between devices  45.8 us (20%)
  other arithmetic  18.8 us (8%)
  matrix products  17 us (7%)
  local copies, waits for them, and re-layouts  9.43 us (4%)
    ppermute x19, waiting for transfers between devices, moved(): return lax.ppermute(value, 'snp', pairs)  98.1 us
    ppermute x8, waiting for transfers between devices, second_level(): last = lax.ppermute(pick(c, 2, 3, 0, 1) + onward, 'samp', across)  35.9 us
    ppermute x19, starting transfers between devices, moved(): return lax.ppermute(value, 'snp', pairs)  22.7 us
    dot_general x8, matrix products, finish(): jnp.einsum('ab,cb->ac', own_block, blocks, preferred_element_type=jnp.flo...  17 us
    ppermute x8, starting transfers between devices, second_level(): last = lax.ppermute(pick(c, 2, 3, 0, 1) + onward, 'samp', across)  16.9 us
    ppermute x6, starting transfers between devices, standard_rows(): lax.ppermute(moments, 'samp', [(j, j ^ i) for j in range(groups)])  5.12 us
    reduce_sum x2, other arithmetic, local_moments(): return (jnp.sum(values, axis=1), jnp.sum(values * values, axis=1))  5.07 us
    convert_element_type x2, other arithmetic, standardize(): ((values - mean[:, None]) * lax.rsqrt(variance + 1e-05)[:, None]).astype(...  4.84 us
  transfers between devices with their start and end apart: 41, of which 26 were waited for; matrix products, arithmetic and copies ran while one was open for 13% of the time, Pallas kernels for 0%

profile of v11, /device:TPU:0, one launch (start us, length us, event | category | flops | bytes accessed | tf_op | source)
XLA Modules:
  0.0 228.8 jit_solution(3833284649198477902)
XLA Ops:
  0.0 3.7 %slice_reduce_fusion = (f32[768]{0:T(1024)S(1)}, f32[768]{0:T(1024)S(1)}) fusion(f32[896,2048]{1,0:T(8,128)} %param.1), kind=kLoop, calls=%fused_computation.2 | loop fusion | flops 4717056 | bytes 6297600 | tf_op jit(solution)/shard_map/reduce_sum | solution.py:21
  3.7 2.4 %collective-permute-start.3 = (f32[2,768]{1,0:T(2,128)S(1)}, f32[2,768]{1,0:T(2,128)S(1)}, u32[]{:S(2)}, u32[]{:S(2)}) collective-permute-start(f32[2,768]{1,0:T(2,128)S(1)} %pad_maximum_fusion.7), channel_id=1, source_target_pairs={{0,3},{1,2},{2,1},{3,0},{4,7},{5,6},{6,5},{7,4},{8,11},{9,10},{10,... | collective-permute-start | bytes 18440 | tf_op jit(solution)/shard_map/ppermute | solution.py:55
  17.7 3.4 %multiply_convert_fusion = bf16[768,2048]{1,0:T(8,128)(2,1)S(1)} fusion(f32[896,2048]{1,0:T(8,128)} %param.1, f32[768]{0:T(1024)S(1)} %add_rsqrt_fusion, f32[768]{0:T(1024)S(1)} %get-tuple-element.237), kind=kLoop, calls=%fused_computation | loop fusion | flops 4718592 | bytes 9443328 | tf_op jit(solution)/shard_map/convert_element_type | solution.py:17
  22.5 5.1 %collective-permute-done.6 = bf16[128,2048]{1,0:T(8,128)(2,1)S(1)} collective-permute-done((bf16[128,2048]{1,0:T(8,128)(2,1)S(1)}, bf16[128,2048]{1,0:T(8,128)(2,1)S(1)}, u32[]{:S(2)}, u32[]{:S(2)}) %collective-permute-start.6) | collective-permute-done | bytes 524320 | tf_op jit(solution)/shard_map/ppermute | solution.py:11
  27.5 3.1 %collective-permute-done.7 = bf16[128,2048]{1,0:T(8,128)(2,1)S(1)} collective-permute-done((bf16[128,2048]{1,0:T(8,128)(2,1)S(1)}, bf16[128,2048]{1,0:T(8,128)(2,1)S(1)}, u32[]{:S(2)}, u32[]{:S(2)}) %collective-permute-start.7) | collective-permute-done | bytes 524320 | tf_op jit(solution)/shard_map/ppermute | solution.py:11
  32.7 9.8 %collective-permute-done.8 = bf16[128,2048]{1,0:T(8,128)(2,1)S(1)} collective-permute-done((bf16[128,2048]{1,0:T(8,128)(2,1)S(1)}, bf16[128,2048]{1,0:T(8,128)(2,1)S(1)}, u32[]{:S(2)}, u32[]{:S(2)}) %collective-permute-start.8) | collective-permute-done | bytes 524320 | tf_op jit(solution)/shard_map/ppermute | solution.py:11
  48.0 8.9 %collective-permute-done.10 = bf16[112,2048]{1,0:T(8,128)(2,1)} collective-permute-done((bf16[112,2048]{1,0:T(8,128)(2,1)}, bf16[112,2048]{1,0:T(8,128)(2,1)}, u32[]{:S(2)}, u32[]{:S(2)}) %collective-permute-start.10) | collective-permute-done | bytes 458784 | tf_op jit(solution)/shard_map/ppermute | solution.py:11
  57.9 9.9 %collective-permute-done.11 = bf16[240,2048]{1,0:T(8,128)(2,1)} collective-permute-done((bf16[240,2048]{1,0:T(8,128)(2,1)}, bf16[240,2048]{1,0:T(8,128)(2,1)}, u32[]{:S(2)}, u32[]{:S(2)}) %collective-permute-start.11) | collective-permute-done | bytes 983072 | tf_op jit(solution)/shard_map/ppermute | solution.py:11
  71.9 2.4 %fusion = f32[896,512]{0,1:T(8,128)S(1)} fusion(bf16[128,2048]{1,0:T(8,128)(2,1)S(1)} %slice.326, bf16[128,2048]{1,0:T(8,128)(2,1)S(1)} %copy-done.12, bf16[128,2048]{1,0:T(8,128)(2,1)S(1)} %copy-done.7, bf16[128,2048]{1,0:T(8,128)(2,1)S(1)} %copy-done.14, bf16[768,2048]{1,0:T(8,128)(2,1)S(1)} %multiply_convert_fusion), kind=kOutput, calls=%fused_computation.4 | convolution fusion | flops 1894776832 | bytes 7077888 | tf_op jit(solution)/shard_map/ab,cb->ac/dot_general | solution.py:90
  74.6 5.3 %collective-permute-done.13 = bf16[112,2048]{1,0:T(8,128)(2,1)S(1)} collective-permute-done((bf16[112,2048]{1,0:T(8,128)(2,1)S(1)}, bf16[112,2048]{1,0:T(8,128)(2,1)S(1)}, u32[]{:S(2)}, u32[]{:S(2)}) %collective-permute-start.13) | collective-permute-done | bytes 458784 | tf_op jit(solution)/shard_map/ppermute | solution.py:11
  81.0 9.2 %collective-permute-done.14 = bf16[224,2048]{1,0:T(8,128)(2,1)S(1)} collective-permute-done((bf16[224,2048]{1,0:T(8,128)(2,1)S(1)}, bf16[224,2048]{1,0:T(8,128)(2,1)S(1)}, u32[]{:S(2)}, u32[]{:S(2)}) %collective-permute-start.14) | collective-permute-done | bytes 917536 | tf_op jit(solution)/shard_map/ppermute | solution.py:11
  92.0 2.3 %collective-permute-start.17 = (f32[896,128]{0,1:T(8,128)S(1)}, f32[896,128]{0,1:T(8,128)S(1)}, u32[]{:S(2)}, u32[]{:S(2)}) collective-permute-start(f32[896,128]{0,1:T(8,128)S(1)} %select_add_fusion), channel_id=1, source_target_pairs={{0,2},{1,3},{2,0},{3,1},{4,6},{5,7},{6,4},{7,5},{8,10},{9,11},{10,... | collective-permute-start | bytes 1376264 | tf_op jit(solution)/shard_map/ppermute | solution.py:109
  98.1 4.8 %collective-permute-done.16 = bf16[112,2048]{1,0:T(8,128)(2,1)S(1)} collective-permute-done((bf16[112,2048]{1,0:T(8,128)(2,1)S(1)}, bf16[112,2048]{1,0:T(8,128)(2,1)S(1)}, u32[]{:S(2)}, u32[]{:S(2)}) %collective-permute-start.16) | collective-permute-done | bytes 458784 | tf_op jit(solution)/shard_map/ppermute | solution.py:11
  103.2 7.5 %collective-permute-done.18 = bf16[224,2048]{1,0:T(8,128)(2,1)S(1)} collective-permute-done((bf16[224,2048]{1,0:T(8,128)(2,1)S(1)}, bf16[224,2048]{1,0:T(8,128)(2,1)S(1)}, u32[]{:S(2)}, u32[]{:S(2)}) %collective-permute-start.18) | collective-permute-done | bytes 917536 | tf_op jit(solution)/shard_map/ppermute | solution.py:11
  112.7 2.3 %collective-permute-start.21 = (f32[896,112]{0,1:T(8,128)S(1)}, f32[896,112]{0,1:T(8,128)S(1)}, u32[]{:S(2)}, u32[]{:S(2)}) collective-permute-start(f32[896,112]{0,1:T(8,128)S(1)} %select_add_fusion.6), channel_id=1, source_target_pairs={{0,2},{1,3},{2,0},{3,1},{4,6},{5,7},{6,4},{7,5},{8,10},{9,11},{10,... | collective-permute-start | bytes 1204232 | tf_op jit(solution)/shard_map/ppermute | solution.py:109
  121.0 2.6 %collective-permute-done.20 = bf16[112,2048]{1,0:T(8,128)(2,1)S(1)} collective-permute-done((bf16[112,2048]{1,0:T(8,128)(2,1)S(1)}, bf16[112,2048]{1,0:T(8,128)(2,1)S(1)}, u32[]{:S(2)}, u32[]{:S(2)}) %collective-permute-start.20) | collective-permute-done | bytes 458784 | tf_op jit(solution)/shard_map/ppermute | solution.py:11
  123.6 7.8 %collective-permute-done.22 = bf16[224,2048]{1,0:T(8,128)(2,1)S(1)} collective-permute-done((bf16[224,2048]{1,0:T(8,128)(2,1)S(1)}, bf16[224,2048]{1,0:T(8,128)(2,1)S(1)}, u32[]{:S(2)}, u32[]{:S(2)}) %collective-permute-start.22) | collective-permute-done | bytes 917536 | tf_op jit(solution)/shard_map/ppermute | solution.py:11
  133.0 2.3 %collective-permute-start.25 = (f32[896,112]{0,1:T(8,128)S(1)}, f32[896,112]{0,1:T(8,128)S(1)}, u32[]{:S(2)}, u32[]{:S(2)}) collective-permute-start(f32[896,112]{0,1:T(8,128)S(1)} %select_add_fusion.5), channel_id=1, source_target_pairs={{0,2},{1,3},{2,0},{3,1},{4,6},{5,7},{6,4},{7,5},{8,10},{9,11},{10,... | collective-permute-start | bytes 1204232 | tf_op jit(solution)/shard_map/ppermute | solution.py:109
  141.3 2.6 %collective-permute-done.24 = bf16[112,2048]{1,0:T(8,128)(2,1)S(1)} collective-permute-done((bf16[112,2048]{1,0:T(8,128)(2,1)S(1)}, bf16[112,2048]{1,0:T(8,128)(2,1)S(1)}, u32[]{:S(2)}, u32[]{:S(2)}) %collective-permute-start.24) | collective-permute-done | bytes 458784 | tf_op jit(solution)/shard_map/ppermute | solution.py:11
  144.0 7.0 %collective-permute-done.26 = bf16[224,2048]{1,0:T(8,128)(2,1)S(1)} collective-permute-done((bf16[224,2048]{1,0:T(8,128)(2,1)S(1)}, bf16[224,2048]{1,0:T(8,128)(2,1)S(1)}, u32[]{:S(2)}, u32[]{:S(2)}) %collective-permute-start.26) | collective-permute-done | bytes 917536 | tf_op jit(solution)/shard_map/ppermute | solution.py:11
  152.6 3.3 %collective-permute-start.29 = (f32[896,112]{0,1:T(8,128)S(1)}, f32[896,112]{0,1:T(8,128)S(1)}, u32[]{:S(2)}, u32[]{:S(2)}) collective-permute-start(f32[896,112]{0,1:T(8,128)S(1)} %select_add_fusion.4), channel_id=1, source_target_pairs={{0,2},{1,3},{2,0},{3,1},{4,6},{5,7},{6,4},{7,5},{8,10},{9,11},{10,... | collective-permute-start | bytes 1204232 | tf_op jit(solution)/shard_map/ppermute | solution.py:109
  161.9 2.6 %collective-permute-done.28 = bf16[112,2048]{1,0:T(8,128)(2,1)S(1)} collective-permute-done((bf16[112,2048]{1,0:T(8,128)(2,1)S(1)}, bf16[112,2048]{1,0:T(8,128)(2,1)S(1)}, u32[]{:S(2)}, u32[]{:S(2)}) %collective-permute-start.28) | collective-permute-done | bytes 458784 | tf_op jit(solution)/shard_map/ppermute | solution.py:11
  164.6 2.7 %collective-permute-done.30 = bf16[208,2048]{1,0:T(8,128)(2,1)S(1)} collective-permute-done((bf16[208,2048]{1,0:T(8,128)(2,1)S(1)}, bf16[208,2048]{1,0:T(8,128)(2,1)S(1)}, u32[]{:S(2)}, u32[]{:S(2)}) %collective-permute-start.30) | collective-permute-done | bytes 852000 | tf_op jit(solution)/shard_map/ppermute | solution.py:11
  171.7 4.2 %collective-permute-start.33 = (f32[896,112]{0,1:T(8,128)S(1)}, f32[896,112]{0,1:T(8,128)S(1)}, u32[]{:S(2)}, u32[]{:S(2)}) collective-permute-start(f32[896,112]{0,1:T(8,128)S(1)} %select_add_fusion.3), channel_id=1, source_target_pairs={{0,2},{1,3},{2,0},{3,1},{4,6},{5,7},{6,4},{7,5},{8,10},{9,11},{10,... | collective-permute-start | bytes 1204232 | tf_op jit(solution)/shard_map/ppermute | solution.py:109
  177.4 2.7 %collective-permute-done.32 = bf16[96,2048]{1,0:T(8,128)(2,1)S(1)} collective-permute-done((bf16[96,2048]{1,0:T(8,128)(2,1)S(1)}, bf16[96,2048]{1,0:T(8,128)(2,1)S(1)}, u32[]{:S(2)}, u32[]{:S(2)}) %collective-permute-start.32) | collective-permute-done | bytes 393248 | tf_op jit(solution)/shard_map/ppermute | solution.py:11
  180.2 5.7 %collective-permute-done.33 = f32[896,112]{0,1:T(8,128)S(1)} collective-permute-done((f32[896,112]{0,1:T(8,128)S(1)}, f32[896,112]{0,1:T(8,128)S(1)}, u32[]{:S(2)}, u32[]{:S(2)}) %collective-permute-start.33) | collective-permute-done | bytes 401440 | tf_op jit(solution)/shard_map/ppermute | solution.py:109
  186.0 6.7 %collective-permute-done.34 = bf16[112,2048]{1,0:T(8,128)(2,1)S(1)} collective-permute-done((bf16[112,2048]{1,0:T(8,128)(2,1)S(1)}, bf16[112,2048]{1,0:T(8,128)(2,1)S(1)}, u32[]{:S(2)}, u32[]{:S(2)}) %collective-permute-start.34) | collective-permute-done | bytes 458784 | tf_op jit(solution)/shard_map/ppermute | solution.py:11
  194.9 2.1 fusion.48
  200.7 9.5 %collective-permute-done.38 = f32[896,112]{0,1:T(8,128)S(1)} collective-permute-done((f32[896,112]{0,1:T(8,128)S(1)}, f32[896,112]{0,1:T(8,128)S(1)}, u32[]{:S(2)}, u32[]{:S(2)}) %collective-permute-start.38) | collective-permute-done | bytes 401440 | tf_op jit(solution)/shard_map/ppermute | solution.py:109
  210.4 7.1 %collective-permute-done.40 = f32[896,96]{0,1:T(8,128)S(1)} collective-permute-done((f32[896,96]{0,1:T(8,128)S(1)}, f32[896,96]{0,1:T(8,128)S(1)}, u32[]{:S(2)}, u32[]{:S(2)}) %collective-permute-start.40) | collective-permute-done | bytes 344096 | tf_op jit(solution)/shard_map/ppermute | solution.py:109
  217.7 7.5 %collective-permute-done.39 = f32[896,112]{0,1:T(8,128)S(1)} collective-permute-done((f32[896,112]{0,1:T(8,128)S(1)}, f32[896,112]{0,1:T(8,128)S(1)}, u32[]{:S(2)}, u32[]{:S(2)}) %collective-permute-start.39) | collective-permute-done | bytes 401440 | tf_op jit(solution)/shard_map/ppermute | solution.py:109
  225.9 3.0 %copy.2 = f32[896,896]{1,0:T(8,128)} copy(f32[896,896]{0,1:T(8,128)S(1)} %broadcast_multiply_fusion) | data formatting | bytes 6422528 | tf_op jit(solution)/shard_map/div | solution.py:148
  (179 shorter events, 68.7 us)
Async XLA Ops:
  3.7 13.9 %collective-permute-start.3 = (f32[2,768]{1,0:T(2,128)S(1)}, f32[2,768]{1,0:T(2,128)S(1)}, u32[]{:S(2)}, u32[]{:S(2)}) collective-permute-start(f32[2,768]{1,0:T(2,128)S(1)} %pad_maximum_fusion.7), channel_id=1, source_target_pairs={{0,3},{1,2},{2,1},{3,0},{4,7},{5,6},{6,5},{7,4},{8,11},{9,10},{10,... | collective-permute-start | bytes 18440 | tf_op jit(solution)/shard_map/ppermute | solution.py:55
  6.2 11.5 %collective-permute-start.4 = (f32[2,768]{1,0:T(2,128)S(1)}, f32[2,768]{1,0:T(2,128)S(1)}, u32[]{:S(2)}, u32[]{:S(2)}) collective-permute-start(f32[2,768]{1,0:T(2,128)S(1)} %pad_maximum_fusion.7), channel_id=1, source_target_pairs={{0,2},{1,3},{2,0},{3,1},{4,6},{5,7},{6,4},{7,5},{8,10},{9,11},{10,... | collective-permute-start | bytes 18440 | tf_op jit(solution)/shard_map/ppermute | solution.py:55
  14.7 12.8 %collective-permute-start.6 = (bf16[128,2048]{1,0:T(8,128)(2,1)S(1)}, bf16[128,2048]{1,0:T(8,128)(2,1)S(1)}, u32[]{:S(2)}, u32[]{:S(2)}) collective-permute-start(bf16[128,2048]{1,0:T(8,128)(2,1)S(1)} %multiply_convert_fusion.1), channel_id=1, source_target_pairs={{4,0},{12,8},{20,16},{28,24},{0,4},{8,12},{16,20},{24,28},{5,1},{1... | collective-permute-start | bytes 1572872 | tf_op jit(solution)/shard_map/ppermute | solution.py:11
  16.3 14.4 %collective-permute-start.7 = (bf16[128,2048]{1,0:T(8,128)(2,1)S(1)}, bf16[128,2048]{1,0:T(8,128)(2,1)S(1)}, u32[]{:S(2)}, u32[]{:S(2)}) collective-permute-start(bf16[128,2048]{1,0:T(8,128)(2,1)S(1)} %multiply_convert_fusion.1), channel_id=1, source_target_pairs={{8,0},{12,4},{16,8},{20,12},{24,16},{28,20},{9,1},{13,5},{17,9},{2... | collective-permute-start | bytes 1572872 | tf_op jit(solution)/shard_map/ppermute | solution.py:11
  30.8 11.6 %collective-permute-start.8 = (bf16[128,2048]{1,0:T(8,128)(2,1)S(1)}, bf16[128,2048]{1,0:T(8,128)(2,1)S(1)}, u32[]{:S(2)}, u32[]{:S(2)}) collective-permute-start(bf16[128,2048]{1,0:T(8,128)(2,1)S(1)} %pad_select_fusion), channel_id=1, source_target_pairs={{4,0},{12,8},{20,16},{28,24},{0,4},{8,12},{16,20},{24,28},{5,1},{1... | collective-permute-start | bytes 1572872 | tf_op jit(solution)/shard_map/ppermute | solution.py:11
  31.4 11.9 %collective-permute-start.9 = (bf16[112,2048]{1,0:T(8,128)(2,1)S(1)}, bf16[112,2048]{1,0:T(8,128)(2,1)S(1)}, u32[]{:S(2)}, u32[]{:S(2)}) collective-permute-start(bf16[112,2048]{1,0:T(8,128)(2,1)S(1)} %get-tuple-element.121), channel_id=1, source_target_pairs={{8,0},{12,4},{16,8},{20,12},{24,16},{28,20},{9,1},{13,5},{17,9},{2... | collective-permute-start | bytes 1376264 | tf_op jit(solution)/shard_map/ppermute | solution.py:11
  45.1 22.7 %collective-permute-start.11 = (bf16[240,2048]{1,0:T(8,128)(2,1)}, bf16[240,2048]{1,0:T(8,128)(2,1)}, u32[]{:S(2)}, u32[]{:S(2)}) collective-permute-start(bf16[240,2048]{1,0:T(8,128)(2,1)} %pad_maximum_fusion.1), channel_id=1, source_target_pairs={{8,0},{12,4},{16,8},{20,12},{24,16},{28,20},{9,1},{13,5},{17,9},{2... | collective-permute-start | bytes 2949128 | tf_op jit(solution)/shard_map/ppermute | solution.py:11
  47.2 9.6 %collective-permute-start.10 = (bf16[112,2048]{1,0:T(8,128)(2,1)}, bf16[112,2048]{1,0:T(8,128)(2,1)}, u32[]{:S(2)}, u32[]{:S(2)}) collective-permute-start(bf16[112,2048]{1,0:T(8,128)(2,1)} %broadcast_select_fusion.10), channel_id=1, source_target_pairs={{4,0},{12,8},{20,16},{28,24},{0,4},{8,12},{16,20},{24,28},{5,1},{1... | collective-permute-start | bytes 1376264 | tf_op jit(solution)/shard_map/ppermute | solution.py:11
  70.0 20.2 %collective-permute-start.14 = (bf16[224,2048]{1,0:T(8,128)(2,1)S(1)}, bf16[224,2048]{1,0:T(8,128)(2,1)S(1)}, u32[]{:S(2)}, u32[]{:S(2)}) collective-permute-start(bf16[224,2048]{1,0:T(8,128)(2,1)S(1)} %pad_maximum_fusion.2), channel_id=1, source_target_pairs={{8,0},{12,4},{16,8},{20,12},{24,16},{28,20},{9,1},{13,5},{17,9},{2... | collective-permute-start | bytes 2752520 | tf_op jit(solution)/shard_map/ppermute | solution.py:11
  71.4 8.5 %collective-permute-start.13 = (bf16[112,2048]{1,0:T(8,128)(2,1)S(1)}, bf16[112,2048]{1,0:T(8,128)(2,1)S(1)}, u32[]{:S(2)}, u32[]{:S(2)}) collective-permute-start(bf16[112,2048]{1,0:T(8,128)(2,1)S(1)} %broadcast_select_fusion.9), channel_id=1, source_target_pairs={{4,0},{12,8},{20,16},{28,24},{0,4},{8,12},{16,20},{24,28},{5,1},{1... | collective-permute-start | bytes 1376264 | tf_op jit(solution)/shard_map/ppermute | solution.py:11
  74.6 15.7 %collective-permute-start.12 = (f32[896,256]{0,1:T(8,128)S(1)}, f32[896,256]{0,1:T(8,128)S(1)}, u32[]{:S(2)}, u32[]{:S(2)}) collective-permute-start(f32[896,256]{0,1:T(8,128)S(1)} %maximum_select_fusion), channel_id=1, source_target_pairs={{0,1},{1,0},{2,3},{3,2},{4,5},{5,4},{6,7},{7,6},{8,9},{9,8},{10,11... | collective-permute-start | bytes 2752520 | tf_op jit(solution)/shard_map/ppermute | solution.py:96
  90.4 20.3 %collective-permute-start.18 = (bf16[224,2048]{1,0:T(8,128)(2,1)S(1)}, bf16[224,2048]{1,0:T(8,128)(2,1)S(1)}, u32[]{:S(2)}, u32[]{:S(2)}) collective-permute-start(bf16[224,2048]{1,0:T(8,128)(2,1)S(1)} %pad_maximum_fusion.3), channel_id=1, source_target_pairs={{8,0},{12,4},{16,8},{20,12},{24,16},{28,20},{9,1},{13,5},{17,9},{2... | collective-permute-start | bytes 2752520 | tf_op jit(solution)/shard_map/ppermute | solution.py:11
  92.0 11.0 %collective-permute-start.17 = (f32[896,128]{0,1:T(8,128)S(1)}, f32[896,128]{0,1:T(8,128)S(1)}, u32[]{:S(2)}, u32[]{:S(2)}) collective-permute-start(f32[896,128]{0,1:T(8,128)S(1)} %select_add_fusion), channel_id=1, source_target_pairs={{0,2},{1,3},{2,0},{3,1},{4,6},{5,7},{6,4},{7,5},{8,10},{9,11},{10,... | collective-permute-start | bytes 1376264 | tf_op jit(solution)/shard_map/ppermute | solution.py:109
  94.3 8.5 %collective-permute-start.16 = (bf16[112,2048]{1,0:T(8,128)(2,1)S(1)}, bf16[112,2048]{1,0:T(8,128)(2,1)S(1)}, u32[]{:S(2)}, u32[]{:S(2)}) collective-permute-start(bf16[112,2048]{1,0:T(8,128)(2,1)S(1)} %broadcast_select_fusion.7), channel_id=1, source_target_pairs={{4,0},{12,8},{20,16},{28,24},{0,4},{8,12},{16,20},{24,28},{5,1},{1... | collective-permute-start | bytes 1376264 | tf_op jit(solution)/shard_map/ppermute | solution.py:11
  98.1 12.8 %collective-permute-start.15 = (f32[896,224]{0,1:T(8,128)S(1)}, f32[896,224]{0,1:T(8,128)S(1)}, u32[]{:S(2)}, u32[]{:S(2)}) collective-permute-start(f32[896,224]{0,1:T(8,128)S(1)} %maximum_select_fusion.1), channel_id=1, source_target_pairs={{0,1},{1,0},{2,3},{3,2},{4,5},{5,4},{6,7},{7,6},{8,9},{9,8},{10,11... | collective-permute-start | bytes 2408456 | tf_op jit(solution)/shard_map/ppermute | solution.py:96
  110.9 20.5 %collective-permute-start.22 = (bf16[224,2048]{1,0:T(8,128)(2,1)S(1)}, bf16[224,2048]{1,0:T(8,128)(2,1)S(1)}, u32[]{:S(2)}, u32[]{:S(2)}) collective-permute-start(bf16[224,2048]{1,0:T(8,128)(2,1)S(1)} %pad_maximum_fusion.4), channel_id=1, source_target_pairs={{8,0},{12,4},{16,8},{20,12},{24,16},{28,20},{9,1},{13,5},{17,9},{2... | collective-permute-start | bytes 2752520 | tf_op jit(solution)/shard_map/ppermute | solution.py:11
  115.0 8.5 %collective-permute-start.20 = (bf16[112,2048]{1,0:T(8,128)(2,1)S(1)}, bf16[112,2048]{1,0:T(8,128)(2,1)S(1)}, u32[]{:S(2)}, u32[]{:S(2)}) collective-permute-start(bf16[112,2048]{1,0:T(8,128)(2,1)S(1)} %broadcast_select_fusion.5), channel_id=1, source_target_pairs={{4,0},{12,8},{20,16},{28,24},{0,4},{8,12},{16,20},{24,28},{5,1},{1... | collective-permute-start | bytes 1376264 | tf_op jit(solution)/shard_map/ppermute | solution.py:11
  118.7 12.7 %collective-permute-start.19 = (f32[896,224]{0,1:T(8,128)S(1)}, f32[896,224]{0,1:T(8,128)S(1)}, u32[]{:S(2)}, u32[]{:S(2)}) collective-permute-start(f32[896,224]{0,1:T(8,128)S(1)} %maximum_select_fusion.2), channel_id=1, source_target_pairs={{0,1},{1,0},{2,3},{3,2},{4,5},{5,4},{6,7},{7,6},{8,9},{9,8},{10,11... | collective-permute-start | bytes 2408456 | tf_op jit(solution)/shard_map/ppermute | solution.py:96
  131.6 19.4 %collective-permute-start.26 = (bf16[224,2048]{1,0:T(8,128)(2,1)S(1)}, bf16[224,2048]{1,0:T(8,128)(2,1)S(1)}, u32[]{:S(2)}, u32[]{:S(2)}) collective-permute-start(bf16[224,2048]{1,0:T(8,128)(2,1)S(1)} %pad_maximum_fusion.5), channel_id=1, source_target_pairs={{8,0},{12,4},{16,8},{20,12},{24,16},{28,20},{9,1},{13,5},{17,9},{2... | collective-permute-start | bytes 2752520 | tf_op jit(solution)/shard_map/ppermute | solution.py:11
  135.4 8.5 %collective-permute-start.24 = (bf16[112,2048]{1,0:T(8,128)(2,1)S(1)}, bf16[112,2048]{1,0:T(8,128)(2,1)S(1)}, u32[]{:S(2)}, u32[]{:S(2)}) collective-permute-start(bf16[112,2048]{1,0:T(8,128)(2,1)S(1)} %broadcast_select_fusion.3), channel_id=1, source_target_pairs={{4,0},{12,8},{20,16},{28,24},{0,4},{8,12},{16,20},{24,28},{5,1},{1... | collective-permute-start | bytes 1376264 | tf_op jit(solution)/shard_map/ppermute | solution.py:11
  139.0 12.0 %collective-permute-start.23 = (f32[896,224]{0,1:T(8,128)S(1)}, f32[896,224]{0,1:T(8,128)S(1)}, u32[]{:S(2)}, u32[]{:S(2)}) collective-permute-start(f32[896,224]{0,1:T(8,128)S(1)} %maximum_select_fusion.3), channel_id=1, source_target_pairs={{0,1},{1,0},{2,3},{3,2},{4,5},{5,4},{6,7},{7,6},{8,9},{9,8},{10,11... | collective-permute-start | bytes 2408456 | tf_op jit(solution)/shard_map/ppermute | solution.py:96
  151.1 16.2 %collective-permute-start.30 = (bf16[208,2048]{1,0:T(8,128)(2,1)S(1)}, bf16[208,2048]{1,0:T(8,128)(2,1)S(1)}, u32[]{:S(2)}, u32[]{:S(2)}) collective-permute-start(bf16[208,2048]{1,0:T(8,128)(2,1)S(1)} %pad_maximum_fusion.6), channel_id=1, source_target_pairs={{8,0},{12,4},{16,8},{20,12},{24,16},{28,20},{9,1},{13,5},{17,9},{2... | collective-permute-start | bytes 2555912 | tf_op jit(solution)/shard_map/ppermute | solution.py:11
  152.6 9.1 %collective-permute-start.29 = (f32[896,112]{0,1:T(8,128)S(1)}, f32[896,112]{0,1:T(8,128)S(1)}, u32[]{:S(2)}, u32[]{:S(2)}) collective-permute-start(f32[896,112]{0,1:T(8,128)S(1)} %select_add_fusion.4), channel_id=1, source_target_pairs={{0,2},{1,3},{2,0},{3,1},{4,6},{5,7},{6,4},{7,5},{8,10},{9,11},{10,... | collective-permute-start | bytes 1204232 | tf_op jit(solution)/shard_map/ppermute | solution.py:109
  156.0 8.5 %collective-permute-start.28 = (bf16[112,2048]{1,0:T(8,128)(2,1)S(1)}, bf16[112,2048]{1,0:T(8,128)(2,1)S(1)}, u32[]{:S(2)}, u32[]{:S(2)}) collective-permute-start(bf16[112,2048]{1,0:T(8,128)(2,1)S(1)} %pad_select_fusion.1), channel_id=1, source_target_pairs={{4,0},{12,8},{20,16},{28,24},{0,4},{8,12},{16,20},{24,28},{5,1},{1... | collective-permute-start | bytes 1376264 | tf_op jit(solution)/shard_map/ppermute | solution.py:11
  167.4 12.8 %collective-permute-start.32 = (bf16[96,2048]{1,0:T(8,128)(2,1)S(1)}, bf16[96,2048]{1,0:T(8,128)(2,1)S(1)}, u32[]{:S(2)}, u32[]{:S(2)}) collective-permute-start(bf16[96,2048]{1,0:T(8,128)(2,1)S(1)} %slice.362), channel_id=1, source_target_pairs={{4,0},{12,8},{20,16},{28,24},{0,4},{8,12},{16,20},{24,28},{5,1},{1... | collective-permute-start | bytes 1179656 | tf_op jit(solution)/shard_map/ppermute | solution.py:11
  167.8 18.2 %collective-permute-start.35 = (bf16[96,2048]{1,0:T(8,128)(2,1)S(1)}, bf16[96,2048]{1,0:T(8,128)(2,1)S(1)}, u32[]{:S(2)}, u32[]{:S(2)}) collective-permute-start(bf16[96,2048]{1,0:T(8,128)(2,1)S(1)} %slice.362), channel_id=1, source_target_pairs={{4,0},{8,4},{12,8},{16,12},{20,16},{24,20},{28,24},{5,1},{9,5},{13... | collective-permute-start | bytes 1179656 | tf_op jit(solution)/shard_map/ppermute | solution.py:11
  171.4 21.3 %collective-permute-start.31 = (f32[896,224]{0,1:T(8,128)S(1)}, f32[896,224]{0,1:T(8,128)S(1)}, u32[]{:S(2)}, u32[]{:S(2)}) collective-permute-start(f32[896,224]{0,1:T(8,128)S(1)} %maximum_select_fusion.5), channel_id=1, source_target_pairs={{0,1},{1,0},{2,3},{3,2},{4,5},{5,4},{6,7},{7,6},{8,9},{9,8},{10,11... | collective-permute-start | bytes 2408456 | tf_op jit(solution)/shard_map/ppermute | solution.py:96
  171.7 14.2 %collective-permute-start.33 = (f32[896,112]{0,1:T(8,128)S(1)}, f32[896,112]{0,1:T(8,128)S(1)}, u32[]{:S(2)}, u32[]{:S(2)}) collective-permute-start(f32[896,112]{0,1:T(8,128)S(1)} %select_add_fusion.3), channel_id=1, source_target_pairs={{0,2},{1,3},{2,0},{3,1},{4,6},{5,7},{6,4},{7,5},{8,10},{9,11},{10,... | collective-permute-start | bytes 1204232 | tf_op jit(solution)/shard_map/ppermute | solution.py:109
  175.9 16.9 %collective-permute-start.34 = (bf16[112,2048]{1,0:T(8,128)(2,1)S(1)}, bf16[112,2048]{1,0:T(8,128)(2,1)S(1)}, u32[]{:S(2)}, u32[]{:S(2)}) collective-permute-start(bf16[112,2048]{1,0:T(8,128)(2,1)S(1)} %broadcast_select_fusion.1), channel_id=1, source_target_pairs={{8,0},{12,4},{16,8},{20,12},{24,16},{28,20},{9,1},{13,5},{17,9},{2... | collective-permute-start | bytes 1376264 | tf_op jit(solution)/shard_map/ppermute | solution.py:11
  198.0 12.2 %collective-permute-start.38 = (f32[896,112]{0,1:T(8,128)S(1)}, f32[896,112]{0,1:T(8,128)S(1)}, u32[]{:S(2)}, u32[]{:S(2)}) collective-permute-start(f32[896,112]{0,1:T(8,128)S(1)} %select_add_fusion.2), channel_id=1, source_target_pairs={{0,2},{1,3},{2,0},{3,1},{4,6},{5,7},{6,4},{7,5},{8,10},{9,11},{10,... | collective-permute-start | bytes 1204232 | tf_op jit(solution)/shard_map/ppermute | solution.py:109
  198.4 19.1 %collective-permute-start.40 = (f32[896,96]{0,1:T(8,128)S(1)}, f32[896,96]{0,1:T(8,128)S(1)}, u32[]{:S(2)}, u32[]{:S(2)}) collective-permute-start(f32[896,96]{0,1:T(8,128)S(1)} %select_add_fusion.7), channel_id=1, source_target_pairs={{0,2},{1,3},{2,0},{3,1},{4,6},{5,7},{6,4},{7,5},{8,10},{9,11},{10,... | collective-permute-start | bytes 1032200 | tf_op jit(solution)/shard_map/ppermute | solution.py:109
  200.4 24.9 %collective-permute-start.39 = (f32[896,112]{0,1:T(8,128)S(1)}, f32[896,112]{0,1:T(8,128)S(1)}, u32[]{:S(2)}, u32[]{:S(2)}) collective-permute-start(f32[896,112]{0,1:T(8,128)S(1)} %select_add_fusion.1), channel_id=1, source_target_pairs={{0,2},{1,3},{2,0},{3,1},{4,6},{5,7},{6,4},{7,5},{8,10},{9,11},{10,... | collective-permute-start | bytes 1204232 | tf_op jit(solution)/shard_map/ppermute | solution.py:109
  (26 other events, 275.7 us)

commit v12 on v11

--- a/solution.py
+++ b/solution.py
@@ -94,7 +94,7 @@
         payload = jnp.where(even_me, jnp.concatenate([tiles[1], tiles[3]], axis=1),
                             jnp.concatenate([tiles[0], tiles[2]], axis=1))
         state["first"][c] = lax.ppermute(payload, "samp", partner)
-        if c >= CHUNKS - 2:
+        if c >= CHUNKS - 3:
             second_level(c)
 
     def pick(c, a, b, d, e):
@@ -136,7 +136,7 @@
             state["three"][second] = moved(state["two"][second], one_down)
         for c in [c for c in range(CHUNKS) if ready[c] == t]:
             finish(c)
-        if 0 <= t - 4 < CHUNKS - 2:
+        if 0 <= t - 4 < CHUNKS - 3:
             second_level(t - 4)
         flat, tree = jax.tree.flatten(state)
         following = pieces[t + 1] if t + 1 < CHUNKS else own_block[:8]

time: 230 us -> 223 us (0.970)
  waiting for transfers between devices: 137 us -> 129 us
    ppermute x8, waiting for transfers between devices: 35.9 us -> 26.8 us  [second_level(): last = lax.ppermute(pick(c, 2, 3, 0, 1) + onward, 'samp', across)]
  transfers between devices with their start and end apart: 41 -> 41, of which waited for: 26 -> 25; matrix products, arithmetic and copies ran while one was open for 13% -> 13% of each run, Pallas kernels for 0% -> 0%
where the time goes in v12:
time: 223 us
  waiting for transfers between devices  129 us (58%)
  starting transfers between devices  47.7 us (21%)
  other arithmetic  18.8 us (8%)
  matrix products  16.8 us (8%)
  local copies, waits for them, and re-layouts  9.46 us (4%)
    ppermute x19, waiting for transfers between devices, moved(): return lax.ppermute(value, 'snp', pairs)  99.2 us
    ppermute x8, waiting for transfers between devices, second_level(): last = lax.ppermute(pick(c, 2, 3, 0, 1) + onward, 'samp', across)  26.8 us
    ppermute x19, starting transfers between devices, moved(): return lax.ppermute(value, 'snp', pairs)  22.7 us
    ppermute x8, starting transfers between devices, second_level(): last = lax.ppermute(pick(c, 2, 3, 0, 1) + onward, 'samp', across)  18.8 us
    dot_general x8, matrix products, finish(): jnp.einsum('ab,cb->ac', own_block, blocks, preferred_element_type=jnp.flo...  16.8 us
    ppermute x6, starting transfers between devices, standard_rows(): lax.ppermute(moments, 'samp', [(j, j ^ i) for j in range(groups)])  5.12 us
    reduce_sum x2, other arithmetic, local_moments(): return (jnp.sum(values, axis=1), jnp.sum(values * values, axis=1))  5.07 us
    convert_element_type x2, other arithmetic, standardize(): ((values - mean[:, None]) * lax.rsqrt(variance + 1e-05)[:, None]).astype(...  4.84 us
  transfers between devices with their start and end apart: 41, of which 25 were waited for; matrix products, arithmetic and copies ran while one was open for 13% of the time, Pallas kernels for 0%

profile of v12, /device:TPU:0, one launch (start us, length us, event | category | flops | bytes accessed | tf_op | source)
XLA Modules:
  0.0 222.6 jit_solution(11385507172876100060)
XLA Ops:
  0.0 3.7 %slice_reduce_fusion = (f32[768]{0:T(1024)S(1)}, f32[768]{0:T(1024)S(1)}) fusion(f32[896,2048]{1,0:T(8,128)} %param.1), kind=kLoop, calls=%fused_computation.2 | loop fusion | flops 4717056 | bytes 6297600 | tf_op jit(solution)/shard_map/reduce_sum | solution.py:21
  3.7 2.4 %collective-permute-start.3 = (f32[2,768]{1,0:T(2,128)S(1)}, f32[2,768]{1,0:T(2,128)S(1)}, u32[]{:S(2)}, u32[]{:S(2)}) collective-permute-start(f32[2,768]{1,0:T(2,128)S(1)} %pad_maximum_fusion.7), channel_id=1, source_target_pairs={{0,3},{1,2},{2,1},{3,0},{4,7},{5,6},{6,5},{7,4},{8,11},{9,10},{10,... | collective-permute-start | bytes 18440 | tf_op jit(solution)/shard_map/ppermute | solution.py:55
  17.7 3.4 %multiply_convert_fusion = bf16[768,2048]{1,0:T(8,128)(2,1)S(1)} fusion(f32[896,2048]{1,0:T(8,128)} %param.1, f32[768]{0:T(1024)S(1)} %add_rsqrt_fusion, f32[768]{0:T(1024)S(1)} %get-tuple-element.229), kind=kLoop, calls=%fused_computation | loop fusion | flops 4718592 | bytes 9443328 | tf_op jit(solution)/shard_map/convert_element_type | solution.py:17
  22.5 5.1 %collective-permute-done.6 = bf16[128,2048]{1,0:T(8,128)(2,1)S(1)} collective-permute-done((bf16[128,2048]{1,0:T(8,128)(2,1)S(1)}, bf16[128,2048]{1,0:T(8,128)(2,1)S(1)}, u32[]{:S(2)}, u32[]{:S(2)}) %collective-permute-start.6) | collective-permute-done | bytes 524320 | tf_op jit(solution)/shard_map/ppermute | solution.py:11
  27.5 3.1 %collective-permute-done.7 = bf16[128,2048]{1,0:T(8,128)(2,1)S(1)} collective-permute-done((bf16[128,2048]{1,0:T(8,128)(2,1)S(1)}, bf16[128,2048]{1,0:T(8,128)(2,1)S(1)}, u32[]{:S(2)}, u32[]{:S(2)}) %collective-permute-start.7) | collective-permute-done | bytes 524320 | tf_op jit(solution)/shard_map/ppermute | solution.py:11
  32.7 9.8 %collective-permute-done.8 = bf16[128,2048]{1,0:T(8,128)(2,1)S(1)} collective-permute-done((bf16[128,2048]{1,0:T(8,128)(2,1)S(1)}, bf16[128,2048]{1,0:T(8,128)(2,1)S(1)}, u32[]{:S(2)}, u32[]{:S(2)}) %collective-permute-start.8) | collective-permute-done | bytes 524320 | tf_op jit(solution)/shard_map/ppermute | solution.py:11
  48.0 8.9 %collective-permute-done.10 = bf16[112,2048]{1,0:T(8,128)(2,1)} collective-permute-done((bf16[112,2048]{1,0:T(8,128)(2,1)}, bf16[112,2048]{1,0:T(8,128)(2,1)}, u32[]{:S(2)}, u32[]{:S(2)}) %collective-permute-start.10) | collective-permute-done | bytes 458784 | tf_op jit(solution)/shard_map/ppermute | solution.py:11
  57.9 9.9 %collective-permute-done.11 = bf16[240,2048]{1,0:T(8,128)(2,1)} collective-permute-done((bf16[240,2048]{1,0:T(8,128)(2,1)}, bf16[240,2048]{1,0:T(8,128)(2,1)}, u32[]{:S(2)}, u32[]{:S(2)}) %collective-permute-start.11) | collective-permute-done | bytes 983072 | tf_op jit(solution)/shard_map/ppermute | solution.py:11
  71.9 2.4 %fusion = f32[896,512]{0,1:T(8,128)S(1)} fusion(bf16[128,2048]{1,0:T(8,128)(2,1)S(1)} %slice.326, bf16[128,2048]{1,0:T(8,128)(2,1)S(1)} %copy-done.12, bf16[128,2048]{1,0:T(8,128)(2,1)S(1)} %copy-done.7, bf16[128,2048]{1,0:T(8,128)(2,1)S(1)} %copy-done.14, bf16[768,2048]{1,0:T(8,128)(2,1)S(1)} %multiply_convert_fusion), kind=kOutput, calls=%fused_computation.4 | convolution fusion | flops 1894776832 | bytes 7077888 | tf_op jit(solution)/shard_map/ab,cb->ac/dot_general | solution.py:90
  74.6 5.3 %collective-permute-done.13 = bf16[112,2048]{1,0:T(8,128)(2,1)S(1)} collective-permute-done((bf16[112,2048]{1,0:T(8,128)(2,1)S(1)}, bf16[112,2048]{1,0:T(8,128)(2,1)S(1)}, u32[]{:S(2)}, u32[]{:S(2)}) %collective-permute-start.13) | collective-permute-done | bytes 458784 | tf_op jit(solution)/shard_map/ppermute | solution.py:11
  81.0 9.2 %collective-permute-done.14 = bf16[224,2048]{1,0:T(8,128)(2,1)S(1)} collective-permute-done((bf16[224,2048]{1,0:T(8,128)(2,1)S(1)}, bf16[224,2048]{1,0:T(8,128)(2,1)S(1)}, u32[]{:S(2)}, u32[]{:S(2)}) %collective-permute-start.14) | collective-permute-done | bytes 917536 | tf_op jit(solution)/shard_map/ppermute | solution.py:11
  92.0 2.3 %collective-permute-start.17 = (f32[896,128]{0,1:T(8,128)S(1)}, f32[896,128]{0,1:T(8,128)S(1)}, u32[]{:S(2)}, u32[]{:S(2)}) collective-permute-start(f32[896,128]{0,1:T(8,128)S(1)} %select_add_fusion), channel_id=1, source_target_pairs={{0,2},{1,3},{2,0},{3,1},{4,6},{5,7},{6,4},{7,5},{8,10},{9,11},{10,... | collective-permute-start | bytes 1376264 | tf_op jit(solution)/shard_map/ppermute | solution.py:109
  95.7 2.1 fusion.8
  98.1 4.8 %collective-permute-done.16 = bf16[112,2048]{1,0:T(8,128)(2,1)S(1)} collective-permute-done((bf16[112,2048]{1,0:T(8,128)(2,1)S(1)}, bf16[112,2048]{1,0:T(8,128)(2,1)S(1)}, u32[]{:S(2)}, u32[]{:S(2)}) %collective-permute-start.16) | collective-permute-done | bytes 458784 | tf_op jit(solution)/shard_map/ppermute | solution.py:11
  103.2 7.5 %collective-permute-done.18 = bf16[224,2048]{1,0:T(8,128)(2,1)S(1)} collective-permute-done((bf16[224,2048]{1,0:T(8,128)(2,1)S(1)}, bf16[224,2048]{1,0:T(8,128)(2,1)S(1)}, u32[]{:S(2)}, u32[]{:S(2)}) %collective-permute-start.18) | collective-permute-done | bytes 917536 | tf_op jit(solution)/shard_map/ppermute | solution.py:11
  112.7 2.3 %collective-permute-start.21 = (f32[896,112]{0,1:T(8,128)S(1)}, f32[896,112]{0,1:T(8,128)S(1)}, u32[]{:S(2)}, u32[]{:S(2)}) collective-permute-start(f32[896,112]{0,1:T(8,128)S(1)} %select_add_fusion.6), channel_id=1, source_target_pairs={{0,2},{1,3},{2,0},{3,1},{4,6},{5,7},{6,4},{7,5},{8,10},{9,11},{10,... | collective-permute-start | bytes 1204232 | tf_op jit(solution)/shard_map/ppermute | solution.py:109
  121.0 2.6 %collective-permute-done.20 = bf16[112,2048]{1,0:T(8,128)(2,1)S(1)} collective-permute-done((bf16[112,2048]{1,0:T(8,128)(2,1)S(1)}, bf16[112,2048]{1,0:T(8,128)(2,1)S(1)}, u32[]{:S(2)}, u32[]{:S(2)}) %collective-permute-start.20) | collective-permute-done | bytes 458784 | tf_op jit(solution)/shard_map/ppermute | solution.py:11
  123.7 7.7 %collective-permute-done.22 = bf16[224,2048]{1,0:T(8,128)(2,1)S(1)} collective-permute-done((bf16[224,2048]{1,0:T(8,128)(2,1)S(1)}, bf16[224,2048]{1,0:T(8,128)(2,1)S(1)}, u32[]{:S(2)}, u32[]{:S(2)}) %collective-permute-start.22) | collective-permute-done | bytes 917536 | tf_op jit(solution)/shard_map/ppermute | solution.py:11
  133.0 2.3 %collective-permute-start.25 = (f32[896,112]{0,1:T(8,128)S(1)}, f32[896,112]{0,1:T(8,128)S(1)}, u32[]{:S(2)}, u32[]{:S(2)}) collective-permute-start(f32[896,112]{0,1:T(8,128)S(1)} %select_add_fusion.5), channel_id=1, source_target_pairs={{0,2},{1,3},{2,0},{3,1},{4,6},{5,7},{6,4},{7,5},{8,10},{9,11},{10,... | collective-permute-start | bytes 1204232 | tf_op jit(solution)/shard_map/ppermute | solution.py:109
  141.4 2.6 %collective-permute-done.24 = bf16[112,2048]{1,0:T(8,128)(2,1)S(1)} collective-permute-done((bf16[112,2048]{1,0:T(8,128)(2,1)S(1)}, bf16[112,2048]{1,0:T(8,128)(2,1)S(1)}, u32[]{:S(2)}, u32[]{:S(2)}) %collective-permute-start.24) | collective-permute-done | bytes 458784 | tf_op jit(solution)/shard_map/ppermute | solution.py:11
  144.0 7.0 %collective-permute-done.26 = bf16[224,2048]{1,0:T(8,128)(2,1)S(1)} collective-permute-done((bf16[224,2048]{1,0:T(8,128)(2,1)S(1)}, bf16[224,2048]{1,0:T(8,128)(2,1)S(1)}, u32[]{:S(2)}, u32[]{:S(2)}) %collective-permute-start.26) | collective-permute-done | bytes 917536 | tf_op jit(solution)/shard_map/ppermute | solution.py:11
  152.6 3.3 %collective-permute-start.29 = (f32[896,112]{0,1:T(8,128)S(1)}, f32[896,112]{0,1:T(8,128)S(1)}, u32[]{:S(2)}, u32[]{:S(2)}) collective-permute-start(f32[896,112]{0,1:T(8,128)S(1)} %select_add_fusion.4), channel_id=1, source_target_pairs={{0,2},{1,3},{2,0},{3,1},{4,6},{5,7},{6,4},{7,5},{8,10},{9,11},{10,... | collective-permute-start | bytes 1204232 | tf_op jit(solution)/shard_map/ppermute | solution.py:109
  161.9 2.6 %collective-permute-done.28 = bf16[112,2048]{1,0:T(8,128)(2,1)S(1)} collective-permute-done((bf16[112,2048]{1,0:T(8,128)(2,1)S(1)}, bf16[112,2048]{1,0:T(8,128)(2,1)S(1)}, u32[]{:S(2)}, u32[]{:S(2)}) %collective-permute-start.28) | collective-permute-done | bytes 458784 | tf_op jit(solution)/shard_map/ppermute | solution.py:11
  164.6 2.7 %collective-permute-done.30 = bf16[208,2048]{1,0:T(8,128)(2,1)S(1)} collective-permute-done((bf16[208,2048]{1,0:T(8,128)(2,1)S(1)}, bf16[208,2048]{1,0:T(8,128)(2,1)S(1)}, u32[]{:S(2)}, u32[]{:S(2)}) %collective-permute-start.30) | collective-permute-done | bytes 852000 | tf_op jit(solution)/shard_map/ppermute | solution.py:11
  171.7 3.9 %collective-permute-start.33 = (f32[896,112]{0,1:T(8,128)S(1)}, f32[896,112]{0,1:T(8,128)S(1)}, u32[]{:S(2)}, u32[]{:S(2)}) collective-permute-start(f32[896,112]{0,1:T(8,128)S(1)} %select_add_fusion.3), channel_id=1, source_target_pairs={{0,2},{1,3},{2,0},{3,1},{4,6},{5,7},{6,4},{7,5},{8,10},{9,11},{10,... | collective-permute-start | bytes 1204232 | tf_op jit(solution)/shard_map/ppermute | solution.py:109
  177.2 10.3 %collective-permute-done.32 = bf16[96,2048]{1,0:T(8,128)(2,1)S(1)} collective-permute-done((bf16[96,2048]{1,0:T(8,128)(2,1)S(1)}, bf16[96,2048]{1,0:T(8,128)(2,1)S(1)}, u32[]{:S(2)}, u32[]{:S(2)}) %collective-permute-start.32) | collective-permute-done | bytes 393248 | tf_op jit(solution)/shard_map/ppermute | solution.py:11
  187.9 5.9 %collective-permute-done.34 = f32[896,112]{0,1:T(8,128)S(1)} collective-permute-done((f32[896,112]{0,1:T(8,128)S(1)}, f32[896,112]{0,1:T(8,128)S(1)}, u32[]{:S(2)}, u32[]{:S(2)}) %collective-permute-start.34) | collective-permute-done | bytes 401440 | tf_op jit(solution)/shard_map/ppermute | solution.py:109
  196.3 2.1 fusion.48
  199.3 2.7 %collective-permute-start.40 = (f32[896,96]{0,1:T(8,128)S(1)}, f32[896,96]{0,1:T(8,128)S(1)}, u32[]{:S(2)}, u32[]{:S(2)}) collective-permute-start(f32[896,96]{0,1:T(8,128)S(1)} %select_add_fusion.7), channel_id=1, source_target_pairs={{0,2},{1,3},{2,0},{3,1},{4,6},{5,7},{6,4},{7,5},{8,10},{9,11},{10,... | collective-permute-start | bytes 1032200 | tf_op jit(solution)/shard_map/ppermute | solution.py:109
  204.0 6.9 %collective-permute-done.40 = f32[896,96]{0,1:T(8,128)S(1)} collective-permute-done((f32[896,96]{0,1:T(8,128)S(1)}, f32[896,96]{0,1:T(8,128)S(1)}, u32[]{:S(2)}, u32[]{:S(2)}) %collective-permute-start.40) | collective-permute-done | bytes 344096 | tf_op jit(solution)/shard_map/ppermute | solution.py:109
  211.1 7.8 %collective-permute-done.39 = f32[896,112]{0,1:T(8,128)S(1)} collective-permute-done((f32[896,112]{0,1:T(8,128)S(1)}, f32[896,112]{0,1:T(8,128)S(1)}, u32[]{:S(2)}, u32[]{:S(2)}) %collective-permute-start.39) | collective-permute-done | bytes 401440 | tf_op jit(solution)/shard_map/ppermute | solution.py:109
  219.6 3.0 %copy.2 = f32[896,896]{1,0:T(8,128)} copy(f32[896,896]{0,1:T(8,128)S(1)} %broadcast_multiply_fusion) | data formatting | bytes 6422528 | tf_op jit(solution)/shard_map/div | solution.py:148
  (179 shorter events, 66.2 us)
Async XLA Ops:
  3.7 13.9 %collective-permute-start.3 = (f32[2,768]{1,0:T(2,128)S(1)}, f32[2,768]{1,0:T(2,128)S(1)}, u32[]{:S(2)}, u32[]{:S(2)}) collective-permute-start(f32[2,768]{1,0:T(2,128)S(1)} %pad_maximum_fusion.7), channel_id=1, source_target_pairs={{0,3},{1,2},{2,1},{3,0},{4,7},{5,6},{6,5},{7,4},{8,11},{9,10},{10,... | collective-permute-start | bytes 18440 | tf_op jit(solution)/shard_map/ppermute | solution.py:55
  6.2 11.5 %collective-permute-start.4 = (f32[2,768]{1,0:T(2,128)S(1)}, f32[2,768]{1,0:T(2,128)S(1)}, u32[]{:S(2)}, u32[]{:S(2)}) collective-permute-start(f32[2,768]{1,0:T(2,128)S(1)} %pad_maximum_fusion.7), channel_id=1, source_target_pairs={{0,2},{1,3},{2,0},{3,1},{4,6},{5,7},{6,4},{7,5},{8,10},{9,11},{10,... | collective-permute-start | bytes 18440 | tf_op jit(solution)/shard_map/ppermute | solution.py:55
  14.7 12.8 %collective-permute-start.6 = (bf16[128,2048]{1,0:T(8,128)(2,1)S(1)}, bf16[128,2048]{1,0:T(8,128)(2,1)S(1)}, u32[]{:S(2)}, u32[]{:S(2)}) collective-permute-start(bf16[128,2048]{1,0:T(8,128)(2,1)S(1)} %multiply_convert_fusion.1), channel_id=1, source_target_pairs={{4,0},{12,8},{20,16},{28,24},{0,4},{8,12},{16,20},{24,28},{5,1},{1... | collective-permute-start | bytes 1572872 | tf_op jit(solution)/shard_map/ppermute | solution.py:11
  16.3 14.4 %collective-permute-start.7 = (bf16[128,2048]{1,0:T(8,128)(2,1)S(1)}, bf16[128,2048]{1,0:T(8,128)(2,1)S(1)}, u32[]{:S(2)}, u32[]{:S(2)}) collective-permute-start(bf16[128,2048]{1,0:T(8,128)(2,1)S(1)} %multiply_convert_fusion.1), channel_id=1, source_target_pairs={{8,0},{12,4},{16,8},{20,12},{24,16},{28,20},{9,1},{13,5},{17,9},{2... | collective-permute-start | bytes 1572872 | tf_op jit(solution)/shard_map/ppermute | solution.py:11
  30.8 11.6 %collective-permute-start.8 = (bf16[128,2048]{1,0:T(8,128)(2,1)S(1)}, bf16[128,2048]{1,0:T(8,128)(2,1)S(1)}, u32[]{:S(2)}, u32[]{:S(2)}) collective-permute-start(bf16[128,2048]{1,0:T(8,128)(2,1)S(1)} %pad_select_fusion), channel_id=1, source_target_pairs={{4,0},{12,8},{20,16},{28,24},{0,4},{8,12},{16,20},{24,28},{5,1},{1... | collective-permute-start | bytes 1572872 | tf_op jit(solution)/shard_map/ppermute | solution.py:11
  31.4 11.9 %collective-permute-start.9 = (bf16[112,2048]{1,0:T(8,128)(2,1)S(1)}, bf16[112,2048]{1,0:T(8,128)(2,1)S(1)}, u32[]{:S(2)}, u32[]{:S(2)}) collective-permute-start(bf16[112,2048]{1,0:T(8,128)(2,1)S(1)} %get-tuple-element.117), channel_id=1, source_target_pairs={{8,0},{12,4},{16,8},{20,12},{24,16},{28,20},{9,1},{13,5},{17,9},{2... | collective-permute-start | bytes 1376264 | tf_op jit(solution)/shard_map/ppermute | solution.py:11
  45.1 22.7 %collective-permute-start.11 = (bf16[240,2048]{1,0:T(8,128)(2,1)}, bf16[240,2048]{1,0:T(8,128)(2,1)}, u32[]{:S(2)}, u32[]{:S(2)}) collective-permute-start(bf16[240,2048]{1,0:T(8,128)(2,1)} %pad_maximum_fusion.1), channel_id=1, source_target_pairs={{8,0},{12,4},{16,8},{20,12},{24,16},{28,20},{9,1},{13,5},{17,9},{2... | collective-permute-start | bytes 2949128 | tf_op jit(solution)/shard_map/ppermute | solution.py:11
  47.2 9.6 %collective-permute-start.10 = (bf16[112,2048]{1,0:T(8,128)(2,1)}, bf16[112,2048]{1,0:T(8,128)(2,1)}, u32[]{:S(2)}, u32[]{:S(2)}) collective-permute-start(bf16[112,2048]{1,0:T(8,128)(2,1)} %broadcast_select_fusion.10), channel_id=1, source_target_pairs={{4,0},{12,8},{20,16},{28,24},{0,4},{8,12},{16,20},{24,28},{5,1},{1... | collective-permute-start | bytes 1376264 | tf_op jit(solution)/shard_map/ppermute | solution.py:11
  70.0 20.2 %collective-permute-start.14 = (bf16[224,2048]{1,0:T(8,128)(2,1)S(1)}, bf16[224,2048]{1,0:T(8,128)(2,1)S(1)}, u32[]{:S(2)}, u32[]{:S(2)}) collective-permute-start(bf16[224,2048]{1,0:T(8,128)(2,1)S(1)} %pad_maximum_fusion.2), channel_id=1, source_target_pairs={{8,0},{12,4},{16,8},{20,12},{24,16},{28,20},{9,1},{13,5},{17,9},{2... | collective-permute-start | bytes 2752520 | tf_op jit(solution)/shard_map/ppermute | solution.py:11
  71.3 8.5 %collective-permute-start.13 = (bf16[112,2048]{1,0:T(8,128)(2,1)S(1)}, bf16[112,2048]{1,0:T(8,128)(2,1)S(1)}, u32[]{:S(2)}, u32[]{:S(2)}) collective-permute-start(bf16[112,2048]{1,0:T(8,128)(2,1)S(1)} %broadcast_select_fusion.9), channel_id=1, source_target_pairs={{4,0},{12,8},{20,16},{28,24},{0,4},{8,12},{16,20},{24,28},{5,1},{1... | collective-permute-start | bytes 1376264 | tf_op jit(solution)/shard_map/ppermute | solution.py:11
  74.6 15.7 %collective-permute-start.12 = (f32[896,256]{0,1:T(8,128)S(1)}, f32[896,256]{0,1:T(8,128)S(1)}, u32[]{:S(2)}, u32[]{:S(2)}) collective-permute-start(f32[896,256]{0,1:T(8,128)S(1)} %maximum_select_fusion), channel_id=1, source_target_pairs={{0,1},{1,0},{2,3},{3,2},{4,5},{5,4},{6,7},{7,6},{8,9},{9,8},{10,11... | collective-permute-start | bytes 2752520 | tf_op jit(solution)/shard_map/ppermute | solution.py:96
  90.4 20.3 %collective-permute-start.18 = (bf16[224,2048]{1,0:T(8,128)(2,1)S(1)}, bf16[224,2048]{1,0:T(8,128)(2,1)S(1)}, u32[]{:S(2)}, u32[]{:S(2)}) collective-permute-start(bf16[224,2048]{1,0:T(8,128)(2,1)S(1)} %pad_maximum_fusion.3), channel_id=1, source_target_pairs={{8,0},{12,4},{16,8},{20,12},{24,16},{28,20},{9,1},{13,5},{17,9},{2... | collective-permute-start | bytes 2752520 | tf_op jit(solution)/shard_map/ppermute | solution.py:11
  92.0 11.0 %collective-permute-start.17 = (f32[896,128]{0,1:T(8,128)S(1)}, f32[896,128]{0,1:T(8,128)S(1)}, u32[]{:S(2)}, u32[]{:S(2)}) collective-permute-start(f32[896,128]{0,1:T(8,128)S(1)} %select_add_fusion), channel_id=1, source_target_pairs={{0,2},{1,3},{2,0},{3,1},{4,6},{5,7},{6,4},{7,5},{8,10},{9,11},{10,... | collective-permute-start | bytes 1376264 | tf_op jit(solution)/shard_map/ppermute | solution.py:109
  94.4 8.5 %collective-permute-start.16 = (bf16[112,2048]{1,0:T(8,128)(2,1)S(1)}, bf16[112,2048]{1,0:T(8,128)(2,1)S(1)}, u32[]{:S(2)}, u32[]{:S(2)}) collective-permute-start(bf16[112,2048]{1,0:T(8,128)(2,1)S(1)} %broadcast_select_fusion.7), channel_id=1, source_target_pairs={{4,0},{12,8},{20,16},{28,24},{0,4},{8,12},{16,20},{24,28},{5,1},{1... | collective-permute-start | bytes 1376264 | tf_op jit(solution)/shard_map/ppermute | solution.py:11
  98.0 12.8 %collective-permute-start.15 = (f32[896,224]{0,1:T(8,128)S(1)}, f32[896,224]{0,1:T(8,128)S(1)}, u32[]{:S(2)}, u32[]{:S(2)}) collective-permute-start(f32[896,224]{0,1:T(8,128)S(1)} %maximum_select_fusion.1), channel_id=1, source_target_pairs={{0,1},{1,0},{2,3},{3,2},{4,5},{5,4},{6,7},{7,6},{8,9},{9,8},{10,11... | collective-permute-start | bytes 2408456 | tf_op jit(solution)/shard_map/ppermute | solution.py:96
  110.9 20.5 %collective-permute-start.22 = (bf16[224,2048]{1,0:T(8,128)(2,1)S(1)}, bf16[224,2048]{1,0:T(8,128)(2,1)S(1)}, u32[]{:S(2)}, u32[]{:S(2)}) collective-permute-start(bf16[224,2048]{1,0:T(8,128)(2,1)S(1)} %pad_maximum_fusion.4), channel_id=1, source_target_pairs={{8,0},{12,4},{16,8},{20,12},{24,16},{28,20},{9,1},{13,5},{17,9},{2... | collective-permute-start | bytes 2752520 | tf_op jit(solution)/shard_map/ppermute | solution.py:11
  112.7 8.2 %collective-permute-start.21 = (f32[896,112]{0,1:T(8,128)S(1)}, f32[896,112]{0,1:T(8,128)S(1)}, u32[]{:S(2)}, u32[]{:S(2)}) collective-permute-start(f32[896,112]{0,1:T(8,128)S(1)} %select_add_fusion.6), channel_id=1, source_target_pairs={{0,2},{1,3},{2,0},{3,1},{4,6},{5,7},{6,4},{7,5},{8,10},{9,11},{10,... | collective-permute-start | bytes 1204232 | tf_op jit(solution)/shard_map/ppermute | solution.py:109
  115.1 8.5 %collective-permute-start.20 = (bf16[112,2048]{1,0:T(8,128)(2,1)S(1)}, bf16[112,2048]{1,0:T(8,128)(2,1)S(1)}, u32[]{:S(2)}, u32[]{:S(2)}) collective-permute-start(bf16[112,2048]{1,0:T(8,128)(2,1)S(1)} %broadcast_select_fusion.5), channel_id=1, source_target_pairs={{4,0},{12,8},{20,16},{28,24},{0,4},{8,12},{16,20},{24,28},{5,1},{1... | collective-permute-start | bytes 1376264 | tf_op jit(solution)/shard_map/ppermute | solution.py:11
  118.7 12.7 %collective-permute-start.19 = (f32[896,224]{0,1:T(8,128)S(1)}, f32[896,224]{0,1:T(8,128)S(1)}, u32[]{:S(2)}, u32[]{:S(2)}) collective-permute-start(f32[896,224]{0,1:T(8,128)S(1)} %maximum_select_fusion.2), channel_id=1, source_target_pairs={{0,1},{1,0},{2,3},{3,2},{4,5},{5,4},{6,7},{7,6},{8,9},{9,8},{10,11... | collective-permute-start | bytes 2408456 | tf_op jit(solution)/shard_map/ppermute | solution.py:96
  131.5 19.4 %collective-permute-start.26 = (bf16[224,2048]{1,0:T(8,128)(2,1)S(1)}, bf16[224,2048]{1,0:T(8,128)(2,1)S(1)}, u32[]{:S(2)}, u32[]{:S(2)}) collective-permute-start(bf16[224,2048]{1,0:T(8,128)(2,1)S(1)} %pad_maximum_fusion.5), channel_id=1, source_target_pairs={{8,0},{12,4},{16,8},{20,12},{24,16},{28,20},{9,1},{13,5},{17,9},{2... | collective-permute-start | bytes 2752520 | tf_op jit(solution)/shard_map/ppermute | solution.py:11
  135.4 8.5 %collective-permute-start.24 = (bf16[112,2048]{1,0:T(8,128)(2,1)S(1)}, bf16[112,2048]{1,0:T(8,128)(2,1)S(1)}, u32[]{:S(2)}, u32[]{:S(2)}) collective-permute-start(bf16[112,2048]{1,0:T(8,128)(2,1)S(1)} %broadcast_select_fusion.3), channel_id=1, source_target_pairs={{4,0},{12,8},{20,16},{28,24},{0,4},{8,12},{16,20},{24,28},{5,1},{1... | collective-permute-start | bytes 1376264 | tf_op jit(solution)/shard_map/ppermute | solution.py:11
  139.0 12.0 %collective-permute-start.23 = (f32[896,224]{0,1:T(8,128)S(1)}, f32[896,224]{0,1:T(8,128)S(1)}, u32[]{:S(2)}, u32[]{:S(2)}) collective-permute-start(f32[896,224]{0,1:T(8,128)S(1)} %maximum_select_fusion.3), channel_id=1, source_target_pairs={{0,1},{1,0},{2,3},{3,2},{4,5},{5,4},{6,7},{7,6},{8,9},{9,8},{10,11... | collective-permute-start | bytes 2408456 | tf_op jit(solution)/shard_map/ppermute | solution.py:96
  151.1 16.2 %collective-permute-start.30 = (bf16[208,2048]{1,0:T(8,128)(2,1)S(1)}, bf16[208,2048]{1,0:T(8,128)(2,1)S(1)}, u32[]{:S(2)}, u32[]{:S(2)}) collective-permute-start(bf16[208,2048]{1,0:T(8,128)(2,1)S(1)} %pad_maximum_fusion.6), channel_id=1, source_target_pairs={{8,0},{12,4},{16,8},{20,12},{24,16},{28,20},{9,1},{13,5},{17,9},{2... | collective-permute-start | bytes 2555912 | tf_op jit(solution)/shard_map/ppermute | solution.py:11
  152.6 9.1 %collective-permute-start.29 = (f32[896,112]{0,1:T(8,128)S(1)}, f32[896,112]{0,1:T(8,128)S(1)}, u32[]{:S(2)}, u32[]{:S(2)}) collective-permute-start(f32[896,112]{0,1:T(8,128)S(1)} %select_add_fusion.4), channel_id=1, source_target_pairs={{0,2},{1,3},{2,0},{3,1},{4,6},{5,7},{6,4},{7,5},{8,10},{9,11},{10,... | collective-permute-start | bytes 1204232 | tf_op jit(solution)/shard_map/ppermute | solution.py:109
  156.0 8.5 %collective-permute-start.28 = (bf16[112,2048]{1,0:T(8,128)(2,1)S(1)}, bf16[112,2048]{1,0:T(8,128)(2,1)S(1)}, u32[]{:S(2)}, u32[]{:S(2)}) collective-permute-start(bf16[112,2048]{1,0:T(8,128)(2,1)S(1)} %pad_select_fusion.1), channel_id=1, source_target_pairs={{4,0},{12,8},{20,16},{28,24},{0,4},{8,12},{16,20},{24,28},{5,1},{1... | collective-permute-start | bytes 1376264 | tf_op jit(solution)/shard_map/ppermute | solution.py:11
  169.7 17.9 %collective-permute-start.32 = (bf16[96,2048]{1,0:T(8,128)(2,1)S(1)}, bf16[96,2048]{1,0:T(8,128)(2,1)S(1)}, u32[]{:S(2)}, u32[]{:S(2)}) collective-permute-start(bf16[96,2048]{1,0:T(8,128)(2,1)S(1)} %slice.362), channel_id=1, source_target_pairs={{4,0},{12,8},{20,16},{28,24},{0,4},{8,12},{16,20},{24,28},{5,1},{1... | collective-permute-start | bytes 1179656 | tf_op jit(solution)/shard_map/ppermute | solution.py:11
  170.2 23.7 %collective-permute-start.36 = (bf16[96,2048]{1,0:T(8,128)(2,1)S(1)}, bf16[96,2048]{1,0:T(8,128)(2,1)S(1)}, u32[]{:S(2)}, u32[]{:S(2)}) collective-permute-start(bf16[96,2048]{1,0:T(8,128)(2,1)S(1)} %slice.362), channel_id=1, source_target_pairs={{4,0},{8,4},{12,8},{16,12},{20,16},{24,20},{28,24},{5,1},{9,5},{13... | collective-permute-start | bytes 1179656 | tf_op jit(solution)/shard_map/ppermute | solution.py:11
  171.7 16.0 %collective-permute-start.33 = (f32[896,112]{0,1:T(8,128)S(1)}, f32[896,112]{0,1:T(8,128)S(1)}, u32[]{:S(2)}, u32[]{:S(2)}) collective-permute-start(f32[896,112]{0,1:T(8,128)S(1)} %select_add_fusion.3), channel_id=1, source_target_pairs={{0,2},{1,3},{2,0},{3,1},{4,6},{5,7},{6,4},{7,5},{8,10},{9,11},{10,... | collective-permute-start | bytes 1204232 | tf_op jit(solution)/shard_map/ppermute | solution.py:109
  175.5 18.7 %collective-permute-start.35 = (bf16[112,2048]{1,0:T(8,128)(2,1)S(1)}, bf16[112,2048]{1,0:T(8,128)(2,1)S(1)}, u32[]{:S(2)}, u32[]{:S(2)}) collective-permute-start(bf16[112,2048]{1,0:T(8,128)(2,1)S(1)} %broadcast_select_fusion.1), channel_id=1, source_target_pairs={{8,0},{12,4},{16,8},{20,12},{24,16},{28,20},{9,1},{13,5},{17,9},{2... | collective-permute-start | bytes 1376264 | tf_op jit(solution)/shard_map/ppermute | solution.py:11
  177.2 16.6 %collective-permute-start.34 = (f32[896,112]{0,1:T(8,128)S(1)}, f32[896,112]{0,1:T(8,128)S(1)}, u32[]{:S(2)}, u32[]{:S(2)}) collective-permute-start(f32[896,112]{0,1:T(8,128)S(1)} %select_add_fusion.2), channel_id=1, source_target_pairs={{0,2},{1,3},{2,0},{3,1},{4,6},{5,7},{6,4},{7,5},{8,10},{9,11},{10,... | collective-permute-start | bytes 1204232 | tf_op jit(solution)/shard_map/ppermute | solution.py:109
  199.3 11.6 %collective-permute-start.40 = (f32[896,96]{0,1:T(8,128)S(1)}, f32[896,96]{0,1:T(8,128)S(1)}, u32[]{:S(2)}, u32[]{:S(2)}) collective-permute-start(f32[896,96]{0,1:T(8,128)S(1)} %select_add_fusion.7), channel_id=1, source_target_pairs={{0,2},{1,3},{2,0},{3,1},{4,6},{5,7},{6,4},{7,5},{8,10},{9,11},{10,... | collective-permute-start | bytes 1032200 | tf_op jit(solution)/shard_map/ppermute | solution.py:109
  202.2 16.7 %collective-permute-start.39 = (f32[896,112]{0,1:T(8,128)S(1)}, f32[896,112]{0,1:T(8,128)S(1)}, u32[]{:S(2)}, u32[]{:S(2)}) collective-permute-start(f32[896,112]{0,1:T(8,128)S(1)} %select_add_fusion.1), channel_id=1, source_target_pairs={{0,2},{1,3},{2,0},{3,1},{4,6},{5,7},{6,4},{7,5},{8,10},{9,11},{10,... | collective-permute-start | bytes 1204232 | tf_op jit(solution)/shard_map/ppermute | solution.py:109
  (26 other events, 274.8 us)

commit v13 on v12

--- a/solution.py
+++ b/solution.py
@@ -94,7 +94,7 @@
         payload = jnp.where(even_me, jnp.concatenate([tiles[1], tiles[3]], axis=1),
                             jnp.concatenate([tiles[0], tiles[2]], axis=1))
         state["first"][c] = lax.ppermute(payload, "samp", partner)
-        if c >= CHUNKS - 3:
+        if c >= CHUNKS - 4:
             second_level(c)
 
     def pick(c, a, b, d, e):
@@ -136,7 +136,7 @@
             state["three"][second] = moved(state["two"][second], one_down)
         for c in [c for c in range(CHUNKS) if ready[c] == t]:
             finish(c)
-        if 0 <= t - 4 < CHUNKS - 3:
+        if 0 <= t - 4 < CHUNKS - 4:
             second_level(t - 4)
         flat, tree = jax.tree.flatten(state)
         following = pieces[t + 1] if t + 1 < CHUNKS else own_block[:8]

time: 223 us -> 236 us (1.058)
  waiting for transfers between devices: 129 us -> 142 us
    ppermute x8, waiting for transfers between devices: 26.8 us -> 36 us  [second_level(): last = lax.ppermute(pick(c, 2, 3, 0, 1) + onward, 'samp', across)]
    ppermute x19, waiting for transfers between devices: 99.2 us -> 103 us  [moved(): return lax.ppermute(value, 'snp', pairs)]
  transfers between devices with their start and end apart: 41 -> 41, of which waited for: 25 -> 26; matrix products, arithmetic and copies ran while one was open for 13% -> 12% of each run, Pallas kernels for 0% -> 0%
where the time goes in v13:
time: 236 us; the launch traced here: 235 us
  waiting for transfers between devices  142 us (60%)
  starting transfers between devices  46.7 us (20%)
  other arithmetic  18.7 us (8%)
  matrix products  16.8 us (7%)
  local copies, waits for them, and re-layouts  9.46 us (4%)
    ppermute x19, waiting for transfers between devices, moved(): return lax.ppermute(value, 'snp', pairs)  103 us
    ppermute x8, waiting for transfers between devices, second_level(): last = lax.ppermute(pick(c, 2, 3, 0, 1) + onward, 'samp', across)  36 us
    ppermute x19, starting transfers between devices, moved(): return lax.ppermute(value, 'snp', pairs)  23.6 us
    ppermute x8, starting transfers between devices, second_level(): last = lax.ppermute(pick(c, 2, 3, 0, 1) + onward, 'samp', across)  16.9 us
    dot_general x8, matrix products, finish(): jnp.einsum('ab,cb->ac', own_block, blocks, preferred_element_type=jnp.flo...  16.8 us
    ppermute x6, starting transfers between devices, standard_rows(): lax.ppermute(moments, 'samp', [(j, j ^ i) for j in range(groups)])  5.12 us
    reduce_sum x2, other arithmetic, local_moments(): return (jnp.sum(values, axis=1), jnp.sum(values * values, axis=1))  5.07 us
    convert_element_type x2, other arithmetic, standardize(): ((values - mean[:, None]) * lax.rsqrt(variance + 1e-05)[:, None]).astype(...  4.84 us
  transfers between devices with their start and end apart: 41, of which 26 were waited for; matrix products, arithmetic and copies ran while one was open for 12% of the time, Pallas kernels for 0%

profile of v13, /device:TPU:0, one launch (start us, length us, event | category | flops | bytes accessed | tf_op | source)
XLA Modules:
  0.0 234.8 jit_solution(10184140933452557309)
XLA Ops:
  0.0 3.7 %slice_reduce_fusion = (f32[768]{0:T(1024)S(1)}, f32[768]{0:T(1024)S(1)}) fusion(f32[896,2048]{1,0:T(8,128)} %param.1), kind=kLoop, calls=%fused_computation.2 | loop fusion | flops 4717056 | bytes 6297600 | tf_op jit(solution)/shard_map/reduce_sum | solution.py:21
  3.7 2.4 %collective-permute-start.3 = (f32[2,768]{1,0:T(2,128)S(1)}, f32[2,768]{1,0:T(2,128)S(1)}, u32[]{:S(2)}, u32[]{:S(2)}) collective-permute-start(f32[2,768]{1,0:T(2,128)S(1)} %pad_maximum_fusion.7), channel_id=1, source_target_pairs={{0,3},{1,2},{2,1},{3,0},{4,7},{5,6},{6,5},{7,4},{8,11},{9,10},{10,... | collective-permute-start | bytes 18440 | tf_op jit(solution)/shard_map/ppermute | solution.py:55
  17.7 3.4 %multiply_convert_fusion = bf16[768,2048]{1,0:T(8,128)(2,1)S(1)} fusion(f32[896,2048]{1,0:T(8,128)} %param.1, f32[768]{0:T(1024)S(1)} %add_rsqrt_fusion, f32[768]{0:T(1024)S(1)} %get-tuple-element.221), kind=kLoop, calls=%fused_computation | loop fusion | flops 4718592 | bytes 9443328 | tf_op jit(solution)/shard_map/convert_element_type | solution.py:17
  22.5 5.1 %collective-permute-done.6 = bf16[128,2048]{1,0:T(8,128)(2,1)S(1)} collective-permute-done((bf16[128,2048]{1,0:T(8,128)(2,1)S(1)}, bf16[128,2048]{1,0:T(8,128)(2,1)S(1)}, u32[]{:S(2)}, u32[]{:S(2)}) %collective-permute-start.6) | collective-permute-done | bytes 524320 | tf_op jit(solution)/shard_map/ppermute | solution.py:11
  27.5 3.1 %collective-permute-done.7 = bf16[128,2048]{1,0:T(8,128)(2,1)S(1)} collective-permute-done((bf16[128,2048]{1,0:T(8,128)(2,1)S(1)}, bf16[128,2048]{1,0:T(8,128)(2,1)S(1)}, u32[]{:S(2)}, u32[]{:S(2)}) %collective-permute-start.7) | collective-permute-done | bytes 524320 | tf_op jit(solution)/shard_map/ppermute | solution.py:11
  32.7 9.8 %collective-permute-done.8 = bf16[128,2048]{1,0:T(8,128)(2,1)S(1)} collective-permute-done((bf16[128,2048]{1,0:T(8,128)(2,1)S(1)}, bf16[128,2048]{1,0:T(8,128)(2,1)S(1)}, u32[]{:S(2)}, u32[]{:S(2)}) %collective-permute-start.8) | collective-permute-done | bytes 524320 | tf_op jit(solution)/shard_map/ppermute | solution.py:11
  48.0 8.9 %collective-permute-done.10 = bf16[112,2048]{1,0:T(8,128)(2,1)} collective-permute-done((bf16[112,2048]{1,0:T(8,128)(2,1)}, bf16[112,2048]{1,0:T(8,128)(2,1)}, u32[]{:S(2)}, u32[]{:S(2)}) %collective-permute-start.10) | collective-permute-done | bytes 458784 | tf_op jit(solution)/shard_map/ppermute | solution.py:11
  57.9 9.9 %collective-permute-done.11 = bf16[240,2048]{1,0:T(8,128)(2,1)} collective-permute-done((bf16[240,2048]{1,0:T(8,128)(2,1)}, bf16[240,2048]{1,0:T(8,128)(2,1)}, u32[]{:S(2)}, u32[]{:S(2)}) %collective-permute-start.11) | collective-permute-done | bytes 983072 | tf_op jit(solution)/shard_map/ppermute | solution.py:11
  71.9 2.4 %fusion = f32[896,512]{0,1:T(8,128)S(1)} fusion(bf16[128,2048]{1,0:T(8,128)(2,1)S(1)} %slice.326, bf16[128,2048]{1,0:T(8,128)(2,1)S(1)} %copy-done.12, bf16[128,2048]{1,0:T(8,128)(2,1)S(1)} %copy-done.7, bf16[128,2048]{1,0:T(8,128)(2,1)S(1)} %copy-done.14, bf16[768,2048]{1,0:T(8,128)(2,1)S(1)} %multiply_convert_fusion), kind=kOutput, calls=%fused_computation.4 | convolution fusion | flops 1894776832 | bytes 7077888 | tf_op jit(solution)/shard_map/ab,cb->ac/dot_general | solution.py:90
  74.6 5.3 %collective-permute-done.13 = bf16[112,2048]{1,0:T(8,128)(2,1)S(1)} collective-permute-done((bf16[112,2048]{1,0:T(8,128)(2,1)S(1)}, bf16[112,2048]{1,0:T(8,128)(2,1)S(1)}, u32[]{:S(2)}, u32[]{:S(2)}) %collective-permute-start.13) | collective-permute-done | bytes 458784 | tf_op jit(solution)/shard_map/ppermute | solution.py:11
  81.0 9.2 %collective-permute-done.14 = bf16[224,2048]{1,0:T(8,128)(2,1)S(1)} collective-permute-done((bf16[224,2048]{1,0:T(8,128)(2,1)S(1)}, bf16[224,2048]{1,0:T(8,128)(2,1)S(1)}, u32[]{:S(2)}, u32[]{:S(2)}) %collective-permute-start.14) | collective-permute-done | bytes 917536 | tf_op jit(solution)/shard_map/ppermute | solution.py:11
  92.0 2.3 collective-permute-start.17
  95.7 2.1 fusion.8
  98.1 4.8 %collective-permute-done.16 = bf16[112,2048]{1,0:T(8,128)(2,1)S(1)} collective-permute-done((bf16[112,2048]{1,0:T(8,128)(2,1)S(1)}, bf16[112,2048]{1,0:T(8,128)(2,1)S(1)}, u32[]{:S(2)}, u32[]{:S(2)}) %collective-permute-start.16) | collective-permute-done | bytes 458784 | tf_op jit(solution)/shard_map/ppermute | solution.py:11
  103.2 7.5 %collective-permute-done.18 = bf16[224,2048]{1,0:T(8,128)(2,1)S(1)} collective-permute-done((bf16[224,2048]{1,0:T(8,128)(2,1)S(1)}, bf16[224,2048]{1,0:T(8,128)(2,1)S(1)}, u32[]{:S(2)}, u32[]{:S(2)}) %collective-permute-start.18) | collective-permute-done | bytes 917536 | tf_op jit(solution)/shard_map/ppermute | solution.py:11
  112.7 2.3 collective-permute-start.21
  121.0 2.6 %collective-permute-done.20 = bf16[112,2048]{1,0:T(8,128)(2,1)S(1)} collective-permute-done((bf16[112,2048]{1,0:T(8,128)(2,1)S(1)}, bf16[112,2048]{1,0:T(8,128)(2,1)S(1)}, u32[]{:S(2)}, u32[]{:S(2)}) %collective-permute-start.20) | collective-permute-done | bytes 458784 | tf_op jit(solution)/shard_map/ppermute | solution.py:11
  123.7 7.7 %collective-permute-done.22 = bf16[224,2048]{1,0:T(8,128)(2,1)S(1)} collective-permute-done((bf16[224,2048]{1,0:T(8,128)(2,1)S(1)}, bf16[224,2048]{1,0:T(8,128)(2,1)S(1)}, u32[]{:S(2)}, u32[]{:S(2)}) %collective-permute-start.22) | collective-permute-done | bytes 917536 | tf_op jit(solution)/shard_map/ppermute | solution.py:11
  133.0 2.3 collective-permute-start.25
  141.4 2.6 %collective-permute-done.24 = bf16[112,2048]{1,0:T(8,128)(2,1)S(1)} collective-permute-done((bf16[112,2048]{1,0:T(8,128)(2,1)S(1)}, bf16[112,2048]{1,0:T(8,128)(2,1)S(1)}, u32[]{:S(2)}, u32[]{:S(2)}) %collective-permute-start.24) | collective-permute-done | bytes 458784 | tf_op jit(solution)/shard_map/ppermute | solution.py:11
  144.0 7.0 %collective-permute-done.26 = bf16[224,2048]{1,0:T(8,128)(2,1)S(1)} collective-permute-done((bf16[224,2048]{1,0:T(8,128)(2,1)S(1)}, bf16[224,2048]{1,0:T(8,128)(2,1)S(1)}, u32[]{:S(2)}, u32[]{:S(2)}) %collective-permute-start.26) | collective-permute-done | bytes 917536 | tf_op jit(solution)/shard_map/ppermute | solution.py:11
  152.4 2.1 fusion.32
  154.9 3.3 %collective-permute-start.29 = (f32[896,112]{0,1:T(8,128)S(1)}, f32[896,112]{0,1:T(8,128)S(1)}, u32[]{:S(2)}, u32[]{:S(2)}) collective-permute-start(f32[896,112]{0,1:T(8,128)S(1)} %select_add_fusion.4), channel_id=1, source_target_pairs={{0,2},{1,3},{2,0},{3,1},{4,6},{5,7},{6,4},{7,5},{8,10},{9,11},{10,... | collective-permute-start | bytes 1204232 | tf_op jit(solution)/shard_map/ppermute | solution.py:109
  159.7 8.5 %collective-permute-done.29 = f32[896,112]{0,1:T(8,128)S(1)} collective-permute-done((f32[896,112]{0,1:T(8,128)S(1)}, f32[896,112]{0,1:T(8,128)S(1)}, u32[]{:S(2)}, u32[]{:S(2)}) %collective-permute-start.29) | collective-permute-done | bytes 401440 | tf_op jit(solution)/shard_map/ppermute | solution.py:109
  171.2 8.4 %collective-permute-done.30 = f32[896,112]{0,1:T(8,128)S(1)} collective-permute-done((f32[896,112]{0,1:T(8,128)S(1)}, f32[896,112]{0,1:T(8,128)S(1)}, u32[]{:S(2)}, u32[]{:S(2)}) %collective-permute-start.30) | collective-permute-done | bytes 401440 | tf_op jit(solution)/shard_map/ppermute | solution.py:109
  179.8 2.1 fusion.40
  188.1 12.8 %collective-permute-done.33 = bf16[96,2048]{1,0:T(8,128)(2,1)S(1)} collective-permute-done((bf16[96,2048]{1,0:T(8,128)(2,1)S(1)}, bf16[96,2048]{1,0:T(8,128)(2,1)S(1)}, u32[]{:S(2)}, u32[]{:S(2)}) %collective-permute-start.33) | collective-permute-done | bytes 393248 | tf_op jit(solution)/shard_map/ppermute | solution.py:11
  202.1 5.2 %collective-permute-done.35 = bf16[112,2048]{1,0:T(8,128)(2,1)S(1)} collective-permute-done((bf16[112,2048]{1,0:T(8,128)(2,1)S(1)}, bf16[112,2048]{1,0:T(8,128)(2,1)S(1)}, u32[]{:S(2)}, u32[]{:S(2)}) %collective-permute-start.35) | collective-permute-done | bytes 458784 | tf_op jit(solution)/shard_map/ppermute | solution.py:11
  209.5 2.1 fusion.48
  216.1 7.4 %collective-permute-done.40 = f32[896,96]{0,1:T(8,128)S(1)} collective-permute-done((f32[896,96]{0,1:T(8,128)S(1)}, f32[896,96]{0,1:T(8,128)S(1)}, u32[]{:S(2)}, u32[]{:S(2)}) %collective-permute-start.40) | collective-permute-done | bytes 344096 | tf_op jit(solution)/shard_map/ppermute | solution.py:109
  223.7 7.5 %collective-permute-done.39 = f32[896,112]{0,1:T(8,128)S(1)} collective-permute-done((f32[896,112]{0,1:T(8,128)S(1)}, f32[896,112]{0,1:T(8,128)S(1)}, u32[]{:S(2)}, u32[]{:S(2)}) %collective-permute-start.39) | collective-permute-done | bytes 401440 | tf_op jit(solution)/shard_map/ppermute | solution.py:109
  231.9 3.0 %copy.2 = f32[896,896]{1,0:T(8,128)} copy(f32[896,896]{0,1:T(8,128)S(1)} %broadcast_multiply_fusion) | data formatting | bytes 6422528 | tf_op jit(solution)/shard_map/div | solution.py:148
  (179 shorter events, 67.2 us)
Async XLA Ops:
  3.7 13.9 %collective-permute-start.3 = (f32[2,768]{1,0:T(2,128)S(1)}, f32[2,768]{1,0:T(2,128)S(1)}, u32[]{:S(2)}, u32[]{:S(2)}) collective-permute-start(f32[2,768]{1,0:T(2,128)S(1)} %pad_maximum_fusion.7), channel_id=1, source_target_pairs={{0,3},{1,2},{2,1},{3,0},{4,7},{5,6},{6,5},{7,4},{8,11},{9,10},{10,... | collective-permute-start | bytes 18440 | tf_op jit(solution)/shard_map/ppermute | solution.py:55
  6.2 11.5 %collective-permute-start.4 = (f32[2,768]{1,0:T(2,128)S(1)}, f32[2,768]{1,0:T(2,128)S(1)}, u32[]{:S(2)}, u32[]{:S(2)}) collective-permute-start(f32[2,768]{1,0:T(2,128)S(1)} %pad_maximum_fusion.7), channel_id=1, source_target_pairs={{0,2},{1,3},{2,0},{3,1},{4,6},{5,7},{6,4},{7,5},{8,10},{9,11},{10,... | collective-permute-start | bytes 18440 | tf_op jit(solution)/shard_map/ppermute | solution.py:55
  14.7 12.8 %collective-permute-start.6 = (bf16[128,2048]{1,0:T(8,128)(2,1)S(1)}, bf16[128,2048]{1,0:T(8,128)(2,1)S(1)}, u32[]{:S(2)}, u32[]{:S(2)}) collective-permute-start(bf16[128,2048]{1,0:T(8,128)(2,1)S(1)} %multiply_convert_fusion.1), channel_id=1, source_target_pairs={{4,0},{12,8},{20,16},{28,24},{0,4},{8,12},{16,20},{24,28},{5,1},{1... | collective-permute-start | bytes 1572872 | tf_op jit(solution)/shard_map/ppermute | solution.py:11
  16.3 14.4 %collective-permute-start.7 = (bf16[128,2048]{1,0:T(8,128)(2,1)S(1)}, bf16[128,2048]{1,0:T(8,128)(2,1)S(1)}, u32[]{:S(2)}, u32[]{:S(2)}) collective-permute-start(bf16[128,2048]{1,0:T(8,128)(2,1)S(1)} %multiply_convert_fusion.1), channel_id=1, source_target_pairs={{8,0},{12,4},{16,8},{20,12},{24,16},{28,20},{9,1},{13,5},{17,9},{2... | collective-permute-start | bytes 1572872 | tf_op jit(solution)/shard_map/ppermute | solution.py:11
  30.8 11.6 %collective-permute-start.8 = (bf16[128,2048]{1,0:T(8,128)(2,1)S(1)}, bf16[128,2048]{1,0:T(8,128)(2,1)S(1)}, u32[]{:S(2)}, u32[]{:S(2)}) collective-permute-start(bf16[128,2048]{1,0:T(8,128)(2,1)S(1)} %pad_select_fusion), channel_id=1, source_target_pairs={{4,0},{12,8},{20,16},{28,24},{0,4},{8,12},{16,20},{24,28},{5,1},{1... | collective-permute-start | bytes 1572872 | tf_op jit(solution)/shard_map/ppermute | solution.py:11
  31.4 11.9 %collective-permute-start.9 = (bf16[112,2048]{1,0:T(8,128)(2,1)S(1)}, bf16[112,2048]{1,0:T(8,128)(2,1)S(1)}, u32[]{:S(2)}, u32[]{:S(2)}) collective-permute-start(bf16[112,2048]{1,0:T(8,128)(2,1)S(1)} %get-tuple-element.113), channel_id=1, source_target_pairs={{8,0},{12,4},{16,8},{20,12},{24,16},{28,20},{9,1},{13,5},{17,9},{2... | collective-permute-start | bytes 1376264 | tf_op jit(solution)/shard_map/ppermute | solution.py:11
  45.1 22.7 %collective-permute-start.11 = (bf16[240,2048]{1,0:T(8,128)(2,1)}, bf16[240,2048]{1,0:T(8,128)(2,1)}, u32[]{:S(2)}, u32[]{:S(2)}) collective-permute-start(bf16[240,2048]{1,0:T(8,128)(2,1)} %pad_maximum_fusion.1), channel_id=1, source_target_pairs={{8,0},{12,4},{16,8},{20,12},{24,16},{28,20},{9,1},{13,5},{17,9},{2... | collective-permute-start | bytes 2949128 | tf_op jit(solution)/shard_map/ppermute | solution.py:11
  47.2 9.6 %collective-permute-start.10 = (bf16[112,2048]{1,0:T(8,128)(2,1)}, bf16[112,2048]{1,0:T(8,128)(2,1)}, u32[]{:S(2)}, u32[]{:S(2)}) collective-permute-start(bf16[112,2048]{1,0:T(8,128)(2,1)} %broadcast_select_fusion.10), channel_id=1, source_target_pairs={{4,0},{12,8},{20,16},{28,24},{0,4},{8,12},{16,20},{24,28},{5,1},{1... | collective-permute-start | bytes 1376264 | tf_op jit(solution)/shard_map/ppermute | solution.py:11
  70.0 20.2 %collective-permute-start.14 = (bf16[224,2048]{1,0:T(8,128)(2,1)S(1)}, bf16[224,2048]{1,0:T(8,128)(2,1)S(1)}, u32[]{:S(2)}, u32[]{:S(2)}) collective-permute-start(bf16[224,2048]{1,0:T(8,128)(2,1)S(1)} %pad_maximum_fusion.2), channel_id=1, source_target_pairs={{8,0},{12,4},{16,8},{20,12},{24,16},{28,20},{9,1},{13,5},{17,9},{2... | collective-permute-start | bytes 2752520 | tf_op jit(solution)/shard_map/ppermute | solution.py:11
  71.3 8.5 %collective-permute-start.13 = (bf16[112,2048]{1,0:T(8,128)(2,1)S(1)}, bf16[112,2048]{1,0:T(8,128)(2,1)S(1)}, u32[]{:S(2)}, u32[]{:S(2)}) collective-permute-start(bf16[112,2048]{1,0:T(8,128)(2,1)S(1)} %broadcast_select_fusion.9), channel_id=1, source_target_pairs={{4,0},{12,8},{20,16},{28,24},{0,4},{8,12},{16,20},{24,28},{5,1},{1... | collective-permute-start | bytes 1376264 | tf_op jit(solution)/shard_map/ppermute | solution.py:11
  74.6 15.7 %collective-permute-start.12 = (f32[896,256]{0,1:T(8,128)S(1)}, f32[896,256]{0,1:T(8,128)S(1)}, u32[]{:S(2)}, u32[]{:S(2)}) collective-permute-start(f32[896,256]{0,1:T(8,128)S(1)} %maximum_select_fusion), channel_id=1, source_target_pairs={{0,1},{1,0},{2,3},{3,2},{4,5},{5,4},{6,7},{7,6},{8,9},{9,8},{10,11... | collective-permute-start | bytes 2752520 | tf_op jit(solution)/shard_map/ppermute | solution.py:96
  90.4 20.3 %collective-permute-start.18 = (bf16[224,2048]{1,0:T(8,128)(2,1)S(1)}, bf16[224,2048]{1,0:T(8,128)(2,1)S(1)}, u32[]{:S(2)}, u32[]{:S(2)}) collective-permute-start(bf16[224,2048]{1,0:T(8,128)(2,1)S(1)} %pad_maximum_fusion.3), channel_id=1, source_target_pairs={{8,0},{12,4},{16,8},{20,12},{24,16},{28,20},{9,1},{13,5},{17,9},{2... | collective-permute-start | bytes 2752520 | tf_op jit(solution)/shard_map/ppermute | solution.py:11
  92.0 11.0 %collective-permute-start.17 = (f32[896,128]{0,1:T(8,128)S(1)}, f32[896,128]{0,1:T(8,128)S(1)}, u32[]{:S(2)}, u32[]{:S(2)}) collective-permute-start(f32[896,128]{0,1:T(8,128)S(1)} %select_add_fusion), channel_id=1, source_target_pairs={{0,2},{1,3},{2,0},{3,1},{4,6},{5,7},{6,4},{7,5},{8,10},{9,11},{10,... | collective-permute-start | bytes 1376264 | tf_op jit(solution)/shard_map/ppermute | solution.py:109
  94.4 8.5 %collective-permute-start.16 = (bf16[112,2048]{1,0:T(8,128)(2,1)S(1)}, bf16[112,2048]{1,0:T(8,128)(2,1)S(1)}, u32[]{:S(2)}, u32[]{:S(2)}) collective-permute-start(bf16[112,2048]{1,0:T(8,128)(2,1)S(1)} %broadcast_select_fusion.7), channel_id=1, source_target_pairs={{4,0},{12,8},{20,16},{28,24},{0,4},{8,12},{16,20},{24,28},{5,1},{1... | collective-permute-start | bytes 1376264 | tf_op jit(solution)/shard_map/ppermute | solution.py:11
  98.0 12.8 %collective-permute-start.15 = (f32[896,224]{0,1:T(8,128)S(1)}, f32[896,224]{0,1:T(8,128)S(1)}, u32[]{:S(2)}, u32[]{:S(2)}) collective-permute-start(f32[896,224]{0,1:T(8,128)S(1)} %maximum_select_fusion.1), channel_id=1, source_target_pairs={{0,1},{1,0},{2,3},{3,2},{4,5},{5,4},{6,7},{7,6},{8,9},{9,8},{10,11... | collective-permute-start | bytes 2408456 | tf_op jit(solution)/shard_map/ppermute | solution.py:96
  110.9 20.5 %collective-permute-start.22 = (bf16[224,2048]{1,0:T(8,128)(2,1)S(1)}, bf16[224,2048]{1,0:T(8,128)(2,1)S(1)}, u32[]{:S(2)}, u32[]{:S(2)}) collective-permute-start(bf16[224,2048]{1,0:T(8,128)(2,1)S(1)} %pad_maximum_fusion.4), channel_id=1, source_target_pairs={{8,0},{12,4},{16,8},{20,12},{24,16},{28,20},{9,1},{13,5},{17,9},{2... | collective-permute-start | bytes 2752520 | tf_op jit(solution)/shard_map/ppermute | solution.py:11
  115.1 8.5 %collective-permute-start.20 = (bf16[112,2048]{1,0:T(8,128)(2,1)S(1)}, bf16[112,2048]{1,0:T(8,128)(2,1)S(1)}, u32[]{:S(2)}, u32[]{:S(2)}) collective-permute-start(bf16[112,2048]{1,0:T(8,128)(2,1)S(1)} %broadcast_select_fusion.5), channel_id=1, source_target_pairs={{4,0},{12,8},{20,16},{28,24},{0,4},{8,12},{16,20},{24,28},{5,1},{1... | collective-permute-start | bytes 1376264 | tf_op jit(solution)/shard_map/ppermute | solution.py:11
  118.7 12.7 %collective-permute-start.19 = (f32[896,224]{0,1:T(8,128)S(1)}, f32[896,224]{0,1:T(8,128)S(1)}, u32[]{:S(2)}, u32[]{:S(2)}) collective-permute-start(f32[896,224]{0,1:T(8,128)S(1)} %maximum_select_fusion.2), channel_id=1, source_target_pairs={{0,1},{1,0},{2,3},{3,2},{4,5},{5,4},{6,7},{7,6},{8,9},{9,8},{10,11... | collective-permute-start | bytes 2408456 | tf_op jit(solution)/shard_map/ppermute | solution.py:96
  131.5 19.4 %collective-permute-start.26 = (bf16[224,2048]{1,0:T(8,128)(2,1)S(1)}, bf16[224,2048]{1,0:T(8,128)(2,1)S(1)}, u32[]{:S(2)}, u32[]{:S(2)}) collective-permute-start(bf16[224,2048]{1,0:T(8,128)(2,1)S(1)} %pad_maximum_fusion.5), channel_id=1, source_target_pairs={{8,0},{12,4},{16,8},{20,12},{24,16},{28,20},{9,1},{13,5},{17,9},{2... | collective-permute-start | bytes 2752520 | tf_op jit(solution)/shard_map/ppermute | solution.py:11
  135.4 8.5 %collective-permute-start.24 = (bf16[112,2048]{1,0:T(8,128)(2,1)S(1)}, bf16[112,2048]{1,0:T(8,128)(2,1)S(1)}, u32[]{:S(2)}, u32[]{:S(2)}) collective-permute-start(bf16[112,2048]{1,0:T(8,128)(2,1)S(1)} %broadcast_select_fusion.3), channel_id=1, source_target_pairs={{4,0},{12,8},{20,16},{28,24},{0,4},{8,12},{16,20},{24,28},{5,1},{1... | collective-permute-start | bytes 1376264 | tf_op jit(solution)/shard_map/ppermute | solution.py:11
  139.0 12.0 %collective-permute-start.23 = (f32[896,224]{0,1:T(8,128)S(1)}, f32[896,224]{0,1:T(8,128)S(1)}, u32[]{:S(2)}, u32[]{:S(2)}) collective-permute-start(f32[896,224]{0,1:T(8,128)S(1)} %maximum_select_fusion.3), channel_id=1, source_target_pairs={{0,1},{1,0},{2,3},{3,2},{4,5},{5,4},{6,7},{7,6},{8,9},{9,8},{10,11... | collective-permute-start | bytes 2408456 | tf_op jit(solution)/shard_map/ppermute | solution.py:96
  151.1 20.0 %collective-permute-start.31 = (bf16[208,2048]{1,0:T(8,128)(2,1)S(1)}, bf16[208,2048]{1,0:T(8,128)(2,1)S(1)}, u32[]{:S(2)}, u32[]{:S(2)}) collective-permute-start(bf16[208,2048]{1,0:T(8,128)(2,1)S(1)} %pad_maximum_fusion.6), channel_id=1, source_target_pairs={{8,0},{12,4},{16,8},{20,12},{24,16},{28,20},{9,1},{13,5},{17,9},{2... | collective-permute-start | bytes 2555912 | tf_op jit(solution)/shard_map/ppermute | solution.py:11
  154.7 13.6 %collective-permute-start.27 = (f32[896,224]{0,1:T(8,128)S(1)}, f32[896,224]{0,1:T(8,128)S(1)}, u32[]{:S(2)}, u32[]{:S(2)}) collective-permute-start(f32[896,224]{0,1:T(8,128)S(1)} %maximum_select_fusion.4), channel_id=1, source_target_pairs={{0,1},{1,0},{2,3},{3,2},{4,5},{5,4},{6,7},{7,6},{8,9},{9,8},{10,11... | collective-permute-start | bytes 2408456 | tf_op jit(solution)/shard_map/ppermute | solution.py:96
  154.9 13.2 %collective-permute-start.29 = (f32[896,112]{0,1:T(8,128)S(1)}, f32[896,112]{0,1:T(8,128)S(1)}, u32[]{:S(2)}, u32[]{:S(2)}) collective-permute-start(f32[896,112]{0,1:T(8,128)S(1)} %select_add_fusion.4), channel_id=1, source_target_pairs={{0,2},{1,3},{2,0},{3,1},{4,6},{5,7},{6,4},{7,5},{8,10},{9,11},{10,... | collective-permute-start | bytes 1204232 | tf_op jit(solution)/shard_map/ppermute | solution.py:109
  158.3 12.7 %collective-permute-start.28 = (bf16[112,2048]{1,0:T(8,128)(2,1)S(1)}, bf16[112,2048]{1,0:T(8,128)(2,1)S(1)}, u32[]{:S(2)}, u32[]{:S(2)}) collective-permute-start(bf16[112,2048]{1,0:T(8,128)(2,1)S(1)} %pad_select_fusion.1), channel_id=1, source_target_pairs={{4,0},{12,8},{20,16},{28,24},{0,4},{8,12},{16,20},{24,28},{5,1},{1... | collective-permute-start | bytes 1376264 | tf_op jit(solution)/shard_map/ppermute | solution.py:11
  168.4 11.2 %collective-permute-start.30 = (f32[896,112]{0,1:T(8,128)S(1)}, f32[896,112]{0,1:T(8,128)S(1)}, u32[]{:S(2)}, u32[]{:S(2)}) collective-permute-start(f32[896,112]{0,1:T(8,128)S(1)} %select_add_fusion.3), channel_id=1, source_target_pairs={{0,2},{1,3},{2,0},{3,1},{4,6},{5,7},{6,4},{7,5},{8,10},{9,11},{10,... | collective-permute-start | bytes 1204232 | tf_op jit(solution)/shard_map/ppermute | solution.py:109
  182.2 18.7 %collective-permute-start.33 = (bf16[96,2048]{1,0:T(8,128)(2,1)S(1)}, bf16[96,2048]{1,0:T(8,128)(2,1)S(1)}, u32[]{:S(2)}, u32[]{:S(2)}) collective-permute-start(bf16[96,2048]{1,0:T(8,128)(2,1)S(1)} %slice.364), channel_id=1, source_target_pairs={{4,0},{12,8},{20,16},{28,24},{0,4},{8,12},{16,20},{24,28},{5,1},{1... | collective-permute-start | bytes 1179656 | tf_op jit(solution)/shard_map/ppermute | solution.py:11
  183.5 18.6 %collective-permute-start.36 = (bf16[96,2048]{1,0:T(8,128)(2,1)S(1)}, bf16[96,2048]{1,0:T(8,128)(2,1)S(1)}, u32[]{:S(2)}, u32[]{:S(2)}) collective-permute-start(bf16[96,2048]{1,0:T(8,128)(2,1)S(1)} %slice.364), channel_id=1, source_target_pairs={{4,0},{8,4},{12,8},{16,12},{20,16},{24,20},{28,24},{5,1},{9,5},{13... | collective-permute-start | bytes 1179656 | tf_op jit(solution)/shard_map/ppermute | solution.py:11
  184.8 22.6 %collective-permute-start.35 = (bf16[112,2048]{1,0:T(8,128)(2,1)S(1)}, bf16[112,2048]{1,0:T(8,128)(2,1)S(1)}, u32[]{:S(2)}, u32[]{:S(2)}) collective-permute-start(bf16[112,2048]{1,0:T(8,128)(2,1)S(1)} %broadcast_select_fusion.1), channel_id=1, source_target_pairs={{8,0},{12,4},{16,8},{20,12},{24,16},{28,20},{9,1},{13,5},{17,9},{2... | collective-permute-start | bytes 1376264 | tf_op jit(solution)/shard_map/ppermute | solution.py:11
  186.5 14.5 %collective-permute-start.34 = (f32[896,112]{0,1:T(8,128)S(1)}, f32[896,112]{0,1:T(8,128)S(1)}, u32[]{:S(2)}, u32[]{:S(2)}) collective-permute-start(f32[896,112]{0,1:T(8,128)S(1)} %select_add_fusion.2), channel_id=1, source_target_pairs={{0,2},{1,3},{2,0},{3,1},{4,6},{5,7},{6,4},{7,5},{8,10},{9,11},{10,... | collective-permute-start | bytes 1204232 | tf_op jit(solution)/shard_map/ppermute | solution.py:109
  212.5 11.0 %collective-permute-start.40 = (f32[896,96]{0,1:T(8,128)S(1)}, f32[896,96]{0,1:T(8,128)S(1)}, u32[]{:S(2)}, u32[]{:S(2)}) collective-permute-start(f32[896,96]{0,1:T(8,128)S(1)} %select_add_fusion.7), channel_id=1, source_target_pairs={{0,2},{1,3},{2,0},{3,1},{4,6},{5,7},{6,4},{7,5},{8,10},{9,11},{10,... | collective-permute-start | bytes 1032200 | tf_op jit(solution)/shard_map/ppermute | solution.py:109
  214.5 16.7 %collective-permute-start.39 = (f32[896,112]{0,1:T(8,128)S(1)}, f32[896,112]{0,1:T(8,128)S(1)}, u32[]{:S(2)}, u32[]{:S(2)}) collective-permute-start(f32[896,112]{0,1:T(8,128)S(1)} %select_add_fusion.1), channel_id=1, source_target_pairs={{0,2},{1,3},{2,0},{3,1},{4,6},{5,7},{6,4},{7,5},{8,10},{9,11},{10,... | collective-permute-start | bytes 1204232 | tf_op jit(solution)/shard_map/ppermute | solution.py:109
  (26 other events, 271.2 us)

commit v14 on v12

--- a/solution.py
+++ b/solution.py
@@ -107,7 +107,7 @@
         mine = jnp.where(low, got[:, :size], got[:, size:])
         onward = jnp.where(low, got[:, size:], got[:, :size])
         last = lax.ppermute(pick(c, 2, 3, 0, 1) + onward, "samp", across)
-        state["results"][c] = pick(c, 0, 1, 2, 3) + mine + last
+        state["results"][c] = (pick(c, 0, 1, 2, 3) + mine + last) / total
 
     ready = [c + 3 for c in range(CHUNKS - 1)] + [CHUNKS + 1]
     for t in range(CHUNKS + 2):
@@ -144,8 +144,7 @@
         state = {k: list(v) for k, v in jax.tree.unflatten(tree, flat).items()}
         if t + 1 < CHUNKS:
             pieces[t + 1] = following
-    summed = jnp.concatenate(state["results"][:CHUNKS], axis=1)
-    return summed / total
+    return jnp.concatenate(state["results"][:CHUNKS], axis=1)
 
 
 def solution(mesh):

time: 223 us -> 223 us (level)
    concatenate x1 -> x2, local copies, waits for them, and re-layouts: 0.03 us -> 2.99 us  [local(): return jnp.concatenate(state['results'][:CHUNKS], axis=1)]
    div x1 -> x0, local copies, waits for them, and re-layouts: 2.97 us -> none  [local(): return summed / total]
where the time goes in v14:
time: 223 us; the launch traced here: 222 us
  waiting for transfers between devices  129 us (58%)
  starting transfers between devices  47.7 us (21%)
  other arithmetic  18.6 us (8%)
  matrix products  16.8 us (8%)
  local copies, waits for them, and re-layouts  9.46 us (4%)
    ppermute x19, waiting for transfers between devices, moved(): return lax.ppermute(value, 'snp', pairs)  99.2 us
    ppermute x8, waiting for transfers between devices, second_level(): last = lax.ppermute(pick(c, 2, 3, 0, 1) + onward, 'samp', across)  26.8 us
    ppermute x19, starting transfers between devices, moved(): return lax.ppermute(value, 'snp', pairs)  22.7 us
    ppermute x8, starting transfers between devices, second_level(): last = lax.ppermute(pick(c, 2, 3, 0, 1) + onward, 'samp', across)  18.8 us
    dot_general x8, matrix products, finish(): jnp.einsum('ab,cb->ac', own_block, blocks, preferred_element_type=jnp.flo...  16.8 us
    ppermute x6, starting transfers between devices, standard_rows(): lax.ppermute(moments, 'samp', [(j, j ^ i) for j in range(groups)])  5.12 us
    reduce_sum x2, other arithmetic, local_moments(): return (jnp.sum(values, axis=1), jnp.sum(values * values, axis=1))  5.07 us
    convert_element_type x2, other arithmetic, standardize(): ((values - mean[:, None]) * lax.rsqrt(variance + 1e-05)[:, None]).astype(...  4.84 us
  transfers between devices with their start and end apart: 41, of which 25 were waited for; matrix products, arithmetic and copies ran while one was open for 13% of the time, Pallas kernels for 0%

profile of v14, /device:TPU:0, one launch (start us, length us, event | category | flops | bytes accessed | tf_op | source)
XLA Modules:
  0.0 222.3 jit_solution(16352670802007579537)
XLA Ops:
  0.0 3.7 %slice_reduce_fusion = (f32[768]{0:T(1024)S(1)}, f32[768]{0:T(1024)S(1)}) fusion(f32[896,2048]{1,0:T(8,128)} %param.1), kind=kLoop, calls=%fused_computation.2 | loop fusion | flops 4717056 | bytes 6297600 | tf_op jit(solution)/shard_map/reduce_sum | solution.py:21
  3.7 2.4 %collective-permute-start.3 = (f32[2,768]{1,0:T(2,128)S(1)}, f32[2,768]{1,0:T(2,128)S(1)}, u32[]{:S(2)}, u32[]{:S(2)}) collective-permute-start(f32[2,768]{1,0:T(2,128)S(1)} %pad_maximum_fusion.7), channel_id=1, source_target_pairs={{0,3},{1,2},{2,1},{3,0},{4,7},{5,6},{6,5},{7,4},{8,11},{9,10},{10,... | collective-permute-start | bytes 18440 | tf_op jit(solution)/shard_map/ppermute | solution.py:55
  17.7 3.4 %multiply_convert_fusion = bf16[768,2048]{1,0:T(8,128)(2,1)S(1)} fusion(f32[896,2048]{1,0:T(8,128)} %param.1, f32[768]{0:T(1024)S(1)} %add_rsqrt_fusion, f32[768]{0:T(1024)S(1)} %get-tuple-element.229), kind=kLoop, calls=%fused_computation | loop fusion | flops 4718592 | bytes 9443328 | tf_op jit(solution)/shard_map/convert_element_type | solution.py:17
  22.5 5.1 %collective-permute-done.6 = bf16[128,2048]{1,0:T(8,128)(2,1)S(1)} collective-permute-done((bf16[128,2048]{1,0:T(8,128)(2,1)S(1)}, bf16[128,2048]{1,0:T(8,128)(2,1)S(1)}, u32[]{:S(2)}, u32[]{:S(2)}) %collective-permute-start.6) | collective-permute-done | bytes 524320 | tf_op jit(solution)/shard_map/ppermute | solution.py:11
  27.5 3.1 %collective-permute-done.7 = bf16[128,2048]{1,0:T(8,128)(2,1)S(1)} collective-permute-done((bf16[128,2048]{1,0:T(8,128)(2,1)S(1)}, bf16[128,2048]{1,0:T(8,128)(2,1)S(1)}, u32[]{:S(2)}, u32[]{:S(2)}) %collective-permute-start.7) | collective-permute-done | bytes 524320 | tf_op jit(solution)/shard_map/ppermute | solution.py:11
  32.7 9.8 %collective-permute-done.8 = bf16[128,2048]{1,0:T(8,128)(2,1)S(1)} collective-permute-done((bf16[128,2048]{1,0:T(8,128)(2,1)S(1)}, bf16[128,2048]{1,0:T(8,128)(2,1)S(1)}, u32[]{:S(2)}, u32[]{:S(2)}) %collective-permute-start.8) | collective-permute-done | bytes 524320 | tf_op jit(solution)/shard_map/ppermute | solution.py:11
  48.0 8.9 %collective-permute-done.10 = bf16[112,2048]{1,0:T(8,128)(2,1)} collective-permute-done((bf16[112,2048]{1,0:T(8,128)(2,1)}, bf16[112,2048]{1,0:T(8,128)(2,1)}, u32[]{:S(2)}, u32[]{:S(2)}) %collective-permute-start.10) | collective-permute-done | bytes 458784 | tf_op jit(solution)/shard_map/ppermute | solution.py:11
  57.9 9.9 %collective-permute-done.11 = bf16[240,2048]{1,0:T(8,128)(2,1)} collective-permute-done((bf16[240,2048]{1,0:T(8,128)(2,1)}, bf16[240,2048]{1,0:T(8,128)(2,1)}, u32[]{:S(2)}, u32[]{:S(2)}) %collective-permute-start.11) | collective-permute-done | bytes 983072 | tf_op jit(solution)/shard_map/ppermute | solution.py:11
  71.9 2.4 %fusion = f32[896,512]{0,1:T(8,128)S(1)} fusion(bf16[128,2048]{1,0:T(8,128)(2,1)S(1)} %slice.326, bf16[128,2048]{1,0:T(8,128)(2,1)S(1)} %copy-done.12, bf16[128,2048]{1,0:T(8,128)(2,1)S(1)} %copy-done.7, bf16[128,2048]{1,0:T(8,128)(2,1)S(1)} %copy-done.14, bf16[768,2048]{1,0:T(8,128)(2,1)S(1)} %multiply_convert_fusion), kind=kOutput, calls=%fused_computation.4 | convolution fusion | flops 1894776832 | bytes 7077888 | tf_op jit(solution)/shard_map/ab,cb->ac/dot_general | solution.py:90
  74.6 5.3 %collective-permute-done.13 = bf16[112,2048]{1,0:T(8,128)(2,1)S(1)} collective-permute-done((bf16[112,2048]{1,0:T(8,128)(2,1)S(1)}, bf16[112,2048]{1,0:T(8,128)(2,1)S(1)}, u32[]{:S(2)}, u32[]{:S(2)}) %collective-permute-start.13) | collective-permute-done | bytes 458784 | tf_op jit(solution)/shard_map/ppermute | solution.py:11
  81.0 9.2 %collective-permute-done.14 = bf16[224,2048]{1,0:T(8,128)(2,1)S(1)} collective-permute-done((bf16[224,2048]{1,0:T(8,128)(2,1)S(1)}, bf16[224,2048]{1,0:T(8,128)(2,1)S(1)}, u32[]{:S(2)}, u32[]{:S(2)}) %collective-permute-start.14) | collective-permute-done | bytes 917536 | tf_op jit(solution)/shard_map/ppermute | solution.py:11
  92.0 2.3 %collective-permute-start.17 = (f32[896,128]{0,1:T(8,128)S(1)}, f32[896,128]{0,1:T(8,128)S(1)}, u32[]{:S(2)}, u32[]{:S(2)}) collective-permute-start(f32[896,128]{0,1:T(8,128)S(1)} %select_add_fusion), channel_id=1, source_target_pairs={{0,2},{1,3},{2,0},{3,1},{4,6},{5,7},{6,4},{7,5},{8,10},{9,11},{10,... | collective-permute-start | bytes 1376264 | tf_op jit(solution)/shard_map/ppermute | solution.py:109
  95.7 2.1 fusion.8
  98.1 4.8 %collective-permute-done.16 = bf16[112,2048]{1,0:T(8,128)(2,1)S(1)} collective-permute-done((bf16[112,2048]{1,0:T(8,128)(2,1)S(1)}, bf16[112,2048]{1,0:T(8,128)(2,1)S(1)}, u32[]{:S(2)}, u32[]{:S(2)}) %collective-permute-start.16) | collective-permute-done | bytes 458784 | tf_op jit(solution)/shard_map/ppermute | solution.py:11
  103.2 7.5 %collective-permute-done.18 = bf16[224,2048]{1,0:T(8,128)(2,1)S(1)} collective-permute-done((bf16[224,2048]{1,0:T(8,128)(2,1)S(1)}, bf16[224,2048]{1,0:T(8,128)(2,1)S(1)}, u32[]{:S(2)}, u32[]{:S(2)}) %collective-permute-start.18) | collective-permute-done | bytes 917536 | tf_op jit(solution)/shard_map/ppermute | solution.py:11
  112.7 2.3 %collective-permute-start.21 = (f32[896,112]{0,1:T(8,128)S(1)}, f32[896,112]{0,1:T(8,128)S(1)}, u32[]{:S(2)}, u32[]{:S(2)}) collective-permute-start(f32[896,112]{0,1:T(8,128)S(1)} %select_add_fusion.6), channel_id=1, source_target_pairs={{0,2},{1,3},{2,0},{3,1},{4,6},{5,7},{6,4},{7,5},{8,10},{9,11},{10,... | collective-permute-start | bytes 1204232 | tf_op jit(solution)/shard_map/ppermute | solution.py:109
  121.0 2.6 %collective-permute-done.20 = bf16[112,2048]{1,0:T(8,128)(2,1)S(1)} collective-permute-done((bf16[112,2048]{1,0:T(8,128)(2,1)S(1)}, bf16[112,2048]{1,0:T(8,128)(2,1)S(1)}, u32[]{:S(2)}, u32[]{:S(2)}) %collective-permute-start.20) | collective-permute-done | bytes 458784 | tf_op jit(solution)/shard_map/ppermute | solution.py:11
  123.7 7.7 %collective-permute-done.22 = bf16[224,2048]{1,0:T(8,128)(2,1)S(1)} collective-permute-done((bf16[224,2048]{1,0:T(8,128)(2,1)S(1)}, bf16[224,2048]{1,0:T(8,128)(2,1)S(1)}, u32[]{:S(2)}, u32[]{:S(2)}) %collective-permute-start.22) | collective-permute-done | bytes 917536 | tf_op jit(solution)/shard_map/ppermute | solution.py:11
  133.0 2.3 %collective-permute-start.25 = (f32[896,112]{0,1:T(8,128)S(1)}, f32[896,112]{0,1:T(8,128)S(1)}, u32[]{:S(2)}, u32[]{:S(2)}) collective-permute-start(f32[896,112]{0,1:T(8,128)S(1)} %select_add_fusion.5), channel_id=1, source_target_pairs={{0,2},{1,3},{2,0},{3,1},{4,6},{5,7},{6,4},{7,5},{8,10},{9,11},{10,... | collective-permute-start | bytes 1204232 | tf_op jit(solution)/shard_map/ppermute | solution.py:109
  141.4 2.6 %collective-permute-done.24 = bf16[112,2048]{1,0:T(8,128)(2,1)S(1)} collective-permute-done((bf16[112,2048]{1,0:T(8,128)(2,1)S(1)}, bf16[112,2048]{1,0:T(8,128)(2,1)S(1)}, u32[]{:S(2)}, u32[]{:S(2)}) %collective-permute-start.24) | collective-permute-done | bytes 458784 | tf_op jit(solution)/shard_map/ppermute | solution.py:11
  144.0 7.0 %collective-permute-done.26 = bf16[224,2048]{1,0:T(8,128)(2,1)S(1)} collective-permute-done((bf16[224,2048]{1,0:T(8,128)(2,1)S(1)}, bf16[224,2048]{1,0:T(8,128)(2,1)S(1)}, u32[]{:S(2)}, u32[]{:S(2)}) %collective-permute-start.26) | collective-permute-done | bytes 917536 | tf_op jit(solution)/shard_map/ppermute | solution.py:11
  152.6 3.3 %collective-permute-start.29 = (f32[896,112]{0,1:T(8,128)S(1)}, f32[896,112]{0,1:T(8,128)S(1)}, u32[]{:S(2)}, u32[]{:S(2)}) collective-permute-start(f32[896,112]{0,1:T(8,128)S(1)} %select_add_fusion.4), channel_id=1, source_target_pairs={{0,2},{1,3},{2,0},{3,1},{4,6},{5,7},{6,4},{7,5},{8,10},{9,11},{10,... | collective-permute-start | bytes 1204232 | tf_op jit(solution)/shard_map/ppermute | solution.py:109
  161.9 2.6 %collective-permute-done.28 = bf16[112,2048]{1,0:T(8,128)(2,1)S(1)} collective-permute-done((bf16[112,2048]{1,0:T(8,128)(2,1)S(1)}, bf16[112,2048]{1,0:T(8,128)(2,1)S(1)}, u32[]{:S(2)}, u32[]{:S(2)}) %collective-permute-start.28) | collective-permute-done | bytes 458784 | tf_op jit(solution)/shard_map/ppermute | solution.py:11
  164.6 2.7 %collective-permute-done.30 = bf16[208,2048]{1,0:T(8,128)(2,1)S(1)} collective-permute-done((bf16[208,2048]{1,0:T(8,128)(2,1)S(1)}, bf16[208,2048]{1,0:T(8,128)(2,1)S(1)}, u32[]{:S(2)}, u32[]{:S(2)}) %collective-permute-start.30) | collective-permute-done | bytes 852000 | tf_op jit(solution)/shard_map/ppermute | solution.py:11
  171.7 3.9 %collective-permute-start.33 = (f32[896,112]{0,1:T(8,128)S(1)}, f32[896,112]{0,1:T(8,128)S(1)}, u32[]{:S(2)}, u32[]{:S(2)}) collective-permute-start(f32[896,112]{0,1:T(8,128)S(1)} %select_add_fusion.3), channel_id=1, source_target_pairs={{0,2},{1,3},{2,0},{3,1},{4,6},{5,7},{6,4},{7,5},{8,10},{9,11},{10,... | collective-permute-start | bytes 1204232 | tf_op jit(solution)/shard_map/ppermute | solution.py:109
  177.2 10.3 %collective-permute-done.32 = bf16[96,2048]{1,0:T(8,128)(2,1)S(1)} collective-permute-done((bf16[96,2048]{1,0:T(8,128)(2,1)S(1)}, bf16[96,2048]{1,0:T(8,128)(2,1)S(1)}, u32[]{:S(2)}, u32[]{:S(2)}) %collective-permute-start.32) | collective-permute-done | bytes 393248 | tf_op jit(solution)/shard_map/ppermute | solution.py:11
  187.9 5.9 %collective-permute-done.34 = f32[896,112]{0,1:T(8,128)S(1)} collective-permute-done((f32[896,112]{0,1:T(8,128)S(1)}, f32[896,112]{0,1:T(8,128)S(1)}, u32[]{:S(2)}, u32[]{:S(2)}) %collective-permute-start.34) | collective-permute-done | bytes 401440 | tf_op jit(solution)/shard_map/ppermute | solution.py:109
  196.3 2.1 fusion.48
  199.3 2.7 %collective-permute-start.40 = (f32[896,96]{0,1:T(8,128)S(1)}, f32[896,96]{0,1:T(8,128)S(1)}, u32[]{:S(2)}, u32[]{:S(2)}) collective-permute-start(f32[896,96]{0,1:T(8,128)S(1)} %select_add_fusion.7), channel_id=1, source_target_pairs={{0,2},{1,3},{2,0},{3,1},{4,6},{5,7},{6,4},{7,5},{8,10},{9,11},{10,... | collective-permute-start | bytes 1032200 | tf_op jit(solution)/shard_map/ppermute | solution.py:109
  204.0 6.9 %collective-permute-done.40 = f32[896,96]{0,1:T(8,128)S(1)} collective-permute-done((f32[896,96]{0,1:T(8,128)S(1)}, f32[896,96]{0,1:T(8,128)S(1)}, u32[]{:S(2)}, u32[]{:S(2)}) %collective-permute-start.40) | collective-permute-done | bytes 344096 | tf_op jit(solution)/shard_map/ppermute | solution.py:109
  211.1 7.8 %collective-permute-done.39 = f32[896,112]{0,1:T(8,128)S(1)} collective-permute-done((f32[896,112]{0,1:T(8,128)S(1)}, f32[896,112]{0,1:T(8,128)S(1)}, u32[]{:S(2)}, u32[]{:S(2)}) %collective-permute-start.39) | collective-permute-done | bytes 401440 | tf_op jit(solution)/shard_map/ppermute | solution.py:109
  219.4 3.0 %copy.2 = f32[896,896]{1,0:T(8,128)} copy(f32[896,896]{0,1:T(8,128)S(1)} %constant_dynamic-update-slice_fusion) | data formatting | bytes 6422528 | tf_op jit(solution)/shard_map/concatenate | solution.py:147
  (178 shorter events, 66.0 us)
Async XLA Ops:
  3.7 13.9 %collective-permute-start.3 = (f32[2,768]{1,0:T(2,128)S(1)}, f32[2,768]{1,0:T(2,128)S(1)}, u32[]{:S(2)}, u32[]{:S(2)}) collective-permute-start(f32[2,768]{1,0:T(2,128)S(1)} %pad_maximum_fusion.7), channel_id=1, source_target_pairs={{0,3},{1,2},{2,1},{3,0},{4,7},{5,6},{6,5},{7,4},{8,11},{9,10},{10,... | collective-permute-start | bytes 18440 | tf_op jit(solution)/shard_map/ppermute | solution.py:55
  6.2 11.5 %collective-permute-start.4 = (f32[2,768]{1,0:T(2,128)S(1)}, f32[2,768]{1,0:T(2,128)S(1)}, u32[]{:S(2)}, u32[]{:S(2)}) collective-permute-start(f32[2,768]{1,0:T(2,128)S(1)} %pad_maximum_fusion.7), channel_id=1, source_target_pairs={{0,2},{1,3},{2,0},{3,1},{4,6},{5,7},{6,4},{7,5},{8,10},{9,11},{10,... | collective-permute-start | bytes 18440 | tf_op jit(solution)/shard_map/ppermute | solution.py:55
  14.7 12.8 %collective-permute-start.6 = (bf16[128,2048]{1,0:T(8,128)(2,1)S(1)}, bf16[128,2048]{1,0:T(8,128)(2,1)S(1)}, u32[]{:S(2)}, u32[]{:S(2)}) collective-permute-start(bf16[128,2048]{1,0:T(8,128)(2,1)S(1)} %multiply_convert_fusion.1), channel_id=1, source_target_pairs={{4,0},{12,8},{20,16},{28,24},{0,4},{8,12},{16,20},{24,28},{5,1},{1... | collective-permute-start | bytes 1572872 | tf_op jit(solution)/shard_map/ppermute | solution.py:11
  16.3 14.4 %collective-permute-start.7 = (bf16[128,2048]{1,0:T(8,128)(2,1)S(1)}, bf16[128,2048]{1,0:T(8,128)(2,1)S(1)}, u32[]{:S(2)}, u32[]{:S(2)}) collective-permute-start(bf16[128,2048]{1,0:T(8,128)(2,1)S(1)} %multiply_convert_fusion.1), channel_id=1, source_target_pairs={{8,0},{12,4},{16,8},{20,12},{24,16},{28,20},{9,1},{13,5},{17,9},{2... | collective-permute-start | bytes 1572872 | tf_op jit(solution)/shard_map/ppermute | solution.py:11
  30.8 11.6 %collective-permute-start.8 = (bf16[128,2048]{1,0:T(8,128)(2,1)S(1)}, bf16[128,2048]{1,0:T(8,128)(2,1)S(1)}, u32[]{:S(2)}, u32[]{:S(2)}) collective-permute-start(bf16[128,2048]{1,0:T(8,128)(2,1)S(1)} %pad_select_fusion), channel_id=1, source_target_pairs={{4,0},{12,8},{20,16},{28,24},{0,4},{8,12},{16,20},{24,28},{5,1},{1... | collective-permute-start | bytes 1572872 | tf_op jit(solution)/shard_map/ppermute | solution.py:11
  31.4 11.9 %collective-permute-start.9 = (bf16[112,2048]{1,0:T(8,128)(2,1)S(1)}, bf16[112,2048]{1,0:T(8,128)(2,1)S(1)}, u32[]{:S(2)}, u32[]{:S(2)}) collective-permute-start(bf16[112,2048]{1,0:T(8,128)(2,1)S(1)} %get-tuple-element.117), channel_id=1, source_target_pairs={{8,0},{12,4},{16,8},{20,12},{24,16},{28,20},{9,1},{13,5},{17,9},{2... | collective-permute-start | bytes 1376264 | tf_op jit(solution)/shard_map/ppermute | solution.py:11
  45.1 22.7 %collective-permute-start.11 = (bf16[240,2048]{1,0:T(8,128)(2,1)}, bf16[240,2048]{1,0:T(8,128)(2,1)}, u32[]{:S(2)}, u32[]{:S(2)}) collective-permute-start(bf16[240,2048]{1,0:T(8,128)(2,1)} %pad_maximum_fusion.1), channel_id=1, source_target_pairs={{8,0},{12,4},{16,8},{20,12},{24,16},{28,20},{9,1},{13,5},{17,9},{2... | collective-permute-start | bytes 2949128 | tf_op jit(solution)/shard_map/ppermute | solution.py:11
  47.2 9.6 %collective-permute-start.10 = (bf16[112,2048]{1,0:T(8,128)(2,1)}, bf16[112,2048]{1,0:T(8,128)(2,1)}, u32[]{:S(2)}, u32[]{:S(2)}) collective-permute-start(bf16[112,2048]{1,0:T(8,128)(2,1)} %broadcast_select_fusion.10), channel_id=1, source_target_pairs={{4,0},{12,8},{20,16},{28,24},{0,4},{8,12},{16,20},{24,28},{5,1},{1... | collective-permute-start | bytes 1376264 | tf_op jit(solution)/shard_map/ppermute | solution.py:11
  70.0 20.2 %collective-permute-start.14 = (bf16[224,2048]{1,0:T(8,128)(2,1)S(1)}, bf16[224,2048]{1,0:T(8,128)(2,1)S(1)}, u32[]{:S(2)}, u32[]{:S(2)}) collective-permute-start(bf16[224,2048]{1,0:T(8,128)(2,1)S(1)} %pad_maximum_fusion.2), channel_id=1, source_target_pairs={{8,0},{12,4},{16,8},{20,12},{24,16},{28,20},{9,1},{13,5},{17,9},{2... | collective-permute-start | bytes 2752520 | tf_op jit(solution)/shard_map/ppermute | solution.py:11
  71.3 8.5 %collective-permute-start.13 = (bf16[112,2048]{1,0:T(8,128)(2,1)S(1)}, bf16[112,2048]{1,0:T(8,128)(2,1)S(1)}, u32[]{:S(2)}, u32[]{:S(2)}) collective-permute-start(bf16[112,2048]{1,0:T(8,128)(2,1)S(1)} %broadcast_select_fusion.9), channel_id=1, source_target_pairs={{4,0},{12,8},{20,16},{28,24},{0,4},{8,12},{16,20},{24,28},{5,1},{1... | collective-permute-start | bytes 1376264 | tf_op jit(solution)/shard_map/ppermute | solution.py:11
  74.6 15.7 %collective-permute-start.12 = (f32[896,256]{0,1:T(8,128)S(1)}, f32[896,256]{0,1:T(8,128)S(1)}, u32[]{:S(2)}, u32[]{:S(2)}) collective-permute-start(f32[896,256]{0,1:T(8,128)S(1)} %maximum_select_fusion), channel_id=1, source_target_pairs={{0,1},{1,0},{2,3},{3,2},{4,5},{5,4},{6,7},{7,6},{8,9},{9,8},{10,11... | collective-permute-start | bytes 2752520 | tf_op jit(solution)/shard_map/ppermute | solution.py:96
  90.4 20.3 %collective-permute-start.18 = (bf16[224,2048]{1,0:T(8,128)(2,1)S(1)}, bf16[224,2048]{1,0:T(8,128)(2,1)S(1)}, u32[]{:S(2)}, u32[]{:S(2)}) collective-permute-start(bf16[224,2048]{1,0:T(8,128)(2,1)S(1)} %pad_maximum_fusion.3), channel_id=1, source_target_pairs={{8,0},{12,4},{16,8},{20,12},{24,16},{28,20},{9,1},{13,5},{17,9},{2... | collective-permute-start | bytes 2752520 | tf_op jit(solution)/shard_map/ppermute | solution.py:11
  92.0 11.0 %collective-permute-start.17 = (f32[896,128]{0,1:T(8,128)S(1)}, f32[896,128]{0,1:T(8,128)S(1)}, u32[]{:S(2)}, u32[]{:S(2)}) collective-permute-start(f32[896,128]{0,1:T(8,128)S(1)} %select_add_fusion), channel_id=1, source_target_pairs={{0,2},{1,3},{2,0},{3,1},{4,6},{5,7},{6,4},{7,5},{8,10},{9,11},{10,... | collective-permute-start | bytes 1376264 | tf_op jit(solution)/shard_map/ppermute | solution.py:109
  94.4 8.5 %collective-permute-start.16 = (bf16[112,2048]{1,0:T(8,128)(2,1)S(1)}, bf16[112,2048]{1,0:T(8,128)(2,1)S(1)}, u32[]{:S(2)}, u32[]{:S(2)}) collective-permute-start(bf16[112,2048]{1,0:T(8,128)(2,1)S(1)} %broadcast_select_fusion.7), channel_id=1, source_target_pairs={{4,0},{12,8},{20,16},{28,24},{0,4},{8,12},{16,20},{24,28},{5,1},{1... | collective-permute-start | bytes 1376264 | tf_op jit(solution)/shard_map/ppermute | solution.py:11
  98.0 12.8 %collective-permute-start.15 = (f32[896,224]{0,1:T(8,128)S(1)}, f32[896,224]{0,1:T(8,128)S(1)}, u32[]{:S(2)}, u32[]{:S(2)}) collective-permute-start(f32[896,224]{0,1:T(8,128)S(1)} %maximum_select_fusion.1), channel_id=1, source_target_pairs={{0,1},{1,0},{2,3},{3,2},{4,5},{5,4},{6,7},{7,6},{8,9},{9,8},{10,11... | collective-permute-start | bytes 2408456 | tf_op jit(solution)/shard_map/ppermute | solution.py:96
  110.9 20.5 %collective-permute-start.22 = (bf16[224,2048]{1,0:T(8,128)(2,1)S(1)}, bf16[224,2048]{1,0:T(8,128)(2,1)S(1)}, u32[]{:S(2)}, u32[]{:S(2)}) collective-permute-start(bf16[224,2048]{1,0:T(8,128)(2,1)S(1)} %pad_maximum_fusion.4), channel_id=1, source_target_pairs={{8,0},{12,4},{16,8},{20,12},{24,16},{28,20},{9,1},{13,5},{17,9},{2... | collective-permute-start | bytes 2752520 | tf_op jit(solution)/shard_map/ppermute | solution.py:11
  112.7 8.2 %collective-permute-start.21 = (f32[896,112]{0,1:T(8,128)S(1)}, f32[896,112]{0,1:T(8,128)S(1)}, u32[]{:S(2)}, u32[]{:S(2)}) collective-permute-start(f32[896,112]{0,1:T(8,128)S(1)} %select_add_fusion.6), channel_id=1, source_target_pairs={{0,2},{1,3},{2,0},{3,1},{4,6},{5,7},{6,4},{7,5},{8,10},{9,11},{10,... | collective-permute-start | bytes 1204232 | tf_op jit(solution)/shard_map/ppermute | solution.py:109
  115.1 8.5 %collective-permute-start.20 = (bf16[112,2048]{1,0:T(8,128)(2,1)S(1)}, bf16[112,2048]{1,0:T(8,128)(2,1)S(1)}, u32[]{:S(2)}, u32[]{:S(2)}) collective-permute-start(bf16[112,2048]{1,0:T(8,128)(2,1)S(1)} %broadcast_select_fusion.5), channel_id=1, source_target_pairs={{4,0},{12,8},{20,16},{28,24},{0,4},{8,12},{16,20},{24,28},{5,1},{1... | collective-permute-start | bytes 1376264 | tf_op jit(solution)/shard_map/ppermute | solution.py:11
  118.7 12.7 %collective-permute-start.19 = (f32[896,224]{0,1:T(8,128)S(1)}, f32[896,224]{0,1:T(8,128)S(1)}, u32[]{:S(2)}, u32[]{:S(2)}) collective-permute-start(f32[896,224]{0,1:T(8,128)S(1)} %maximum_select_fusion.2), channel_id=1, source_target_pairs={{0,1},{1,0},{2,3},{3,2},{4,5},{5,4},{6,7},{7,6},{8,9},{9,8},{10,11... | collective-permute-start | bytes 2408456 | tf_op jit(solution)/shard_map/ppermute | solution.py:96
  131.5 19.4 %collective-permute-start.26 = (bf16[224,2048]{1,0:T(8,128)(2,1)S(1)}, bf16[224,2048]{1,0:T(8,128)(2,1)S(1)}, u32[]{:S(2)}, u32[]{:S(2)}) collective-permute-start(bf16[224,2048]{1,0:T(8,128)(2,1)S(1)} %pad_maximum_fusion.5), channel_id=1, source_target_pairs={{8,0},{12,4},{16,8},{20,12},{24,16},{28,20},{9,1},{13,5},{17,9},{2... | collective-permute-start | bytes 2752520 | tf_op jit(solution)/shard_map/ppermute | solution.py:11
  135.4 8.5 %collective-permute-start.24 = (bf16[112,2048]{1,0:T(8,128)(2,1)S(1)}, bf16[112,2048]{1,0:T(8,128)(2,1)S(1)}, u32[]{:S(2)}, u32[]{:S(2)}) collective-permute-start(bf16[112,2048]{1,0:T(8,128)(2,1)S(1)} %broadcast_select_fusion.3), channel_id=1, source_target_pairs={{4,0},{12,8},{20,16},{28,24},{0,4},{8,12},{16,20},{24,28},{5,1},{1... | collective-permute-start | bytes 1376264 | tf_op jit(solution)/shard_map/ppermute | solution.py:11
  139.0 12.0 %collective-permute-start.23 = (f32[896,224]{0,1:T(8,128)S(1)}, f32[896,224]{0,1:T(8,128)S(1)}, u32[]{:S(2)}, u32[]{:S(2)}) collective-permute-start(f32[896,224]{0,1:T(8,128)S(1)} %maximum_select_fusion.3), channel_id=1, source_target_pairs={{0,1},{1,0},{2,3},{3,2},{4,5},{5,4},{6,7},{7,6},{8,9},{9,8},{10,11... | collective-permute-start | bytes 2408456 | tf_op jit(solution)/shard_map/ppermute | solution.py:96
  151.1 16.2 %collective-permute-start.30 = (bf16[208,2048]{1,0:T(8,128)(2,1)S(1)}, bf16[208,2048]{1,0:T(8,128)(2,1)S(1)}, u32[]{:S(2)}, u32[]{:S(2)}) collective-permute-start(bf16[208,2048]{1,0:T(8,128)(2,1)S(1)} %pad_maximum_fusion.6), channel_id=1, source_target_pairs={{8,0},{12,4},{16,8},{20,12},{24,16},{28,20},{9,1},{13,5},{17,9},{2... | collective-permute-start | bytes 2555912 | tf_op jit(solution)/shard_map/ppermute | solution.py:11
  152.6 9.1 %collective-permute-start.29 = (f32[896,112]{0,1:T(8,128)S(1)}, f32[896,112]{0,1:T(8,128)S(1)}, u32[]{:S(2)}, u32[]{:S(2)}) collective-permute-start(f32[896,112]{0,1:T(8,128)S(1)} %select_add_fusion.4), channel_id=1, source_target_pairs={{0,2},{1,3},{2,0},{3,1},{4,6},{5,7},{6,4},{7,5},{8,10},{9,11},{10,... | collective-permute-start | bytes 1204232 | tf_op jit(solution)/shard_map/ppermute | solution.py:109
  156.0 8.5 %collective-permute-start.28 = (bf16[112,2048]{1,0:T(8,128)(2,1)S(1)}, bf16[112,2048]{1,0:T(8,128)(2,1)S(1)}, u32[]{:S(2)}, u32[]{:S(2)}) collective-permute-start(bf16[112,2048]{1,0:T(8,128)(2,1)S(1)} %pad_select_fusion.1), channel_id=1, source_target_pairs={{4,0},{12,8},{20,16},{28,24},{0,4},{8,12},{16,20},{24,28},{5,1},{1... | collective-permute-start | bytes 1376264 | tf_op jit(solution)/shard_map/ppermute | solution.py:11
  169.7 17.9 %collective-permute-start.32 = (bf16[96,2048]{1,0:T(8,128)(2,1)S(1)}, bf16[96,2048]{1,0:T(8,128)(2,1)S(1)}, u32[]{:S(2)}, u32[]{:S(2)}) collective-permute-start(bf16[96,2048]{1,0:T(8,128)(2,1)S(1)} %slice.362), channel_id=1, source_target_pairs={{4,0},{12,8},{20,16},{28,24},{0,4},{8,12},{16,20},{24,28},{5,1},{1... | collective-permute-start | bytes 1179656 | tf_op jit(solution)/shard_map/ppermute | solution.py:11
  170.2 23.7 %collective-permute-start.36 = (bf16[96,2048]{1,0:T(8,128)(2,1)S(1)}, bf16[96,2048]{1,0:T(8,128)(2,1)S(1)}, u32[]{:S(2)}, u32[]{:S(2)}) collective-permute-start(bf16[96,2048]{1,0:T(8,128)(2,1)S(1)} %slice.362), channel_id=1, source_target_pairs={{4,0},{8,4},{12,8},{16,12},{20,16},{24,20},{28,24},{5,1},{9,5},{13... | collective-permute-start | bytes 1179656 | tf_op jit(solution)/shard_map/ppermute | solution.py:11
  171.7 16.0 %collective-permute-start.33 = (f32[896,112]{0,1:T(8,128)S(1)}, f32[896,112]{0,1:T(8,128)S(1)}, u32[]{:S(2)}, u32[]{:S(2)}) collective-permute-start(f32[896,112]{0,1:T(8,128)S(1)} %select_add_fusion.3), channel_id=1, source_target_pairs={{0,2},{1,3},{2,0},{3,1},{4,6},{5,7},{6,4},{7,5},{8,10},{9,11},{10,... | collective-permute-start | bytes 1204232 | tf_op jit(solution)/shard_map/ppermute | solution.py:109
  175.5 18.7 %collective-permute-start.35 = (bf16[112,2048]{1,0:T(8,128)(2,1)S(1)}, bf16[112,2048]{1,0:T(8,128)(2,1)S(1)}, u32[]{:S(2)}, u32[]{:S(2)}) collective-permute-start(bf16[112,2048]{1,0:T(8,128)(2,1)S(1)} %broadcast_select_fusion.1), channel_id=1, source_target_pairs={{8,0},{12,4},{16,8},{20,12},{24,16},{28,20},{9,1},{13,5},{17,9},{2... | collective-permute-start | bytes 1376264 | tf_op jit(solution)/shard_map/ppermute | solution.py:11
  177.2 16.6 %collective-permute-start.34 = (f32[896,112]{0,1:T(8,128)S(1)}, f32[896,112]{0,1:T(8,128)S(1)}, u32[]{:S(2)}, u32[]{:S(2)}) collective-permute-start(f32[896,112]{0,1:T(8,128)S(1)} %select_add_fusion.2), channel_id=1, source_target_pairs={{0,2},{1,3},{2,0},{3,1},{4,6},{5,7},{6,4},{7,5},{8,10},{9,11},{10,... | collective-permute-start | bytes 1204232 | tf_op jit(solution)/shard_map/ppermute | solution.py:109
  199.3 11.6 %collective-permute-start.40 = (f32[896,96]{0,1:T(8,128)S(1)}, f32[896,96]{0,1:T(8,128)S(1)}, u32[]{:S(2)}, u32[]{:S(2)}) collective-permute-start(f32[896,96]{0,1:T(8,128)S(1)} %select_add_fusion.7), channel_id=1, source_target_pairs={{0,2},{1,3},{2,0},{3,1},{4,6},{5,7},{6,4},{7,5},{8,10},{9,11},{10,... | collective-permute-start | bytes 1032200 | tf_op jit(solution)/shard_map/ppermute | solution.py:109
  202.2 16.7 %collective-permute-start.39 = (f32[896,112]{0,1:T(8,128)S(1)}, f32[896,112]{0,1:T(8,128)S(1)}, u32[]{:S(2)}, u32[]{:S(2)}) collective-permute-start(f32[896,112]{0,1:T(8,128)S(1)} %select_add_fusion.1), channel_id=1, source_target_pairs={{0,2},{1,3},{2,0},{3,1},{4,6},{5,7},{6,4},{7,5},{8,10},{9,11},{10,... | collective-permute-start | bytes 1204232 | tf_op jit(solution)/shard_map/ppermute | solution.py:109
  (26 other events, 274.8 us)

commit v15 on v14

--- a/solution.py
+++ b/solution.py
@@ -94,7 +94,7 @@
         payload = jnp.where(even_me, jnp.concatenate([tiles[1], tiles[3]], axis=1),
                             jnp.concatenate([tiles[0], tiles[2]], axis=1))
         state["first"][c] = lax.ppermute(payload, "samp", partner)
-        if c >= CHUNKS - 3:
+        if c >= CHUNKS - 2:
             second_level(c)
 
     def pick(c, a, b, d, e):
@@ -109,11 +109,11 @@
         last = lax.ppermute(pick(c, 2, 3, 0, 1) + onward, "samp", across)
         state["results"][c] = (pick(c, 0, 1, 2, 3) + mine + last) / total
 
-    ready = [c + 3 for c in range(CHUNKS - 1)] + [CHUNKS + 1]
+    ready = [c + 3 for c in range(CHUNKS - 2)] + [CHUNKS, CHUNKS + 1]
     for t in range(CHUNKS + 2):
         new = t if t < CHUNKS else None
         second = t - 1 if 0 <= t - 1 < CHUNKS else None
-        third = t - 2 if 0 <= t - 2 < CHUNKS - 1 else None
+        third = t - 2 if 0 <= t - 2 < CHUNKS - 2 else None
         if new is not None or third is not None:
             sent = moved(joined([pieces[new] if new is not None else None,
                                  state["one"][third] if third is not None else None]), z_down)
@@ -132,11 +132,11 @@
         if second is not None:
             size = sizes[second]
             state["one"][second] = jnp.where(even_snp, state["swapped"][second][:size], state["swapped"][t][:size])
-        if second == CHUNKS - 1:
+        if second is not None and second >= CHUNKS - 2:
             state["three"][second] = moved(state["two"][second], one_down)
         for c in [c for c in range(CHUNKS) if ready[c] == t]:
             finish(c)
-        if 0 <= t - 4 < CHUNKS - 3:
+        if 0 <= t - 4 < CHUNKS - 2:
             second_level(t - 4)
         flat, tree = jax.tree.flatten(state)
         following = pieces[t + 1] if t + 1 < CHUNKS else own_block[:8]

time: 223 us -> 230 us (1.031)
  waiting for transfers between devices: 129 us -> 134 us
    ppermute x19, starting transfers between devices: 22.7 us -> 26.4 us  [moved(): return lax.ppermute(value, 'snp', pairs)]
    ppermute x8, waiting for transfers between devices: 26.8 us -> 29.7 us  [second_level(): last = lax.ppermute(pick(c, 2, 3, 0, 1) + onward, 'samp', across)]
  transfers between devices with their start and end apart: 41 -> 41, of which waited for: 25 -> 27; matrix products, arithmetic and copies ran while one was open for 13% -> 13% of each run, Pallas kernels for 0% -> 0%
where the time goes in v15:
time: 230 us; the launch traced here: 229 us
  waiting for transfers between devices  134 us (58%)
  starting transfers between devices  49.4 us (21%)
  other arithmetic  18.7 us (8%)
  matrix products  16.8 us (7%)
  local copies, waits for them, and re-layouts  9.44 us (4%)
    ppermute x19, waiting for transfers between devices, moved(): return lax.ppermute(value, 'snp', pairs)  101 us
    ppermute x8, waiting for transfers between devices, second_level(): last = lax.ppermute(pick(c, 2, 3, 0, 1) + onward, 'samp', across)  29.7 us
    ppermute x19, starting transfers between devices, moved(): return lax.ppermute(value, 'snp', pairs)  26.4 us
    ppermute x8, starting transfers between devices, second_level(): last = lax.ppermute(pick(c, 2, 3, 0, 1) + onward, 'samp', across)  17.2 us
    dot_general x8, matrix products, finish(): jnp.einsum('ab,cb->ac', own_block, blocks, preferred_element_type=jnp.flo...  16.8 us
    ppermute x6, starting transfers between devices, standard_rows(): lax.ppermute(moments, 'samp', [(j, j ^ i) for j in range(groups)])  5.12 us
    reduce_sum x2, other arithmetic, local_moments(): return (jnp.sum(values, axis=1), jnp.sum(values * values, axis=1))  5.07 us
    convert_element_type x2, other arithmetic, standardize(): ((values - mean[:, None]) * lax.rsqrt(variance + 1e-05)[:, None]).astype(...  4.84 us
  transfers between devices with their start and end apart: 41, of which 27 were waited for; matrix products, arithmetic and copies ran while one was open for 13% of the time, Pallas kernels for 0%

profile of v15, /device:TPU:0, one launch (start us, length us, event | category | flops | bytes accessed | tf_op | source)
XLA Modules:
  0.0 229.1 jit_solution(9705932461824671720)
XLA Ops:
  0.0 3.7 %slice_reduce_fusion = (f32[768]{0:T(1024)S(1)}, f32[768]{0:T(1024)S(1)}) fusion(f32[896,2048]{1,0:T(8,128)} %param.1), kind=kLoop, calls=%fused_computation.2 | loop fusion | flops 4717056 | bytes 6297600 | tf_op jit(solution)/shard_map/reduce_sum | solution.py:21
  3.7 2.4 %collective-permute-start.3 = (f32[2,768]{1,0:T(2,128)S(1)}, f32[2,768]{1,0:T(2,128)S(1)}, u32[]{:S(2)}, u32[]{:S(2)}) collective-permute-start(f32[2,768]{1,0:T(2,128)S(1)} %pad_maximum_fusion.7), channel_id=1, source_target_pairs={{0,3},{1,2},{2,1},{3,0},{4,7},{5,6},{6,5},{7,4},{8,11},{9,10},{10,... | collective-permute-start | bytes 18440 | tf_op jit(solution)/shard_map/ppermute | solution.py:55
  17.7 3.4 %multiply_convert_fusion = bf16[768,2048]{1,0:T(8,128)(2,1)S(1)} fusion(f32[896,2048]{1,0:T(8,128)} %param.1, f32[768]{0:T(1024)S(1)} %add_rsqrt_fusion, f32[768]{0:T(1024)S(1)} %get-tuple-element.235), kind=kLoop, calls=%fused_computation | loop fusion | flops 4718592 | bytes 9443328 | tf_op jit(solution)/shard_map/convert_element_type | solution.py:17
  22.5 5.1 %collective-permute-done.6 = bf16[128,2048]{1,0:T(8,128)(2,1)S(1)} collective-permute-done((bf16[128,2048]{1,0:T(8,128)(2,1)S(1)}, bf16[128,2048]{1,0:T(8,128)(2,1)S(1)}, u32[]{:S(2)}, u32[]{:S(2)}) %collective-permute-start.6) | collective-permute-done | bytes 524320 | tf_op jit(solution)/shard_map/ppermute | solution.py:11
  27.5 3.1 %collective-permute-done.7 = bf16[128,2048]{1,0:T(8,128)(2,1)S(1)} collective-permute-done((bf16[128,2048]{1,0:T(8,128)(2,1)S(1)}, bf16[128,2048]{1,0:T(8,128)(2,1)S(1)}, u32[]{:S(2)}, u32[]{:S(2)}) %collective-permute-start.7) | collective-permute-done | bytes 524320 | tf_op jit(solution)/shard_map/ppermute | solution.py:11
  32.7 9.8 %collective-permute-done.8 = bf16[128,2048]{1,0:T(8,128)(2,1)S(1)} collective-permute-done((bf16[128,2048]{1,0:T(8,128)(2,1)S(1)}, bf16[128,2048]{1,0:T(8,128)(2,1)S(1)}, u32[]{:S(2)}, u32[]{:S(2)}) %collective-permute-start.8) | collective-permute-done | bytes 524320 | tf_op jit(solution)/shard_map/ppermute | solution.py:11
  48.0 8.8 %collective-permute-done.10 = bf16[112,2048]{1,0:T(8,128)(2,1)} collective-permute-done((bf16[112,2048]{1,0:T(8,128)(2,1)}, bf16[112,2048]{1,0:T(8,128)(2,1)}, u32[]{:S(2)}, u32[]{:S(2)}) %collective-permute-start.10) | collective-permute-done | bytes 458784 | tf_op jit(solution)/shard_map/ppermute | solution.py:11
  57.9 9.9 %collective-permute-done.11 = bf16[240,2048]{1,0:T(8,128)(2,1)} collective-permute-done((bf16[240,2048]{1,0:T(8,128)(2,1)}, bf16[240,2048]{1,0:T(8,128)(2,1)}, u32[]{:S(2)}, u32[]{:S(2)}) %collective-permute-start.11) | collective-permute-done | bytes 983072 | tf_op jit(solution)/shard_map/ppermute | solution.py:11
  71.9 2.4 %fusion = f32[896,512]{0,1:T(8,128)S(1)} fusion(bf16[128,2048]{1,0:T(8,128)(2,1)S(1)} %slice.326, bf16[128,2048]{1,0:T(8,128)(2,1)S(1)} %copy-done.13, bf16[128,2048]{1,0:T(8,128)(2,1)S(1)} %copy-done.7, bf16[128,2048]{1,0:T(8,128)(2,1)S(1)} %copy-done.15, bf16[768,2048]{1,0:T(8,128)(2,1)S(1)} %multiply_convert_fusion), kind=kOutput, calls=%fused_computation.4 | convolution fusion | flops 1894776832 | bytes 7077888 | tf_op jit(solution)/shard_map/ab,cb->ac/dot_general | solution.py:90
  74.6 5.3 %collective-permute-done.13 = bf16[112,2048]{1,0:T(8,128)(2,1)S(1)} collective-permute-done((bf16[112,2048]{1,0:T(8,128)(2,1)S(1)}, bf16[112,2048]{1,0:T(8,128)(2,1)S(1)}, u32[]{:S(2)}, u32[]{:S(2)}) %collective-permute-start.13) | collective-permute-done | bytes 458784 | tf_op jit(solution)/shard_map/ppermute | solution.py:11
  81.0 9.2 %collective-permute-done.14 = bf16[224,2048]{1,0:T(8,128)(2,1)S(1)} collective-permute-done((bf16[224,2048]{1,0:T(8,128)(2,1)S(1)}, bf16[224,2048]{1,0:T(8,128)(2,1)S(1)}, u32[]{:S(2)}, u32[]{:S(2)}) %collective-permute-start.14) | collective-permute-done | bytes 917536 | tf_op jit(solution)/shard_map/ppermute | solution.py:11
  92.0 2.3 %collective-permute-start.17 = (f32[896,128]{0,1:T(8,128)S(1)}, f32[896,128]{0,1:T(8,128)S(1)}, u32[]{:S(2)}, u32[]{:S(2)}) collective-permute-start(f32[896,128]{0,1:T(8,128)S(1)} %select_add_fusion), channel_id=1, source_target_pairs={{0,2},{1,3},{2,0},{3,1},{4,6},{5,7},{6,4},{7,5},{8,10},{9,11},{10,... | collective-permute-start | bytes 1376264 | tf_op jit(solution)/shard_map/ppermute | solution.py:109
  98.1 4.8 %collective-permute-done.16 = bf16[112,2048]{1,0:T(8,128)(2,1)S(1)} collective-permute-done((bf16[112,2048]{1,0:T(8,128)(2,1)S(1)}, bf16[112,2048]{1,0:T(8,128)(2,1)S(1)}, u32[]{:S(2)}, u32[]{:S(2)}) %collective-permute-start.16) | collective-permute-done | bytes 458784 | tf_op jit(solution)/shard_map/ppermute | solution.py:11
  103.2 7.5 %collective-permute-done.18 = bf16[224,2048]{1,0:T(8,128)(2,1)S(1)} collective-permute-done((bf16[224,2048]{1,0:T(8,128)(2,1)S(1)}, bf16[224,2048]{1,0:T(8,128)(2,1)S(1)}, u32[]{:S(2)}, u32[]{:S(2)}) %collective-permute-start.18) | collective-permute-done | bytes 917536 | tf_op jit(solution)/shard_map/ppermute | solution.py:11
  112.7 2.3 %collective-permute-start.21 = (f32[896,112]{0,1:T(8,128)S(1)}, f32[896,112]{0,1:T(8,128)S(1)}, u32[]{:S(2)}, u32[]{:S(2)}) collective-permute-start(f32[896,112]{0,1:T(8,128)S(1)} %select_add_fusion.6), channel_id=1, source_target_pairs={{0,2},{1,3},{2,0},{3,1},{4,6},{5,7},{6,4},{7,5},{8,10},{9,11},{10,... | collective-permute-start | bytes 1204232 | tf_op jit(solution)/shard_map/ppermute | solution.py:109
  121.0 2.6 %collective-permute-done.20 = bf16[112,2048]{1,0:T(8,128)(2,1)S(1)} collective-permute-done((bf16[112,2048]{1,0:T(8,128)(2,1)S(1)}, bf16[112,2048]{1,0:T(8,128)(2,1)S(1)}, u32[]{:S(2)}, u32[]{:S(2)}) %collective-permute-start.20) | collective-permute-done | bytes 458784 | tf_op jit(solution)/shard_map/ppermute | solution.py:11
  123.7 7.7 %collective-permute-done.22 = bf16[224,2048]{1,0:T(8,128)(2,1)S(1)} collective-permute-done((bf16[224,2048]{1,0:T(8,128)(2,1)S(1)}, bf16[224,2048]{1,0:T(8,128)(2,1)S(1)}, u32[]{:S(2)}, u32[]{:S(2)}) %collective-permute-start.22) | collective-permute-done | bytes 917536 | tf_op jit(solution)/shard_map/ppermute | solution.py:11
  133.0 2.3 %collective-permute-start.25 = (f32[896,112]{0,1:T(8,128)S(1)}, f32[896,112]{0,1:T(8,128)S(1)}, u32[]{:S(2)}, u32[]{:S(2)}) collective-permute-start(f32[896,112]{0,1:T(8,128)S(1)} %select_add_fusion.5), channel_id=1, source_target_pairs={{0,2},{1,3},{2,0},{3,1},{4,6},{5,7},{6,4},{7,5},{8,10},{9,11},{10,... | collective-permute-start | bytes 1204232 | tf_op jit(solution)/shard_map/ppermute | solution.py:109
  141.4 2.6 %collective-permute-done.24 = bf16[112,2048]{1,0:T(8,128)(2,1)S(1)} collective-permute-done((bf16[112,2048]{1,0:T(8,128)(2,1)S(1)}, bf16[112,2048]{1,0:T(8,128)(2,1)S(1)}, u32[]{:S(2)}, u32[]{:S(2)}) %collective-permute-start.24) | collective-permute-done | bytes 458784 | tf_op jit(solution)/shard_map/ppermute | solution.py:11
  144.0 7.0 %collective-permute-done.26 = bf16[224,2048]{1,0:T(8,128)(2,1)S(1)} collective-permute-done((bf16[224,2048]{1,0:T(8,128)(2,1)S(1)}, bf16[224,2048]{1,0:T(8,128)(2,1)S(1)}, u32[]{:S(2)}, u32[]{:S(2)}) %collective-permute-start.26) | collective-permute-done | bytes 917536 | tf_op jit(solution)/shard_map/ppermute | solution.py:11
  152.6 3.3 %collective-permute-start.29 = (f32[896,112]{0,1:T(8,128)S(1)}, f32[896,112]{0,1:T(8,128)S(1)}, u32[]{:S(2)}, u32[]{:S(2)}) collective-permute-start(f32[896,112]{0,1:T(8,128)S(1)} %select_add_fusion.4), channel_id=1, source_target_pairs={{0,2},{1,3},{2,0},{3,1},{4,6},{5,7},{6,4},{7,5},{8,10},{9,11},{10,... | collective-permute-start | bytes 1204232 | tf_op jit(solution)/shard_map/ppermute | solution.py:109
  161.9 2.6 %collective-permute-done.28 = bf16[112,2048]{1,0:T(8,128)(2,1)S(1)} collective-permute-done((bf16[112,2048]{1,0:T(8,128)(2,1)S(1)}, bf16[112,2048]{1,0:T(8,128)(2,1)S(1)}, u32[]{:S(2)}, u32[]{:S(2)}) %collective-permute-start.28) | collective-permute-done | bytes 458784 | tf_op jit(solution)/shard_map/ppermute | solution.py:11
  164.6 4.3 %collective-permute-done.30 = bf16[208,2048]{1,0:T(8,128)(2,1)S(1)} collective-permute-done((bf16[208,2048]{1,0:T(8,128)(2,1)S(1)}, bf16[208,2048]{1,0:T(8,128)(2,1)S(1)}, u32[]{:S(2)}, u32[]{:S(2)}) %collective-permute-start.30) | collective-permute-done | bytes 852000 | tf_op jit(solution)/shard_map/ppermute | solution.py:11
  168.9 5.5 %collective-permute-done.31 = bf16[112,2048]{1,0:T(8,128)(2,1)S(1)} collective-permute-done((bf16[112,2048]{1,0:T(8,128)(2,1)S(1)}, bf16[112,2048]{1,0:T(8,128)(2,1)S(1)}, u32[]{:S(2)}, u32[]{:S(2)}) %collective-permute-start.31) | collective-permute-done | bytes 458784 | tf_op jit(solution)/shard_map/ppermute | solution.py:11
  174.5 4.1 %collective-permute-start.34 = (bf16[96,2048]{1,0:T(8,128)(2,1)S(1)}, bf16[96,2048]{1,0:T(8,128)(2,1)S(1)}, u32[]{:S(2)}, u32[]{:S(2)}) collective-permute-start(bf16[96,2048]{1,0:T(8,128)(2,1)S(1)} %slice.362), channel_id=1, source_target_pairs={{4,0},{12,8},{20,16},{28,24},{0,4},{8,12},{16,20},{24,28},{5,1},{1... | collective-permute-start | bytes 1179656 | tf_op jit(solution)/shard_map/ppermute | solution.py:11
  180.1 2.1 fusion.48
  182.7 2.8 %collective-permute-start.35 = (f32[896,112]{0,1:T(8,128)S(1)}, f32[896,112]{0,1:T(8,128)S(1)}, u32[]{:S(2)}, u32[]{:S(2)}) collective-permute-start(f32[896,112]{0,1:T(8,128)S(1)} %select_add_fusion.3), channel_id=1, source_target_pairs={{0,2},{1,3},{2,0},{3,1},{4,6},{5,7},{6,4},{7,5},{8,10},{9,11},{10,... | collective-permute-start | bytes 1204232 | tf_op jit(solution)/shard_map/ppermute | solution.py:109
  188.7 5.3 %collective-permute-done.34 = bf16[96,2048]{1,0:T(8,128)(2,1)S(1)} collective-permute-done((bf16[96,2048]{1,0:T(8,128)(2,1)S(1)}, bf16[96,2048]{1,0:T(8,128)(2,1)S(1)}, u32[]{:S(2)}, u32[]{:S(2)}) %collective-permute-start.34) | collective-permute-done | bytes 393248 | tf_op jit(solution)/shard_map/ppermute | solution.py:11
  195.9 8.2 %collective-permute-done.36 = f32[896,112]{0,1:T(8,128)S(1)} collective-permute-done((f32[896,112]{0,1:T(8,128)S(1)}, f32[896,112]{0,1:T(8,128)S(1)}, u32[]{:S(2)}, u32[]{:S(2)}) %collective-permute-start.36) | collective-permute-done | bytes 401440 | tf_op jit(solution)/shard_map/ppermute | solution.py:109
  210.4 8.3 %collective-permute-done.39 = f32[896,112]{0,1:T(8,128)S(1)} collective-permute-done((f32[896,112]{0,1:T(8,128)S(1)}, f32[896,112]{0,1:T(8,128)S(1)}, u32[]{:S(2)}, u32[]{:S(2)}) %collective-permute-start.39) | collective-permute-done | bytes 401440 | tf_op jit(solution)/shard_map/ppermute | solution.py:109
  218.9 6.8 %collective-permute-done.40 = f32[896,96]{0,1:T(8,128)S(1)} collective-permute-done((f32[896,96]{0,1:T(8,128)S(1)}, f32[896,96]{0,1:T(8,128)S(1)}, u32[]{:S(2)}, u32[]{:S(2)}) %collective-permute-start.40) | collective-permute-done | bytes 344096 | tf_op jit(solution)/shard_map/ppermute | solution.py:109
  226.1 3.0 %copy.2 = f32[896,896]{1,0:T(8,128)} copy(f32[896,896]{0,1:T(8,128)S(1)} %constant_dynamic-update-slice_fusion) | data formatting | bytes 6422528 | tf_op jit(solution)/shard_map/concatenate | solution.py:147
  (181 shorter events, 69.8 us)
Async XLA Ops:
  3.7 13.9 %collective-permute-start.3 = (f32[2,768]{1,0:T(2,128)S(1)}, f32[2,768]{1,0:T(2,128)S(1)}, u32[]{:S(2)}, u32[]{:S(2)}) collective-permute-start(f32[2,768]{1,0:T(2,128)S(1)} %pad_maximum_fusion.7), channel_id=1, source_target_pairs={{0,3},{1,2},{2,1},{3,0},{4,7},{5,6},{6,5},{7,4},{8,11},{9,10},{10,... | collective-permute-start | bytes 18440 | tf_op jit(solution)/shard_map/ppermute | solution.py:55
  6.2 11.5 %collective-permute-start.4 = (f32[2,768]{1,0:T(2,128)S(1)}, f32[2,768]{1,0:T(2,128)S(1)}, u32[]{:S(2)}, u32[]{:S(2)}) collective-permute-start(f32[2,768]{1,0:T(2,128)S(1)} %pad_maximum_fusion.7), channel_id=1, source_target_pairs={{0,2},{1,3},{2,0},{3,1},{4,6},{5,7},{6,4},{7,5},{8,10},{9,11},{10,... | collective-permute-start | bytes 18440 | tf_op jit(solution)/shard_map/ppermute | solution.py:55
  14.7 12.8 %collective-permute-start.6 = (bf16[128,2048]{1,0:T(8,128)(2,1)S(1)}, bf16[128,2048]{1,0:T(8,128)(2,1)S(1)}, u32[]{:S(2)}, u32[]{:S(2)}) collective-permute-start(bf16[128,2048]{1,0:T(8,128)(2,1)S(1)} %multiply_convert_fusion.1), channel_id=1, source_target_pairs={{4,0},{12,8},{20,16},{28,24},{0,4},{8,12},{16,20},{24,28},{5,1},{1... | collective-permute-start | bytes 1572872 | tf_op jit(solution)/shard_map/ppermute | solution.py:11
  16.3 14.4 %collective-permute-start.7 = (bf16[128,2048]{1,0:T(8,128)(2,1)S(1)}, bf16[128,2048]{1,0:T(8,128)(2,1)S(1)}, u32[]{:S(2)}, u32[]{:S(2)}) collective-permute-start(bf16[128,2048]{1,0:T(8,128)(2,1)S(1)} %multiply_convert_fusion.1), channel_id=1, source_target_pairs={{8,0},{12,4},{16,8},{20,12},{24,16},{28,20},{9,1},{13,5},{17,9},{2... | collective-permute-start | bytes 1572872 | tf_op jit(solution)/shard_map/ppermute | solution.py:11
  30.8 11.6 %collective-permute-start.8 = (bf16[128,2048]{1,0:T(8,128)(2,1)S(1)}, bf16[128,2048]{1,0:T(8,128)(2,1)S(1)}, u32[]{:S(2)}, u32[]{:S(2)}) collective-permute-start(bf16[128,2048]{1,0:T(8,128)(2,1)S(1)} %pad_select_fusion), channel_id=1, source_target_pairs={{4,0},{12,8},{20,16},{28,24},{0,4},{8,12},{16,20},{24,28},{5,1},{1... | collective-permute-start | bytes 1572872 | tf_op jit(solution)/shard_map/ppermute | solution.py:11
  31.4 11.9 %collective-permute-start.9 = (bf16[112,2048]{1,0:T(8,128)(2,1)S(1)}, bf16[112,2048]{1,0:T(8,128)(2,1)S(1)}, u32[]{:S(2)}, u32[]{:S(2)}) collective-permute-start(bf16[112,2048]{1,0:T(8,128)(2,1)S(1)} %get-tuple-element.120), channel_id=1, source_target_pairs={{8,0},{12,4},{16,8},{20,12},{24,16},{28,20},{9,1},{13,5},{17,9},{2... | collective-permute-start | bytes 1376264 | tf_op jit(solution)/shard_map/ppermute | solution.py:11
  45.1 22.7 %collective-permute-start.11 = (bf16[240,2048]{1,0:T(8,128)(2,1)}, bf16[240,2048]{1,0:T(8,128)(2,1)}, u32[]{:S(2)}, u32[]{:S(2)}) collective-permute-start(bf16[240,2048]{1,0:T(8,128)(2,1)} %pad_maximum_fusion.1), channel_id=1, source_target_pairs={{8,0},{12,4},{16,8},{20,12},{24,16},{28,20},{9,1},{13,5},{17,9},{2... | collective-permute-start | bytes 2949128 | tf_op jit(solution)/shard_map/ppermute | solution.py:11
  47.2 9.6 %collective-permute-start.10 = (bf16[112,2048]{1,0:T(8,128)(2,1)}, bf16[112,2048]{1,0:T(8,128)(2,1)}, u32[]{:S(2)}, u32[]{:S(2)}) collective-permute-start(bf16[112,2048]{1,0:T(8,128)(2,1)} %broadcast_select_fusion.10), channel_id=1, source_target_pairs={{4,0},{12,8},{20,16},{28,24},{0,4},{8,12},{16,20},{24,28},{5,1},{1... | collective-permute-start | bytes 1376264 | tf_op jit(solution)/shard_map/ppermute | solution.py:11
  70.0 20.2 %collective-permute-start.14 = (bf16[224,2048]{1,0:T(8,128)(2,1)S(1)}, bf16[224,2048]{1,0:T(8,128)(2,1)S(1)}, u32[]{:S(2)}, u32[]{:S(2)}) collective-permute-start(bf16[224,2048]{1,0:T(8,128)(2,1)S(1)} %pad_maximum_fusion.2), channel_id=1, source_target_pairs={{8,0},{12,4},{16,8},{20,12},{24,16},{28,20},{9,1},{13,5},{17,9},{2... | collective-permute-start | bytes 2752520 | tf_op jit(solution)/shard_map/ppermute | solution.py:11
  71.4 8.5 %collective-permute-start.13 = (bf16[112,2048]{1,0:T(8,128)(2,1)S(1)}, bf16[112,2048]{1,0:T(8,128)(2,1)S(1)}, u32[]{:S(2)}, u32[]{:S(2)}) collective-permute-start(bf16[112,2048]{1,0:T(8,128)(2,1)S(1)} %broadcast_select_fusion.9), channel_id=1, source_target_pairs={{4,0},{12,8},{20,16},{28,24},{0,4},{8,12},{16,20},{24,28},{5,1},{1... | collective-permute-start | bytes 1376264 | tf_op jit(solution)/shard_map/ppermute | solution.py:11
  74.6 15.7 %collective-permute-start.12 = (f32[896,256]{0,1:T(8,128)S(1)}, f32[896,256]{0,1:T(8,128)S(1)}, u32[]{:S(2)}, u32[]{:S(2)}) collective-permute-start(f32[896,256]{0,1:T(8,128)S(1)} %maximum_select_fusion), channel_id=1, source_target_pairs={{0,1},{1,0},{2,3},{3,2},{4,5},{5,4},{6,7},{7,6},{8,9},{9,8},{10,11... | collective-permute-start | bytes 2752520 | tf_op jit(solution)/shard_map/ppermute | solution.py:96
  90.4 20.3 %collective-permute-start.18 = (bf16[224,2048]{1,0:T(8,128)(2,1)S(1)}, bf16[224,2048]{1,0:T(8,128)(2,1)S(1)}, u32[]{:S(2)}, u32[]{:S(2)}) collective-permute-start(bf16[224,2048]{1,0:T(8,128)(2,1)S(1)} %pad_maximum_fusion.3), channel_id=1, source_target_pairs={{8,0},{12,4},{16,8},{20,12},{24,16},{28,20},{9,1},{13,5},{17,9},{2... | collective-permute-start | bytes 2752520 | tf_op jit(solution)/shard_map/ppermute | solution.py:11
  92.0 11.0 %collective-permute-start.17 = (f32[896,128]{0,1:T(8,128)S(1)}, f32[896,128]{0,1:T(8,128)S(1)}, u32[]{:S(2)}, u32[]{:S(2)}) collective-permute-start(f32[896,128]{0,1:T(8,128)S(1)} %select_add_fusion), channel_id=1, source_target_pairs={{0,2},{1,3},{2,0},{3,1},{4,6},{5,7},{6,4},{7,5},{8,10},{9,11},{10,... | collective-permute-start | bytes 1376264 | tf_op jit(solution)/shard_map/ppermute | solution.py:109
  94.4 8.5 %collective-permute-start.16 = (bf16[112,2048]{1,0:T(8,128)(2,1)S(1)}, bf16[112,2048]{1,0:T(8,128)(2,1)S(1)}, u32[]{:S(2)}, u32[]{:S(2)}) collective-permute-start(bf16[112,2048]{1,0:T(8,128)(2,1)S(1)} %broadcast_select_fusion.7), channel_id=1, source_target_pairs={{4,0},{12,8},{20,16},{28,24},{0,4},{8,12},{16,20},{24,28},{5,1},{1... | collective-permute-start | bytes 1376264 | tf_op jit(solution)/shard_map/ppermute | solution.py:11
  98.0 12.8 %collective-permute-start.15 = (f32[896,224]{0,1:T(8,128)S(1)}, f32[896,224]{0,1:T(8,128)S(1)}, u32[]{:S(2)}, u32[]{:S(2)}) collective-permute-start(f32[896,224]{0,1:T(8,128)S(1)} %maximum_select_fusion.1), channel_id=1, source_target_pairs={{0,1},{1,0},{2,3},{3,2},{4,5},{5,4},{6,7},{7,6},{8,9},{9,8},{10,11... | collective-permute-start | bytes 2408456 | tf_op jit(solution)/shard_map/ppermute | solution.py:96
  110.9 20.5 %collective-permute-start.22 = (bf16[224,2048]{1,0:T(8,128)(2,1)S(1)}, bf16[224,2048]{1,0:T(8,128)(2,1)S(1)}, u32[]{:S(2)}, u32[]{:S(2)}) collective-permute-start(bf16[224,2048]{1,0:T(8,128)(2,1)S(1)} %pad_maximum_fusion.4), channel_id=1, source_target_pairs={{8,0},{12,4},{16,8},{20,12},{24,16},{28,20},{9,1},{13,5},{17,9},{2... | collective-permute-start | bytes 2752520 | tf_op jit(solution)/shard_map/ppermute | solution.py:11
  115.1 8.5 %collective-permute-start.20 = (bf16[112,2048]{1,0:T(8,128)(2,1)S(1)}, bf16[112,2048]{1,0:T(8,128)(2,1)S(1)}, u32[]{:S(2)}, u32[]{:S(2)}) collective-permute-start(bf16[112,2048]{1,0:T(8,128)(2,1)S(1)} %broadcast_select_fusion.5), channel_id=1, source_target_pairs={{4,0},{12,8},{20,16},{28,24},{0,4},{8,12},{16,20},{24,28},{5,1},{1... | collective-permute-start | bytes 1376264 | tf_op jit(solution)/shard_map/ppermute | solution.py:11
  118.7 12.7 %collective-permute-start.19 = (f32[896,224]{0,1:T(8,128)S(1)}, f32[896,224]{0,1:T(8,128)S(1)}, u32[]{:S(2)}, u32[]{:S(2)}) collective-permute-start(f32[896,224]{0,1:T(8,128)S(1)} %maximum_select_fusion.2), channel_id=1, source_target_pairs={{0,1},{1,0},{2,3},{3,2},{4,5},{5,4},{6,7},{7,6},{8,9},{9,8},{10,11... | collective-permute-start | bytes 2408456 | tf_op jit(solution)/shard_map/ppermute | solution.py:96
  131.5 19.4 %collective-permute-start.26 = (bf16[224,2048]{1,0:T(8,128)(2,1)S(1)}, bf16[224,2048]{1,0:T(8,128)(2,1)S(1)}, u32[]{:S(2)}, u32[]{:S(2)}) collective-permute-start(bf16[224,2048]{1,0:T(8,128)(2,1)S(1)} %pad_maximum_fusion.5), channel_id=1, source_target_pairs={{8,0},{12,4},{16,8},{20,12},{24,16},{28,20},{9,1},{13,5},{17,9},{2... | collective-permute-start | bytes 2752520 | tf_op jit(solution)/shard_map/ppermute | solution.py:11
  139.0 12.0 %collective-permute-start.23 = (f32[896,224]{0,1:T(8,128)S(1)}, f32[896,224]{0,1:T(8,128)S(1)}, u32[]{:S(2)}, u32[]{:S(2)}) collective-permute-start(f32[896,224]{0,1:T(8,128)S(1)} %maximum_select_fusion.3), channel_id=1, source_target_pairs={{0,1},{1,0},{2,3},{3,2},{4,5},{5,4},{6,7},{7,6},{8,9},{9,8},{10,11... | collective-permute-start | bytes 2408456 | tf_op jit(solution)/shard_map/ppermute | solution.py:96
  151.1 17.8 %collective-permute-start.30 = (bf16[208,2048]{1,0:T(8,128)(2,1)S(1)}, bf16[208,2048]{1,0:T(8,128)(2,1)S(1)}, u32[]{:S(2)}, u32[]{:S(2)}) collective-permute-start(bf16[208,2048]{1,0:T(8,128)(2,1)S(1)} %pad_maximum_fusion.6), channel_id=1, source_target_pairs={{8,0},{12,4},{16,8},{20,12},{24,16},{28,20},{9,1},{13,5},{17,9},{2... | collective-permute-start | bytes 2555912 | tf_op jit(solution)/shard_map/ppermute | solution.py:11
  152.6 9.1 %collective-permute-start.29 = (f32[896,112]{0,1:T(8,128)S(1)}, f32[896,112]{0,1:T(8,128)S(1)}, u32[]{:S(2)}, u32[]{:S(2)}) collective-permute-start(f32[896,112]{0,1:T(8,128)S(1)} %select_add_fusion.4), channel_id=1, source_target_pairs={{0,2},{1,3},{2,0},{3,1},{4,6},{5,7},{6,4},{7,5},{8,10},{9,11},{10,... | collective-permute-start | bytes 1204232 | tf_op jit(solution)/shard_map/ppermute | solution.py:109
  156.0 8.5 %collective-permute-start.28 = (bf16[112,2048]{1,0:T(8,128)(2,1)S(1)}, bf16[112,2048]{1,0:T(8,128)(2,1)S(1)}, u32[]{:S(2)}, u32[]{:S(2)}) collective-permute-start(bf16[112,2048]{1,0:T(8,128)(2,1)S(1)} %pad_select_fusion.1), channel_id=1, source_target_pairs={{4,0},{12,8},{20,16},{28,24},{0,4},{8,12},{16,20},{24,28},{5,1},{1... | collective-permute-start | bytes 1376264 | tf_op jit(solution)/shard_map/ppermute | solution.py:11
  159.6 14.9 %collective-permute-start.27 = (f32[896,224]{0,1:T(8,128)S(1)}, f32[896,224]{0,1:T(8,128)S(1)}, u32[]{:S(2)}, u32[]{:S(2)}) collective-permute-start(f32[896,224]{0,1:T(8,128)S(1)} %maximum_select_fusion.4), channel_id=1, source_target_pairs={{0,1},{1,0},{2,3},{3,2},{4,5},{5,4},{6,7},{7,6},{8,9},{9,8},{10,11... | collective-permute-start | bytes 2408456 | tf_op jit(solution)/shard_map/ppermute | solution.py:96
  159.7 14.8 %collective-permute-start.31 = (bf16[112,2048]{1,0:T(8,128)(2,1)S(1)}, bf16[112,2048]{1,0:T(8,128)(2,1)S(1)}, u32[]{:S(2)}, u32[]{:S(2)}) collective-permute-start(bf16[112,2048]{1,0:T(8,128)(2,1)S(1)} %get-tuple-element.197), channel_id=1, source_target_pairs={{4,0},{8,4},{12,8},{16,12},{20,16},{24,20},{28,24},{5,1},{9,5},{13... | collective-permute-start | bytes 1376264 | tf_op jit(solution)/shard_map/ppermute | solution.py:11
  174.5 19.5 %collective-permute-start.34 = (bf16[96,2048]{1,0:T(8,128)(2,1)S(1)}, bf16[96,2048]{1,0:T(8,128)(2,1)S(1)}, u32[]{:S(2)}, u32[]{:S(2)}) collective-permute-start(bf16[96,2048]{1,0:T(8,128)(2,1)S(1)} %slice.362), channel_id=1, source_target_pairs={{4,0},{12,8},{20,16},{28,24},{0,4},{8,12},{16,20},{24,28},{5,1},{1... | collective-permute-start | bytes 1179656 | tf_op jit(solution)/shard_map/ppermute | solution.py:11
  178.6 25.6 %collective-permute-start.37 = (bf16[96,2048]{1,0:T(8,128)(2,1)S(1)}, bf16[96,2048]{1,0:T(8,128)(2,1)S(1)}, u32[]{:S(2)}, u32[]{:S(2)}) collective-permute-start(bf16[96,2048]{1,0:T(8,128)(2,1)S(1)} %slice.362), channel_id=1, source_target_pairs={{4,0},{8,4},{12,8},{16,12},{20,16},{24,20},{28,24},{5,1},{9,5},{13... | collective-permute-start | bytes 1179656 | tf_op jit(solution)/shard_map/ppermute | solution.py:11
  182.7 13.0 %collective-permute-start.35 = (f32[896,112]{0,1:T(8,128)S(1)}, f32[896,112]{0,1:T(8,128)S(1)}, u32[]{:S(2)}, u32[]{:S(2)}) collective-permute-start(f32[896,112]{0,1:T(8,128)S(1)} %select_add_fusion.3), channel_id=1, source_target_pairs={{0,2},{1,3},{2,0},{3,1},{4,6},{5,7},{6,4},{7,5},{8,10},{9,11},{10,... | collective-permute-start | bytes 1204232 | tf_op jit(solution)/shard_map/ppermute | solution.py:109
  187.8 16.4 %collective-permute-start.32 = (f32[896,224]{0,1:T(8,128)S(1)}, f32[896,224]{0,1:T(8,128)S(1)}, u32[]{:S(2)}, u32[]{:S(2)}) collective-permute-start(f32[896,224]{0,1:T(8,128)S(1)} %maximum_select_fusion.5), channel_id=1, source_target_pairs={{0,1},{1,0},{2,3},{3,2},{4,5},{5,4},{6,7},{7,6},{8,9},{9,8},{10,11... | collective-permute-start | bytes 2408456 | tf_op jit(solution)/shard_map/ppermute | solution.py:96
  188.2 15.8 %collective-permute-start.36 = (f32[896,112]{0,1:T(8,128)S(1)}, f32[896,112]{0,1:T(8,128)S(1)}, u32[]{:S(2)}, u32[]{:S(2)}) collective-permute-start(f32[896,112]{0,1:T(8,128)S(1)} %select_add_fusion.2), channel_id=1, source_target_pairs={{0,2},{1,3},{2,0},{3,1},{4,6},{5,7},{6,4},{7,5},{8,10},{9,11},{10,... | collective-permute-start | bytes 1204232 | tf_op jit(solution)/shard_map/ppermute | solution.py:109
  206.5 12.1 %collective-permute-start.39 = (f32[896,112]{0,1:T(8,128)S(1)}, f32[896,112]{0,1:T(8,128)S(1)}, u32[]{:S(2)}, u32[]{:S(2)}) collective-permute-start(f32[896,112]{0,1:T(8,128)S(1)} %select_add_fusion.1), channel_id=1, source_target_pairs={{0,2},{1,3},{2,0},{3,1},{4,6},{5,7},{6,4},{7,5},{8,10},{9,11},{10,... | collective-permute-start | bytes 1204232 | tf_op jit(solution)/shard_map/ppermute | solution.py:109
  208.6 17.0 %collective-permute-start.40 = (f32[896,96]{0,1:T(8,128)S(1)}, f32[896,96]{0,1:T(8,128)S(1)}, u32[]{:S(2)}, u32[]{:S(2)}) collective-permute-start(f32[896,96]{0,1:T(8,128)S(1)} %select_add_fusion.7), channel_id=1, source_target_pairs={{0,2},{1,3},{2,0},{3,1},{4,6},{5,7},{6,4},{7,5},{8,10},{9,11},{10,... | collective-permute-start | bytes 1032200 | tf_op jit(solution)/shard_map/ppermute | solution.py:109
  (28 other events, 294.4 us)
